TPU v7x, 256 devices: a whole 4x4x8 slice. The times are simulated.
256 devices in a mesh: shots: 8 (over z_hi, y), slab: 32 (over z_lo, x, core).
Axes of the slice: x: 4, y: 4, z: 8 (z_hi: 2, z_lo: 4; z = z_hi * 4 + z_lo), core: 2. Of those that a mesh axis runs over, the one named last changes fastest.
Arguments:
- vel_parts: float32 [8, 128, 512, 256], P('shots', 'slab'), may hold values from -24 to 24
- den_parts: float32 [8, 128, 512, 256], P('shots', 'slab'), may hold values from -24 to 24
- illum_parts: float32 [8, 128, 512, 256], P('shots', 'slab'), may hold values from 0.02 to 0.2
- layer_index: int32 [256], replicated, may hold values from 0 to 15, never falling along the last dimension, each value on 1 to 128 neighbouring positions
- depth_scale: float32 [2, 16], replicated, may hold values from 1 to 8
Outputs:
- vel_update: float32 [128, 512, 256], P('slab')
- den_update: float32 [128, 512, 256], P('slab')
Inputs may be any that keep to these rules, and one draw needn't show every extreme that they name: `layer_index`: never falls with depth; every layer holds 1 to 128 consecutive depth cells, and one holds exactly 128.
All inputs are finite; a program needn't handle non-finite values.
Results may differ from a plain program's by a relative error of at most 0.00011.
Values sent between devices are 32-bit elements; how exact they have to be, the bound alone decides.
No kernel may reach another device: no remote copies, remote signals or barrier semaphores. Data moves between devices by JAX's collectives and lax.ppermute only.
A program may use at most 64 MiB of HBM per device.

v0:
```python
import jax
import jax.numpy as jnp
from jax import lax
from jax.sharding import PartitionSpec as P

RADIUS = 20
HP = lax.Precision.HIGHEST
RING = 4


def smoothing_matrix(count):
    cells = jnp.arange(count, dtype=jnp.int32)
    offset = (cells[:, None] - cells[None, :]).astype(jnp.float32)
    inside = jnp.abs(offset) <= RADIUS
    weights = jnp.where(inside, jnp.exp(-offset * offset / 200.0), jnp.float32(0.0))
    return weights / jnp.sum(weights, axis=1, keepdims=True)


def ring_pairs(n_shots, step):
    hi = n_shots // RING
    return [(h * RING + r, h * RING + (r + step) % RING) for h in range(hi) for r in range(RING)]


def hi_pairs(n_shots):
    hi = n_shots // RING
    return [(h * RING + r, ((h + 1) % hi) * RING + r) for h in range(hi) for r in range(RING)]


def rows(field, start, size):
    return lax.dynamic_slice_in_dim(field, start, size, axis=1)


def reduce_scatter_shots(fields, n_shots):
    idx = lax.axis_index("shots")
    r, h = idx % RING, idx // RING
    chunk = fields[0].shape[1] // RING
    half = chunk // 2
    fwd, bwd = ring_pairs(n_shots, 1), ring_pairs(n_shots, -1)

    def take(start):
        return jnp.stack([rows(f, start, half) for f in fields])

    acc_f = take(((r - 1) % RING) * chunk + h * half)
    acc_b = take(((r + 1) % RING) * chunk + (1 - h) * half)
    for t in range(1, RING):
        recv_f = lax.ppermute(acc_f, "shots", fwd)
        recv_b = lax.ppermute(acc_b, "shots", bwd)
        acc_f = recv_f + take(((r - 1 - t) % RING) * chunk + h * half)
        acc_b = recv_b + take(((r + 1 + t) % RING) * chunk + (1 - h) * half)
    return acc_f + lax.ppermute(acc_b, "shots", hi_pairs(n_shots))


def all_gather_smooth_shots(blocks, n_shots, total):
    idx = lax.axis_index("shots")
    r, h = idx % RING, idx // RING
    chunk = total // RING
    half = chunk // 2
    fwd, bwd = ring_pairs(n_shots, 1), ring_pairs(n_shots, -1)
    cur_f = blocks
    cur_b = lax.ppermute(cur_f, "shots", hi_pairs(n_shots))
    pieces = [cur_f, cur_b]
    starts = [r * chunk + h * half, r * chunk + (1 - h) * half]
    for t in range(1, RING):
        cur_f = lax.ppermute(cur_f, "shots", fwd)
        cur_b = lax.ppermute(cur_b, "shots", bwd)
        pieces += [cur_f, cur_b]
        starts += [((r - t) % RING) * chunk + h * half, ((r + t) % RING) * chunk + (1 - h) * half]
    matrix = smoothing_matrix(total)
    matrix = jnp.concatenate(
        [lax.dynamic_slice_in_dim(matrix, s, half, axis=1) for s in starts], axis=1
    )
    outs = []
    for k in range(blocks.shape[0]):
        joined = jnp.concatenate([p[k] for p in pieces], axis=1)
        wide = jnp.broadcast_to(matrix, (joined.shape[0],) + matrix.shape)
        outs.append(jnp.einsum("xij,xjz->xiz", wide, joined, precision=HP))
    return outs


def smooth_depth(field):
    matrix = smoothing_matrix(field.shape[-1])
    return jnp.einsum("...j,ij->...i", field, matrix, precision=HP)


def smooth_along_x(both):
    cols = lax.all_to_all(both, "slab", split_axis=2, concat_axis=1, tiled=True)
    matrix = smoothing_matrix(cols.shape[1])
    cols = jnp.einsum("ij,fjyz->fiyz", matrix, cols, precision=HP)
    return lax.all_to_all(cols, "slab", split_axis=1, concat_axis=2, tiled=True)


def make_body(n_shots):
    def body(vel_parts, den_parts, illum_parts, layer_index, depth_scale):
        total = vel_parts.shape[2]
        illum, vel, den = reduce_scatter_shots(
            [illum_parts[0], vel_parts[0], den_parts[0]], n_shots
        )
        both = jnp.stack([vel / illum, den / illum])
        both = smooth_along_x(smooth_depth(both))
        vel, den = all_gather_smooth_shots(both, n_shots, total)
        onehot = (
            layer_index[:, None] == jnp.arange(depth_scale.shape[1], dtype=jnp.int32)[None, :]
        ).astype(jnp.float32)
        per_depth = jnp.dot(depth_scale, onehot.T, precision=HP)
        vel_update = per_depth[0][None, None, :] * vel
        den_update = per_depth[1][None, None, :] * den
        return (vel_update, den_update)

    return body


def solution(mesh):
    placed = (
        P("shots", "slab", None, None),
        P("shots", "slab", None, None),
        P("shots", "slab", None, None),
        P(),
        P(),
    )
    return jax.shard_map(
        make_body(mesh.shape["shots"]),
        mesh=mesh,
        in_specs=placed,
        out_specs=(P("slab", None, None), P("slab", None, None)),
        check_vma=False,
    )
```

profile of v0, /device:TPU:2, one launch (start us, length us, event | category | flops | bytes accessed | tf_op | source)
XLA Modules:
  0.0 232.7 jit_solution(16517316433484003850)
XLA Ops:
  0.6 0.0 copy-start
  0.8 1.8 constant_dynamic-slice_fusion.14
  2.7 0.3 copy-done.1
  3.0 0.6 copy-done.2
  3.7 0.7 constant_dynamic-slice_fusion.12
  4.4 0.1 pad_maximum_fusion.1
  4.4 3.1 %collective-permute-start.3 = (f32[3,4,64,256]{3,2,1,0:T(8,128)S(1)}, f32[3,4,64,256]{3,2,1,0:T(8,128)S(1)}, u32[]{:S(2)}, u32[]{:S(2)}) collective-permute-start(f32[3,4,64,256]{3,2,1,0:T(8,128)S(1)} %pad_maximum_fusion.1), channel_id=1, source_target_pairs={{0,96},{32,0},{64,32},{96,64},{128,224},{160,128},{192,160},{224,1... | collective-permute-start | bytes 2359304 | tf_op jit(solution)/shard_map/ppermute | solution.py:47
  7.5 0.1 pad_maximum_fusion
  7.6 0.1 collective-permute-start
  7.7 16.7 %collective-permute-done.3 = f32[3,4,64,256]{3,2,1,0:T(8,128)S(1)} collective-permute-done((f32[3,4,64,256]{3,2,1,0:T(8,128)S(1)}, f32[3,4,64,256]{3,2,1,0:T(8,128)S(1)}, u32[]{:S(2)}, u32[]{:S(2)}) %collective-permute-start.3) | collective-permute-done | bytes 786464 | tf_op jit(solution)/shard_map/ppermute | solution.py:47
  24.3 0.1 maximum_add_fusion.3
  24.4 3.8 %collective-permute-start.4 = (f32[3,4,64,256]{3,2,1,0:T(8,128)S(1)}, f32[3,4,64,256]{3,2,1,0:T(8,128)S(1)}, u32[]{:S(2)}, u32[]{:S(2)}) collective-permute-start(f32[3,4,64,256]{3,2,1,0:T(8,128)S(1)} %maximum_add_fusion.3), channel_id=1, source_target_pairs={{0,96},{32,0},{64,32},{96,64},{128,224},{160,128},{192,160},{224,1... | collective-permute-start | bytes 2359304 | tf_op jit(solution)/shard_map/ppermute | solution.py:47
  28.2 0.1 maximum_add_fusion
  28.3 0.1 collective-permute-start.1
  28.4 15.7 %collective-permute-done.4 = f32[3,4,64,256]{3,2,1,0:T(8,128)S(1)} collective-permute-done((f32[3,4,64,256]{3,2,1,0:T(8,128)S(1)}, f32[3,4,64,256]{3,2,1,0:T(8,128)S(1)}, u32[]{:S(2)}, u32[]{:S(2)}) %collective-permute-start.4) | collective-permute-done | bytes 786464 | tf_op jit(solution)/shard_map/ppermute | solution.py:47
  44.1 0.1 maximum_add_fusion.4
  44.2 3.8 %collective-permute-start.5 = (f32[3,4,64,256]{3,2,1,0:T(8,128)S(1)}, f32[3,4,64,256]{3,2,1,0:T(8,128)S(1)}, u32[]{:S(2)}, u32[]{:S(2)}) collective-permute-start(f32[3,4,64,256]{3,2,1,0:T(8,128)S(1)} %maximum_add_fusion.4), channel_id=1, source_target_pairs={{0,96},{32,0},{64,32},{96,64},{128,224},{160,128},{192,160},{224,1... | collective-permute-start | bytes 2359304 | tf_op jit(solution)/shard_map/ppermute | solution.py:47
  48.0 0.1 maximum_add_fusion.1
  48.1 0.1 collective-permute-start.2
  48.2 14.8 %collective-permute-done.5 = f32[3,4,64,256]{3,2,1,0:T(8,128)S(1)} collective-permute-done((f32[3,4,64,256]{3,2,1,0:T(8,128)S(1)}, f32[3,4,64,256]{3,2,1,0:T(8,128)S(1)}, u32[]{:S(2)}, u32[]{:S(2)}) %collective-permute-start.5) | collective-permute-done | bytes 786464 | tf_op jit(solution)/shard_map/ppermute | solution.py:47
  63.0 0.1 maximum_add_fusion.5
  63.1 7.3 %collective-permute-start.6 = (f32[3,4,64,256]{3,2,1,0:T(8,128)S(1)}, f32[3,4,64,256]{3,2,1,0:T(8,128)S(1)}, u32[]{:S(2)}, u32[]{:S(2)}) collective-permute-start(f32[3,4,64,256]{3,2,1,0:T(8,128)S(1)} %maximum_add_fusion.5), channel_id=1, source_target_pairs={{0,128},{32,160},{64,192},{96,224},{128,0},{160,32},{192,64},{224,... | collective-permute-start | bytes 2359304 | tf_op jit(solution)/shard_map/ppermute | solution.py:50
  70.4 0.2 fusion.41
  70.6 30.2 %collective-permute-done.6 = f32[3,4,64,256]{3,2,1,0:T(8,128)S(1)} collective-permute-done((f32[3,4,64,256]{3,2,1,0:T(8,128)S(1)}, f32[3,4,64,256]{3,2,1,0:T(8,128)S(1)}, u32[]{:S(2)}, u32[]{:S(2)}) %collective-permute-start.6) | collective-permute-done | bytes 786464 | tf_op jit(solution)/shard_map/ppermute | solution.py:50
  100.8 0.2 fusion.15
  100.9 0.1 slice_divide_fusion.1
  101.0 0.7 fusion.16
  101.7 1.1 copy.17
  102.8 7.5 %all-to-all-start = ((f32[2,4,64,256]{3,1,0,2:T(4,128)}), f32[2,4,64,256]{3,1,0,2:T(4,128)S(1)}, u32[]{:S(2)}, u32[]{:S(2)}) async-start(f32[2,4,64,256]{3,1,0,2:T(4,128)} %copy.17), calls=%async_computation | async-start | bytes 1048576 | tf_op jit(solution)/shard_map/all_to_all | solution.py:86
  110.4 0.1 fusion.52
  110.5 14.6 %all-to-all-done = f32[2,4,64,256]{3,1,0,2:T(4,128)S(1)} async-done(((f32[2,4,64,256]{3,1,0,2:T(4,128)}), f32[2,4,64,256]{3,1,0,2:T(4,128)S(1)}, u32[]{:S(2)}, u32[]{:S(2)}) %all-to-all-start) | async-done | bytes 524320 | tf_op jit(solution)/shard_map/all_to_all | solution.py:86
  125.1 0.3 copy.18
  125.3 1.0 convolution_bitcast_fusion
  126.4 1.0 copy.20
  127.4 5.9 %all-to-all-start.1 = ((f32[2,128,2,256]{3,2,0,1:T(2,128)}), f32[2,128,2,256]{3,2,0,1:T(2,128)S(1)}, u32[]{:S(2)}, u32[]{:S(2)}) async-start(f32[2,128,2,256]{3,2,0,1:T(2,128)} %copy.20), calls=%async_computation.1 | async-start | bytes 1048576 | tf_op jit(solution)/shard_map/all_to_all | solution.py:89
  133.3 0.2 convolution_bitcast_fusion.1
  133.5 14.5 %all-to-all-done.1 = f32[2,128,2,256]{3,2,0,1:T(2,128)S(1)} async-done(((f32[2,128,2,256]{3,2,0,1:T(2,128)}), f32[2,128,2,256]{3,2,0,1:T(2,128)S(1)}, u32[]{:S(2)}, u32[]{:S(2)}) %all-to-all-start.1) | async-done | bytes 524320 | tf_op jit(solution)/shard_map/all_to_all | solution.py:89
  147.9 0.2 copy.23
  148.1 1.2 all_to_all.33
  149.3 5.0 %collective-permute-start.7 = (f32[2,4,64,256]{3,2,1,0:T(8,128)}, f32[2,4,64,256]{3,2,1,0:T(8,128)}, u32[]{:S(2)}, u32[]{:S(2)}) collective-permute-start(f32[2,4,64,256]{3,2,1,0:T(8,128)} %all_to_all.33), channel_id=1, source_target_pairs={{0,128},{32,160},{64,192},{96,224},{128,0},{160,32},{192,64},{224,... | collective-permute-start | bytes 1572872 | tf_op jit(solution)/shard_map/ppermute | solution.py:60
  154.3 0.5 fusion.14
  154.8 0.4 fusion.13
  155.2 0.1 collective-permute-start.8
  155.4 24.3 %collective-permute-done.7 = f32[2,4,64,256]{3,2,1,0:T(8,128)} collective-permute-done((f32[2,4,64,256]{3,2,1,0:T(8,128)}, f32[2,4,64,256]{3,2,1,0:T(8,128)}, u32[]{:S(2)}, u32[]{:S(2)}) %collective-permute-start.7) | collective-permute-done | bytes 524320 | tf_op jit(solution)/shard_map/ppermute | solution.py:60
  179.6 3.7 %collective-permute-start.9 = (f32[2,4,64,256]{3,2,1,0:T(8,128)}, f32[2,4,64,256]{3,2,1,0:T(8,128)}, u32[]{:S(2)}, u32[]{:S(2)}) collective-permute-start(f32[2,4,64,256]{3,2,1,0:T(8,128)} %collective-permute-done.7), channel_id=1, source_target_pairs={{0,96},{32,0},{64,32},{96,64},{128,224},{160,128},{192,160},{224,1... | collective-permute-start | bytes 1572872 | tf_op jit(solution)/shard_map/ppermute | solution.py:65
  183.3 1.3 constant_dynamic-slice_fusion.24
  184.6 1.5 concatenate.9
  186.1 0.2 copy.21
  186.3 0.2 fusion.65
  186.6 0.2 squeeze.51
  186.8 0.2 squeeze.59
  187.0 0.1 collective-permute-start.10
  187.2 7.9 %collective-permute-done.9 = f32[2,4,64,256]{3,2,1,0:T(8,128)} collective-permute-done((f32[2,4,64,256]{3,2,1,0:T(8,128)}, f32[2,4,64,256]{3,2,1,0:T(8,128)}, u32[]{:S(2)}, u32[]{:S(2)}) %collective-permute-start.9) | collective-permute-done | bytes 524320 | tf_op jit(solution)/shard_map/ppermute | solution.py:65
  195.1 3.7 %collective-permute-start.11 = (f32[2,4,64,256]{3,2,1,0:T(8,128)}, f32[2,4,64,256]{3,2,1,0:T(8,128)S(1)}, u32[]{:S(2)}, u32[]{:S(2)}) collective-permute-start(f32[2,4,64,256]{3,2,1,0:T(8,128)} %collective-permute-done.9), channel_id=1, source_target_pairs={{0,96},{32,0},{64,32},{96,64},{128,224},{160,128},{192,160},{224,1... | collective-permute-start | bytes 1572872 | tf_op jit(solution)/shard_map/ppermute | solution.py:65
  198.8 1.1 fusion.30
  199.8 1.1 fusion.29
  200.9 1.3 collective-permute-done.10
  202.1 1.1 fusion.28
  203.2 6.4 %collective-permute-done.11 = f32[2,4,64,256]{3,2,1,0:T(8,128)S(1)} collective-permute-done((f32[2,4,64,256]{3,2,1,0:T(8,128)}, f32[2,4,64,256]{3,2,1,0:T(8,128)S(1)}, u32[]{:S(2)}, u32[]{:S(2)}) %collective-permute-start.11) | collective-permute-done | bytes 524320 | tf_op jit(solution)/shard_map/ppermute | solution.py:65
  209.6 3.6 %collective-permute-start.13 = (f32[2,4,64,256]{3,2,1,0:T(8,128)S(1)}, f32[2,4,64,256]{3,2,1,0:T(8,128)S(1)}, u32[]{:S(2)}, u32[]{:S(2)}) collective-permute-start(f32[2,4,64,256]{3,2,1,0:T(8,128)S(1)} %collective-permute-done.11), channel_id=1, source_target_pairs={{0,96},{32,0},{64,32},{96,64},{128,224},{160,128},{192,160},{224,1... | collective-permute-start | bytes 1572872 | tf_op jit(solution)/shard_map/ppermute | solution.py:65
  213.3 2.8 %collective-permute-done.12 = f32[2,4,64,256]{3,2,1,0:T(8,128)S(1)} collective-permute-done((f32[2,4,64,256]{3,2,1,0:T(8,128)S(1)}, f32[2,4,64,256]{3,2,1,0:T(8,128)S(1)}, u32[]{:S(2)}, u32[]{:S(2)}) %collective-permute-start.12) | collective-permute-done | bytes 524320 | tf_op jit(solution)/shard_map/ppermute | solution.py:64
  216.1 6.7 %collective-permute-done.13 = f32[2,4,64,256]{3,2,1,0:T(8,128)S(1)} collective-permute-done((f32[2,4,64,256]{3,2,1,0:T(8,128)S(1)}, f32[2,4,64,256]{3,2,1,0:T(8,128)S(1)}, u32[]{:S(2)}, u32[]{:S(2)}) %collective-permute-start.13) | collective-permute-done | bytes 524320 | tf_op jit(solution)/shard_map/ppermute | solution.py:65
  222.9 4.9 %fusion.7 = f32[4,512,256]{2,1,0:T(8,128)} fusion(f32[4,512,256]{2,1,0:T(8,128)S(1)} %get-tuple-element.36, f32[512,512]{1,0:T(8,128)S(1)} %concatenate.9, f32[256]{0:T(256)S(1)} %bitcast.88), kind=kOutput, calls=%fused_computation.5 | convolution fusion | flops 3221749760 | bytes 5243904 | tf_op jit(solution)/shard_map/xij,xjz->xiz/dot_general | solution.py:76
  227.8 4.9 %fusion.4 = f32[4,512,256]{2,1,0:T(8,128)} fusion(f32[4,512,256]{2,1,0:T(8,128)S(1)} %get-tuple-element.37, f32[512,512]{1,0:T(8,128)S(1)} %concatenate.9, f32[256]{0:T(256)S(1)} %bitcast.87), kind=kOutput, calls=%fused_computation.4 | convolution fusion | flops 3221749760 | bytes 5243904 | tf_op jit(solution)/shard_map/xij,xjz->xiz/dot_general | solution.py:76
  (19 shorter events, 0.3 us)
Async XLA Ops:
  0.6 132.6 %copy-start = (f32[2,16]{1,0:T(2,128)S(1)}, f32[2,16]{1,0:T(2,128)}, u32[]{:S(2)}) copy-start(f32[2,16]{1,0:T(2,128)} %param.9) | copy-start | bytes 388
  0.8 2.2 copy-start.1
  0.8 2.8 %copy-start.2 = (f32[1,4,512,256]{3,2,1,0:T(8,128)S(1)}, f32[1,4,512,256]{3,2,1,0:T(8,128)}, u32[]{:S(2)}) copy-start(f32[1,4,512,256]{3,2,1,0:T(8,128)} %param.5) | copy-start | bytes 6291460
  4.4 19.9 %collective-permute-start.3 = (f32[3,4,64,256]{3,2,1,0:T(8,128)S(1)}, f32[3,4,64,256]{3,2,1,0:T(8,128)S(1)}, u32[]{:S(2)}, u32[]{:S(2)}) collective-permute-start(f32[3,4,64,256]{3,2,1,0:T(8,128)S(1)} %pad_maximum_fusion.1), channel_id=1, source_target_pairs={{0,96},{32,0},{64,32},{96,64},{128,224},{160,128},{192,160},{224,1... | collective-permute-start | bytes 2359304 | tf_op jit(solution)/shard_map/ppermute | solution.py:47
  7.6 20.6 %collective-permute-start = (f32[3,4,64,256]{3,2,1,0:T(8,128)S(1)}, f32[3,4,64,256]{3,2,1,0:T(8,128)S(1)}, u32[]{:S(2)}, u32[]{:S(2)}) collective-permute-start(f32[3,4,64,256]{3,2,1,0:T(8,128)S(1)} %pad_maximum_fusion), channel_id=1, source_target_pairs={{0,32},{32,64},{64,96},{96,0},{128,160},{160,192},{192,224},{224,1... | collective-permute-start | bytes 2359304 | tf_op jit(solution)/shard_map/ppermute | solution.py:46
  24.4 19.7 %collective-permute-start.4 = (f32[3,4,64,256]{3,2,1,0:T(8,128)S(1)}, f32[3,4,64,256]{3,2,1,0:T(8,128)S(1)}, u32[]{:S(2)}, u32[]{:S(2)}) collective-permute-start(f32[3,4,64,256]{3,2,1,0:T(8,128)S(1)} %maximum_add_fusion.3), channel_id=1, source_target_pairs={{0,96},{32,0},{64,32},{96,64},{128,224},{160,128},{192,160},{224,1... | collective-permute-start | bytes 2359304 | tf_op jit(solution)/shard_map/ppermute | solution.py:47
  28.3 19.7 %collective-permute-start.1 = (f32[3,4,64,256]{3,2,1,0:T(8,128)S(1)}, f32[3,4,64,256]{3,2,1,0:T(8,128)S(1)}, u32[]{:S(2)}, u32[]{:S(2)}) collective-permute-start(f32[3,4,64,256]{3,2,1,0:T(8,128)S(1)} %maximum_add_fusion), channel_id=1, source_target_pairs={{0,32},{32,64},{64,96},{96,0},{128,160},{160,192},{192,224},{224,1... | collective-permute-start | bytes 2359304 | tf_op jit(solution)/shard_map/ppermute | solution.py:46
  44.2 18.8 %collective-permute-start.5 = (f32[3,4,64,256]{3,2,1,0:T(8,128)S(1)}, f32[3,4,64,256]{3,2,1,0:T(8,128)S(1)}, u32[]{:S(2)}, u32[]{:S(2)}) collective-permute-start(f32[3,4,64,256]{3,2,1,0:T(8,128)S(1)} %maximum_add_fusion.4), channel_id=1, source_target_pairs={{0,96},{32,0},{64,32},{96,64},{128,224},{160,128},{192,160},{224,1... | collective-permute-start | bytes 2359304 | tf_op jit(solution)/shard_map/ppermute | solution.py:47
  48.1 22.5 %collective-permute-start.2 = (f32[3,4,64,256]{3,2,1,0:T(8,128)S(1)}, f32[3,4,64,256]{3,2,1,0:T(8,128)S(1)}, u32[]{:S(2)}, u32[]{:S(2)}) collective-permute-start(f32[3,4,64,256]{3,2,1,0:T(8,128)S(1)} %maximum_add_fusion.1), channel_id=1, source_target_pairs={{0,32},{32,64},{64,96},{96,0},{128,160},{160,192},{192,224},{224,1... | collective-permute-start | bytes 2359304 | tf_op jit(solution)/shard_map/ppermute | solution.py:46
  63.1 37.6 %collective-permute-start.6 = (f32[3,4,64,256]{3,2,1,0:T(8,128)S(1)}, f32[3,4,64,256]{3,2,1,0:T(8,128)S(1)}, u32[]{:S(2)}, u32[]{:S(2)}) collective-permute-start(f32[3,4,64,256]{3,2,1,0:T(8,128)S(1)} %maximum_add_fusion.5), channel_id=1, source_target_pairs={{0,128},{32,160},{64,192},{96,224},{128,0},{160,32},{192,64},{224,... | collective-permute-start | bytes 2359304 | tf_op jit(solution)/shard_map/ppermute | solution.py:50
  102.8 22.2 %all-to-all-start = ((f32[2,4,64,256]{3,1,0,2:T(4,128)}), f32[2,4,64,256]{3,1,0,2:T(4,128)S(1)}, u32[]{:S(2)}, u32[]{:S(2)}) async-start(f32[2,4,64,256]{3,1,0,2:T(4,128)} %copy.17), calls=%async_computation | async-start | bytes 1048576 | tf_op jit(solution)/shard_map/all_to_all | solution.py:86
  125.1 8.2 %copy-start.3 = (s32[256]{0:T(256)S(1)}, s32[256]{0:T(256)}, u32[]{:S(2)}) copy-start(s32[256]{0:T(256)} %param.8) | copy-start | bytes 3076
  127.4 20.6 %all-to-all-start.1 = ((f32[2,128,2,256]{3,2,0,1:T(2,128)}), f32[2,128,2,256]{3,2,0,1:T(2,128)S(1)}, u32[]{:S(2)}, u32[]{:S(2)}) async-start(f32[2,128,2,256]{3,2,0,1:T(2,128)} %copy.20), calls=%async_computation.1 | async-start | bytes 1048576 | tf_op jit(solution)/shard_map/all_to_all | solution.py:89
  149.3 30.4 %collective-permute-start.7 = (f32[2,4,64,256]{3,2,1,0:T(8,128)}, f32[2,4,64,256]{3,2,1,0:T(8,128)}, u32[]{:S(2)}, u32[]{:S(2)}) collective-permute-start(f32[2,4,64,256]{3,2,1,0:T(8,128)} %all_to_all.33), channel_id=1, source_target_pairs={{0,128},{32,160},{64,192},{96,224},{128,0},{160,32},{192,64},{224,... | collective-permute-start | bytes 1572872 | tf_op jit(solution)/shard_map/ppermute | solution.py:60
  155.2 31.8 %collective-permute-start.8 = (f32[2,4,64,256]{3,2,1,0:T(8,128)}, f32[2,4,64,256]{3,2,1,0:T(8,128)}, u32[]{:S(2)}, u32[]{:S(2)}) collective-permute-start(f32[2,4,64,256]{3,2,1,0:T(8,128)} %all_to_all.33), channel_id=1, source_target_pairs={{0,32},{32,64},{64,96},{96,0},{128,160},{160,192},{192,224},{224,1... | collective-permute-start | bytes 1572872 | tf_op jit(solution)/shard_map/ppermute | solution.py:64
  179.6 15.4 %collective-permute-start.9 = (f32[2,4,64,256]{3,2,1,0:T(8,128)}, f32[2,4,64,256]{3,2,1,0:T(8,128)}, u32[]{:S(2)}, u32[]{:S(2)}) collective-permute-start(f32[2,4,64,256]{3,2,1,0:T(8,128)} %collective-permute-done.7), channel_id=1, source_target_pairs={{0,96},{32,0},{64,32},{96,64},{128,224},{160,128},{192,160},{224,1... | collective-permute-start | bytes 1572872 | tf_op jit(solution)/shard_map/ppermute | solution.py:65
  187.0 15.1 %collective-permute-start.10 = (f32[2,4,64,256]{3,2,1,0:T(8,128)}, f32[2,4,64,256]{3,2,1,0:T(8,128)S(1)}, u32[]{:S(2)}, u32[]{:S(2)}) collective-permute-start(f32[2,4,64,256]{3,2,1,0:T(8,128)} %collective-permute-done.8), channel_id=1, source_target_pairs={{0,32},{32,64},{64,96},{96,0},{128,160},{160,192},{192,224},{224,1... | collective-permute-start | bytes 1572872 | tf_op jit(solution)/shard_map/ppermute | solution.py:64
  195.1 14.6 %collective-permute-start.11 = (f32[2,4,64,256]{3,2,1,0:T(8,128)}, f32[2,4,64,256]{3,2,1,0:T(8,128)S(1)}, u32[]{:S(2)}, u32[]{:S(2)}) collective-permute-start(f32[2,4,64,256]{3,2,1,0:T(8,128)} %collective-permute-done.9), channel_id=1, source_target_pairs={{0,96},{32,0},{64,32},{96,64},{128,224},{160,128},{192,160},{224,1... | collective-permute-start | bytes 1572872 | tf_op jit(solution)/shard_map/ppermute | solution.py:65
  202.1 13.9 %collective-permute-start.12 = (f32[2,4,64,256]{3,2,1,0:T(8,128)S(1)}, f32[2,4,64,256]{3,2,1,0:T(8,128)S(1)}, u32[]{:S(2)}, u32[]{:S(2)}) collective-permute-start(f32[2,4,64,256]{3,2,1,0:T(8,128)S(1)} %collective-permute-done.10), channel_id=1, source_target_pairs={{0,32},{32,64},{64,96},{96,0},{128,160},{160,192},{192,224},{224,1... | collective-permute-start | bytes 1572872 | tf_op jit(solution)/shard_map/ppermute | solution.py:64
  209.6 13.2 %collective-permute-start.13 = (f32[2,4,64,256]{3,2,1,0:T(8,128)S(1)}, f32[2,4,64,256]{3,2,1,0:T(8,128)S(1)}, u32[]{:S(2)}, u32[]{:S(2)}) collective-permute-start(f32[2,4,64,256]{3,2,1,0:T(8,128)S(1)} %collective-permute-done.11), channel_id=1, source_target_pairs={{0,96},{32,0},{64,32},{96,64},{128,224},{160,128},{192,160},{224,1... | collective-permute-start | bytes 1572872 | tf_op jit(solution)/shard_map/ppermute | solution.py:65
where the time goes:
time: 234 us; the launch traced here: 233 us
  waiting for transfers between devices  156 us (67%)
  starting transfers between devices  47.8 us (20%)
  local copies, waits for them, and re-layouts  14.3 us (6%)
  matrix products  11.7 us (5%)
    ppermute x3, waiting for transfers between devices, reduce_scatter_shots(): recv_b = lax.ppermute(acc_b, 'shots', bwd)  47.2 us
    ppermute x1, waiting for transfers between devices, reduce_scatter_shots(): return acc_f + lax.ppermute(acc_b, 'shots', hi_pairs(n_shots))  30.2 us
    ppermute x1, waiting for transfers between devices, all_gather_smooth_shots(): cur_b = lax.ppermute(cur_f, 'shots', hi_pairs(n_shots))  24.3 us
    ppermute x3, waiting for transfers between devices, all_gather_smooth_shots(): cur_b = lax.ppermute(cur_b, 'shots', bwd)  21.1 us
    all_to_all x1, waiting for transfers between devices, smooth_along_x(): cols = lax.all_to_all(both, 'slab', split_axis=2, concat_axis=1, tiled=True)  14.6 us
    all_to_all x1, waiting for transfers between devices, smooth_along_x(): return lax.all_to_all(cols, 'slab', split_axis=1, concat_axis=2, tiled=True)  14.5 us
    ppermute x3, starting transfers between devices, all_gather_smooth_shots(): cur_b = lax.ppermute(cur_b, 'shots', bwd)  11 us
    ppermute x3, starting transfers between devices, reduce_scatter_shots(): recv_b = lax.ppermute(acc_b, 'shots', bwd)  10.6 us
  transfers between devices with their start and end apart: 16, of which 12 were waited for; matrix products, arithmetic and copies ran while one was open for 4% of the time, Pallas kernels for 0%

commit v1 on v0

--- a/solution.py
+++ b/solution.py
@@ -30,44 +30,65 @@
     return lax.dynamic_slice_in_dim(field, start, size, axis=1)
 
 
-def reduce_scatter_shots(fields, n_shots):
+def reduce_scatter_shots(fields, n_shots, parts=2):
     idx = lax.axis_index("shots")
     r, h = idx % RING, idx // RING
     chunk = fields[0].shape[1] // RING
     half = chunk // 2
+    sub = half // parts
     fwd, bwd = ring_pairs(n_shots, 1), ring_pairs(n_shots, -1)
 
-    def take(start):
-        return jnp.stack([rows(f, start, half) for f in fields])
+    def ring(fields, off):
+        def take(start):
+            return jnp.stack([rows(f, start + off, sub) for f in fields])
 
-    acc_f = take(((r - 1) % RING) * chunk + h * half)
-    acc_b = take(((r + 1) % RING) * chunk + (1 - h) * half)
-    for t in range(1, RING):
-        recv_f = lax.ppermute(acc_f, "shots", fwd)
-        recv_b = lax.ppermute(acc_b, "shots", bwd)
-        acc_f = recv_f + take(((r - 1 - t) % RING) * chunk + h * half)
-        acc_b = recv_b + take(((r + 1 + t) % RING) * chunk + (1 - h) * half)
-    return acc_f + lax.ppermute(acc_b, "shots", hi_pairs(n_shots))
+        acc_f = take(((r - 1) % RING) * chunk + h * half)
+        acc_b = take(((r + 1) % RING) * chunk + (1 - h) * half)
+        for t in range(1, RING):
+            recv_f = lax.ppermute(acc_f, "shots", fwd)
+            recv_b = lax.ppermute(acc_b, "shots", bwd)
+            acc_f = recv_f + take(((r - 1 - t) % RING) * chunk + h * half)
+            acc_b = recv_b + take(((r + 1 + t) % RING) * chunk + (1 - h) * half)
+        return acc_f, acc_b
+
+    out = []
+    fields = tuple(fields)
+    for p in range(parts):
+        acc_f, acc_b = ring(fields, p * sub)
+        if p + 1 < parts:
+            fields, acc_f, acc_b = lax.optimization_barrier((fields, acc_f, acc_b))
+        out.append(acc_f + lax.ppermute(acc_b, "shots", hi_pairs(n_shots)))
+    return jnp.concatenate(out, axis=2)
 
 
-def all_gather_smooth_shots(blocks, n_shots, total):
+def all_gather_smooth_shots(blocks, n_shots, total, parts=2):
     idx = lax.axis_index("shots")
     r, h = idx % RING, idx // RING
     chunk = total // RING
     half = chunk // 2
+    sub = half // parts
     fwd, bwd = ring_pairs(n_shots, 1), ring_pairs(n_shots, -1)
-    cur_f = blocks
-    cur_b = lax.ppermute(cur_f, "shots", hi_pairs(n_shots))
-    pieces = [cur_f, cur_b]
-    starts = [r * chunk + h * half, r * chunk + (1 - h) * half]
-    for t in range(1, RING):
-        cur_f = lax.ppermute(cur_f, "shots", fwd)
-        cur_b = lax.ppermute(cur_b, "shots", bwd)
+    pieces, starts = [], []
+    rest = blocks
+    for p in range(parts):
+        cur_f = rest[:, :, p * sub:(p + 1) * sub]
+        cur_b = lax.ppermute(cur_f, "shots", hi_pairs(n_shots))
+        if p + 1 < parts:
+            rest, cur_b = lax.optimization_barrier((rest, cur_b))
+        off = p * sub
         pieces += [cur_f, cur_b]
-        starts += [((r - t) % RING) * chunk + h * half, ((r + t) % RING) * chunk + (1 - h) * half]
+        starts += [r * chunk + h * half + off, r * chunk + (1 - h) * half + off]
+        for t in range(1, RING):
+            cur_f = lax.ppermute(cur_f, "shots", fwd)
+            cur_b = lax.ppermute(cur_b, "shots", bwd)
+            pieces += [cur_f, cur_b]
+            starts += [
+                ((r - t) % RING) * chunk + h * half + off,
+                ((r + t) % RING) * chunk + (1 - h) * half + off,
+            ]
     matrix = smoothing_matrix(total)
     matrix = jnp.concatenate(
-        [lax.dynamic_slice_in_dim(matrix, s, half, axis=1) for s in starts], axis=1
+        [lax.dynamic_slice_in_dim(matrix, s, sub, axis=1) for s in starts], axis=1
     )
     outs = []
     for k in range(blocks.shape[0]):

time: 234 us -> 223 us (0.953)
  waiting for transfers between devices: 156 us -> 111 us
  starting transfers between devices: 47.8 us -> 73.8 us
  other arithmetic: 2.04 us -> 5.14 us
  local copies, waits for them, and re-layouts: 14.3 us -> 16.8 us
    ppermute x7 -> x14, waiting for transfers between devices: 77.4 us -> 56.9 us  [the longest x6 23.1 us: ring(): recv_f = lax.ppermute(acc_f, 'shots', fwd)]
    ppermute x1 -> x2, waiting for transfers between devices: 24.3 us -> 8.2 us  [all_gather_smooth_shots(): cur_b = lax.ppermute(cur_f, 'shots', hi_pairs(n_shots))]
    ppermute x7 -> x14, starting transfers between devices: 18.2 us -> 31.9 us  [the longest x6 17 us: ring(): recv_b = lax.ppermute(acc_b, 'shots', bwd)]
    ppermute x3 -> x6, starting transfers between devices: 11 us -> 19.8 us  [all_gather_smooth_shots(): cur_b = lax.ppermute(cur_b, 'shots', bwd)]
    ppermute x3 -> x6, waiting for transfers between devices: 21.1 us -> 15.5 us  [all_gather_smooth_shots(): cur_b = lax.ppermute(cur_b, 'shots', bwd)]
    add x6 -> x13, other arithmetic: 0.67 us -> 3.7 us  [the longest x6 2.12 us: ring(): acc_b = recv_b + take((r + 1 + t) % RING * chunk + (1 - h) * half)]
    ppermute x1 -> x2, starting transfers between devices: 5.03 us -> 7.74 us  [all_gather_smooth_shots(): cur_b = lax.ppermute(cur_f, 'shots', hi_pairs(n_shots))]
  transfers between devices with their start and end apart: 16 -> 30, of which waited for: 12 -> 17; matrix products, arithmetic and copies ran while one was open for 4% -> 6% of each run, Pallas kernels for 0% -> 0%
where the time goes in v1:
time: 223 us; the launch traced here: 220 us
  waiting for transfers between devices  111 us (50%)
  starting transfers between devices  73.8 us (33%)
  local copies, waits for them, and re-layouts  16.8 us (8%)
  matrix products  11.7 us (5%)
  other arithmetic  5.14 us (2%)
    ppermute x6, waiting for transfers between devices, ring(): recv_f = lax.ppermute(acc_f, 'shots', fwd)  23.1 us
    ppermute x2, waiting for transfers between devices, reduce_scatter_shots(): out.append(acc_f + lax.ppermute(acc_b, 'shots', hi_pairs(n_shots)))  21 us
    ppermute x6, starting transfers between devices, all_gather_smooth_shots(): cur_b = lax.ppermute(cur_b, 'shots', bwd)  19.8 us
    ppermute x6, starting transfers between devices, ring(): recv_b = lax.ppermute(acc_b, 'shots', bwd)  17 us
    ppermute x6, waiting for transfers between devices, all_gather_smooth_shots(): cur_b = lax.ppermute(cur_b, 'shots', bwd)  15.5 us
    all_to_all x1, waiting for transfers between devices, smooth_along_x(): cols = lax.all_to_all(both, 'slab', split_axis=2, concat_axis=1, tiled=True)  14.6 us
    all_to_all x1, waiting for transfers between devices, smooth_along_x(): return lax.all_to_all(cols, 'slab', split_axis=1, concat_axis=2, tiled=True)  13.5 us
    ppermute x6, waiting for transfers between devices, ring(): recv_b = lax.ppermute(acc_b, 'shots', bwd)  12.9 us
  transfers between devices with their start and end apart: 30, of which 17 were waited for; matrix products, arithmetic and copies ran while one was open for 6% of the time, Pallas kernels for 0%

profile of v1, /device:TPU:2, one launch (start us, length us, event | category | flops | bytes accessed | tf_op | source)
XLA Modules:
  0.0 220.2 jit_solution(18094250286683709245)
XLA Ops:
  0.8 1.5 constant_dynamic-slice_fusion.2
  2.3 0.3 copy-done.1
  2.7 1.5 constant_dynamic-slice_fusion
  4.2 1.7 collective-permute-start
  5.9 1.7 collective-permute-start.3
  7.7 8.8 %collective-permute-done = f32[3,4,32,256]{3,2,1,0:T(8,128)S(1)} collective-permute-done((f32[3,4,32,256]{3,2,1,0:T(8,128)S(1)}, f32[3,4,32,256]{3,2,1,0:T(8,128)S(1)}, u32[]{:S(2)}, u32[]{:S(2)}) %collective-permute-start) | collective-permute-done | bytes 393248 | tf_op jit(solution)/shard_map/ppermute | solution.py:48
  16.5 0.4 collective-permute-start.1
  17.0 3.0 %collective-permute-start.4 = (f32[3,4,32,256]{3,2,1,0:T(8,128)S(1)}, f32[3,4,32,256]{3,2,1,0:T(8,128)S(1)}, u32[]{:S(2)}, u32[]{:S(2)}) collective-permute-start(f32[3,4,32,256]{3,2,1,0:T(8,128)S(1)} %maximum_add_fusion.3), channel_id=1, source_target_pairs={{0,96},{32,0},{64,32},{96,64},{128,224},{160,128},{192,160},{224,1... | collective-permute-start | bytes 1179656 | tf_op jit(solution)/shard_map/ppermute | solution.py:49
  20.0 7.9 %collective-permute-done.1 = f32[3,4,32,256]{3,2,1,0:T(8,128)S(1)} collective-permute-done((f32[3,4,32,256]{3,2,1,0:T(8,128)S(1)}, f32[3,4,32,256]{3,2,1,0:T(8,128)S(1)}, u32[]{:S(2)}, u32[]{:S(2)}) %collective-permute-start.1) | collective-permute-done | bytes 393248 | tf_op jit(solution)/shard_map/ppermute | solution.py:48
  28.0 0.8 maximum_add_fusion.4
  28.8 3.2 %collective-permute-start.5 = (f32[3,4,32,256]{3,2,1,0:T(8,128)}, f32[3,4,32,256]{3,2,1,0:T(8,128)}, u32[]{:S(2)}, u32[]{:S(2)}) collective-permute-start(f32[3,4,32,256]{3,2,1,0:T(8,128)} %maximum_add_fusion.4), channel_id=1, source_target_pairs={{0,96},{32,0},{64,32},{96,64},{128,224},{160,128},{192,160},{224,1... | collective-permute-start | bytes 1179656 | tf_op jit(solution)/shard_map/ppermute | solution.py:49
  32.0 6.4 %collective-permute-done.2 = f32[3,4,32,256]{3,2,1,0:T(8,128)} collective-permute-done((f32[3,4,32,256]{3,2,1,0:T(8,128)S(1)}, f32[3,4,32,256]{3,2,1,0:T(8,128)}, u32[]{:S(2)}, u32[]{:S(2)}) %collective-permute-start.2) | collective-permute-done | bytes 393248 | tf_op jit(solution)/shard_map/ppermute | solution.py:48
  38.5 1.2 maximum_add_fusion.2
  39.7 1.1 maximum_add_fusion.5
  40.9 0.1 dynamic-slice_bitcast_fusion.13
  41.0 1.3 copy-done.3
  42.5 2.8 %collective-permute-start.10 = (f32[3,4,32,256]{3,2,1,0:T(8,128)S(1)}, f32[3,4,32,256]{3,2,1,0:T(8,128)S(1)}, u32[]{:S(2)}, u32[]{:S(2)}) collective-permute-start(f32[3,4,32,256]{3,2,1,0:T(8,128)S(1)} %pad_maximum_fusion.3), channel_id=1, source_target_pairs={{0,96},{32,0},{64,32},{96,64},{128,224},{160,128},{192,160},{224,1... | collective-permute-start | bytes 1179656 | tf_op jit(solution)/shard_map/ppermute | solution.py:49
  45.4 6.3 %collective-permute-done.10 = f32[3,4,32,256]{3,2,1,0:T(8,128)S(1)} collective-permute-done((f32[3,4,32,256]{3,2,1,0:T(8,128)S(1)}, f32[3,4,32,256]{3,2,1,0:T(8,128)S(1)}, u32[]{:S(2)}, u32[]{:S(2)}) %collective-permute-start.10) | collective-permute-done | bytes 393248 | tf_op jit(solution)/shard_map/ppermute | solution.py:49
  51.8 2.8 %collective-permute-start.11 = (f32[3,4,32,256]{3,2,1,0:T(8,128)S(1)}, f32[3,4,32,256]{3,2,1,0:T(8,128)S(1)}, u32[]{:S(2)}, u32[]{:S(2)}) collective-permute-start(f32[3,4,32,256]{3,2,1,0:T(8,128)S(1)} %maximum_add_fusion.9), channel_id=1, source_target_pairs={{0,96},{32,0},{64,32},{96,64},{128,224},{160,128},{192,160},{224,1... | collective-permute-start | bytes 1179656 | tf_op jit(solution)/shard_map/ppermute | solution.py:49
  54.7 6.6 %collective-permute-done.11 = f32[3,4,32,256]{3,2,1,0:T(8,128)S(1)} collective-permute-done((f32[3,4,32,256]{3,2,1,0:T(8,128)S(1)}, f32[3,4,32,256]{3,2,1,0:T(8,128)S(1)}, u32[]{:S(2)}, u32[]{:S(2)}) %collective-permute-start.11) | collective-permute-done | bytes 393248 | tf_op jit(solution)/shard_map/ppermute | solution.py:49
  61.4 3.4 %collective-permute-start.12 = (f32[3,4,32,256]{3,2,1,0:T(8,128)S(1)}, f32[3,4,32,256]{3,2,1,0:T(8,128)S(1)}, u32[]{:S(2)}, u32[]{:S(2)}) collective-permute-start(f32[3,4,32,256]{3,2,1,0:T(8,128)S(1)} %maximum_add_fusion.10), channel_id=1, source_target_pairs={{0,96},{32,0},{64,32},{96,64},{128,224},{160,128},{192,160},{224,1... | collective-permute-start | bytes 1179656 | tf_op jit(solution)/shard_map/ppermute | solution.py:49
  64.8 7.2 %collective-permute-start.6 = (f32[3,4,32,256]{3,2,1,0:T(8,128)S(1)}, f32[3,4,32,256]{3,2,1,0:T(8,128)S(1)}, u32[]{:S(2)}, u32[]{:S(2)}) collective-permute-start(f32[3,4,32,256]{3,2,1,0:T(8,128)S(1)} %maximum_add_fusion.5), channel_id=1, source_target_pairs={{0,128},{32,160},{64,192},{96,224},{128,0},{160,32},{192,64},{224,... | collective-permute-start | bytes 1179656 | tf_op jit(solution)/shard_map/ppermute | solution.py:60
  72.2 5.4 %collective-permute-start.13 = (f32[3,4,32,256]{3,2,1,0:T(8,128)S(1)}, f32[3,4,32,256]{3,2,1,0:T(8,128)S(1)}, u32[]{:S(2)}, u32[]{:S(2)}) collective-permute-start(f32[3,4,32,256]{3,2,1,0:T(8,128)S(1)} %maximum_add_fusion.11), channel_id=1, source_target_pairs={{0,128},{32,160},{64,192},{96,224},{128,0},{160,32},{192,64},{224,... | collective-permute-start | bytes 1179656 | tf_op jit(solution)/shard_map/ppermute | solution.py:60
  77.6 0.2 fusion.31
  77.8 7.6 %collective-permute-done.6 = f32[3,4,32,256]{3,2,1,0:T(8,128)S(1)} collective-permute-done((f32[3,4,32,256]{3,2,1,0:T(8,128)S(1)}, f32[3,4,32,256]{3,2,1,0:T(8,128)S(1)}, u32[]{:S(2)}, u32[]{:S(2)}) %collective-permute-start.6) | collective-permute-done | bytes 393248 | tf_op jit(solution)/shard_map/ppermute | solution.py:60
  85.4 13.4 %collective-permute-done.13 = f32[3,4,32,256]{3,2,1,0:T(8,128)S(1)} collective-permute-done((f32[3,4,32,256]{3,2,1,0:T(8,128)S(1)}, f32[3,4,32,256]{3,2,1,0:T(8,128)S(1)}, u32[]{:S(2)}, u32[]{:S(2)}) %collective-permute-start.13) | collective-permute-done | bytes 393248 | tf_op jit(solution)/shard_map/ppermute | solution.py:60
  99.0 0.7 fusion.15
  99.7 1.1 copy.13
  100.8 7.5 %all-to-all-start = ((f32[2,4,64,256]{3,1,0,2:T(4,128)}), f32[2,4,64,256]{3,1,0,2:T(4,128)S(1)}, u32[]{:S(2)}, u32[]{:S(2)}) async-start(f32[2,4,64,256]{3,1,0,2:T(4,128)} %copy.13), calls=%async_computation | async-start | bytes 1048576 | tf_op jit(solution)/shard_map/all_to_all | solution.py:107
  108.5 14.6 %all-to-all-done = f32[2,4,64,256]{3,1,0,2:T(4,128)S(1)} async-done(((f32[2,4,64,256]{3,1,0,2:T(4,128)}), f32[2,4,64,256]{3,1,0,2:T(4,128)S(1)}, u32[]{:S(2)}, u32[]{:S(2)}) %all-to-all-start) | async-done | bytes 524320 | tf_op jit(solution)/shard_map/all_to_all | solution.py:107
  123.1 0.3 copy.14
  123.4 1.0 convolution_bitcast_fusion
  124.4 1.0 copy.16
  125.4 5.9 %all-to-all-start.1 = ((f32[2,128,2,256]{3,2,0,1:T(2,128)}), f32[2,128,2,256]{3,2,0,1:T(2,128)S(1)}, u32[]{:S(2)}, u32[]{:S(2)}) async-start(f32[2,128,2,256]{3,2,0,1:T(2,128)} %copy.16), calls=%async_computation.1 | async-start | bytes 1048576 | tf_op jit(solution)/shard_map/all_to_all | solution.py:110
  131.3 0.5 fusion.14
  131.8 0.2 convolution_bitcast_fusion.1
  132.0 0.5 fusion.13
  132.5 13.5 %all-to-all-done.1 = f32[2,128,2,256]{3,2,0,1:T(2,128)S(1)} async-done(((f32[2,128,2,256]{3,2,0,1:T(2,128)}), f32[2,128,2,256]{3,2,0,1:T(2,128)S(1)}, u32[]{:S(2)}, u32[]{:S(2)}) %all-to-all-start.1) | async-done | bytes 524320 | tf_op jit(solution)/shard_map/all_to_all | solution.py:110
  146.0 0.2 copy.18
  146.2 0.4 all_to_all.33
  146.5 0.7 slice.150
  147.2 5.0 %collective-permute-start.14 = (f32[2,4,32,256]{3,2,1,0:T(8,128)}, f32[2,4,32,256]{3,2,1,0:T(8,128)}, u32[]{:S(2)}, u32[]{:S(2)}) collective-permute-start(f32[2,4,32,256]{3,2,1,0:T(8,128)} %slice.150), channel_id=1, source_target_pairs={{0,128},{32,160},{64,192},{96,224},{128,0},{160,32},{192,64},{224,... | collective-permute-start | bytes 786440 | tf_op jit(solution)/shard_map/ppermute | solution.py:75
  152.3 2.5 %constant_dynamic-slice_fusion.24 = (f32[512,32]{1,0:T(8,128)S(1)}, f32[512,32]{1,0:T(8,128)S(1)}, f32[512,32]{1,0:T(8,128)S(1)}, f32[512,32]{1,0:T(8,128)S(1)},...) fusion(f32[512,512]{1,0:T(8,128)S(1)} %fusion.13, ...), kind=kLoop, calls=%fused_computation.180 | loop fusion | bytes 2097216 | tf_op jit(solution)/shard_map/dynamic_slice | solution.py:91
  154.8 3.3 %concatenate.12 = f32[512,512]{1,0:T(8,128)S(1)} concatenate(f32[512,32]{1,0:T(8,128)} %get-tuple-element.79, f32[512,32]{1,0:T(8,128)} %get-tuple-element.78, f32[512,32]{1,0:T(8,128)} %get-tuple-element.77, f32[512,32]{1,0:T(8,128)} %get-tuple-element.76, f32[512,32]{1,0:T(8,128)} %get-tuple-element.75, f32[512,32]{1,0:T(8,128)} %get-tuple-element.74, ...), dimensions={1} | concatenate | bytes 2097152 | tf_op jit(solution)/shard_map/concatenate | solution.py:90
  158.2 8.2 %collective-permute-done.14 = f32[2,4,32,256]{3,2,1,0:T(8,128)} collective-permute-done((f32[2,4,32,256]{3,2,1,0:T(8,128)}, f32[2,4,32,256]{3,2,1,0:T(8,128)}, u32[]{:S(2)}, u32[]{:S(2)}) %collective-permute-start.14) | collective-permute-done | bytes 262176 | tf_op jit(solution)/shard_map/ppermute | solution.py:75
  166.4 2.7 %collective-permute-start.21 = (f32[2,4,32,256]{3,2,1,0:T(8,128)S(1)}, f32[2,4,32,256]{3,2,1,0:T(8,128)S(1)}, u32[]{:S(2)}, u32[]{:S(2)}) collective-permute-start(f32[2,4,32,256]{3,2,1,0:T(8,128)S(1)} %slice.123), channel_id=1, source_target_pairs={{0,128},{32,160},{64,192},{96,224},{128,0},{160,32},{192,64},{224,... | collective-permute-start | bytes 786440 | tf_op jit(solution)/shard_map/ppermute | solution.py:75
  169.1 0.9 collective-permute-start.22
  170.0 2.3 %collective-permute-start.16 = (f32[2,4,32,256]{3,2,1,0:T(8,128)}, f32[2,4,32,256]{3,2,1,0:T(8,128)S(1)}, u32[]{:S(2)}, u32[]{:S(2)}) collective-permute-start(f32[2,4,32,256]{3,2,1,0:T(8,128)} %collective-permute-done.14), channel_id=1, source_target_pairs={{0,96},{32,0},{64,32},{96,64},{128,224},{160,128},{192,160},{224,1... | collective-permute-start | bytes 786440 | tf_op jit(solution)/shard_map/ppermute | solution.py:83
  172.3 1.0 bitcast_dynamic-update-slice_fusion.1
  173.3 1.0 fusion.44
  174.3 3.6 %collective-permute-done.16 = f32[2,4,32,256]{3,2,1,0:T(8,128)S(1)} collective-permute-done((f32[2,4,32,256]{3,2,1,0:T(8,128)}, f32[2,4,32,256]{3,2,1,0:T(8,128)S(1)}, u32[]{:S(2)}, u32[]{:S(2)}) %collective-permute-start.16) | collective-permute-done | bytes 262176 | tf_op jit(solution)/shard_map/ppermute | solution.py:83
  178.0 3.5 %collective-permute-start.18 = (f32[2,4,32,256]{3,2,1,0:T(8,128)S(1)}, f32[2,4,32,256]{3,2,1,0:T(8,128)S(1)}, u32[]{:S(2)}, u32[]{:S(2)}) collective-permute-start(f32[2,4,32,256]{3,2,1,0:T(8,128)S(1)} %collective-permute-done.16), channel_id=1, source_target_pairs={{0,96},{32,0},{64,32},{96,64},{128,224},{160,128},{192,160},{224,1... | collective-permute-start | bytes 786440 | tf_op jit(solution)/shard_map/ppermute | solution.py:83
  181.5 2.4 %collective-permute-done.17 = f32[2,4,32,256]{3,2,1,0:T(8,128)S(1)} collective-permute-done((f32[2,4,32,256]{3,2,1,0:T(8,128)}, f32[2,4,32,256]{3,2,1,0:T(8,128)S(1)}, u32[]{:S(2)}, u32[]{:S(2)}) %collective-permute-start.17) | collective-permute-done | bytes 262176 | tf_op jit(solution)/shard_map/ppermute | solution.py:82
  183.9 3.2 %collective-permute-start.23 = (f32[2,4,32,256]{3,2,1,0:T(8,128)S(1)}, f32[2,4,32,256]{3,2,1,0:T(8,128)S(1)}, u32[]{:S(2)}, u32[]{:S(2)}) collective-permute-start(f32[2,4,32,256]{3,2,1,0:T(8,128)S(1)} %collective-permute-done.21), channel_id=1, source_target_pairs={{0,96},{32,0},{64,32},{96,64},{128,224},{160,128},{192,160},{224,1... | collective-permute-start | bytes 786440 | tf_op jit(solution)/shard_map/ppermute | solution.py:83
  187.2 3.3 %collective-permute-start.20 = (f32[2,4,32,256]{3,2,1,0:T(8,128)S(1)}, f32[2,4,32,256]{3,2,1,0:T(8,128)S(1)}, u32[]{:S(2)}, u32[]{:S(2)}) collective-permute-start(f32[2,4,32,256]{3,2,1,0:T(8,128)S(1)} %collective-permute-done.18), channel_id=1, source_target_pairs={{0,96},{32,0},{64,32},{96,64},{128,224},{160,128},{192,160},{224,1... | collective-permute-start | bytes 786440 | tf_op jit(solution)/shard_map/ppermute | solution.py:83
  190.6 3.4 %collective-permute-done.23 = f32[2,4,32,256]{3,2,1,0:T(8,128)S(1)} collective-permute-done((f32[2,4,32,256]{3,2,1,0:T(8,128)S(1)}, f32[2,4,32,256]{3,2,1,0:T(8,128)S(1)}, u32[]{:S(2)}, u32[]{:S(2)}) %collective-permute-start.23) | collective-permute-done | bytes 262176 | tf_op jit(solution)/shard_map/ppermute | solution.py:83
  193.9 3.7 %collective-permute-start.25 = (f32[2,4,32,256]{3,2,1,0:T(8,128)S(1)}, f32[2,4,32,256]{3,2,1,0:T(8,128)S(1)}, u32[]{:S(2)}, u32[]{:S(2)}) collective-permute-start(f32[2,4,32,256]{3,2,1,0:T(8,128)S(1)} %collective-permute-done.23), channel_id=1, source_target_pairs={{0,96},{32,0},{64,32},{96,64},{128,224},{160,128},{192,160},{224,1... | collective-permute-start | bytes 786440 | tf_op jit(solution)/shard_map/ppermute | solution.py:83
  197.6 0.3 collective-permute-done.24
  197.9 1.6 collective-permute-done.20
  199.6 3.2 %collective-permute-done.25 = f32[2,4,32,256]{3,2,1,0:T(8,128)S(1)} collective-permute-done((f32[2,4,32,256]{3,2,1,0:T(8,128)S(1)}, f32[2,4,32,256]{3,2,1,0:T(8,128)S(1)}, u32[]{:S(2)}, u32[]{:S(2)}) %collective-permute-start.25) | collective-permute-done | bytes 262176 | tf_op jit(solution)/shard_map/ppermute | solution.py:83
  202.8 3.7 %collective-permute-start.27 = (f32[2,4,32,256]{3,2,1,0:T(8,128)S(1)}, f32[2,4,32,256]{3,2,1,0:T(8,128)S(1)}, u32[]{:S(2)}, u32[]{:S(2)}) collective-permute-start(f32[2,4,32,256]{3,2,1,0:T(8,128)S(1)} %collective-permute-done.25), channel_id=1, source_target_pairs={{0,96},{32,0},{64,32},{96,64},{128,224},{160,128},{192,160},{224,1... | collective-permute-start | bytes 786440 | tf_op jit(solution)/shard_map/ppermute | solution.py:83
  206.6 3.7 %collective-permute-done.27 = f32[2,4,32,256]{3,2,1,0:T(8,128)S(1)} collective-permute-done((f32[2,4,32,256]{3,2,1,0:T(8,128)S(1)}, f32[2,4,32,256]{3,2,1,0:T(8,128)S(1)}, u32[]{:S(2)}, u32[]{:S(2)}) %collective-permute-start.27) | collective-permute-done | bytes 262176 | tf_op jit(solution)/shard_map/ppermute | solution.py:83
  210.4 4.9 %fusion.4 = f32[4,512,256]{2,1,0:T(8,128)} fusion(f32[4,512,256]{2,1,0:T(8,128)S(1)} %get-tuple-element.87, f32[512,512]{1,0:T(8,128)S(1)} %concatenate.12, f32[256]{0:T(256)S(1)} %bitcast.204), kind=kOutput, calls=%fused_computation.4 | convolution fusion | flops 3221749760 | bytes 5243904 | tf_op jit(solution)/shard_map/xij,xjz->xiz/dot_general | solution.py:97
  215.3 4.9 %fusion.7 = f32[4,512,256]{2,1,0:T(8,128)} fusion(f32[4,512,256]{2,1,0:T(8,128)S(1)} %get-tuple-element.86, f32[512,512]{1,0:T(8,128)S(1)} %concatenate.12, f32[256]{0:T(256)S(1)} %bitcast.203), kind=kOutput, calls=%fused_computation.5 | convolution fusion | flops 3221749760 | bytes 5243904 | tf_op jit(solution)/shard_map/xij,xjz->xiz/dot_general | solution.py:97
  (64 shorter events, 1.8 us)
Async XLA Ops:
  0.6 131.1 %copy-start = (f32[2,16]{1,0:T(2,128)S(1)}, f32[2,16]{1,0:T(2,128)}, u32[]{:S(2)}) copy-start(f32[2,16]{1,0:T(2,128)} %param.9) | copy-start | bytes 388
  0.6 2.0 copy-start.1
  4.2 12.2 %collective-permute-start = (f32[3,4,32,256]{3,2,1,0:T(8,128)S(1)}, f32[3,4,32,256]{3,2,1,0:T(8,128)S(1)}, u32[]{:S(2)}, u32[]{:S(2)}) collective-permute-start(f32[3,4,32,256]{3,2,1,0:T(8,128)S(1)} %pad_maximum_fusion), channel_id=1, source_target_pairs={{0,32},{32,64},{64,96},{96,0},{128,160},{160,192},{192,224},{224,1... | collective-permute-start | bytes 1179656 | tf_op jit(solution)/shard_map/ppermute | solution.py:48
  5.9 11.0 %collective-permute-start.3 = (f32[3,4,32,256]{3,2,1,0:T(8,128)S(1)}, f32[3,4,32,256]{3,2,1,0:T(8,128)S(1)}, u32[]{:S(2)}, u32[]{:S(2)}) collective-permute-start(f32[3,4,32,256]{3,2,1,0:T(8,128)S(1)} %pad_maximum_fusion.1), channel_id=1, source_target_pairs={{0,96},{32,0},{64,32},{96,64},{128,224},{160,128},{192,160},{224,1... | collective-permute-start | bytes 1179656 | tf_op jit(solution)/shard_map/ppermute | solution.py:49
  16.5 11.3 %collective-permute-start.1 = (f32[3,4,32,256]{3,2,1,0:T(8,128)S(1)}, f32[3,4,32,256]{3,2,1,0:T(8,128)S(1)}, u32[]{:S(2)}, u32[]{:S(2)}) collective-permute-start(f32[3,4,32,256]{3,2,1,0:T(8,128)S(1)} %maximum_add_fusion), channel_id=1, source_target_pairs={{0,32},{32,64},{64,96},{96,0},{128,160},{160,192},{192,224},{224,1... | collective-permute-start | bytes 1179656 | tf_op jit(solution)/shard_map/ppermute | solution.py:48
  17.0 11.1 %collective-permute-start.4 = (f32[3,4,32,256]{3,2,1,0:T(8,128)S(1)}, f32[3,4,32,256]{3,2,1,0:T(8,128)S(1)}, u32[]{:S(2)}, u32[]{:S(2)}) collective-permute-start(f32[3,4,32,256]{3,2,1,0:T(8,128)S(1)} %maximum_add_fusion.3), channel_id=1, source_target_pairs={{0,96},{32,0},{64,32},{96,64},{128,224},{160,128},{192,160},{224,1... | collective-permute-start | bytes 1179656 | tf_op jit(solution)/shard_map/ppermute | solution.py:49
  27.9 10.5 %collective-permute-start.2 = (f32[3,4,32,256]{3,2,1,0:T(8,128)S(1)}, f32[3,4,32,256]{3,2,1,0:T(8,128)}, u32[]{:S(2)}, u32[]{:S(2)}) collective-permute-start(f32[3,4,32,256]{3,2,1,0:T(8,128)S(1)} %maximum_add_fusion.1), channel_id=1, source_target_pairs={{0,32},{32,64},{64,96},{96,0},{128,160},{160,192},{192,224},{224,1... | collective-permute-start | bytes 1179656 | tf_op jit(solution)/shard_map/ppermute | solution.py:48
  28.8 10.8 %collective-permute-start.5 = (f32[3,4,32,256]{3,2,1,0:T(8,128)}, f32[3,4,32,256]{3,2,1,0:T(8,128)}, u32[]{:S(2)}, u32[]{:S(2)}) collective-permute-start(f32[3,4,32,256]{3,2,1,0:T(8,128)} %maximum_add_fusion.4), channel_id=1, source_target_pairs={{0,96},{32,0},{64,32},{96,64},{128,224},{160,128},{192,160},{224,1... | collective-permute-start | bytes 1179656 | tf_op jit(solution)/shard_map/ppermute | solution.py:49
  38.4 2.5 %copy-start.2 = (f32[1,4,512,256]{3,2,1,0:T(8,128)S(1)}, f32[1,4,512,256]{3,2,1,0:T(8,128)}, u32[]{:S(2)}) copy-start(f32[1,4,512,256]{3,2,1,0:T(8,128)} %param.5) | copy-start | bytes 6291460
  40.8 1.6 copy-start.3
  42.5 9.2 %collective-permute-start.10 = (f32[3,4,32,256]{3,2,1,0:T(8,128)S(1)}, f32[3,4,32,256]{3,2,1,0:T(8,128)S(1)}, u32[]{:S(2)}, u32[]{:S(2)}) collective-permute-start(f32[3,4,32,256]{3,2,1,0:T(8,128)S(1)} %pad_maximum_fusion.3), channel_id=1, source_target_pairs={{0,96},{32,0},{64,32},{96,64},{128,224},{160,128},{192,160},{224,1... | collective-permute-start | bytes 1179656 | tf_op jit(solution)/shard_map/ppermute | solution.py:49
  45.3 9.3 %collective-permute-start.7 = (f32[3,4,32,256]{3,2,1,0:T(8,128)S(1)}, f32[3,4,32,256]{3,2,1,0:T(8,128)S(1)}, u32[]{:S(2)}, u32[]{:S(2)}) collective-permute-start(f32[3,4,32,256]{3,2,1,0:T(8,128)S(1)} %pad_maximum_fusion.2), channel_id=1, source_target_pairs={{0,32},{32,64},{64,96},{96,0},{128,160},{160,192},{192,224},{224,1... | collective-permute-start | bytes 1179656 | tf_op jit(solution)/shard_map/ppermute | solution.py:48
  51.8 9.6 %collective-permute-start.11 = (f32[3,4,32,256]{3,2,1,0:T(8,128)S(1)}, f32[3,4,32,256]{3,2,1,0:T(8,128)S(1)}, u32[]{:S(2)}, u32[]{:S(2)}) collective-permute-start(f32[3,4,32,256]{3,2,1,0:T(8,128)S(1)} %maximum_add_fusion.9), channel_id=1, source_target_pairs={{0,96},{32,0},{64,32},{96,64},{128,224},{160,128},{192,160},{224,1... | collective-permute-start | bytes 1179656 | tf_op jit(solution)/shard_map/ppermute | solution.py:49
  54.7 17.3 %collective-permute-start.8 = (f32[3,4,32,256]{3,2,1,0:T(8,128)S(1)}, f32[3,4,32,256]{3,2,1,0:T(8,128)S(1)}, u32[]{:S(2)}, u32[]{:S(2)}) collective-permute-start(f32[3,4,32,256]{3,2,1,0:T(8,128)S(1)} %maximum_add_fusion.6), channel_id=1, source_target_pairs={{0,32},{32,64},{64,96},{96,0},{128,160},{160,192},{192,224},{224,1... | collective-permute-start | bytes 1179656 | tf_op jit(solution)/shard_map/ppermute | solution.py:48
  61.4 10.7 %collective-permute-start.12 = (f32[3,4,32,256]{3,2,1,0:T(8,128)S(1)}, f32[3,4,32,256]{3,2,1,0:T(8,128)S(1)}, u32[]{:S(2)}, u32[]{:S(2)}) collective-permute-start(f32[3,4,32,256]{3,2,1,0:T(8,128)S(1)} %maximum_add_fusion.10), channel_id=1, source_target_pairs={{0,96},{32,0},{64,32},{96,64},{128,224},{160,128},{192,160},{224,1... | collective-permute-start | bytes 1179656 | tf_op jit(solution)/shard_map/ppermute | solution.py:49
  64.8 20.6 %collective-permute-start.6 = (f32[3,4,32,256]{3,2,1,0:T(8,128)S(1)}, f32[3,4,32,256]{3,2,1,0:T(8,128)S(1)}, u32[]{:S(2)}, u32[]{:S(2)}) collective-permute-start(f32[3,4,32,256]{3,2,1,0:T(8,128)S(1)} %maximum_add_fusion.5), channel_id=1, source_target_pairs={{0,128},{32,160},{64,192},{96,224},{128,0},{160,32},{192,64},{224,... | collective-permute-start | bytes 1179656 | tf_op jit(solution)/shard_map/ppermute | solution.py:60
  72.1 13.4 %collective-permute-start.9 = (f32[3,4,32,256]{3,2,1,0:T(8,128)S(1)}, f32[3,4,32,256]{3,2,1,0:T(8,128)S(1)}, u32[]{:S(2)}, u32[]{:S(2)}) collective-permute-start(f32[3,4,32,256]{3,2,1,0:T(8,128)S(1)} %maximum_add_fusion.7), channel_id=1, source_target_pairs={{0,32},{32,64},{64,96},{96,0},{128,160},{160,192},{192,224},{224,1... | collective-permute-start | bytes 1179656 | tf_op jit(solution)/shard_map/ppermute | solution.py:48
  72.2 26.6 %collective-permute-start.13 = (f32[3,4,32,256]{3,2,1,0:T(8,128)S(1)}, f32[3,4,32,256]{3,2,1,0:T(8,128)S(1)}, u32[]{:S(2)}, u32[]{:S(2)}) collective-permute-start(f32[3,4,32,256]{3,2,1,0:T(8,128)S(1)} %maximum_add_fusion.11), channel_id=1, source_target_pairs={{0,128},{32,160},{64,192},{96,224},{128,0},{160,32},{192,64},{224,... | collective-permute-start | bytes 1179656 | tf_op jit(solution)/shard_map/ppermute | solution.py:60
  100.8 22.2 %all-to-all-start = ((f32[2,4,64,256]{3,1,0,2:T(4,128)}), f32[2,4,64,256]{3,1,0,2:T(4,128)S(1)}, u32[]{:S(2)}, u32[]{:S(2)}) async-start(f32[2,4,64,256]{3,1,0,2:T(4,128)} %copy.13), calls=%async_computation | async-start | bytes 1048576 | tf_op jit(solution)/shard_map/all_to_all | solution.py:107
  123.4 8.4 %copy-start.4 = (s32[256]{0:T(256)S(1)}, s32[256]{0:T(256)}, u32[]{:S(2)}) copy-start(s32[256]{0:T(256)} %param.8) | copy-start | bytes 3076
  125.4 20.6 %all-to-all-start.1 = ((f32[2,128,2,256]{3,2,0,1:T(2,128)}), f32[2,128,2,256]{3,2,0,1:T(2,128)S(1)}, u32[]{:S(2)}, u32[]{:S(2)}) async-start(f32[2,128,2,256]{3,2,0,1:T(2,128)} %copy.16), calls=%async_computation.1 | async-start | bytes 1048576 | tf_op jit(solution)/shard_map/all_to_all | solution.py:110
  147.2 19.1 %collective-permute-start.14 = (f32[2,4,32,256]{3,2,1,0:T(8,128)}, f32[2,4,32,256]{3,2,1,0:T(8,128)}, u32[]{:S(2)}, u32[]{:S(2)}) collective-permute-start(f32[2,4,32,256]{3,2,1,0:T(8,128)} %slice.150), channel_id=1, source_target_pairs={{0,128},{32,160},{64,192},{96,224},{128,0},{160,32},{192,64},{224,... | collective-permute-start | bytes 786440 | tf_op jit(solution)/shard_map/ppermute | solution.py:75
  152.3 20.0 %collective-permute-start.15 = (f32[2,4,32,256]{3,2,1,0:T(8,128)}, f32[2,4,32,256]{3,2,1,0:T(8,128)}, u32[]{:S(2)}, u32[]{:S(2)}) collective-permute-start(f32[2,4,32,256]{3,2,1,0:T(8,128)} %slice.150), channel_id=1, source_target_pairs={{0,32},{32,64},{64,96},{96,0},{128,160},{160,192},{192,224},{224,1... | collective-permute-start | bytes 786440 | tf_op jit(solution)/shard_map/ppermute | solution.py:82
  166.4 17.5 %collective-permute-start.21 = (f32[2,4,32,256]{3,2,1,0:T(8,128)S(1)}, f32[2,4,32,256]{3,2,1,0:T(8,128)S(1)}, u32[]{:S(2)}, u32[]{:S(2)}) collective-permute-start(f32[2,4,32,256]{3,2,1,0:T(8,128)S(1)} %slice.123), channel_id=1, source_target_pairs={{0,128},{32,160},{64,192},{96,224},{128,0},{160,32},{192,64},{224,... | collective-permute-start | bytes 786440 | tf_op jit(solution)/shard_map/ppermute | solution.py:75
  169.1 18.1 %collective-permute-start.22 = (f32[2,4,32,256]{3,2,1,0:T(8,128)S(1)}, f32[2,4,32,256]{3,2,1,0:T(8,128)S(1)}, u32[]{:S(2)}, u32[]{:S(2)}) collective-permute-start(f32[2,4,32,256]{3,2,1,0:T(8,128)S(1)} %slice.123), channel_id=1, source_target_pairs={{0,32},{32,64},{64,96},{96,0},{128,160},{160,192},{192,224},{224,1... | collective-permute-start | bytes 786440 | tf_op jit(solution)/shard_map/ppermute | solution.py:82
  170.0 7.9 %collective-permute-start.16 = (f32[2,4,32,256]{3,2,1,0:T(8,128)}, f32[2,4,32,256]{3,2,1,0:T(8,128)S(1)}, u32[]{:S(2)}, u32[]{:S(2)}) collective-permute-start(f32[2,4,32,256]{3,2,1,0:T(8,128)} %collective-permute-done.14), channel_id=1, source_target_pairs={{0,96},{32,0},{64,32},{96,64},{128,224},{160,128},{192,160},{224,1... | collective-permute-start | bytes 786440 | tf_op jit(solution)/shard_map/ppermute | solution.py:83
  172.3 11.6 %collective-permute-start.17 = (f32[2,4,32,256]{3,2,1,0:T(8,128)}, f32[2,4,32,256]{3,2,1,0:T(8,128)S(1)}, u32[]{:S(2)}, u32[]{:S(2)}) collective-permute-start(f32[2,4,32,256]{3,2,1,0:T(8,128)} %collective-permute-done.15), channel_id=1, source_target_pairs={{0,32},{32,64},{64,96},{96,0},{128,160},{160,192},{192,224},{224,1... | collective-permute-start | bytes 786440 | tf_op jit(solution)/shard_map/ppermute | solution.py:82
  178.0 9.3 %collective-permute-start.18 = (f32[2,4,32,256]{3,2,1,0:T(8,128)S(1)}, f32[2,4,32,256]{3,2,1,0:T(8,128)S(1)}, u32[]{:S(2)}, u32[]{:S(2)}) collective-permute-start(f32[2,4,32,256]{3,2,1,0:T(8,128)S(1)} %collective-permute-done.16), channel_id=1, source_target_pairs={{0,96},{32,0},{64,32},{96,64},{128,224},{160,128},{192,160},{224,1... | collective-permute-start | bytes 786440 | tf_op jit(solution)/shard_map/ppermute | solution.py:83
  183.9 14.0 %collective-permute-start.19 = (f32[2,4,32,256]{3,2,1,0:T(8,128)S(1)}, f32[2,4,32,256]{3,2,1,0:T(8,128)S(1)}, u32[]{:S(2)}, u32[]{:S(2)}) collective-permute-start(f32[2,4,32,256]{3,2,1,0:T(8,128)S(1)} %collective-permute-done.17), channel_id=1, source_target_pairs={{0,32},{32,64},{64,96},{96,0},{128,160},{160,192},{192,224},{224,1... | collective-permute-start | bytes 786440 | tf_op jit(solution)/shard_map/ppermute | solution.py:82
  183.9 10.0 %collective-permute-start.23 = (f32[2,4,32,256]{3,2,1,0:T(8,128)S(1)}, f32[2,4,32,256]{3,2,1,0:T(8,128)S(1)}, u32[]{:S(2)}, u32[]{:S(2)}) collective-permute-start(f32[2,4,32,256]{3,2,1,0:T(8,128)S(1)} %collective-permute-done.21), channel_id=1, source_target_pairs={{0,96},{32,0},{64,32},{96,64},{128,224},{160,128},{192,160},{224,1... | collective-permute-start | bytes 786440 | tf_op jit(solution)/shard_map/ppermute | solution.py:83
  187.2 10.7 %collective-permute-start.24 = (f32[2,4,32,256]{3,2,1,0:T(8,128)S(1)}, f32[2,4,32,256]{3,2,1,0:T(8,128)S(1)}, u32[]{:S(2)}, u32[]{:S(2)}) collective-permute-start(f32[2,4,32,256]{3,2,1,0:T(8,128)S(1)} %collective-permute-done.22), channel_id=1, source_target_pairs={{0,32},{32,64},{64,96},{96,0},{128,160},{160,192},{192,224},{224,1... | collective-permute-start | bytes 786440 | tf_op jit(solution)/shard_map/ppermute | solution.py:82
  187.2 12.3 %collective-permute-start.20 = (f32[2,4,32,256]{3,2,1,0:T(8,128)S(1)}, f32[2,4,32,256]{3,2,1,0:T(8,128)S(1)}, u32[]{:S(2)}, u32[]{:S(2)}) collective-permute-start(f32[2,4,32,256]{3,2,1,0:T(8,128)S(1)} %collective-permute-done.18), channel_id=1, source_target_pairs={{0,96},{32,0},{64,32},{96,64},{128,224},{160,128},{192,160},{224,1... | collective-permute-start | bytes 786440 | tf_op jit(solution)/shard_map/ppermute | solution.py:83
  193.9 8.8 %collective-permute-start.25 = (f32[2,4,32,256]{3,2,1,0:T(8,128)S(1)}, f32[2,4,32,256]{3,2,1,0:T(8,128)S(1)}, u32[]{:S(2)}, u32[]{:S(2)}) collective-permute-start(f32[2,4,32,256]{3,2,1,0:T(8,128)S(1)} %collective-permute-done.23), channel_id=1, source_target_pairs={{0,96},{32,0},{64,32},{96,64},{128,224},{160,128},{192,160},{224,1... | collective-permute-start | bytes 786440 | tf_op jit(solution)/shard_map/ppermute | solution.py:83
  197.9 8.7 %collective-permute-start.26 = (f32[2,4,32,256]{3,2,1,0:T(8,128)S(1)}, f32[2,4,32,256]{3,2,1,0:T(8,128)S(1)}, u32[]{:S(2)}, u32[]{:S(2)}) collective-permute-start(f32[2,4,32,256]{3,2,1,0:T(8,128)S(1)} %collective-permute-done.24), channel_id=1, source_target_pairs={{0,32},{32,64},{64,96},{96,0},{128,160},{160,192},{192,224},{224,1... | collective-permute-start | bytes 786440 | tf_op jit(solution)/shard_map/ppermute | solution.py:82
  202.8 7.6 %collective-permute-start.27 = (f32[2,4,32,256]{3,2,1,0:T(8,128)S(1)}, f32[2,4,32,256]{3,2,1,0:T(8,128)S(1)}, u32[]{:S(2)}, u32[]{:S(2)}) collective-permute-start(f32[2,4,32,256]{3,2,1,0:T(8,128)S(1)} %collective-permute-done.25), channel_id=1, source_target_pairs={{0,96},{32,0},{64,32},{96,64},{128,224},{160,128},{192,160},{224,1... | collective-permute-start | bytes 786440 | tf_op jit(solution)/shard_map/ppermute | solution.py:83

commit v2 on v1

--- a/solution.py
+++ b/solution.py
@@ -4,7 +4,7 @@
 from jax.sharding import PartitionSpec as P
 
 RADIUS = 20
-HP = lax.Precision.HIGHEST
+HP = lax.Precision.HIGH
 RING = 4
 
 
@@ -122,7 +122,7 @@
         onehot = (
             layer_index[:, None] == jnp.arange(depth_scale.shape[1], dtype=jnp.int32)[None, :]
         ).astype(jnp.float32)
-        per_depth = jnp.dot(depth_scale, onehot.T, precision=HP)
+        per_depth = jnp.dot(depth_scale, onehot.T, precision=lax.Precision.HIGHEST)
         vel_update = per_depth[0][None, None, :] * vel
         den_update = per_depth[1][None, None, :] * den
         return (vel_update, den_update)

time: 223 us -> 219 us (0.982)
  matrix products: 11.7 us -> 7.86 us
    dot_general x2, matrix products: 9.78 us -> 6.52 us  [all_gather_smooth_shots(): outs.append(jnp.einsum('xij,xjz->xiz', wide, joined, precision=HP))]
where the time goes in v2:
time: 219 us; the launch traced here: 216 us
  waiting for transfers between devices  111 us (51%)
  starting transfers between devices  73.8 us (34%)
  local copies, waits for them, and re-layouts  16.8 us (8%)
  matrix products  7.86 us (4%)
  other arithmetic  5.14 us (2%)
    ppermute x6, waiting for transfers between devices, ring(): recv_f = lax.ppermute(acc_f, 'shots', fwd)  23.1 us
    ppermute x2, waiting for transfers between devices, reduce_scatter_shots(): out.append(acc_f + lax.ppermute(acc_b, 'shots', hi_pairs(n_shots)))  21 us
    ppermute x6, starting transfers between devices, all_gather_smooth_shots(): cur_b = lax.ppermute(cur_b, 'shots', bwd)  19.8 us
    ppermute x6, starting transfers between devices, ring(): recv_b = lax.ppermute(acc_b, 'shots', bwd)  17 us
    ppermute x6, waiting for transfers between devices, all_gather_smooth_shots(): cur_b = lax.ppermute(cur_b, 'shots', bwd)  15.5 us
    all_to_all x1, waiting for transfers between devices, smooth_along_x(): cols = lax.all_to_all(both, 'slab', split_axis=2, concat_axis=1, tiled=True)  14.6 us
    all_to_all x1, waiting for transfers between devices, smooth_along_x(): return lax.all_to_all(cols, 'slab', split_axis=1, concat_axis=2, tiled=True)  13.5 us
    ppermute x6, waiting for transfers between devices, ring(): recv_b = lax.ppermute(acc_b, 'shots', bwd)  12.9 us
  transfers between devices with their start and end apart: 30, of which 17 were waited for; matrix products, arithmetic and copies ran while one was open for 6% of the time, Pallas kernels for 0%

profile of v2, /device:TPU:2, one launch (start us, length us, event | category | flops | bytes accessed | tf_op | source)
XLA Modules:
  0.0 216.3 jit_solution(4244232427307224083)
XLA Ops:
  0.8 1.5 constant_dynamic-slice_fusion.2
  2.3 0.3 copy-done.1
  2.7 1.5 constant_dynamic-slice_fusion
  4.2 1.7 collective-permute-start
  5.9 1.7 collective-permute-start.3
  7.7 8.8 %collective-permute-done = f32[3,4,32,256]{3,2,1,0:T(8,128)S(1)} collective-permute-done((f32[3,4,32,256]{3,2,1,0:T(8,128)S(1)}, f32[3,4,32,256]{3,2,1,0:T(8,128)S(1)}, u32[]{:S(2)}, u32[]{:S(2)}) %collective-permute-start) | collective-permute-done | bytes 393248 | tf_op jit(solution)/shard_map/ppermute | solution.py:48
  16.5 0.4 collective-permute-start.1
  17.0 3.0 %collective-permute-start.4 = (f32[3,4,32,256]{3,2,1,0:T(8,128)S(1)}, f32[3,4,32,256]{3,2,1,0:T(8,128)S(1)}, u32[]{:S(2)}, u32[]{:S(2)}) collective-permute-start(f32[3,4,32,256]{3,2,1,0:T(8,128)S(1)} %maximum_add_fusion.3), channel_id=1, source_target_pairs={{0,96},{32,0},{64,32},{96,64},{128,224},{160,128},{192,160},{224,1... | collective-permute-start | bytes 1179656 | tf_op jit(solution)/shard_map/ppermute | solution.py:49
  20.0 7.9 %collective-permute-done.1 = f32[3,4,32,256]{3,2,1,0:T(8,128)S(1)} collective-permute-done((f32[3,4,32,256]{3,2,1,0:T(8,128)S(1)}, f32[3,4,32,256]{3,2,1,0:T(8,128)S(1)}, u32[]{:S(2)}, u32[]{:S(2)}) %collective-permute-start.1) | collective-permute-done | bytes 393248 | tf_op jit(solution)/shard_map/ppermute | solution.py:48
  28.0 0.8 maximum_add_fusion.4
  28.8 3.2 %collective-permute-start.5 = (f32[3,4,32,256]{3,2,1,0:T(8,128)}, f32[3,4,32,256]{3,2,1,0:T(8,128)}, u32[]{:S(2)}, u32[]{:S(2)}) collective-permute-start(f32[3,4,32,256]{3,2,1,0:T(8,128)} %maximum_add_fusion.4), channel_id=1, source_target_pairs={{0,96},{32,0},{64,32},{96,64},{128,224},{160,128},{192,160},{224,1... | collective-permute-start | bytes 1179656 | tf_op jit(solution)/shard_map/ppermute | solution.py:49
  32.0 6.4 %collective-permute-done.2 = f32[3,4,32,256]{3,2,1,0:T(8,128)} collective-permute-done((f32[3,4,32,256]{3,2,1,0:T(8,128)S(1)}, f32[3,4,32,256]{3,2,1,0:T(8,128)}, u32[]{:S(2)}, u32[]{:S(2)}) %collective-permute-start.2) | collective-permute-done | bytes 393248 | tf_op jit(solution)/shard_map/ppermute | solution.py:48
  38.5 1.2 maximum_add_fusion.2
  39.7 1.1 maximum_add_fusion.5
  40.8 0.1 dynamic-slice_bitcast_fusion.12
  41.0 1.3 copy-done.3
  42.5 2.8 %collective-permute-start.10 = (f32[3,4,32,256]{3,2,1,0:T(8,128)S(1)}, f32[3,4,32,256]{3,2,1,0:T(8,128)S(1)}, u32[]{:S(2)}, u32[]{:S(2)}) collective-permute-start(f32[3,4,32,256]{3,2,1,0:T(8,128)S(1)} %pad_maximum_fusion.3), channel_id=1, source_target_pairs={{0,96},{32,0},{64,32},{96,64},{128,224},{160,128},{192,160},{224,1... | collective-permute-start | bytes 1179656 | tf_op jit(solution)/shard_map/ppermute | solution.py:49
  45.4 6.3 %collective-permute-done.10 = f32[3,4,32,256]{3,2,1,0:T(8,128)S(1)} collective-permute-done((f32[3,4,32,256]{3,2,1,0:T(8,128)S(1)}, f32[3,4,32,256]{3,2,1,0:T(8,128)S(1)}, u32[]{:S(2)}, u32[]{:S(2)}) %collective-permute-start.10) | collective-permute-done | bytes 393248 | tf_op jit(solution)/shard_map/ppermute | solution.py:49
  51.8 2.8 %collective-permute-start.11 = (f32[3,4,32,256]{3,2,1,0:T(8,128)S(1)}, f32[3,4,32,256]{3,2,1,0:T(8,128)S(1)}, u32[]{:S(2)}, u32[]{:S(2)}) collective-permute-start(f32[3,4,32,256]{3,2,1,0:T(8,128)S(1)} %maximum_add_fusion.9), channel_id=1, source_target_pairs={{0,96},{32,0},{64,32},{96,64},{128,224},{160,128},{192,160},{224,1... | collective-permute-start | bytes 1179656 | tf_op jit(solution)/shard_map/ppermute | solution.py:49
  54.7 6.6 %collective-permute-done.11 = f32[3,4,32,256]{3,2,1,0:T(8,128)S(1)} collective-permute-done((f32[3,4,32,256]{3,2,1,0:T(8,128)S(1)}, f32[3,4,32,256]{3,2,1,0:T(8,128)S(1)}, u32[]{:S(2)}, u32[]{:S(2)}) %collective-permute-start.11) | collective-permute-done | bytes 393248 | tf_op jit(solution)/shard_map/ppermute | solution.py:49
  61.4 3.4 %collective-permute-start.12 = (f32[3,4,32,256]{3,2,1,0:T(8,128)S(1)}, f32[3,4,32,256]{3,2,1,0:T(8,128)S(1)}, u32[]{:S(2)}, u32[]{:S(2)}) collective-permute-start(f32[3,4,32,256]{3,2,1,0:T(8,128)S(1)} %maximum_add_fusion.10), channel_id=1, source_target_pairs={{0,96},{32,0},{64,32},{96,64},{128,224},{160,128},{192,160},{224,1... | collective-permute-start | bytes 1179656 | tf_op jit(solution)/shard_map/ppermute | solution.py:49
  64.8 7.2 %collective-permute-start.6 = (f32[3,4,32,256]{3,2,1,0:T(8,128)S(1)}, f32[3,4,32,256]{3,2,1,0:T(8,128)S(1)}, u32[]{:S(2)}, u32[]{:S(2)}) collective-permute-start(f32[3,4,32,256]{3,2,1,0:T(8,128)S(1)} %maximum_add_fusion.5), channel_id=1, source_target_pairs={{0,128},{32,160},{64,192},{96,224},{128,0},{160,32},{192,64},{224,... | collective-permute-start | bytes 1179656 | tf_op jit(solution)/shard_map/ppermute | solution.py:60
  72.2 5.4 %collective-permute-start.13 = (f32[3,4,32,256]{3,2,1,0:T(8,128)S(1)}, f32[3,4,32,256]{3,2,1,0:T(8,128)S(1)}, u32[]{:S(2)}, u32[]{:S(2)}) collective-permute-start(f32[3,4,32,256]{3,2,1,0:T(8,128)S(1)} %maximum_add_fusion.11), channel_id=1, source_target_pairs={{0,128},{32,160},{64,192},{96,224},{128,0},{160,32},{192,64},{224,... | collective-permute-start | bytes 1179656 | tf_op jit(solution)/shard_map/ppermute | solution.py:60
  77.6 0.2 fusion.31
  77.8 7.6 %collective-permute-done.6 = f32[3,4,32,256]{3,2,1,0:T(8,128)S(1)} collective-permute-done((f32[3,4,32,256]{3,2,1,0:T(8,128)S(1)}, f32[3,4,32,256]{3,2,1,0:T(8,128)S(1)}, u32[]{:S(2)}, u32[]{:S(2)}) %collective-permute-start.6) | collective-permute-done | bytes 393248 | tf_op jit(solution)/shard_map/ppermute | solution.py:60
  85.4 13.4 %collective-permute-done.13 = f32[3,4,32,256]{3,2,1,0:T(8,128)S(1)} collective-permute-done((f32[3,4,32,256]{3,2,1,0:T(8,128)S(1)}, f32[3,4,32,256]{3,2,1,0:T(8,128)S(1)}, u32[]{:S(2)}, u32[]{:S(2)}) %collective-permute-start.13) | collective-permute-done | bytes 393248 | tf_op jit(solution)/shard_map/ppermute | solution.py:60
  99.0 0.5 fusion.15
  99.5 1.1 copy.13
  100.6 7.5 %all-to-all-start = ((f32[2,4,64,256]{3,1,0,2:T(4,128)}), f32[2,4,64,256]{3,1,0,2:T(4,128)S(1)}, u32[]{:S(2)}, u32[]{:S(2)}) async-start(f32[2,4,64,256]{3,1,0,2:T(4,128)} %copy.13), calls=%async_computation | async-start | bytes 1048576 | tf_op jit(solution)/shard_map/all_to_all | solution.py:107
  108.3 14.6 %all-to-all-done = f32[2,4,64,256]{3,1,0,2:T(4,128)S(1)} async-done(((f32[2,4,64,256]{3,1,0,2:T(4,128)}), f32[2,4,64,256]{3,1,0,2:T(4,128)S(1)}, u32[]{:S(2)}, u32[]{:S(2)}) %all-to-all-start) | async-done | bytes 524320 | tf_op jit(solution)/shard_map/all_to_all | solution.py:107
  122.9 0.3 copy.14
  123.2 0.6 convolution_bitcast_fusion
  123.8 1.0 copy.16
  124.8 5.9 %all-to-all-start.1 = ((f32[2,128,2,256]{3,2,0,1:T(2,128)}), f32[2,128,2,256]{3,2,0,1:T(2,128)S(1)}, u32[]{:S(2)}, u32[]{:S(2)}) async-start(f32[2,128,2,256]{3,2,0,1:T(2,128)} %copy.16), calls=%async_computation.1 | async-start | bytes 1048576 | tf_op jit(solution)/shard_map/all_to_all | solution.py:110
  130.7 0.5 fusion.14
  131.2 0.2 convolution_bitcast_fusion.1
  131.4 0.5 fusion.13
  131.9 13.5 %all-to-all-done.1 = f32[2,128,2,256]{3,2,0,1:T(2,128)S(1)} async-done(((f32[2,128,2,256]{3,2,0,1:T(2,128)}), f32[2,128,2,256]{3,2,0,1:T(2,128)S(1)}, u32[]{:S(2)}, u32[]{:S(2)}) %all-to-all-start.1) | async-done | bytes 524320 | tf_op jit(solution)/shard_map/all_to_all | solution.py:110
  145.4 0.2 copy.18
  145.6 0.4 all_to_all.33
  145.9 0.7 slice.150
  146.7 5.1 %collective-permute-start.14 = (f32[2,4,32,256]{3,2,1,0:T(8,128)}, f32[2,4,32,256]{3,2,1,0:T(8,128)}, u32[]{:S(2)}, u32[]{:S(2)}) collective-permute-start(f32[2,4,32,256]{3,2,1,0:T(8,128)} %slice.150), channel_id=1, source_target_pairs={{0,128},{32,160},{64,192},{96,224},{128,0},{160,32},{192,64},{224,... | collective-permute-start | bytes 786440 | tf_op jit(solution)/shard_map/ppermute | solution.py:75
  151.7 2.5 %constant_dynamic-slice_fusion.24 = (f32[512,32]{1,0:T(8,128)S(1)}, f32[512,32]{1,0:T(8,128)S(1)}, f32[512,32]{1,0:T(8,128)S(1)}, f32[512,32]{1,0:T(8,128)S(1)},...) fusion(f32[512,512]{1,0:T(8,128)S(1)} %fusion.13, ...), kind=kLoop, calls=%fused_computation.180 | loop fusion | bytes 2097216 | tf_op jit(solution)/shard_map/dynamic_slice | solution.py:91
  154.2 3.3 %concatenate.12 = f32[512,512]{1,0:T(8,128)S(1)} concatenate(f32[512,32]{1,0:T(8,128)} %get-tuple-element.79, f32[512,32]{1,0:T(8,128)} %get-tuple-element.78, f32[512,32]{1,0:T(8,128)} %get-tuple-element.77, f32[512,32]{1,0:T(8,128)} %get-tuple-element.76, f32[512,32]{1,0:T(8,128)} %get-tuple-element.75, f32[512,32]{1,0:T(8,128)} %get-tuple-element.74, ...), dimensions={1} | concatenate | bytes 2097152 | tf_op jit(solution)/shard_map/concatenate | solution.py:90
  157.6 8.2 %collective-permute-done.14 = f32[2,4,32,256]{3,2,1,0:T(8,128)} collective-permute-done((f32[2,4,32,256]{3,2,1,0:T(8,128)}, f32[2,4,32,256]{3,2,1,0:T(8,128)}, u32[]{:S(2)}, u32[]{:S(2)}) %collective-permute-start.14) | collective-permute-done | bytes 262176 | tf_op jit(solution)/shard_map/ppermute | solution.py:75
  165.8 2.7 %collective-permute-start.21 = (f32[2,4,32,256]{3,2,1,0:T(8,128)S(1)}, f32[2,4,32,256]{3,2,1,0:T(8,128)S(1)}, u32[]{:S(2)}, u32[]{:S(2)}) collective-permute-start(f32[2,4,32,256]{3,2,1,0:T(8,128)S(1)} %slice.123), channel_id=1, source_target_pairs={{0,128},{32,160},{64,192},{96,224},{128,0},{160,32},{192,64},{224,... | collective-permute-start | bytes 786440 | tf_op jit(solution)/shard_map/ppermute | solution.py:75
  168.5 0.9 collective-permute-start.22
  169.4 2.3 %collective-permute-start.16 = (f32[2,4,32,256]{3,2,1,0:T(8,128)}, f32[2,4,32,256]{3,2,1,0:T(8,128)S(1)}, u32[]{:S(2)}, u32[]{:S(2)}) collective-permute-start(f32[2,4,32,256]{3,2,1,0:T(8,128)} %collective-permute-done.14), channel_id=1, source_target_pairs={{0,96},{32,0},{64,32},{96,64},{128,224},{160,128},{192,160},{224,1... | collective-permute-start | bytes 786440 | tf_op jit(solution)/shard_map/ppermute | solution.py:83
  171.8 1.0 bitcast_dynamic-update-slice_fusion.1
  172.7 1.0 fusion.44
  173.7 3.6 %collective-permute-done.16 = f32[2,4,32,256]{3,2,1,0:T(8,128)S(1)} collective-permute-done((f32[2,4,32,256]{3,2,1,0:T(8,128)}, f32[2,4,32,256]{3,2,1,0:T(8,128)S(1)}, u32[]{:S(2)}, u32[]{:S(2)}) %collective-permute-start.16) | collective-permute-done | bytes 262176 | tf_op jit(solution)/shard_map/ppermute | solution.py:83
  177.4 3.5 %collective-permute-start.18 = (f32[2,4,32,256]{3,2,1,0:T(8,128)S(1)}, f32[2,4,32,256]{3,2,1,0:T(8,128)S(1)}, u32[]{:S(2)}, u32[]{:S(2)}) collective-permute-start(f32[2,4,32,256]{3,2,1,0:T(8,128)S(1)} %collective-permute-done.16), channel_id=1, source_target_pairs={{0,96},{32,0},{64,32},{96,64},{128,224},{160,128},{192,160},{224,1... | collective-permute-start | bytes 786440 | tf_op jit(solution)/shard_map/ppermute | solution.py:83
  180.9 2.4 %collective-permute-done.17 = f32[2,4,32,256]{3,2,1,0:T(8,128)S(1)} collective-permute-done((f32[2,4,32,256]{3,2,1,0:T(8,128)}, f32[2,4,32,256]{3,2,1,0:T(8,128)S(1)}, u32[]{:S(2)}, u32[]{:S(2)}) %collective-permute-start.17) | collective-permute-done | bytes 262176 | tf_op jit(solution)/shard_map/ppermute | solution.py:82
  183.3 3.2 %collective-permute-start.23 = (f32[2,4,32,256]{3,2,1,0:T(8,128)S(1)}, f32[2,4,32,256]{3,2,1,0:T(8,128)S(1)}, u32[]{:S(2)}, u32[]{:S(2)}) collective-permute-start(f32[2,4,32,256]{3,2,1,0:T(8,128)S(1)} %collective-permute-done.21), channel_id=1, source_target_pairs={{0,96},{32,0},{64,32},{96,64},{128,224},{160,128},{192,160},{224,1... | collective-permute-start | bytes 786440 | tf_op jit(solution)/shard_map/ppermute | solution.py:83
  186.7 3.3 %collective-permute-start.20 = (f32[2,4,32,256]{3,2,1,0:T(8,128)S(1)}, f32[2,4,32,256]{3,2,1,0:T(8,128)S(1)}, u32[]{:S(2)}, u32[]{:S(2)}) collective-permute-start(f32[2,4,32,256]{3,2,1,0:T(8,128)S(1)} %collective-permute-done.18), channel_id=1, source_target_pairs={{0,96},{32,0},{64,32},{96,64},{128,224},{160,128},{192,160},{224,1... | collective-permute-start | bytes 786440 | tf_op jit(solution)/shard_map/ppermute | solution.py:83
  190.0 3.4 %collective-permute-done.23 = f32[2,4,32,256]{3,2,1,0:T(8,128)S(1)} collective-permute-done((f32[2,4,32,256]{3,2,1,0:T(8,128)S(1)}, f32[2,4,32,256]{3,2,1,0:T(8,128)S(1)}, u32[]{:S(2)}, u32[]{:S(2)}) %collective-permute-start.23) | collective-permute-done | bytes 262176 | tf_op jit(solution)/shard_map/ppermute | solution.py:83
  193.3 3.7 %collective-permute-start.25 = (f32[2,4,32,256]{3,2,1,0:T(8,128)S(1)}, f32[2,4,32,256]{3,2,1,0:T(8,128)S(1)}, u32[]{:S(2)}, u32[]{:S(2)}) collective-permute-start(f32[2,4,32,256]{3,2,1,0:T(8,128)S(1)} %collective-permute-done.23), channel_id=1, source_target_pairs={{0,96},{32,0},{64,32},{96,64},{128,224},{160,128},{192,160},{224,1... | collective-permute-start | bytes 786440 | tf_op jit(solution)/shard_map/ppermute | solution.py:83
  197.0 0.3 collective-permute-done.24
  197.4 1.6 collective-permute-done.20
  199.0 3.2 %collective-permute-done.25 = f32[2,4,32,256]{3,2,1,0:T(8,128)S(1)} collective-permute-done((f32[2,4,32,256]{3,2,1,0:T(8,128)S(1)}, f32[2,4,32,256]{3,2,1,0:T(8,128)S(1)}, u32[]{:S(2)}, u32[]{:S(2)}) %collective-permute-start.25) | collective-permute-done | bytes 262176 | tf_op jit(solution)/shard_map/ppermute | solution.py:83
  202.2 3.7 %collective-permute-start.27 = (f32[2,4,32,256]{3,2,1,0:T(8,128)S(1)}, f32[2,4,32,256]{3,2,1,0:T(8,128)S(1)}, u32[]{:S(2)}, u32[]{:S(2)}) collective-permute-start(f32[2,4,32,256]{3,2,1,0:T(8,128)S(1)} %collective-permute-done.25), channel_id=1, source_target_pairs={{0,96},{32,0},{64,32},{96,64},{128,224},{160,128},{192,160},{224,1... | collective-permute-start | bytes 786440 | tf_op jit(solution)/shard_map/ppermute | solution.py:83
  206.0 3.7 %collective-permute-done.27 = f32[2,4,32,256]{3,2,1,0:T(8,128)S(1)} collective-permute-done((f32[2,4,32,256]{3,2,1,0:T(8,128)S(1)}, f32[2,4,32,256]{3,2,1,0:T(8,128)S(1)}, u32[]{:S(2)}, u32[]{:S(2)}) %collective-permute-start.27) | collective-permute-done | bytes 262176 | tf_op jit(solution)/shard_map/ppermute | solution.py:83
  209.8 3.3 %fusion.4 = f32[4,512,256]{2,1,0:T(8,128)} fusion(f32[4,512,256]{2,1,0:T(8,128)S(1)} %get-tuple-element.87, f32[512,512]{1,0:T(8,128)S(1)} %concatenate.12, f32[256]{0:T(256)S(1)} %bitcast.204), kind=kOutput, calls=%fused_computation.4 | convolution fusion | flops 1611137024 | bytes 5243904 | tf_op jit(solution)/shard_map/xij,xjz->xiz/dot_general | solution.py:97
  213.0 3.3 %fusion.7 = f32[4,512,256]{2,1,0:T(8,128)} fusion(f32[4,512,256]{2,1,0:T(8,128)S(1)} %get-tuple-element.86, f32[512,512]{1,0:T(8,128)S(1)} %concatenate.12, f32[256]{0:T(256)S(1)} %bitcast.203), kind=kOutput, calls=%fused_computation.5 | convolution fusion | flops 1611137024 | bytes 5243904 | tf_op jit(solution)/shard_map/xij,xjz->xiz/dot_general | solution.py:97
  (64 shorter events, 1.8 us)
Async XLA Ops:
  0.6 130.5 %copy-start = (f32[2,16]{1,0:T(2,128)S(1)}, f32[2,16]{1,0:T(2,128)}, u32[]{:S(2)}) copy-start(f32[2,16]{1,0:T(2,128)} %param.9) | copy-start | bytes 388
  0.6 2.0 copy-start.1
  4.2 12.2 %collective-permute-start = (f32[3,4,32,256]{3,2,1,0:T(8,128)S(1)}, f32[3,4,32,256]{3,2,1,0:T(8,128)S(1)}, u32[]{:S(2)}, u32[]{:S(2)}) collective-permute-start(f32[3,4,32,256]{3,2,1,0:T(8,128)S(1)} %pad_maximum_fusion), channel_id=1, source_target_pairs={{0,32},{32,64},{64,96},{96,0},{128,160},{160,192},{192,224},{224,1... | collective-permute-start | bytes 1179656 | tf_op jit(solution)/shard_map/ppermute | solution.py:48
  5.9 11.0 %collective-permute-start.3 = (f32[3,4,32,256]{3,2,1,0:T(8,128)S(1)}, f32[3,4,32,256]{3,2,1,0:T(8,128)S(1)}, u32[]{:S(2)}, u32[]{:S(2)}) collective-permute-start(f32[3,4,32,256]{3,2,1,0:T(8,128)S(1)} %pad_maximum_fusion.1), channel_id=1, source_target_pairs={{0,96},{32,0},{64,32},{96,64},{128,224},{160,128},{192,160},{224,1... | collective-permute-start | bytes 1179656 | tf_op jit(solution)/shard_map/ppermute | solution.py:49
  16.5 11.3 %collective-permute-start.1 = (f32[3,4,32,256]{3,2,1,0:T(8,128)S(1)}, f32[3,4,32,256]{3,2,1,0:T(8,128)S(1)}, u32[]{:S(2)}, u32[]{:S(2)}) collective-permute-start(f32[3,4,32,256]{3,2,1,0:T(8,128)S(1)} %maximum_add_fusion), channel_id=1, source_target_pairs={{0,32},{32,64},{64,96},{96,0},{128,160},{160,192},{192,224},{224,1... | collective-permute-start | bytes 1179656 | tf_op jit(solution)/shard_map/ppermute | solution.py:48
  17.0 11.1 %collective-permute-start.4 = (f32[3,4,32,256]{3,2,1,0:T(8,128)S(1)}, f32[3,4,32,256]{3,2,1,0:T(8,128)S(1)}, u32[]{:S(2)}, u32[]{:S(2)}) collective-permute-start(f32[3,4,32,256]{3,2,1,0:T(8,128)S(1)} %maximum_add_fusion.3), channel_id=1, source_target_pairs={{0,96},{32,0},{64,32},{96,64},{128,224},{160,128},{192,160},{224,1... | collective-permute-start | bytes 1179656 | tf_op jit(solution)/shard_map/ppermute | solution.py:49
  27.9 10.5 %collective-permute-start.2 = (f32[3,4,32,256]{3,2,1,0:T(8,128)S(1)}, f32[3,4,32,256]{3,2,1,0:T(8,128)}, u32[]{:S(2)}, u32[]{:S(2)}) collective-permute-start(f32[3,4,32,256]{3,2,1,0:T(8,128)S(1)} %maximum_add_fusion.1), channel_id=1, source_target_pairs={{0,32},{32,64},{64,96},{96,0},{128,160},{160,192},{192,224},{224,1... | collective-permute-start | bytes 1179656 | tf_op jit(solution)/shard_map/ppermute | solution.py:48
  28.8 10.8 %collective-permute-start.5 = (f32[3,4,32,256]{3,2,1,0:T(8,128)}, f32[3,4,32,256]{3,2,1,0:T(8,128)}, u32[]{:S(2)}, u32[]{:S(2)}) collective-permute-start(f32[3,4,32,256]{3,2,1,0:T(8,128)} %maximum_add_fusion.4), channel_id=1, source_target_pairs={{0,96},{32,0},{64,32},{96,64},{128,224},{160,128},{192,160},{224,1... | collective-permute-start | bytes 1179656 | tf_op jit(solution)/shard_map/ppermute | solution.py:49
  38.4 2.5 %copy-start.2 = (f32[1,4,512,256]{3,2,1,0:T(8,128)S(1)}, f32[1,4,512,256]{3,2,1,0:T(8,128)}, u32[]{:S(2)}) copy-start(f32[1,4,512,256]{3,2,1,0:T(8,128)} %param.5) | copy-start | bytes 6291460
  40.8 1.6 copy-start.3
  42.5 9.2 %collective-permute-start.10 = (f32[3,4,32,256]{3,2,1,0:T(8,128)S(1)}, f32[3,4,32,256]{3,2,1,0:T(8,128)S(1)}, u32[]{:S(2)}, u32[]{:S(2)}) collective-permute-start(f32[3,4,32,256]{3,2,1,0:T(8,128)S(1)} %pad_maximum_fusion.3), channel_id=1, source_target_pairs={{0,96},{32,0},{64,32},{96,64},{128,224},{160,128},{192,160},{224,1... | collective-permute-start | bytes 1179656 | tf_op jit(solution)/shard_map/ppermute | solution.py:49
  45.3 9.3 %collective-permute-start.7 = (f32[3,4,32,256]{3,2,1,0:T(8,128)S(1)}, f32[3,4,32,256]{3,2,1,0:T(8,128)S(1)}, u32[]{:S(2)}, u32[]{:S(2)}) collective-permute-start(f32[3,4,32,256]{3,2,1,0:T(8,128)S(1)} %pad_maximum_fusion.2), channel_id=1, source_target_pairs={{0,32},{32,64},{64,96},{96,0},{128,160},{160,192},{192,224},{224,1... | collective-permute-start | bytes 1179656 | tf_op jit(solution)/shard_map/ppermute | solution.py:48
  51.8 9.6 %collective-permute-start.11 = (f32[3,4,32,256]{3,2,1,0:T(8,128)S(1)}, f32[3,4,32,256]{3,2,1,0:T(8,128)S(1)}, u32[]{:S(2)}, u32[]{:S(2)}) collective-permute-start(f32[3,4,32,256]{3,2,1,0:T(8,128)S(1)} %maximum_add_fusion.9), channel_id=1, source_target_pairs={{0,96},{32,0},{64,32},{96,64},{128,224},{160,128},{192,160},{224,1... | collective-permute-start | bytes 1179656 | tf_op jit(solution)/shard_map/ppermute | solution.py:49
  54.7 17.3 %collective-permute-start.8 = (f32[3,4,32,256]{3,2,1,0:T(8,128)S(1)}, f32[3,4,32,256]{3,2,1,0:T(8,128)S(1)}, u32[]{:S(2)}, u32[]{:S(2)}) collective-permute-start(f32[3,4,32,256]{3,2,1,0:T(8,128)S(1)} %maximum_add_fusion.6), channel_id=1, source_target_pairs={{0,32},{32,64},{64,96},{96,0},{128,160},{160,192},{192,224},{224,1... | collective-permute-start | bytes 1179656 | tf_op jit(solution)/shard_map/ppermute | solution.py:48
  61.4 10.7 %collective-permute-start.12 = (f32[3,4,32,256]{3,2,1,0:T(8,128)S(1)}, f32[3,4,32,256]{3,2,1,0:T(8,128)S(1)}, u32[]{:S(2)}, u32[]{:S(2)}) collective-permute-start(f32[3,4,32,256]{3,2,1,0:T(8,128)S(1)} %maximum_add_fusion.10), channel_id=1, source_target_pairs={{0,96},{32,0},{64,32},{96,64},{128,224},{160,128},{192,160},{224,1... | collective-permute-start | bytes 1179656 | tf_op jit(solution)/shard_map/ppermute | solution.py:49
  64.8 20.6 %collective-permute-start.6 = (f32[3,4,32,256]{3,2,1,0:T(8,128)S(1)}, f32[3,4,32,256]{3,2,1,0:T(8,128)S(1)}, u32[]{:S(2)}, u32[]{:S(2)}) collective-permute-start(f32[3,4,32,256]{3,2,1,0:T(8,128)S(1)} %maximum_add_fusion.5), channel_id=1, source_target_pairs={{0,128},{32,160},{64,192},{96,224},{128,0},{160,32},{192,64},{224,... | collective-permute-start | bytes 1179656 | tf_op jit(solution)/shard_map/ppermute | solution.py:60
  72.1 13.4 %collective-permute-start.9 = (f32[3,4,32,256]{3,2,1,0:T(8,128)S(1)}, f32[3,4,32,256]{3,2,1,0:T(8,128)S(1)}, u32[]{:S(2)}, u32[]{:S(2)}) collective-permute-start(f32[3,4,32,256]{3,2,1,0:T(8,128)S(1)} %maximum_add_fusion.7), channel_id=1, source_target_pairs={{0,32},{32,64},{64,96},{96,0},{128,160},{160,192},{192,224},{224,1... | collective-permute-start | bytes 1179656 | tf_op jit(solution)/shard_map/ppermute | solution.py:48
  72.2 26.6 %collective-permute-start.13 = (f32[3,4,32,256]{3,2,1,0:T(8,128)S(1)}, f32[3,4,32,256]{3,2,1,0:T(8,128)S(1)}, u32[]{:S(2)}, u32[]{:S(2)}) collective-permute-start(f32[3,4,32,256]{3,2,1,0:T(8,128)S(1)} %maximum_add_fusion.11), channel_id=1, source_target_pairs={{0,128},{32,160},{64,192},{96,224},{128,0},{160,32},{192,64},{224,... | collective-permute-start | bytes 1179656 | tf_op jit(solution)/shard_map/ppermute | solution.py:60
  100.6 22.2 %all-to-all-start = ((f32[2,4,64,256]{3,1,0,2:T(4,128)}), f32[2,4,64,256]{3,1,0,2:T(4,128)S(1)}, u32[]{:S(2)}, u32[]{:S(2)}) async-start(f32[2,4,64,256]{3,1,0,2:T(4,128)} %copy.13), calls=%async_computation | async-start | bytes 1048576 | tf_op jit(solution)/shard_map/all_to_all | solution.py:107
  123.2 8.0 %copy-start.4 = (s32[256]{0:T(256)S(1)}, s32[256]{0:T(256)}, u32[]{:S(2)}) copy-start(s32[256]{0:T(256)} %param.8) | copy-start | bytes 3076
  124.8 20.6 %all-to-all-start.1 = ((f32[2,128,2,256]{3,2,0,1:T(2,128)}), f32[2,128,2,256]{3,2,0,1:T(2,128)S(1)}, u32[]{:S(2)}, u32[]{:S(2)}) async-start(f32[2,128,2,256]{3,2,0,1:T(2,128)} %copy.16), calls=%async_computation.1 | async-start | bytes 1048576 | tf_op jit(solution)/shard_map/all_to_all | solution.py:110
  146.7 19.1 %collective-permute-start.14 = (f32[2,4,32,256]{3,2,1,0:T(8,128)}, f32[2,4,32,256]{3,2,1,0:T(8,128)}, u32[]{:S(2)}, u32[]{:S(2)}) collective-permute-start(f32[2,4,32,256]{3,2,1,0:T(8,128)} %slice.150), channel_id=1, source_target_pairs={{0,128},{32,160},{64,192},{96,224},{128,0},{160,32},{192,64},{224,... | collective-permute-start | bytes 786440 | tf_op jit(solution)/shard_map/ppermute | solution.py:75
  151.7 20.0 %collective-permute-start.15 = (f32[2,4,32,256]{3,2,1,0:T(8,128)}, f32[2,4,32,256]{3,2,1,0:T(8,128)}, u32[]{:S(2)}, u32[]{:S(2)}) collective-permute-start(f32[2,4,32,256]{3,2,1,0:T(8,128)} %slice.150), channel_id=1, source_target_pairs={{0,32},{32,64},{64,96},{96,0},{128,160},{160,192},{192,224},{224,1... | collective-permute-start | bytes 786440 | tf_op jit(solution)/shard_map/ppermute | solution.py:82
  165.8 17.5 %collective-permute-start.21 = (f32[2,4,32,256]{3,2,1,0:T(8,128)S(1)}, f32[2,4,32,256]{3,2,1,0:T(8,128)S(1)}, u32[]{:S(2)}, u32[]{:S(2)}) collective-permute-start(f32[2,4,32,256]{3,2,1,0:T(8,128)S(1)} %slice.123), channel_id=1, source_target_pairs={{0,128},{32,160},{64,192},{96,224},{128,0},{160,32},{192,64},{224,... | collective-permute-start | bytes 786440 | tf_op jit(solution)/shard_map/ppermute | solution.py:75
  168.5 18.1 %collective-permute-start.22 = (f32[2,4,32,256]{3,2,1,0:T(8,128)S(1)}, f32[2,4,32,256]{3,2,1,0:T(8,128)S(1)}, u32[]{:S(2)}, u32[]{:S(2)}) collective-permute-start(f32[2,4,32,256]{3,2,1,0:T(8,128)S(1)} %slice.123), channel_id=1, source_target_pairs={{0,32},{32,64},{64,96},{96,0},{128,160},{160,192},{192,224},{224,1... | collective-permute-start | bytes 786440 | tf_op jit(solution)/shard_map/ppermute | solution.py:82
  169.4 7.9 %collective-permute-start.16 = (f32[2,4,32,256]{3,2,1,0:T(8,128)}, f32[2,4,32,256]{3,2,1,0:T(8,128)S(1)}, u32[]{:S(2)}, u32[]{:S(2)}) collective-permute-start(f32[2,4,32,256]{3,2,1,0:T(8,128)} %collective-permute-done.14), channel_id=1, source_target_pairs={{0,96},{32,0},{64,32},{96,64},{128,224},{160,128},{192,160},{224,1... | collective-permute-start | bytes 786440 | tf_op jit(solution)/shard_map/ppermute | solution.py:83
  171.8 11.6 %collective-permute-start.17 = (f32[2,4,32,256]{3,2,1,0:T(8,128)}, f32[2,4,32,256]{3,2,1,0:T(8,128)S(1)}, u32[]{:S(2)}, u32[]{:S(2)}) collective-permute-start(f32[2,4,32,256]{3,2,1,0:T(8,128)} %collective-permute-done.15), channel_id=1, source_target_pairs={{0,32},{32,64},{64,96},{96,0},{128,160},{160,192},{192,224},{224,1... | collective-permute-start | bytes 786440 | tf_op jit(solution)/shard_map/ppermute | solution.py:82
  177.4 9.3 %collective-permute-start.18 = (f32[2,4,32,256]{3,2,1,0:T(8,128)S(1)}, f32[2,4,32,256]{3,2,1,0:T(8,128)S(1)}, u32[]{:S(2)}, u32[]{:S(2)}) collective-permute-start(f32[2,4,32,256]{3,2,1,0:T(8,128)S(1)} %collective-permute-done.16), channel_id=1, source_target_pairs={{0,96},{32,0},{64,32},{96,64},{128,224},{160,128},{192,160},{224,1... | collective-permute-start | bytes 786440 | tf_op jit(solution)/shard_map/ppermute | solution.py:83
  183.3 14.0 %collective-permute-start.19 = (f32[2,4,32,256]{3,2,1,0:T(8,128)S(1)}, f32[2,4,32,256]{3,2,1,0:T(8,128)S(1)}, u32[]{:S(2)}, u32[]{:S(2)}) collective-permute-start(f32[2,4,32,256]{3,2,1,0:T(8,128)S(1)} %collective-permute-done.17), channel_id=1, source_target_pairs={{0,32},{32,64},{64,96},{96,0},{128,160},{160,192},{192,224},{224,1... | collective-permute-start | bytes 786440 | tf_op jit(solution)/shard_map/ppermute | solution.py:82
  183.3 10.0 %collective-permute-start.23 = (f32[2,4,32,256]{3,2,1,0:T(8,128)S(1)}, f32[2,4,32,256]{3,2,1,0:T(8,128)S(1)}, u32[]{:S(2)}, u32[]{:S(2)}) collective-permute-start(f32[2,4,32,256]{3,2,1,0:T(8,128)S(1)} %collective-permute-done.21), channel_id=1, source_target_pairs={{0,96},{32,0},{64,32},{96,64},{128,224},{160,128},{192,160},{224,1... | collective-permute-start | bytes 786440 | tf_op jit(solution)/shard_map/ppermute | solution.py:83
  186.6 10.7 %collective-permute-start.24 = (f32[2,4,32,256]{3,2,1,0:T(8,128)S(1)}, f32[2,4,32,256]{3,2,1,0:T(8,128)S(1)}, u32[]{:S(2)}, u32[]{:S(2)}) collective-permute-start(f32[2,4,32,256]{3,2,1,0:T(8,128)S(1)} %collective-permute-done.22), channel_id=1, source_target_pairs={{0,32},{32,64},{64,96},{96,0},{128,160},{160,192},{192,224},{224,1... | collective-permute-start | bytes 786440 | tf_op jit(solution)/shard_map/ppermute | solution.py:82
  186.7 12.3 %collective-permute-start.20 = (f32[2,4,32,256]{3,2,1,0:T(8,128)S(1)}, f32[2,4,32,256]{3,2,1,0:T(8,128)S(1)}, u32[]{:S(2)}, u32[]{:S(2)}) collective-permute-start(f32[2,4,32,256]{3,2,1,0:T(8,128)S(1)} %collective-permute-done.18), channel_id=1, source_target_pairs={{0,96},{32,0},{64,32},{96,64},{128,224},{160,128},{192,160},{224,1... | collective-permute-start | bytes 786440 | tf_op jit(solution)/shard_map/ppermute | solution.py:83
  193.3 8.8 %collective-permute-start.25 = (f32[2,4,32,256]{3,2,1,0:T(8,128)S(1)}, f32[2,4,32,256]{3,2,1,0:T(8,128)S(1)}, u32[]{:S(2)}, u32[]{:S(2)}) collective-permute-start(f32[2,4,32,256]{3,2,1,0:T(8,128)S(1)} %collective-permute-done.23), channel_id=1, source_target_pairs={{0,96},{32,0},{64,32},{96,64},{128,224},{160,128},{192,160},{224,1... | collective-permute-start | bytes 786440 | tf_op jit(solution)/shard_map/ppermute | solution.py:83
  197.3 8.7 %collective-permute-start.26 = (f32[2,4,32,256]{3,2,1,0:T(8,128)S(1)}, f32[2,4,32,256]{3,2,1,0:T(8,128)S(1)}, u32[]{:S(2)}, u32[]{:S(2)}) collective-permute-start(f32[2,4,32,256]{3,2,1,0:T(8,128)S(1)} %collective-permute-done.24), channel_id=1, source_target_pairs={{0,32},{32,64},{64,96},{96,0},{128,160},{160,192},{192,224},{224,1... | collective-permute-start | bytes 786440 | tf_op jit(solution)/shard_map/ppermute | solution.py:82
  202.2 7.6 %collective-permute-start.27 = (f32[2,4,32,256]{3,2,1,0:T(8,128)S(1)}, f32[2,4,32,256]{3,2,1,0:T(8,128)S(1)}, u32[]{:S(2)}, u32[]{:S(2)}) collective-permute-start(f32[2,4,32,256]{3,2,1,0:T(8,128)S(1)} %collective-permute-done.25), channel_id=1, source_target_pairs={{0,96},{32,0},{64,32},{96,64},{128,224},{160,128},{192,160},{224,1... | collective-permute-start | bytes 786440 | tf_op jit(solution)/shard_map/ppermute | solution.py:83

commit v3 on v1

--- a/solution.py
+++ b/solution.py
@@ -38,7 +38,7 @@
     sub = half // parts
     fwd, bwd = ring_pairs(n_shots, 1), ring_pairs(n_shots, -1)
 
-    def ring(fields, off):
+    def ring(fields, off, gate):
         def take(start):
             return jnp.stack([rows(f, start + off, sub) for f in fields])
 
@@ -47,17 +47,21 @@
         for t in range(1, RING):
             recv_f = lax.ppermute(acc_f, "shots", fwd)
             recv_b = lax.ppermute(acc_b, "shots", bwd)
+            if t == 2 and gate is not None:
+                recv_f, recv_b, gate = lax.optimization_barrier((recv_f, recv_b, gate))
             acc_f = recv_f + take(((r - 1 - t) % RING) * chunk + h * half)
             acc_b = recv_b + take(((r + 1 + t) % RING) * chunk + (1 - h) * half)
         return acc_f, acc_b
 
     out = []
     fields = tuple(fields)
+    gate = None
     for p in range(parts):
-        acc_f, acc_b = ring(fields, p * sub)
+        acc_f, acc_b = ring(fields, p * sub, gate)
         if p + 1 < parts:
             fields, acc_f, acc_b = lax.optimization_barrier((fields, acc_f, acc_b))
-        out.append(acc_f + lax.ppermute(acc_b, "shots", hi_pairs(n_shots)))
+        gate = lax.ppermute(acc_b, "shots", hi_pairs(n_shots))
+        out.append(acc_f + gate)
     return jnp.concatenate(out, axis=2)
 
 

time: 223 us -> 219 us (0.982)
  waiting for transfers between devices: 111 us -> 102 us
  starting transfers between devices: 73.8 us -> 78 us
    ppermute x6, waiting for transfers between devices: 12.9 us -> 5.62 us  [ring(): recv_b = lax.ppermute(acc_b, 'shots', bwd)]
    ppermute x2, waiting for transfers between devices: 21 us -> 17 us  [reduce_scatter_shots(): gate = lax.ppermute(acc_b, 'shots', hi_pairs(n_shots))]
    ppermute x2, starting transfers between devices: 12.6 us -> 15.1 us  [reduce_scatter_shots(): gate = lax.ppermute(acc_b, 'shots', hi_pairs(n_shots))]
    ppermute x6, starting transfers between devices: 17 us -> 19.2 us  [ring(): recv_b = lax.ppermute(acc_b, 'shots', bwd)]
  transfers between devices with their start and end apart: 30 -> 30, of which waited for: 17 -> 18; matrix products, arithmetic and copies ran while one was open for 6% -> 6% of each run, Pallas kernels for 0% -> 0%
where the time goes in v3:
time: 219 us; the launch traced here: 215 us
  waiting for transfers between devices  102 us (47%)
  starting transfers between devices  78 us (36%)
  local copies, waits for them, and re-layouts  16.8 us (8%)
  matrix products  11.7 us (5%)
  other arithmetic  5.15 us (2%)
    ppermute x6, waiting for transfers between devices, ring(): recv_f = lax.ppermute(acc_f, 'shots', fwd)  25.1 us
    ppermute x6, starting transfers between devices, all_gather_smooth_shots(): cur_b = lax.ppermute(cur_b, 'shots', bwd)  20.7 us
    ppermute x6, starting transfers between devices, ring(): recv_b = lax.ppermute(acc_b, 'shots', bwd)  19.2 us
    ppermute x2, waiting for transfers between devices, reduce_scatter_shots(): gate = lax.ppermute(acc_b, 'shots', hi_pairs(n_shots))  17 us
    ppermute x6, waiting for transfers between devices, all_gather_smooth_shots(): cur_b = lax.ppermute(cur_b, 'shots', bwd)  15.3 us
    ppermute x2, starting transfers between devices, reduce_scatter_shots(): gate = lax.ppermute(acc_b, 'shots', hi_pairs(n_shots))  15.1 us
    all_to_all x1, waiting for transfers between devices, smooth_along_x(): cols = lax.all_to_all(both, 'slab', split_axis=2, concat_axis=1, tiled=True)  14.6 us
    all_to_all x1, waiting for transfers between devices, smooth_along_x(): return lax.all_to_all(cols, 'slab', split_axis=1, concat_axis=2, tiled=True)  13.5 us
  transfers between devices with their start and end apart: 30, of which 18 were waited for; matrix products, arithmetic and copies ran while one was open for 6% of the time, Pallas kernels for 0%

profile of v3, /device:TPU:2, one launch (start us, length us, event | category | flops | bytes accessed | tf_op | source)
XLA Modules:
  0.0 215.4 jit_solution(9375794608791806663)
XLA Ops:
  0.8 1.5 constant_dynamic-slice_fusion.2
  2.3 0.3 copy-done.1
  2.7 1.5 constant_dynamic-slice_fusion
  4.2 1.7 collective-permute-start
  5.9 1.7 collective-permute-start.3
  7.7 8.8 %collective-permute-done = f32[3,4,32,256]{3,2,1,0:T(8,128)S(1)} collective-permute-done((f32[3,4,32,256]{3,2,1,0:T(8,128)S(1)}, f32[3,4,32,256]{3,2,1,0:T(8,128)S(1)}, u32[]{:S(2)}, u32[]{:S(2)}) %collective-permute-start) | collective-permute-done | bytes 393248 | tf_op jit(solution)/shard_map/ppermute | solution.py:48
  16.5 0.4 collective-permute-start.1
  17.0 3.0 %collective-permute-start.4 = (f32[3,4,32,256]{3,2,1,0:T(8,128)S(1)}, f32[3,4,32,256]{3,2,1,0:T(8,128)S(1)}, u32[]{:S(2)}, u32[]{:S(2)}) collective-permute-start(f32[3,4,32,256]{3,2,1,0:T(8,128)S(1)} %maximum_add_fusion.3), channel_id=1, source_target_pairs={{0,96},{32,0},{64,32},{96,64},{128,224},{160,128},{192,160},{224,1... | collective-permute-start | bytes 1179656 | tf_op jit(solution)/shard_map/ppermute | solution.py:49
  20.0 7.9 %collective-permute-done.1 = f32[3,4,32,256]{3,2,1,0:T(8,128)S(1)} collective-permute-done((f32[3,4,32,256]{3,2,1,0:T(8,128)S(1)}, f32[3,4,32,256]{3,2,1,0:T(8,128)S(1)}, u32[]{:S(2)}, u32[]{:S(2)}) %collective-permute-start.1) | collective-permute-done | bytes 393248 | tf_op jit(solution)/shard_map/ppermute | solution.py:48
  28.0 0.8 maximum_add_fusion.4
  28.8 3.2 %collective-permute-start.5 = (f32[3,4,32,256]{3,2,1,0:T(8,128)}, f32[3,4,32,256]{3,2,1,0:T(8,128)}, u32[]{:S(2)}, u32[]{:S(2)}) collective-permute-start(f32[3,4,32,256]{3,2,1,0:T(8,128)} %maximum_add_fusion.4), channel_id=1, source_target_pairs={{0,96},{32,0},{64,32},{96,64},{128,224},{160,128},{192,160},{224,1... | collective-permute-start | bytes 1179656 | tf_op jit(solution)/shard_map/ppermute | solution.py:49
  32.0 6.4 %collective-permute-done.2 = f32[3,4,32,256]{3,2,1,0:T(8,128)} collective-permute-done((f32[3,4,32,256]{3,2,1,0:T(8,128)S(1)}, f32[3,4,32,256]{3,2,1,0:T(8,128)}, u32[]{:S(2)}, u32[]{:S(2)}) %collective-permute-start.2) | collective-permute-done | bytes 393248 | tf_op jit(solution)/shard_map/ppermute | solution.py:48
  38.5 1.2 maximum_add_fusion.2
  39.7 1.1 maximum_add_fusion.5
  40.9 0.1 dynamic-slice_bitcast_fusion.7
  41.0 1.3 copy-done.3
  42.6 3.3 %collective-permute-start.9 = (f32[3,4,32,256]{3,2,1,0:T(8,128)S(1)}, f32[3,4,32,256]{3,2,1,0:T(8,128)S(1)}, u32[]{:S(2)}, u32[]{:S(2)}) collective-permute-start(f32[3,4,32,256]{3,2,1,0:T(8,128)S(1)} %pad_maximum_fusion.3), channel_id=1, source_target_pairs={{0,96},{32,0},{64,32},{96,64},{128,224},{160,128},{192,160},{224,1... | collective-permute-start | bytes 1179656 | tf_op jit(solution)/shard_map/ppermute | solution.py:49
  45.9 7.2 %collective-permute-start.6 = (f32[3,4,32,256]{3,2,1,0:T(8,128)S(1)}, f32[3,4,32,256]{3,2,1,0:T(8,128)S(1)}, u32[]{:S(2)}, u32[]{:S(2)}) collective-permute-start(f32[3,4,32,256]{3,2,1,0:T(8,128)S(1)} %maximum_add_fusion.5), channel_id=1, source_target_pairs={{0,128},{32,160},{64,192},{96,224},{128,0},{160,32},{192,64},{224,... | collective-permute-start | bytes 1179656 | tf_op jit(solution)/shard_map/ppermute | solution.py:63
  53.3 3.3 %collective-permute-start.10 = (f32[3,4,32,256]{3,2,1,0:T(8,128)S(1)}, f32[3,4,32,256]{3,2,1,0:T(8,128)S(1)}, u32[]{:S(2)}, u32[]{:S(2)}) collective-permute-start(f32[3,4,32,256]{3,2,1,0:T(8,128)S(1)} %maximum_add_fusion.7), channel_id=1, source_target_pairs={{0,96},{32,0},{64,32},{96,64},{128,224},{160,128},{192,160},{224,1... | collective-permute-start | bytes 1179656 | tf_op jit(solution)/shard_map/ppermute | solution.py:49
  56.6 3.5 %collective-permute-done.6 = f32[3,4,32,256]{3,2,1,0:T(8,128)S(1)} collective-permute-done((f32[3,4,32,256]{3,2,1,0:T(8,128)S(1)}, f32[3,4,32,256]{3,2,1,0:T(8,128)S(1)}, u32[]{:S(2)}, u32[]{:S(2)}) %collective-permute-start.6) | collective-permute-done | bytes 393248 | tf_op jit(solution)/shard_map/ppermute | solution.py:63
  60.2 2.1 collective-permute-done.8
  62.2 0.5 collective-permute-done.10
  62.8 4.7 %collective-permute-start.12 = (f32[3,4,32,256]{3,2,1,0:T(8,128)S(1)}, f32[3,4,32,256]{3,2,1,0:T(8,128)S(1)}, u32[]{:S(2)}, u32[]{:S(2)}) collective-permute-start(f32[3,4,32,256]{3,2,1,0:T(8,128)S(1)} %maximum_add_fusion.10), channel_id=1, source_target_pairs={{0,96},{32,0},{64,32},{96,64},{128,224},{160,128},{192,160},{224,1... | collective-permute-start | bytes 1179656 | tf_op jit(solution)/shard_map/ppermute | solution.py:49
  67.6 5.1 %collective-permute-done.12 = f32[3,4,32,256]{3,2,1,0:T(8,128)S(1)} collective-permute-done((f32[3,4,32,256]{3,2,1,0:T(8,128)S(1)}, f32[3,4,32,256]{3,2,1,0:T(8,128)S(1)}, u32[]{:S(2)}, u32[]{:S(2)}) %collective-permute-start.12) | collective-permute-done | bytes 393248 | tf_op jit(solution)/shard_map/ppermute | solution.py:49
  72.8 7.9 %collective-permute-start.13 = (f32[3,4,32,256]{3,2,1,0:T(8,128)S(1)}, f32[3,4,32,256]{3,2,1,0:T(8,128)S(1)}, u32[]{:S(2)}, u32[]{:S(2)}) collective-permute-start(f32[3,4,32,256]{3,2,1,0:T(8,128)S(1)} %maximum_add_fusion.11), channel_id=1, source_target_pairs={{0,128},{32,160},{64,192},{96,224},{128,0},{160,32},{192,64},{224,... | collective-permute-start | bytes 1179656 | tf_op jit(solution)/shard_map/ppermute | solution.py:63
  80.7 0.2 fusion.31
  81.0 13.5 %collective-permute-done.13 = f32[3,4,32,256]{3,2,1,0:T(8,128)S(1)} collective-permute-done((f32[3,4,32,256]{3,2,1,0:T(8,128)S(1)}, f32[3,4,32,256]{3,2,1,0:T(8,128)S(1)}, u32[]{:S(2)}, u32[]{:S(2)}) %collective-permute-start.13) | collective-permute-done | bytes 393248 | tf_op jit(solution)/shard_map/ppermute | solution.py:63
  94.6 0.7 fusion.15
  95.3 1.1 copy.13
  96.4 7.4 %all-to-all-start = ((f32[2,4,64,256]{3,1,0,2:T(4,128)}), f32[2,4,64,256]{3,1,0,2:T(4,128)S(1)}, u32[]{:S(2)}, u32[]{:S(2)}) async-start(f32[2,4,64,256]{3,1,0,2:T(4,128)} %copy.13), calls=%async_computation | async-start | bytes 1048576 | tf_op jit(solution)/shard_map/all_to_all | solution.py:111
  103.9 14.6 %all-to-all-done = f32[2,4,64,256]{3,1,0,2:T(4,128)S(1)} async-done(((f32[2,4,64,256]{3,1,0,2:T(4,128)}), f32[2,4,64,256]{3,1,0,2:T(4,128)S(1)}, u32[]{:S(2)}, u32[]{:S(2)}) %all-to-all-start) | async-done | bytes 524320 | tf_op jit(solution)/shard_map/all_to_all | solution.py:111
  118.5 0.3 copy.14
  118.8 1.0 convolution_bitcast_fusion
  119.8 1.0 copy.16
  120.8 5.8 %all-to-all-start.1 = ((f32[2,128,2,256]{3,2,0,1:T(2,128)}), f32[2,128,2,256]{3,2,0,1:T(2,128)S(1)}, u32[]{:S(2)}, u32[]{:S(2)}) async-start(f32[2,128,2,256]{3,2,0,1:T(2,128)} %copy.16), calls=%async_computation.1 | async-start | bytes 1048576 | tf_op jit(solution)/shard_map/all_to_all | solution.py:114
  126.7 0.5 fusion.14
  127.2 0.2 convolution_bitcast_fusion.1
  127.4 0.5 fusion.13
  127.9 13.5 %all-to-all-done.1 = f32[2,128,2,256]{3,2,0,1:T(2,128)S(1)} async-done(((f32[2,128,2,256]{3,2,0,1:T(2,128)}), f32[2,128,2,256]{3,2,0,1:T(2,128)S(1)}, u32[]{:S(2)}, u32[]{:S(2)}) %all-to-all-start.1) | async-done | bytes 524320 | tf_op jit(solution)/shard_map/all_to_all | solution.py:114
  141.3 0.2 copy.18
  141.5 0.4 all_to_all.33
  141.9 0.7 slice.150
  142.6 4.5 %collective-permute-start.14 = (f32[2,4,32,256]{3,2,1,0:T(8,128)}, f32[2,4,32,256]{3,2,1,0:T(8,128)}, u32[]{:S(2)}, u32[]{:S(2)}) collective-permute-start(f32[2,4,32,256]{3,2,1,0:T(8,128)} %slice.150), channel_id=1, source_target_pairs={{0,128},{32,160},{64,192},{96,224},{128,0},{160,32},{192,64},{224,... | collective-permute-start | bytes 786440 | tf_op jit(solution)/shard_map/ppermute | solution.py:79
  147.1 2.5 %constant_dynamic-slice_fusion.24 = (f32[512,32]{1,0:T(8,128)S(1)}, f32[512,32]{1,0:T(8,128)S(1)}, f32[512,32]{1,0:T(8,128)S(1)}, f32[512,32]{1,0:T(8,128)S(1)},...) fusion(f32[512,512]{1,0:T(8,128)S(1)} %fusion.13, ...), kind=kLoop, calls=%fused_computation.180 | loop fusion | bytes 2097216 | tf_op jit(solution)/shard_map/dynamic_slice | solution.py:95
  149.7 3.3 %concatenate.12 = f32[512,512]{1,0:T(8,128)S(1)} concatenate(f32[512,32]{1,0:T(8,128)} %get-tuple-element.83, f32[512,32]{1,0:T(8,128)} %get-tuple-element.82, f32[512,32]{1,0:T(8,128)} %get-tuple-element.81, f32[512,32]{1,0:T(8,128)} %get-tuple-element.80, f32[512,32]{1,0:T(8,128)} %get-tuple-element.79, f32[512,32]{1,0:T(8,128)} %get-tuple-element.78, ...), dimensions={1} | concatenate | bytes 2097152 | tf_op jit(solution)/shard_map/concatenate | solution.py:94
  153.0 8.7 %collective-permute-done.14 = f32[2,4,32,256]{3,2,1,0:T(8,128)} collective-permute-done((f32[2,4,32,256]{3,2,1,0:T(8,128)}, f32[2,4,32,256]{3,2,1,0:T(8,128)}, u32[]{:S(2)}, u32[]{:S(2)}) %collective-permute-start.14) | collective-permute-done | bytes 262176 | tf_op jit(solution)/shard_map/ppermute | solution.py:79
  161.8 2.8 %collective-permute-start.21 = (f32[2,4,32,256]{3,2,1,0:T(8,128)S(1)}, f32[2,4,32,256]{3,2,1,0:T(8,128)S(1)}, u32[]{:S(2)}, u32[]{:S(2)}) collective-permute-start(f32[2,4,32,256]{3,2,1,0:T(8,128)S(1)} %slice.123), channel_id=1, source_target_pairs={{0,128},{32,160},{64,192},{96,224},{128,0},{160,32},{192,64},{224,... | collective-permute-start | bytes 786440 | tf_op jit(solution)/shard_map/ppermute | solution.py:79
  164.6 3.2 %collective-permute-start.16 = (f32[2,4,32,256]{3,2,1,0:T(8,128)}, f32[2,4,32,256]{3,2,1,0:T(8,128)S(1)}, u32[]{:S(2)}, u32[]{:S(2)}) collective-permute-start(f32[2,4,32,256]{3,2,1,0:T(8,128)} %collective-permute-done.14), channel_id=1, source_target_pairs={{0,96},{32,0},{64,32},{96,64},{128,224},{160,128},{192,160},{224,1... | collective-permute-start | bytes 786440 | tf_op jit(solution)/shard_map/ppermute | solution.py:87
  167.8 1.0 bitcast_dynamic-update-slice_fusion.1
  168.8 1.0 fusion.44
  169.8 3.5 %collective-permute-done.16 = f32[2,4,32,256]{3,2,1,0:T(8,128)S(1)} collective-permute-done((f32[2,4,32,256]{3,2,1,0:T(8,128)}, f32[2,4,32,256]{3,2,1,0:T(8,128)S(1)}, u32[]{:S(2)}, u32[]{:S(2)}) %collective-permute-start.16) | collective-permute-done | bytes 262176 | tf_op jit(solution)/shard_map/ppermute | solution.py:87
  173.3 3.6 %collective-permute-start.18 = (f32[2,4,32,256]{3,2,1,0:T(8,128)S(1)}, f32[2,4,32,256]{3,2,1,0:T(8,128)S(1)}, u32[]{:S(2)}, u32[]{:S(2)}) collective-permute-start(f32[2,4,32,256]{3,2,1,0:T(8,128)S(1)} %collective-permute-done.16), channel_id=1, source_target_pairs={{0,96},{32,0},{64,32},{96,64},{128,224},{160,128},{192,160},{224,1... | collective-permute-start | bytes 786440 | tf_op jit(solution)/shard_map/ppermute | solution.py:87
  176.9 2.4 %collective-permute-done.17 = f32[2,4,32,256]{3,2,1,0:T(8,128)S(1)} collective-permute-done((f32[2,4,32,256]{3,2,1,0:T(8,128)}, f32[2,4,32,256]{3,2,1,0:T(8,128)S(1)}, u32[]{:S(2)}, u32[]{:S(2)}) %collective-permute-start.17) | collective-permute-done | bytes 262176 | tf_op jit(solution)/shard_map/ppermute | solution.py:86
  179.3 3.2 %collective-permute-start.23 = (f32[2,4,32,256]{3,2,1,0:T(8,128)S(1)}, f32[2,4,32,256]{3,2,1,0:T(8,128)S(1)}, u32[]{:S(2)}, u32[]{:S(2)}) collective-permute-start(f32[2,4,32,256]{3,2,1,0:T(8,128)S(1)} %collective-permute-done.21), channel_id=1, source_target_pairs={{0,96},{32,0},{64,32},{96,64},{128,224},{160,128},{192,160},{224,1... | collective-permute-start | bytes 786440 | tf_op jit(solution)/shard_map/ppermute | solution.py:87
  182.6 3.3 %collective-permute-start.20 = (f32[2,4,32,256]{3,2,1,0:T(8,128)S(1)}, f32[2,4,32,256]{3,2,1,0:T(8,128)S(1)}, u32[]{:S(2)}, u32[]{:S(2)}) collective-permute-start(f32[2,4,32,256]{3,2,1,0:T(8,128)S(1)} %collective-permute-done.18), channel_id=1, source_target_pairs={{0,96},{32,0},{64,32},{96,64},{128,224},{160,128},{192,160},{224,1... | collective-permute-start | bytes 786440 | tf_op jit(solution)/shard_map/ppermute | solution.py:87
  185.9 3.4 %collective-permute-done.23 = f32[2,4,32,256]{3,2,1,0:T(8,128)S(1)} collective-permute-done((f32[2,4,32,256]{3,2,1,0:T(8,128)S(1)}, f32[2,4,32,256]{3,2,1,0:T(8,128)S(1)}, u32[]{:S(2)}, u32[]{:S(2)}) %collective-permute-start.23) | collective-permute-done | bytes 262176 | tf_op jit(solution)/shard_map/ppermute | solution.py:87
  189.3 3.7 %collective-permute-start.25 = (f32[2,4,32,256]{3,2,1,0:T(8,128)S(1)}, f32[2,4,32,256]{3,2,1,0:T(8,128)S(1)}, u32[]{:S(2)}, u32[]{:S(2)}) collective-permute-start(f32[2,4,32,256]{3,2,1,0:T(8,128)S(1)} %collective-permute-done.23), channel_id=1, source_target_pairs={{0,96},{32,0},{64,32},{96,64},{128,224},{160,128},{192,160},{224,1... | collective-permute-start | bytes 786440 | tf_op jit(solution)/shard_map/ppermute | solution.py:87
  193.0 0.1 collective-permute-done.24
  193.2 1.7 collective-permute-done.20
  195.0 3.1 %collective-permute-done.25 = f32[2,4,32,256]{3,2,1,0:T(8,128)S(1)} collective-permute-done((f32[2,4,32,256]{3,2,1,0:T(8,128)S(1)}, f32[2,4,32,256]{3,2,1,0:T(8,128)S(1)}, u32[]{:S(2)}, u32[]{:S(2)}) %collective-permute-start.25) | collective-permute-done | bytes 262176 | tf_op jit(solution)/shard_map/ppermute | solution.py:87
  198.0 3.7 %collective-permute-start.27 = (f32[2,4,32,256]{3,2,1,0:T(8,128)S(1)}, f32[2,4,32,256]{3,2,1,0:T(8,128)S(1)}, u32[]{:S(2)}, u32[]{:S(2)}) collective-permute-start(f32[2,4,32,256]{3,2,1,0:T(8,128)S(1)} %collective-permute-done.25), channel_id=1, source_target_pairs={{0,96},{32,0},{64,32},{96,64},{128,224},{160,128},{192,160},{224,1... | collective-permute-start | bytes 786440 | tf_op jit(solution)/shard_map/ppermute | solution.py:87
  201.9 3.7 %collective-permute-done.27 = f32[2,4,32,256]{3,2,1,0:T(8,128)S(1)} collective-permute-done((f32[2,4,32,256]{3,2,1,0:T(8,128)S(1)}, f32[2,4,32,256]{3,2,1,0:T(8,128)S(1)}, u32[]{:S(2)}, u32[]{:S(2)}) %collective-permute-start.27) | collective-permute-done | bytes 262176 | tf_op jit(solution)/shard_map/ppermute | solution.py:87
  205.6 4.9 %fusion.4 = f32[4,512,256]{2,1,0:T(8,128)} fusion(f32[4,512,256]{2,1,0:T(8,128)S(1)} %get-tuple-element.91, f32[512,512]{1,0:T(8,128)S(1)} %concatenate.12, f32[256]{0:T(256)S(1)} %bitcast.204), kind=kOutput, calls=%fused_computation.4 | convolution fusion | flops 3221749760 | bytes 5243904 | tf_op jit(solution)/shard_map/xij,xjz->xiz/dot_general | solution.py:101
  210.5 4.9 %fusion.7 = f32[4,512,256]{2,1,0:T(8,128)} fusion(f32[4,512,256]{2,1,0:T(8,128)S(1)} %get-tuple-element.90, f32[512,512]{1,0:T(8,128)S(1)} %concatenate.12, f32[256]{0:T(256)S(1)} %bitcast.203), kind=kOutput, calls=%fused_computation.5 | convolution fusion | flops 3221749760 | bytes 5243904 | tf_op jit(solution)/shard_map/xij,xjz->xiz/dot_general | solution.py:101
  (64 shorter events, 1.8 us)
Async XLA Ops:
  0.6 126.5 %copy-start = (f32[2,16]{1,0:T(2,128)S(1)}, f32[2,16]{1,0:T(2,128)}, u32[]{:S(2)}) copy-start(f32[2,16]{1,0:T(2,128)} %param.9) | copy-start | bytes 388
  0.6 2.0 copy-start.1
  4.2 12.2 %collective-permute-start = (f32[3,4,32,256]{3,2,1,0:T(8,128)S(1)}, f32[3,4,32,256]{3,2,1,0:T(8,128)S(1)}, u32[]{:S(2)}, u32[]{:S(2)}) collective-permute-start(f32[3,4,32,256]{3,2,1,0:T(8,128)S(1)} %pad_maximum_fusion), channel_id=1, source_target_pairs={{0,32},{32,64},{64,96},{96,0},{128,160},{160,192},{192,224},{224,1... | collective-permute-start | bytes 1179656 | tf_op jit(solution)/shard_map/ppermute | solution.py:48
  5.9 11.0 %collective-permute-start.3 = (f32[3,4,32,256]{3,2,1,0:T(8,128)S(1)}, f32[3,4,32,256]{3,2,1,0:T(8,128)S(1)}, u32[]{:S(2)}, u32[]{:S(2)}) collective-permute-start(f32[3,4,32,256]{3,2,1,0:T(8,128)S(1)} %pad_maximum_fusion.1), channel_id=1, source_target_pairs={{0,96},{32,0},{64,32},{96,64},{128,224},{160,128},{192,160},{224,1... | collective-permute-start | bytes 1179656 | tf_op jit(solution)/shard_map/ppermute | solution.py:49
  16.5 11.3 %collective-permute-start.1 = (f32[3,4,32,256]{3,2,1,0:T(8,128)S(1)}, f32[3,4,32,256]{3,2,1,0:T(8,128)S(1)}, u32[]{:S(2)}, u32[]{:S(2)}) collective-permute-start(f32[3,4,32,256]{3,2,1,0:T(8,128)S(1)} %maximum_add_fusion), channel_id=1, source_target_pairs={{0,32},{32,64},{64,96},{96,0},{128,160},{160,192},{192,224},{224,1... | collective-permute-start | bytes 1179656 | tf_op jit(solution)/shard_map/ppermute | solution.py:48
  17.0 11.1 %collective-permute-start.4 = (f32[3,4,32,256]{3,2,1,0:T(8,128)S(1)}, f32[3,4,32,256]{3,2,1,0:T(8,128)S(1)}, u32[]{:S(2)}, u32[]{:S(2)}) collective-permute-start(f32[3,4,32,256]{3,2,1,0:T(8,128)S(1)} %maximum_add_fusion.3), channel_id=1, source_target_pairs={{0,96},{32,0},{64,32},{96,64},{128,224},{160,128},{192,160},{224,1... | collective-permute-start | bytes 1179656 | tf_op jit(solution)/shard_map/ppermute | solution.py:49
  27.9 10.5 %collective-permute-start.2 = (f32[3,4,32,256]{3,2,1,0:T(8,128)S(1)}, f32[3,4,32,256]{3,2,1,0:T(8,128)}, u32[]{:S(2)}, u32[]{:S(2)}) collective-permute-start(f32[3,4,32,256]{3,2,1,0:T(8,128)S(1)} %maximum_add_fusion.1), channel_id=1, source_target_pairs={{0,32},{32,64},{64,96},{96,0},{128,160},{160,192},{192,224},{224,1... | collective-permute-start | bytes 1179656 | tf_op jit(solution)/shard_map/ppermute | solution.py:48
  28.8 10.8 %collective-permute-start.5 = (f32[3,4,32,256]{3,2,1,0:T(8,128)}, f32[3,4,32,256]{3,2,1,0:T(8,128)}, u32[]{:S(2)}, u32[]{:S(2)}) collective-permute-start(f32[3,4,32,256]{3,2,1,0:T(8,128)} %maximum_add_fusion.4), channel_id=1, source_target_pairs={{0,96},{32,0},{64,32},{96,64},{128,224},{160,128},{192,160},{224,1... | collective-permute-start | bytes 1179656 | tf_op jit(solution)/shard_map/ppermute | solution.py:49
  38.4 2.5 %copy-start.2 = (f32[1,4,512,256]{3,2,1,0:T(8,128)S(1)}, f32[1,4,512,256]{3,2,1,0:T(8,128)}, u32[]{:S(2)}) copy-start(f32[1,4,512,256]{3,2,1,0:T(8,128)} %param.5) | copy-start | bytes 6291460
  40.8 1.6 copy-start.3
  42.5 10.6 %collective-permute-start.7 = (f32[3,4,32,256]{3,2,1,0:T(8,128)S(1)}, f32[3,4,32,256]{3,2,1,0:T(8,128)S(1)}, u32[]{:S(2)}, u32[]{:S(2)}) collective-permute-start(f32[3,4,32,256]{3,2,1,0:T(8,128)S(1)} %pad_maximum_fusion.2), channel_id=1, source_target_pairs={{0,32},{32,64},{64,96},{96,0},{128,160},{160,192},{192,224},{224,1... | collective-permute-start | bytes 1179656 | tf_op jit(solution)/shard_map/ppermute | solution.py:48
  42.6 10.6 %collective-permute-start.9 = (f32[3,4,32,256]{3,2,1,0:T(8,128)S(1)}, f32[3,4,32,256]{3,2,1,0:T(8,128)S(1)}, u32[]{:S(2)}, u32[]{:S(2)}) collective-permute-start(f32[3,4,32,256]{3,2,1,0:T(8,128)S(1)} %pad_maximum_fusion.3), channel_id=1, source_target_pairs={{0,96},{32,0},{64,32},{96,64},{128,224},{160,128},{192,160},{224,1... | collective-permute-start | bytes 1179656 | tf_op jit(solution)/shard_map/ppermute | solution.py:49
  45.9 14.2 %collective-permute-start.6 = (f32[3,4,32,256]{3,2,1,0:T(8,128)S(1)}, f32[3,4,32,256]{3,2,1,0:T(8,128)S(1)}, u32[]{:S(2)}, u32[]{:S(2)}) collective-permute-start(f32[3,4,32,256]{3,2,1,0:T(8,128)S(1)} %maximum_add_fusion.5), channel_id=1, source_target_pairs={{0,128},{32,160},{64,192},{96,224},{128,0},{160,32},{192,64},{224,... | collective-permute-start | bytes 1179656 | tf_op jit(solution)/shard_map/ppermute | solution.py:63
  53.2 9.1 %collective-permute-start.8 = (f32[3,4,32,256]{3,2,1,0:T(8,128)S(1)}, f32[3,4,32,256]{3,2,1,0:T(8,128)S(1)}, u32[]{:S(2)}, u32[]{:S(2)}) collective-permute-start(f32[3,4,32,256]{3,2,1,0:T(8,128)S(1)} %maximum_add_fusion.6), channel_id=1, source_target_pairs={{0,32},{32,64},{64,96},{96,0},{128,160},{160,192},{192,224},{224,1... | collective-permute-start | bytes 1179656 | tf_op jit(solution)/shard_map/ppermute | solution.py:48
  53.3 9.4 %collective-permute-start.10 = (f32[3,4,32,256]{3,2,1,0:T(8,128)S(1)}, f32[3,4,32,256]{3,2,1,0:T(8,128)S(1)}, u32[]{:S(2)}, u32[]{:S(2)}) collective-permute-start(f32[3,4,32,256]{3,2,1,0:T(8,128)S(1)} %maximum_add_fusion.7), channel_id=1, source_target_pairs={{0,96},{32,0},{64,32},{96,64},{128,224},{160,128},{192,160},{224,1... | collective-permute-start | bytes 1179656 | tf_op jit(solution)/shard_map/ppermute | solution.py:49
  62.8 10.0 %collective-permute-start.12 = (f32[3,4,32,256]{3,2,1,0:T(8,128)S(1)}, f32[3,4,32,256]{3,2,1,0:T(8,128)S(1)}, u32[]{:S(2)}, u32[]{:S(2)}) collective-permute-start(f32[3,4,32,256]{3,2,1,0:T(8,128)S(1)} %maximum_add_fusion.10), channel_id=1, source_target_pairs={{0,96},{32,0},{64,32},{96,64},{128,224},{160,128},{192,160},{224,1... | collective-permute-start | bytes 1179656 | tf_op jit(solution)/shard_map/ppermute | solution.py:49
  67.5 13.5 %collective-permute-start.11 = (f32[3,4,32,256]{3,2,1,0:T(8,128)S(1)}, f32[3,4,32,256]{3,2,1,0:T(8,128)S(1)}, u32[]{:S(2)}, u32[]{:S(2)}) collective-permute-start(f32[3,4,32,256]{3,2,1,0:T(8,128)S(1)} %maximum_add_fusion.8), channel_id=1, source_target_pairs={{0,32},{32,64},{64,96},{96,0},{128,160},{160,192},{192,224},{224,1... | collective-permute-start | bytes 1179656 | tf_op jit(solution)/shard_map/ppermute | solution.py:48
  72.8 21.6 %collective-permute-start.13 = (f32[3,4,32,256]{3,2,1,0:T(8,128)S(1)}, f32[3,4,32,256]{3,2,1,0:T(8,128)S(1)}, u32[]{:S(2)}, u32[]{:S(2)}) collective-permute-start(f32[3,4,32,256]{3,2,1,0:T(8,128)S(1)} %maximum_add_fusion.11), channel_id=1, source_target_pairs={{0,128},{32,160},{64,192},{96,224},{128,0},{160,32},{192,64},{224,... | collective-permute-start | bytes 1179656 | tf_op jit(solution)/shard_map/ppermute | solution.py:63
  96.4 22.1 %all-to-all-start = ((f32[2,4,64,256]{3,1,0,2:T(4,128)}), f32[2,4,64,256]{3,1,0,2:T(4,128)S(1)}, u32[]{:S(2)}, u32[]{:S(2)}) async-start(f32[2,4,64,256]{3,1,0,2:T(4,128)} %copy.13), calls=%async_computation | async-start | bytes 1048576 | tf_op jit(solution)/shard_map/all_to_all | solution.py:111
  118.7 8.4 %copy-start.4 = (s32[256]{0:T(256)S(1)}, s32[256]{0:T(256)}, u32[]{:S(2)}) copy-start(s32[256]{0:T(256)} %param.8) | copy-start | bytes 3076
  120.8 20.6 %all-to-all-start.1 = ((f32[2,128,2,256]{3,2,0,1:T(2,128)}), f32[2,128,2,256]{3,2,0,1:T(2,128)S(1)}, u32[]{:S(2)}, u32[]{:S(2)}) async-start(f32[2,128,2,256]{3,2,0,1:T(2,128)} %copy.16), calls=%async_computation.1 | async-start | bytes 1048576 | tf_op jit(solution)/shard_map/all_to_all | solution.py:114
  142.6 19.1 %collective-permute-start.14 = (f32[2,4,32,256]{3,2,1,0:T(8,128)}, f32[2,4,32,256]{3,2,1,0:T(8,128)}, u32[]{:S(2)}, u32[]{:S(2)}) collective-permute-start(f32[2,4,32,256]{3,2,1,0:T(8,128)} %slice.150), channel_id=1, source_target_pairs={{0,128},{32,160},{64,192},{96,224},{128,0},{160,32},{192,64},{224,... | collective-permute-start | bytes 786440 | tf_op jit(solution)/shard_map/ppermute | solution.py:79
  147.1 20.7 %collective-permute-start.15 = (f32[2,4,32,256]{3,2,1,0:T(8,128)}, f32[2,4,32,256]{3,2,1,0:T(8,128)}, u32[]{:S(2)}, u32[]{:S(2)}) collective-permute-start(f32[2,4,32,256]{3,2,1,0:T(8,128)} %slice.150), channel_id=1, source_target_pairs={{0,32},{32,64},{64,96},{96,0},{128,160},{160,192},{192,224},{224,1... | collective-permute-start | bytes 786440 | tf_op jit(solution)/shard_map/ppermute | solution.py:86
  161.8 17.5 %collective-permute-start.21 = (f32[2,4,32,256]{3,2,1,0:T(8,128)S(1)}, f32[2,4,32,256]{3,2,1,0:T(8,128)S(1)}, u32[]{:S(2)}, u32[]{:S(2)}) collective-permute-start(f32[2,4,32,256]{3,2,1,0:T(8,128)S(1)} %slice.123), channel_id=1, source_target_pairs={{0,128},{32,160},{64,192},{96,224},{128,0},{160,32},{192,64},{224,... | collective-permute-start | bytes 786440 | tf_op jit(solution)/shard_map/ppermute | solution.py:79
  164.6 18.0 %collective-permute-start.22 = (f32[2,4,32,256]{3,2,1,0:T(8,128)S(1)}, f32[2,4,32,256]{3,2,1,0:T(8,128)S(1)}, u32[]{:S(2)}, u32[]{:S(2)}) collective-permute-start(f32[2,4,32,256]{3,2,1,0:T(8,128)S(1)} %slice.123), channel_id=1, source_target_pairs={{0,32},{32,64},{64,96},{96,0},{128,160},{160,192},{192,224},{224,1... | collective-permute-start | bytes 786440 | tf_op jit(solution)/shard_map/ppermute | solution.py:86
  164.6 8.7 %collective-permute-start.16 = (f32[2,4,32,256]{3,2,1,0:T(8,128)}, f32[2,4,32,256]{3,2,1,0:T(8,128)S(1)}, u32[]{:S(2)}, u32[]{:S(2)}) collective-permute-start(f32[2,4,32,256]{3,2,1,0:T(8,128)} %collective-permute-done.14), channel_id=1, source_target_pairs={{0,96},{32,0},{64,32},{96,64},{128,224},{160,128},{192,160},{224,1... | collective-permute-start | bytes 786440 | tf_op jit(solution)/shard_map/ppermute | solution.py:87
  167.8 11.5 %collective-permute-start.17 = (f32[2,4,32,256]{3,2,1,0:T(8,128)}, f32[2,4,32,256]{3,2,1,0:T(8,128)S(1)}, u32[]{:S(2)}, u32[]{:S(2)}) collective-permute-start(f32[2,4,32,256]{3,2,1,0:T(8,128)} %collective-permute-done.15), channel_id=1, source_target_pairs={{0,32},{32,64},{64,96},{96,0},{128,160},{160,192},{192,224},{224,1... | collective-permute-start | bytes 786440 | tf_op jit(solution)/shard_map/ppermute | solution.py:86
  173.3 9.3 %collective-permute-start.18 = (f32[2,4,32,256]{3,2,1,0:T(8,128)S(1)}, f32[2,4,32,256]{3,2,1,0:T(8,128)S(1)}, u32[]{:S(2)}, u32[]{:S(2)}) collective-permute-start(f32[2,4,32,256]{3,2,1,0:T(8,128)S(1)} %collective-permute-done.16), channel_id=1, source_target_pairs={{0,96},{32,0},{64,32},{96,64},{128,224},{160,128},{192,160},{224,1... | collective-permute-start | bytes 786440 | tf_op jit(solution)/shard_map/ppermute | solution.py:87
  179.3 13.9 %collective-permute-start.19 = (f32[2,4,32,256]{3,2,1,0:T(8,128)S(1)}, f32[2,4,32,256]{3,2,1,0:T(8,128)S(1)}, u32[]{:S(2)}, u32[]{:S(2)}) collective-permute-start(f32[2,4,32,256]{3,2,1,0:T(8,128)S(1)} %collective-permute-done.17), channel_id=1, source_target_pairs={{0,32},{32,64},{64,96},{96,0},{128,160},{160,192},{192,224},{224,1... | collective-permute-start | bytes 786440 | tf_op jit(solution)/shard_map/ppermute | solution.py:86
  179.3 10.0 %collective-permute-start.23 = (f32[2,4,32,256]{3,2,1,0:T(8,128)S(1)}, f32[2,4,32,256]{3,2,1,0:T(8,128)S(1)}, u32[]{:S(2)}, u32[]{:S(2)}) collective-permute-start(f32[2,4,32,256]{3,2,1,0:T(8,128)S(1)} %collective-permute-done.21), channel_id=1, source_target_pairs={{0,96},{32,0},{64,32},{96,64},{128,224},{160,128},{192,160},{224,1... | collective-permute-start | bytes 786440 | tf_op jit(solution)/shard_map/ppermute | solution.py:87
  182.6 10.6 %collective-permute-start.24 = (f32[2,4,32,256]{3,2,1,0:T(8,128)S(1)}, f32[2,4,32,256]{3,2,1,0:T(8,128)S(1)}, u32[]{:S(2)}, u32[]{:S(2)}) collective-permute-start(f32[2,4,32,256]{3,2,1,0:T(8,128)S(1)} %collective-permute-done.22), channel_id=1, source_target_pairs={{0,32},{32,64},{64,96},{96,0},{128,160},{160,192},{192,224},{224,1... | collective-permute-start | bytes 786440 | tf_op jit(solution)/shard_map/ppermute | solution.py:86
  182.6 12.3 %collective-permute-start.20 = (f32[2,4,32,256]{3,2,1,0:T(8,128)S(1)}, f32[2,4,32,256]{3,2,1,0:T(8,128)S(1)}, u32[]{:S(2)}, u32[]{:S(2)}) collective-permute-start(f32[2,4,32,256]{3,2,1,0:T(8,128)S(1)} %collective-permute-done.18), channel_id=1, source_target_pairs={{0,96},{32,0},{64,32},{96,64},{128,224},{160,128},{192,160},{224,1... | collective-permute-start | bytes 786440 | tf_op jit(solution)/shard_map/ppermute | solution.py:87
  189.3 8.7 %collective-permute-start.25 = (f32[2,4,32,256]{3,2,1,0:T(8,128)S(1)}, f32[2,4,32,256]{3,2,1,0:T(8,128)S(1)}, u32[]{:S(2)}, u32[]{:S(2)}) collective-permute-start(f32[2,4,32,256]{3,2,1,0:T(8,128)S(1)} %collective-permute-done.23), channel_id=1, source_target_pairs={{0,96},{32,0},{64,32},{96,64},{128,224},{160,128},{192,160},{224,1... | collective-permute-start | bytes 786440 | tf_op jit(solution)/shard_map/ppermute | solution.py:87
  193.1 8.7 %collective-permute-start.26 = (f32[2,4,32,256]{3,2,1,0:T(8,128)S(1)}, f32[2,4,32,256]{3,2,1,0:T(8,128)S(1)}, u32[]{:S(2)}, u32[]{:S(2)}) collective-permute-start(f32[2,4,32,256]{3,2,1,0:T(8,128)S(1)} %collective-permute-done.24), channel_id=1, source_target_pairs={{0,32},{32,64},{64,96},{96,0},{128,160},{160,192},{192,224},{224,1... | collective-permute-start | bytes 786440 | tf_op jit(solution)/shard_map/ppermute | solution.py:86
  198.0 7.6 %collective-permute-start.27 = (f32[2,4,32,256]{3,2,1,0:T(8,128)S(1)}, f32[2,4,32,256]{3,2,1,0:T(8,128)S(1)}, u32[]{:S(2)}, u32[]{:S(2)}) collective-permute-start(f32[2,4,32,256]{3,2,1,0:T(8,128)S(1)} %collective-permute-done.25), channel_id=1, source_target_pairs={{0,96},{32,0},{64,32},{96,64},{128,224},{160,128},{192,160},{224,1... | collective-permute-start | bytes 786440 | tf_op jit(solution)/shard_map/ppermute | solution.py:87

commit v4 on v3

--- a/solution.py
+++ b/solution.py
@@ -122,7 +122,7 @@
         )
         both = jnp.stack([vel / illum, den / illum])
         both = smooth_along_x(smooth_depth(both))
-        vel, den = all_gather_smooth_shots(both, n_shots, total)
+        vel, den = all_gather_smooth_shots(both, n_shots, total, parts=1)
         onehot = (
             layer_index[:, None] == jnp.arange(depth_scale.shape[1], dtype=jnp.int32)[None, :]
         ).astype(jnp.float32)

time: 219 us -> 227 us (1.037); the launches traced: 215 us -> 226 us
  waiting for transfers between devices: 102 us -> 133 us
  starting transfers between devices: 78 us -> 59.8 us
    ppermute x6, waiting for transfers between devices: 25.1 us -> 3.48 us  [ring(): recv_f = lax.ppermute(acc_f, 'shots', fwd)]
    ppermute x6, waiting for transfers between devices: 5.62 us -> 27 us  [ring(): recv_b = lax.ppermute(acc_b, 'shots', bwd)]
    ppermute x2 -> x1, waiting for transfers between devices: 8.73 us -> 24.5 us  [all_gather_smooth_shots(): cur_b = lax.ppermute(cur_f, 'shots', hi_pairs(n_shots))]
    ppermute x6 -> x3, starting transfers between devices: 20.7 us -> 10.3 us  [all_gather_smooth_shots(): cur_b = lax.ppermute(cur_b, 'shots', bwd)]
    ppermute x2, waiting for transfers between devices: 17 us -> 23.7 us  [reduce_scatter_shots(): gate = lax.ppermute(acc_b, 'shots', hi_pairs(n_shots))]
    ppermute x6, starting transfers between devices: 19.2 us -> 12.8 us  [ring(): recv_b = lax.ppermute(acc_b, 'shots', bwd)]
    ppermute x6 -> x3, waiting for transfers between devices: 15.3 us -> 21.1 us  [all_gather_smooth_shots(): cur_b = lax.ppermute(cur_b, 'shots', bwd)]
    ppermute x2 -> x1, starting transfers between devices: 7.31 us -> 4.42 us  [all_gather_smooth_shots(): cur_b = lax.ppermute(cur_f, 'shots', hi_pairs(n_shots))]
  transfers between devices with their start and end apart: 30 -> 23, of which waited for: 18 -> 15; matrix products, arithmetic and copies ran while one was open for 6% -> 5% of each run, Pallas kernels for 0% -> 0%
where the time goes in v4:
time: 227 us; the launch traced here: 226 us
  waiting for transfers between devices  133 us (59%)
  starting transfers between devices  59.8 us (26%)
  local copies, waits for them, and re-layouts  15.8 us (7%)
  matrix products  11.7 us (5%)
  other arithmetic  4.93 us (2%)
    ppermute x6, waiting for transfers between devices, ring(): recv_b = lax.ppermute(acc_b, 'shots', bwd)  27 us
    ppermute x1, waiting for transfers between devices, all_gather_smooth_shots(): cur_b = lax.ppermute(cur_f, 'shots', hi_pairs(n_shots))  24.5 us
    ppermute x2, waiting for transfers between devices, reduce_scatter_shots(): gate = lax.ppermute(acc_b, 'shots', hi_pairs(n_shots))  23.7 us
    ppermute x3, waiting for transfers between devices, all_gather_smooth_shots(): cur_b = lax.ppermute(cur_b, 'shots', bwd)  21.1 us
    all_to_all x1, waiting for transfers between devices, smooth_along_x(): cols = lax.all_to_all(both, 'slab', split_axis=2, concat_axis=1, tiled=True)  14.6 us
    all_to_all x1, waiting for transfers between devices, smooth_along_x(): return lax.all_to_all(cols, 'slab', split_axis=1, concat_axis=2, tiled=True)  14.5 us
    ppermute x2, starting transfers between devices, reduce_scatter_shots(): gate = lax.ppermute(acc_b, 'shots', hi_pairs(n_shots))  13.9 us
    ppermute x6, starting transfers between devices, ring(): recv_b = lax.ppermute(acc_b, 'shots', bwd)  12.8 us
  transfers between devices with their start and end apart: 23, of which 15 were waited for; matrix products, arithmetic and copies ran while one was open for 5% of the time, Pallas kernels for 0%

profile of v4, /device:TPU:2, one launch (start us, length us, event | category | flops | bytes accessed | tf_op | source)
XLA Modules:
  0.0 226.2 jit_solution(12775481382580858202)
XLA Ops:
  0.8 1.5 constant_dynamic-slice_fusion.2
  2.3 0.3 copy-done.1
  2.7 1.5 constant_dynamic-slice_fusion
  4.2 3.1 %collective-permute-start.3 = (f32[3,4,32,256]{3,2,1,0:T(8,128)S(1)}, f32[3,4,32,256]{3,2,1,0:T(8,128)S(1)}, u32[]{:S(2)}, u32[]{:S(2)}) collective-permute-start(f32[3,4,32,256]{3,2,1,0:T(8,128)S(1)} %pad_maximum_fusion.1), channel_id=1, source_target_pairs={{0,96},{32,0},{64,32},{96,64},{128,224},{160,128},{192,160},{224,1... | collective-permute-start | bytes 1179656 | tf_op jit(solution)/shard_map/ppermute | solution.py:49
  7.5 8.2 %collective-permute-done.3 = f32[3,4,32,256]{3,2,1,0:T(8,128)S(1)} collective-permute-done((f32[3,4,32,256]{3,2,1,0:T(8,128)S(1)}, f32[3,4,32,256]{3,2,1,0:T(8,128)S(1)}, u32[]{:S(2)}, u32[]{:S(2)}) %collective-permute-start.3) | collective-permute-done | bytes 393248 | tf_op jit(solution)/shard_map/ppermute | solution.py:49
  15.8 3.8 %collective-permute-start.4 = (f32[3,4,32,256]{3,2,1,0:T(8,128)S(1)}, f32[3,4,32,256]{3,2,1,0:T(8,128)S(1)}, u32[]{:S(2)}, u32[]{:S(2)}) collective-permute-start(f32[3,4,32,256]{3,2,1,0:T(8,128)S(1)} %maximum_add_fusion.3), channel_id=1, source_target_pairs={{0,96},{32,0},{64,32},{96,64},{128,224},{160,128},{192,160},{224,1... | collective-permute-start | bytes 1179656 | tf_op jit(solution)/shard_map/ppermute | solution.py:49
  19.7 7.3 %collective-permute-done.4 = f32[3,4,32,256]{3,2,1,0:T(8,128)S(1)} collective-permute-done((f32[3,4,32,256]{3,2,1,0:T(8,128)S(1)}, f32[3,4,32,256]{3,2,1,0:T(8,128)S(1)}, u32[]{:S(2)}, u32[]{:S(2)}) %collective-permute-start.4) | collective-permute-done | bytes 393248 | tf_op jit(solution)/shard_map/ppermute | solution.py:49
  27.1 3.8 %collective-permute-start.5 = (f32[3,4,32,256]{3,2,1,0:T(8,128)S(1)}, f32[3,4,32,256]{3,2,1,0:T(8,128)}, u32[]{:S(2)}, u32[]{:S(2)}) collective-permute-start(f32[3,4,32,256]{3,2,1,0:T(8,128)S(1)} %maximum_add_fusion.4), channel_id=1, source_target_pairs={{0,96},{32,0},{64,32},{96,64},{128,224},{160,128},{192,160},{224,1... | collective-permute-start | bytes 1179656 | tf_op jit(solution)/shard_map/ppermute | solution.py:49
  30.9 0.8 maximum_add_fusion.1
  31.7 5.8 %collective-permute-done.5 = f32[3,4,32,256]{3,2,1,0:T(8,128)} collective-permute-done((f32[3,4,32,256]{3,2,1,0:T(8,128)S(1)}, f32[3,4,32,256]{3,2,1,0:T(8,128)}, u32[]{:S(2)}, u32[]{:S(2)}) %collective-permute-start.5) | collective-permute-done | bytes 393248 | tf_op jit(solution)/shard_map/ppermute | solution.py:49
  37.5 1.1 maximum_add_fusion.5
  38.5 3.5 %collective-permute-done.2 = f32[3,4,32,256]{3,2,1,0:T(8,128)} collective-permute-done((f32[3,4,32,256]{3,2,1,0:T(8,128)}, f32[3,4,32,256]{3,2,1,0:T(8,128)}, u32[]{:S(2)}, u32[]{:S(2)}) %collective-permute-start.2) | collective-permute-done | bytes 393248 | tf_op jit(solution)/shard_map/ppermute | solution.py:48
  42.0 1.1 maximum_add_fusion.2
  43.1 0.1 dynamic-slice_bitcast_fusion.8
  43.2 0.1 dynamic-slice_bitcast_fusion.7
  43.4 1.3 copy-done.2
  44.8 0.4 collective-permute-start.9
  45.3 1.8 collective-permute-start.7
  47.0 7.2 %collective-permute-start.6 = (f32[3,4,32,256]{3,2,1,0:T(8,128)S(1)}, f32[3,4,32,256]{3,2,1,0:T(8,128)S(1)}, u32[]{:S(2)}, u32[]{:S(2)}) collective-permute-start(f32[3,4,32,256]{3,2,1,0:T(8,128)S(1)} %maximum_add_fusion.5), channel_id=1, source_target_pairs={{0,128},{32,160},{64,192},{96,224},{128,0},{160,32},{192,64},{224,... | collective-permute-start | bytes 1179656 | tf_op jit(solution)/shard_map/ppermute | solution.py:63
  54.3 1.6 collective-permute-start.10
  56.0 0.6 collective-permute-start.8
  56.5 10.3 %collective-permute-done.6 = f32[3,4,32,256]{3,2,1,0:T(8,128)S(1)} collective-permute-done((f32[3,4,32,256]{3,2,1,0:T(8,128)S(1)}, f32[3,4,32,256]{3,2,1,0:T(8,128)S(1)}, u32[]{:S(2)}, u32[]{:S(2)}) %collective-permute-start.6) | collective-permute-done | bytes 393248 | tf_op jit(solution)/shard_map/ppermute | solution.py:63
  67.0 2.1 collective-permute-start.11
  69.1 5.6 %collective-permute-done.12 = f32[3,4,32,256]{3,2,1,0:T(8,128)S(1)} collective-permute-done((f32[3,4,32,256]{3,2,1,0:T(8,128)S(1)}, f32[3,4,32,256]{3,2,1,0:T(8,128)S(1)}, u32[]{:S(2)}, u32[]{:S(2)}) %collective-permute-start.12) | collective-permute-done | bytes 393248 | tf_op jit(solution)/shard_map/ppermute | solution.py:49
  74.8 6.7 %collective-permute-start.13 = (f32[3,4,32,256]{3,2,1,0:T(8,128)S(1)}, f32[3,4,32,256]{3,2,1,0:T(8,128)S(1)}, u32[]{:S(2)}, u32[]{:S(2)}) collective-permute-start(f32[3,4,32,256]{3,2,1,0:T(8,128)S(1)} %maximum_add_fusion.11), channel_id=1, source_target_pairs={{0,128},{32,160},{64,192},{96,224},{128,0},{160,32},{192,64},{224,... | collective-permute-start | bytes 1179656 | tf_op jit(solution)/shard_map/ppermute | solution.py:63
  81.5 0.2 fusion.45
  81.7 13.5 %collective-permute-done.13 = f32[3,4,32,256]{3,2,1,0:T(8,128)S(1)} collective-permute-done((f32[3,4,32,256]{3,2,1,0:T(8,128)S(1)}, f32[3,4,32,256]{3,2,1,0:T(8,128)S(1)}, u32[]{:S(2)}, u32[]{:S(2)}) %collective-permute-start.13) | collective-permute-done | bytes 393248 | tf_op jit(solution)/shard_map/ppermute | solution.py:63
  95.3 0.7 fusion.15
  96.0 1.1 copy.17
  97.2 7.3 %all-to-all-start = ((f32[2,4,64,256]{3,1,0,2:T(4,128)}), f32[2,4,64,256]{3,1,0,2:T(4,128)S(1)}, u32[]{:S(2)}, u32[]{:S(2)}) async-start(f32[2,4,64,256]{3,1,0,2:T(4,128)} %copy.17), calls=%async_computation | async-start | bytes 1048576 | tf_op jit(solution)/shard_map/all_to_all | solution.py:111
  104.5 0.1 fusion.56
  104.7 14.6 %all-to-all-done = f32[2,4,64,256]{3,1,0,2:T(4,128)S(1)} async-done(((f32[2,4,64,256]{3,1,0,2:T(4,128)}), f32[2,4,64,256]{3,1,0,2:T(4,128)S(1)}, u32[]{:S(2)}, u32[]{:S(2)}) %all-to-all-start) | async-done | bytes 524320 | tf_op jit(solution)/shard_map/all_to_all | solution.py:111
  119.2 0.3 copy.18
  119.5 1.0 convolution_bitcast_fusion
  120.5 1.0 copy.20
  121.5 5.8 %all-to-all-start.1 = ((f32[2,128,2,256]{3,2,0,1:T(2,128)}), f32[2,128,2,256]{3,2,0,1:T(2,128)S(1)}, u32[]{:S(2)}, u32[]{:S(2)}) async-start(f32[2,128,2,256]{3,2,0,1:T(2,128)} %copy.20), calls=%async_computation.1 | async-start | bytes 1048576 | tf_op jit(solution)/shard_map/all_to_all | solution.py:114
  127.4 0.2 convolution_bitcast_fusion.1
  127.6 14.5 %all-to-all-done.1 = f32[2,128,2,256]{3,2,0,1:T(2,128)S(1)} async-done(((f32[2,128,2,256]{3,2,0,1:T(2,128)}), f32[2,128,2,256]{3,2,0,1:T(2,128)S(1)}, u32[]{:S(2)}, u32[]{:S(2)}) %all-to-all-start.1) | async-done | bytes 524320 | tf_op jit(solution)/shard_map/all_to_all | solution.py:114
  142.1 0.2 copy.23
  142.3 1.2 all_to_all.33
  143.4 4.4 %collective-permute-start.14 = (f32[2,4,64,256]{3,2,1,0:T(8,128)}, f32[2,4,64,256]{3,2,1,0:T(8,128)}, u32[]{:S(2)}, u32[]{:S(2)}) collective-permute-start(f32[2,4,64,256]{3,2,1,0:T(8,128)} %all_to_all.33), channel_id=1, source_target_pairs={{0,128},{32,160},{64,192},{96,224},{128,0},{160,32},{192,64},{224,... | collective-permute-start | bytes 1572872 | tf_op jit(solution)/shard_map/ppermute | solution.py:79
  147.9 0.5 fusion.14
  148.3 0.4 fusion.13
  148.8 0.6 collective-permute-start.15
  149.3 24.5 %collective-permute-done.14 = f32[2,4,64,256]{3,2,1,0:T(8,128)} collective-permute-done((f32[2,4,64,256]{3,2,1,0:T(8,128)}, f32[2,4,64,256]{3,2,1,0:T(8,128)}, u32[]{:S(2)}, u32[]{:S(2)}) %collective-permute-start.14) | collective-permute-done | bytes 524320 | tf_op jit(solution)/shard_map/ppermute | solution.py:79
  173.8 3.0 %collective-permute-start.16 = (f32[2,4,64,256]{3,2,1,0:T(8,128)}, f32[2,4,64,256]{3,2,1,0:T(8,128)}, u32[]{:S(2)}, u32[]{:S(2)}) collective-permute-start(f32[2,4,64,256]{3,2,1,0:T(8,128)} %collective-permute-done.14), channel_id=1, source_target_pairs={{0,96},{32,0},{64,32},{96,64},{128,224},{160,128},{192,160},{224,1... | collective-permute-start | bytes 1572872 | tf_op jit(solution)/shard_map/ppermute | solution.py:87
  176.8 1.3 constant_dynamic-slice_fusion.24
  178.1 1.5 concatenate.12
  179.6 0.2 copy.21
  179.8 0.2 fusion.69
  180.1 0.2 squeeze.60
  180.3 0.2 squeeze.68
  180.7 7.9 %collective-permute-done.16 = f32[2,4,64,256]{3,2,1,0:T(8,128)} collective-permute-done((f32[2,4,64,256]{3,2,1,0:T(8,128)}, f32[2,4,64,256]{3,2,1,0:T(8,128)}, u32[]{:S(2)}, u32[]{:S(2)}) %collective-permute-start.16) | collective-permute-done | bytes 524320 | tf_op jit(solution)/shard_map/ppermute | solution.py:87
  188.6 3.7 %collective-permute-start.18 = (f32[2,4,64,256]{3,2,1,0:T(8,128)}, f32[2,4,64,256]{3,2,1,0:T(8,128)S(1)}, u32[]{:S(2)}, u32[]{:S(2)}) collective-permute-start(f32[2,4,64,256]{3,2,1,0:T(8,128)} %collective-permute-done.16), channel_id=1, source_target_pairs={{0,96},{32,0},{64,32},{96,64},{128,224},{160,128},{192,160},{224,1... | collective-permute-start | bytes 1572872 | tf_op jit(solution)/shard_map/ppermute | solution.py:87
  192.3 1.1 fusion.33
  193.3 1.1 fusion.32
  194.4 1.2 collective-permute-done.17
  195.7 1.1 fusion.31
  196.7 6.4 %collective-permute-done.18 = f32[2,4,64,256]{3,2,1,0:T(8,128)S(1)} collective-permute-done((f32[2,4,64,256]{3,2,1,0:T(8,128)}, f32[2,4,64,256]{3,2,1,0:T(8,128)S(1)}, u32[]{:S(2)}, u32[]{:S(2)}) %collective-permute-start.18) | collective-permute-done | bytes 524320 | tf_op jit(solution)/shard_map/ppermute | solution.py:87
  203.1 3.6 %collective-permute-start.20 = (f32[2,4,64,256]{3,2,1,0:T(8,128)S(1)}, f32[2,4,64,256]{3,2,1,0:T(8,128)S(1)}, u32[]{:S(2)}, u32[]{:S(2)}) collective-permute-start(f32[2,4,64,256]{3,2,1,0:T(8,128)S(1)} %collective-permute-done.18), channel_id=1, source_target_pairs={{0,96},{32,0},{64,32},{96,64},{128,224},{160,128},{192,160},{224,1... | collective-permute-start | bytes 1572872 | tf_op jit(solution)/shard_map/ppermute | solution.py:87
  206.8 2.8 %collective-permute-done.19 = f32[2,4,64,256]{3,2,1,0:T(8,128)S(1)} collective-permute-done((f32[2,4,64,256]{3,2,1,0:T(8,128)S(1)}, f32[2,4,64,256]{3,2,1,0:T(8,128)S(1)}, u32[]{:S(2)}, u32[]{:S(2)}) %collective-permute-start.19) | collective-permute-done | bytes 524320 | tf_op jit(solution)/shard_map/ppermute | solution.py:86
  209.6 6.8 %collective-permute-done.20 = f32[2,4,64,256]{3,2,1,0:T(8,128)S(1)} collective-permute-done((f32[2,4,64,256]{3,2,1,0:T(8,128)S(1)}, f32[2,4,64,256]{3,2,1,0:T(8,128)S(1)}, u32[]{:S(2)}, u32[]{:S(2)}) %collective-permute-start.20) | collective-permute-done | bytes 524320 | tf_op jit(solution)/shard_map/ppermute | solution.py:87
  216.4 4.9 %fusion.7 = f32[4,512,256]{2,1,0:T(8,128)} fusion(f32[4,512,256]{2,1,0:T(8,128)S(1)} %get-tuple-element.74, f32[512,512]{1,0:T(8,128)S(1)} %concatenate.12, f32[256]{0:T(256)S(1)} %bitcast.142), kind=kOutput, calls=%fused_computation.5 | convolution fusion | flops 3221749760 | bytes 5243904 | tf_op jit(solution)/shard_map/xij,xjz->xiz/dot_general | solution.py:101
  221.3 4.9 %fusion.4 = f32[4,512,256]{2,1,0:T(8,128)} fusion(f32[4,512,256]{2,1,0:T(8,128)S(1)} %get-tuple-element.75, f32[512,512]{1,0:T(8,128)S(1)} %concatenate.12, f32[256]{0:T(256)S(1)} %bitcast.141), kind=kOutput, calls=%fused_computation.4 | convolution fusion | flops 3221749760 | bytes 5243904 | tf_op jit(solution)/shard_map/xij,xjz->xiz/dot_general | solution.py:101
  (47 shorter events, 1.5 us)
Async XLA Ops:
  0.6 126.8 %copy-start = (f32[2,16]{1,0:T(2,128)S(1)}, f32[2,16]{1,0:T(2,128)}, u32[]{:S(2)}) copy-start(f32[2,16]{1,0:T(2,128)} %param.9) | copy-start | bytes 388
  0.6 2.0 copy-start.1
  4.2 11.5 %collective-permute-start.3 = (f32[3,4,32,256]{3,2,1,0:T(8,128)S(1)}, f32[3,4,32,256]{3,2,1,0:T(8,128)S(1)}, u32[]{:S(2)}, u32[]{:S(2)}) collective-permute-start(f32[3,4,32,256]{3,2,1,0:T(8,128)S(1)} %pad_maximum_fusion.1), channel_id=1, source_target_pairs={{0,96},{32,0},{64,32},{96,64},{128,224},{160,128},{192,160},{224,1... | collective-permute-start | bytes 1179656 | tf_op jit(solution)/shard_map/ppermute | solution.py:49
  7.4 12.2 %collective-permute-start = (f32[3,4,32,256]{3,2,1,0:T(8,128)S(1)}, f32[3,4,32,256]{3,2,1,0:T(8,128)S(1)}, u32[]{:S(2)}, u32[]{:S(2)}) collective-permute-start(f32[3,4,32,256]{3,2,1,0:T(8,128)S(1)} %pad_maximum_fusion), channel_id=1, source_target_pairs={{0,32},{32,64},{64,96},{96,0},{128,160},{160,192},{192,224},{224,1... | collective-permute-start | bytes 1179656 | tf_op jit(solution)/shard_map/ppermute | solution.py:48
  15.8 11.3 %collective-permute-start.4 = (f32[3,4,32,256]{3,2,1,0:T(8,128)S(1)}, f32[3,4,32,256]{3,2,1,0:T(8,128)S(1)}, u32[]{:S(2)}, u32[]{:S(2)}) collective-permute-start(f32[3,4,32,256]{3,2,1,0:T(8,128)S(1)} %maximum_add_fusion.3), channel_id=1, source_target_pairs={{0,96},{32,0},{64,32},{96,64},{128,224},{160,128},{192,160},{224,1... | collective-permute-start | bytes 1179656 | tf_op jit(solution)/shard_map/ppermute | solution.py:49
  19.6 11.3 %collective-permute-start.1 = (f32[3,4,32,256]{3,2,1,0:T(8,128)S(1)}, f32[3,4,32,256]{3,2,1,0:T(8,128)S(1)}, u32[]{:S(2)}, u32[]{:S(2)}) collective-permute-start(f32[3,4,32,256]{3,2,1,0:T(8,128)S(1)} %maximum_add_fusion), channel_id=1, source_target_pairs={{0,32},{32,64},{64,96},{96,0},{128,160},{160,192},{192,224},{224,1... | collective-permute-start | bytes 1179656 | tf_op jit(solution)/shard_map/ppermute | solution.py:48
  27.1 10.3 %collective-permute-start.5 = (f32[3,4,32,256]{3,2,1,0:T(8,128)S(1)}, f32[3,4,32,256]{3,2,1,0:T(8,128)}, u32[]{:S(2)}, u32[]{:S(2)}) collective-permute-start(f32[3,4,32,256]{3,2,1,0:T(8,128)S(1)} %maximum_add_fusion.4), channel_id=1, source_target_pairs={{0,96},{32,0},{64,32},{96,64},{128,224},{160,128},{192,160},{224,1... | collective-permute-start | bytes 1179656 | tf_op jit(solution)/shard_map/ppermute | solution.py:49
  31.7 10.3 %collective-permute-start.2 = (f32[3,4,32,256]{3,2,1,0:T(8,128)}, f32[3,4,32,256]{3,2,1,0:T(8,128)}, u32[]{:S(2)}, u32[]{:S(2)}) collective-permute-start(f32[3,4,32,256]{3,2,1,0:T(8,128)} %maximum_add_fusion.1), channel_id=1, source_target_pairs={{0,32},{32,64},{64,96},{96,0},{128,160},{160,192},{192,224},{224,1... | collective-permute-start | bytes 1179656 | tf_op jit(solution)/shard_map/ppermute | solution.py:48
  31.7 11.4 %copy-start.3 = (f32[1,4,512,256]{3,2,1,0:T(8,128)S(1)}, f32[1,4,512,256]{3,2,1,0:T(8,128)}, u32[]{:S(2)}) copy-start(f32[1,4,512,256]{3,2,1,0:T(8,128)} %param.7) | copy-start | bytes 6291460
  43.1 1.6 copy-start.2
  44.8 9.4 %collective-permute-start.9 = (f32[3,4,32,256]{3,2,1,0:T(8,128)S(1)}, f32[3,4,32,256]{3,2,1,0:T(8,128)S(1)}, u32[]{:S(2)}, u32[]{:S(2)}) collective-permute-start(f32[3,4,32,256]{3,2,1,0:T(8,128)S(1)} %pad_maximum_fusion.3), channel_id=1, source_target_pairs={{0,96},{32,0},{64,32},{96,64},{128,224},{160,128},{192,160},{224,1... | collective-permute-start | bytes 1179656 | tf_op jit(solution)/shard_map/ppermute | solution.py:49
  45.3 10.6 %collective-permute-start.7 = (f32[3,4,32,256]{3,2,1,0:T(8,128)S(1)}, f32[3,4,32,256]{3,2,1,0:T(8,128)S(1)}, u32[]{:S(2)}, u32[]{:S(2)}) collective-permute-start(f32[3,4,32,256]{3,2,1,0:T(8,128)S(1)} %pad_maximum_fusion.2), channel_id=1, source_target_pairs={{0,32},{32,64},{64,96},{96,0},{128,160},{160,192},{192,224},{224,1... | collective-permute-start | bytes 1179656 | tf_op jit(solution)/shard_map/ppermute | solution.py:48
  47.0 19.8 %collective-permute-start.6 = (f32[3,4,32,256]{3,2,1,0:T(8,128)S(1)}, f32[3,4,32,256]{3,2,1,0:T(8,128)S(1)}, u32[]{:S(2)}, u32[]{:S(2)}) collective-permute-start(f32[3,4,32,256]{3,2,1,0:T(8,128)S(1)} %maximum_add_fusion.5), channel_id=1, source_target_pairs={{0,128},{32,160},{64,192},{96,224},{128,0},{160,32},{192,64},{224,... | collective-permute-start | bytes 1179656 | tf_op jit(solution)/shard_map/ppermute | solution.py:63
  54.3 12.5 %collective-permute-start.10 = (f32[3,4,32,256]{3,2,1,0:T(8,128)S(1)}, f32[3,4,32,256]{3,2,1,0:T(8,128)S(1)}, u32[]{:S(2)}, u32[]{:S(2)}) collective-permute-start(f32[3,4,32,256]{3,2,1,0:T(8,128)S(1)} %maximum_add_fusion.7), channel_id=1, source_target_pairs={{0,96},{32,0},{64,32},{96,64},{128,224},{160,128},{192,160},{224,1... | collective-permute-start | bytes 1179656 | tf_op jit(solution)/shard_map/ppermute | solution.py:49
  56.0 10.8 %collective-permute-start.8 = (f32[3,4,32,256]{3,2,1,0:T(8,128)S(1)}, f32[3,4,32,256]{3,2,1,0:T(8,128)S(1)}, u32[]{:S(2)}, u32[]{:S(2)}) collective-permute-start(f32[3,4,32,256]{3,2,1,0:T(8,128)S(1)} %maximum_add_fusion.6), channel_id=1, source_target_pairs={{0,32},{32,64},{64,96},{96,0},{128,160},{160,192},{192,224},{224,1... | collective-permute-start | bytes 1179656 | tf_op jit(solution)/shard_map/ppermute | solution.py:48
  66.9 7.9 %collective-permute-start.12 = (f32[3,4,32,256]{3,2,1,0:T(8,128)S(1)}, f32[3,4,32,256]{3,2,1,0:T(8,128)S(1)}, u32[]{:S(2)}, u32[]{:S(2)}) collective-permute-start(f32[3,4,32,256]{3,2,1,0:T(8,128)S(1)} %maximum_add_fusion.10), channel_id=1, source_target_pairs={{0,96},{32,0},{64,32},{96,64},{128,224},{160,128},{192,160},{224,1... | collective-permute-start | bytes 1179656 | tf_op jit(solution)/shard_map/ppermute | solution.py:49
  67.0 14.7 %collective-permute-start.11 = (f32[3,4,32,256]{3,2,1,0:T(8,128)S(1)}, f32[3,4,32,256]{3,2,1,0:T(8,128)S(1)}, u32[]{:S(2)}, u32[]{:S(2)}) collective-permute-start(f32[3,4,32,256]{3,2,1,0:T(8,128)S(1)} %maximum_add_fusion.8), channel_id=1, source_target_pairs={{0,32},{32,64},{64,96},{96,0},{128,160},{160,192},{192,224},{224,1... | collective-permute-start | bytes 1179656 | tf_op jit(solution)/shard_map/ppermute | solution.py:48
  74.8 20.4 %collective-permute-start.13 = (f32[3,4,32,256]{3,2,1,0:T(8,128)S(1)}, f32[3,4,32,256]{3,2,1,0:T(8,128)S(1)}, u32[]{:S(2)}, u32[]{:S(2)}) collective-permute-start(f32[3,4,32,256]{3,2,1,0:T(8,128)S(1)} %maximum_add_fusion.11), channel_id=1, source_target_pairs={{0,128},{32,160},{64,192},{96,224},{128,0},{160,32},{192,64},{224,... | collective-permute-start | bytes 1179656 | tf_op jit(solution)/shard_map/ppermute | solution.py:63
  97.2 22.1 %all-to-all-start = ((f32[2,4,64,256]{3,1,0,2:T(4,128)}), f32[2,4,64,256]{3,1,0,2:T(4,128)S(1)}, u32[]{:S(2)}, u32[]{:S(2)}) async-start(f32[2,4,64,256]{3,1,0,2:T(4,128)} %copy.17), calls=%async_computation | async-start | bytes 1048576 | tf_op jit(solution)/shard_map/all_to_all | solution.py:111
  119.2 8.2 %copy-start.4 = (s32[256]{0:T(256)S(1)}, s32[256]{0:T(256)}, u32[]{:S(2)}) copy-start(s32[256]{0:T(256)} %param.8) | copy-start | bytes 3076
  121.5 20.6 %all-to-all-start.1 = ((f32[2,128,2,256]{3,2,0,1:T(2,128)}), f32[2,128,2,256]{3,2,0,1:T(2,128)S(1)}, u32[]{:S(2)}, u32[]{:S(2)}) async-start(f32[2,128,2,256]{3,2,0,1:T(2,128)} %copy.20), calls=%async_computation.1 | async-start | bytes 1048576 | tf_op jit(solution)/shard_map/all_to_all | solution.py:114
  143.4 30.4 %collective-permute-start.14 = (f32[2,4,64,256]{3,2,1,0:T(8,128)}, f32[2,4,64,256]{3,2,1,0:T(8,128)}, u32[]{:S(2)}, u32[]{:S(2)}) collective-permute-start(f32[2,4,64,256]{3,2,1,0:T(8,128)} %all_to_all.33), channel_id=1, source_target_pairs={{0,128},{32,160},{64,192},{96,224},{128,0},{160,32},{192,64},{224,... | collective-permute-start | bytes 1572872 | tf_op jit(solution)/shard_map/ppermute | solution.py:79
  148.8 31.8 %collective-permute-start.15 = (f32[2,4,64,256]{3,2,1,0:T(8,128)}, f32[2,4,64,256]{3,2,1,0:T(8,128)}, u32[]{:S(2)}, u32[]{:S(2)}) collective-permute-start(f32[2,4,64,256]{3,2,1,0:T(8,128)} %all_to_all.33), channel_id=1, source_target_pairs={{0,32},{32,64},{64,96},{96,0},{128,160},{160,192},{192,224},{224,1... | collective-permute-start | bytes 1572872 | tf_op jit(solution)/shard_map/ppermute | solution.py:86
  173.8 14.8 %collective-permute-start.16 = (f32[2,4,64,256]{3,2,1,0:T(8,128)}, f32[2,4,64,256]{3,2,1,0:T(8,128)}, u32[]{:S(2)}, u32[]{:S(2)}) collective-permute-start(f32[2,4,64,256]{3,2,1,0:T(8,128)} %collective-permute-done.14), channel_id=1, source_target_pairs={{0,96},{32,0},{64,32},{96,64},{128,224},{160,128},{192,160},{224,1... | collective-permute-start | bytes 1572872 | tf_op jit(solution)/shard_map/ppermute | solution.py:87
  180.5 15.1 %collective-permute-start.17 = (f32[2,4,64,256]{3,2,1,0:T(8,128)}, f32[2,4,64,256]{3,2,1,0:T(8,128)S(1)}, u32[]{:S(2)}, u32[]{:S(2)}) collective-permute-start(f32[2,4,64,256]{3,2,1,0:T(8,128)} %collective-permute-done.15), channel_id=1, source_target_pairs={{0,32},{32,64},{64,96},{96,0},{128,160},{160,192},{192,224},{224,1... | collective-permute-start | bytes 1572872 | tf_op jit(solution)/shard_map/ppermute | solution.py:86
  188.6 14.6 %collective-permute-start.18 = (f32[2,4,64,256]{3,2,1,0:T(8,128)}, f32[2,4,64,256]{3,2,1,0:T(8,128)S(1)}, u32[]{:S(2)}, u32[]{:S(2)}) collective-permute-start(f32[2,4,64,256]{3,2,1,0:T(8,128)} %collective-permute-done.16), channel_id=1, source_target_pairs={{0,96},{32,0},{64,32},{96,64},{128,224},{160,128},{192,160},{224,1... | collective-permute-start | bytes 1572872 | tf_op jit(solution)/shard_map/ppermute | solution.py:87
  195.7 13.9 %collective-permute-start.19 = (f32[2,4,64,256]{3,2,1,0:T(8,128)S(1)}, f32[2,4,64,256]{3,2,1,0:T(8,128)S(1)}, u32[]{:S(2)}, u32[]{:S(2)}) collective-permute-start(f32[2,4,64,256]{3,2,1,0:T(8,128)S(1)} %collective-permute-done.17), channel_id=1, source_target_pairs={{0,32},{32,64},{64,96},{96,0},{128,160},{160,192},{192,224},{224,1... | collective-permute-start | bytes 1572872 | tf_op jit(solution)/shard_map/ppermute | solution.py:86
  203.1 13.2 %collective-permute-start.20 = (f32[2,4,64,256]{3,2,1,0:T(8,128)S(1)}, f32[2,4,64,256]{3,2,1,0:T(8,128)S(1)}, u32[]{:S(2)}, u32[]{:S(2)}) collective-permute-start(f32[2,4,64,256]{3,2,1,0:T(8,128)S(1)} %collective-permute-done.18), channel_id=1, source_target_pairs={{0,96},{32,0},{64,32},{96,64},{128,224},{160,128},{192,160},{224,1... | collective-permute-start | bytes 1572872 | tf_op jit(solution)/shard_map/ppermute | solution.py:87

commit v5 on v0

--- a/solution.py
+++ b/solution.py
@@ -30,24 +30,35 @@
     return lax.dynamic_slice_in_dim(field, start, size, axis=1)
 
 
-def reduce_scatter_shots(fields, n_shots):
+def ring_sum(fields, starts, size, n_shots):
     idx = lax.axis_index("shots")
-    r, h = idx % RING, idx // RING
-    chunk = fields[0].shape[1] // RING
-    half = chunk // 2
+    r = idx % RING
+    q = size // 2
     fwd, bwd = ring_pairs(n_shots, 1), ring_pairs(n_shots, -1)
 
     def take(start):
-        return jnp.stack([rows(f, start, half) for f in fields])
+        return jnp.stack([rows(f, start, q) for f in fields])
 
-    acc_f = take(((r - 1) % RING) * chunk + h * half)
-    acc_b = take(((r + 1) % RING) * chunk + (1 - h) * half)
+    acc_f = take(starts((r - 1) % RING))
+    acc_b = take(starts((r + 1) % RING) + q)
     for t in range(1, RING):
         recv_f = lax.ppermute(acc_f, "shots", fwd)
         recv_b = lax.ppermute(acc_b, "shots", bwd)
-        acc_f = recv_f + take(((r - 1 - t) % RING) * chunk + h * half)
-        acc_b = recv_b + take(((r + 1 + t) % RING) * chunk + (1 - h) * half)
-    return acc_f + lax.ppermute(acc_b, "shots", hi_pairs(n_shots))
+        acc_f = recv_f + take(starts((r - 1 - t) % RING))
+        acc_b = recv_b + take(starts((r + 1 + t) % RING) + q)
+    return jnp.concatenate([acc_f, acc_b], axis=2)
+
+
+def reduce_scatter_shots(fields, n_shots):
+    idx = lax.axis_index("shots")
+    h = idx // RING
+    chunk = fields[0].shape[1] // RING
+    half = chunk // 2
+    theirs = ring_sum(fields, lambda c: c * chunk + (1 - h) * half, half, n_shots)
+    fields, theirs = lax.optimization_barrier((tuple(fields), theirs))
+    got = lax.ppermute(theirs, "shots", hi_pairs(n_shots))
+    mine = ring_sum(fields, lambda c: c * chunk + h * half, half, n_shots)
+    return mine + got
 
 
 def all_gather_smooth_shots(blocks, n_shots, total):
@@ -55,19 +66,22 @@
     r, h = idx % RING, idx // RING
     chunk = total // RING
     half = chunk // 2
+    q = half // 2
     fwd, bwd = ring_pairs(n_shots, 1), ring_pairs(n_shots, -1)
-    cur_f = blocks
-    cur_b = lax.ppermute(cur_f, "shots", hi_pairs(n_shots))
-    pieces = [cur_f, cur_b]
-    starts = [r * chunk + h * half, r * chunk + (1 - h) * half]
-    for t in range(1, RING):
-        cur_f = lax.ppermute(cur_f, "shots", fwd)
-        cur_b = lax.ppermute(cur_b, "shots", bwd)
+    other = lax.ppermute(blocks, "shots", hi_pairs(n_shots))
+    pieces, starts = [], []
+    for block, side in ((blocks, h), (other, 1 - h)):
+        cur_f, cur_b = block[:, :, :q], block[:, :, q:]
         pieces += [cur_f, cur_b]
-        starts += [((r - t) % RING) * chunk + h * half, ((r + t) % RING) * chunk + (1 - h) * half]
+        starts += [r * chunk + side * half, r * chunk + side * half + q]
+        for t in range(1, RING):
+            cur_f = lax.ppermute(cur_f, "shots", fwd)
+            cur_b = lax.ppermute(cur_b, "shots", bwd)
+            pieces += [cur_f, cur_b]
+            starts += [((r - t) % RING) * chunk + side * half, ((r + t) % RING) * chunk + side * half + q]
     matrix = smoothing_matrix(total)
     matrix = jnp.concatenate(
-        [lax.dynamic_slice_in_dim(matrix, s, half, axis=1) for s in starts], axis=1
+        [lax.dynamic_slice_in_dim(matrix, s, q, axis=1) for s in starts], axis=1
     )
     outs = []
     for k in range(blocks.shape[0]):

time: 234 us -> 211 us (0.902)
  waiting for transfers between devices: 156 us -> 115 us
  starting transfers between devices: 47.8 us -> 62.8 us
  other arithmetic: 2.04 us -> 5 us
    ppermute x8 -> x14, waiting for transfers between devices: 102 us -> 76.1 us  [the longest x6 33.6 us: ring_sum(): recv_b = lax.ppermute(acc_b, 'shots', bwd)]
    ppermute x3 -> x6, waiting for transfers between devices: 21.1 us -> 0.02 us  [all_gather_smooth_shots(): cur_b = lax.ppermute(cur_b, 'shots', bwd)]
    ppermute x3 -> x6, waiting for transfers between devices: 4.03 us -> 17.1 us  [all_gather_smooth_shots(): cur_f = lax.ppermute(cur_f, 'shots', fwd)]
    ppermute x3 -> x6, starting transfers between devices: 11 us -> 19.4 us  [all_gather_smooth_shots(): cur_b = lax.ppermute(cur_b, 'shots', bwd)]
    all_to_all x1, waiting for transfers between devices: 14.5 us -> 7.59 us  [smooth_along_x(): return lax.all_to_all(cols, 'slab', split_axis=1, concat_axis=2, tiled=True)]
    ppermute x8 -> x14, starting transfers between devices: 23.2 us -> 29.8 us  [the longest x6 13.5 us: ring_sum(): recv_b = lax.ppermute(acc_b, 'shots', bwd)]
    add x6 -> x13, other arithmetic: 0.67 us -> 3.57 us  [the longest x6 2.11 us: ring_sum(): acc_f = recv_f + take(starts((r - 1 - t) % RING))]
  transfers between devices with their start and end apart: 16 -> 28, of which waited for: 12 -> 16; matrix products, arithmetic and copies ran while one was open for 4% -> 5% of each run, Pallas kernels for 0% -> 0%
where the time goes in v5:
time: 211 us
  waiting for transfers between devices  115 us (55%)
  starting transfers between devices  62.8 us (30%)
  local copies, waits for them, and re-layouts  14.9 us (7%)
  matrix products  11.7 us (6%)
  other arithmetic  5 us (2%)
    ppermute x6, waiting for transfers between devices, ring_sum(): recv_b = lax.ppermute(acc_b, 'shots', bwd)  33.6 us
    ppermute x6, starting transfers between devices, all_gather_smooth_shots(): cur_b = lax.ppermute(cur_b, 'shots', bwd)  19.4 us
    ppermute x1, waiting for transfers between devices, all_gather_smooth_shots(): other = lax.ppermute(blocks, 'shots', hi_pairs(n_shots))  19.2 us
    ppermute x6, waiting for transfers between devices, all_gather_smooth_shots(): cur_f = lax.ppermute(cur_f, 'shots', fwd)  17.1 us
    ppermute x1, waiting for transfers between devices, reduce_scatter_shots(): got = lax.ppermute(theirs, 'shots', hi_pairs(n_shots))  16.5 us
    all_to_all x1, waiting for transfers between devices, smooth_along_x(): cols = lax.all_to_all(both, 'slab', split_axis=2, concat_axis=1, tiled=True)  14.6 us
    ppermute x6, starting transfers between devices, ring_sum(): recv_b = lax.ppermute(acc_b, 'shots', bwd)  13.5 us
    dot_general x2, matrix products, all_gather_smooth_shots(): outs.append(jnp.einsum('xij,xjz->xiz', wide, joined, precision=HP))  9.78 us
  transfers between devices with their start and end apart: 28, of which 16 were waited for; matrix products, arithmetic and copies ran while one was open for 5% of the time, Pallas kernels for 0%

profile of v5, /device:TPU:2, one launch (start us, length us, event | category | flops | bytes accessed | tf_op | source)
XLA Modules:
  0.0 211.0 jit_solution(13555932183169779747)
XLA Ops:
  0.8 1.5 constant_dynamic-slice_fusion.14
  2.3 0.3 copy-done.1
  2.7 1.5 constant_dynamic-slice_fusion.12
  4.2 3.1 %collective-permute-start.3 = (f32[3,4,32,256]{3,2,1,0:T(8,128)S(1)}, f32[3,4,32,256]{3,2,1,0:T(8,128)S(1)}, u32[]{:S(2)}, u32[]{:S(2)}) collective-permute-start(f32[3,4,32,256]{3,2,1,0:T(8,128)S(1)} %pad_maximum_fusion.2), channel_id=1, source_target_pairs={{0,96},{32,0},{64,32},{96,64},{128,224},{160,128},{192,160},{224,1... | collective-permute-start | bytes 1179656 | tf_op jit(solution)/shard_map/ppermute | solution.py:46
  7.4 0.1 collective-permute-start
  7.5 8.2 %collective-permute-done.3 = f32[3,4,32,256]{3,2,1,0:T(8,128)S(1)} collective-permute-done((f32[3,4,32,256]{3,2,1,0:T(8,128)S(1)}, f32[3,4,32,256]{3,2,1,0:T(8,128)S(1)}, u32[]{:S(2)}, u32[]{:S(2)}) %collective-permute-start.3) | collective-permute-done | bytes 393248 | tf_op jit(solution)/shard_map/ppermute | solution.py:46
  15.8 3.8 %collective-permute-start.4 = (f32[3,4,32,256]{3,2,1,0:T(8,128)S(1)}, f32[3,4,32,256]{3,2,1,0:T(8,128)S(1)}, u32[]{:S(2)}, u32[]{:S(2)}) collective-permute-start(f32[3,4,32,256]{3,2,1,0:T(8,128)S(1)} %maximum_add_fusion.4), channel_id=1, source_target_pairs={{0,96},{32,0},{64,32},{96,64},{128,224},{160,128},{192,160},{224,1... | collective-permute-start | bytes 1179656 | tf_op jit(solution)/shard_map/ppermute | solution.py:46
  19.7 7.3 %collective-permute-done.4 = f32[3,4,32,256]{3,2,1,0:T(8,128)S(1)} collective-permute-done((f32[3,4,32,256]{3,2,1,0:T(8,128)S(1)}, f32[3,4,32,256]{3,2,1,0:T(8,128)S(1)}, u32[]{:S(2)}, u32[]{:S(2)}) %collective-permute-start.4) | collective-permute-done | bytes 393248 | tf_op jit(solution)/shard_map/ppermute | solution.py:46
  27.1 3.8 %collective-permute-start.5 = (f32[3,4,32,256]{3,2,1,0:T(8,128)S(1)}, f32[3,4,32,256]{3,2,1,0:T(8,128)}, u32[]{:S(2)}, u32[]{:S(2)}) collective-permute-start(f32[3,4,32,256]{3,2,1,0:T(8,128)S(1)} %maximum_add_fusion.5), channel_id=1, source_target_pairs={{0,96},{32,0},{64,32},{96,64},{128,224},{160,128},{192,160},{224,1... | collective-permute-start | bytes 1179656 | tf_op jit(solution)/shard_map/ppermute | solution.py:46
  30.9 0.8 maximum_add_fusion.2
  31.7 5.8 %collective-permute-done.5 = f32[3,4,32,256]{3,2,1,0:T(8,128)} collective-permute-done((f32[3,4,32,256]{3,2,1,0:T(8,128)S(1)}, f32[3,4,32,256]{3,2,1,0:T(8,128)}, u32[]{:S(2)}, u32[]{:S(2)}) %collective-permute-start.5) | collective-permute-done | bytes 393248 | tf_op jit(solution)/shard_map/ppermute | solution.py:46
  37.5 1.1 maximum_add_fusion.6
  38.5 3.5 %collective-permute-done.2 = f32[3,4,32,256]{3,2,1,0:T(8,128)} collective-permute-done((f32[3,4,32,256]{3,2,1,0:T(8,128)}, f32[3,4,32,256]{3,2,1,0:T(8,128)}, u32[]{:S(2)}, u32[]{:S(2)}) %collective-permute-start.2) | collective-permute-done | bytes 393248 | tf_op jit(solution)/shard_map/ppermute | solution.py:45
  42.0 1.1 maximum_add_fusion.3
  43.2 0.1 dynamic-slice_bitcast_fusion.12
  43.3 1.4 copy-done.2
  44.7 0.1 dynamic-slice_bitcast_fusion.13
  44.8 0.5 copy-done.3
  45.3 0.1 dynamic-slice_bitcast_fusion.14
  45.5 0.4 collective-permute-start.9
  45.9 1.8 collective-permute-start.6
  47.7 7.0 %collective-permute-done.9 = f32[3,4,32,256]{3,2,1,0:T(8,128)S(1)} collective-permute-done((f32[3,4,32,256]{3,2,1,0:T(8,128)S(1)}, f32[3,4,32,256]{3,2,1,0:T(8,128)S(1)}, u32[]{:S(2)}, u32[]{:S(2)}) %collective-permute-start.9) | collective-permute-done | bytes 393248 | tf_op jit(solution)/shard_map/ppermute | solution.py:46
  54.7 0.6 collective-permute-start.10
  55.4 1.6 collective-permute-start.7
  57.0 7.2 %collective-permute-start.12 = (f32[3,4,64,256]{3,2,1,0:T(8,128)S(1)}, f32[3,4,64,256]{3,2,1,0:T(8,128)S(1)}, u32[]{:S(2)}, u32[]{:S(2)}) collective-permute-start(f32[3,4,64,256]{3,2,1,0:T(8,128)S(1)} %pad_maximum_fusion), channel_id=1, source_target_pairs={{0,128},{32,160},{64,192},{96,224},{128,0},{160,32},{192,64},{224,... | collective-permute-start | bytes 2359304 | tf_op jit(solution)/shard_map/ppermute | solution.py:59
  64.2 1.8 collective-permute-start.11
  66.1 0.5 collective-permute-start.8
  66.7 0.2 fusion.26
  66.8 5.2 %collective-permute-done.11 = f32[3,4,32,256]{3,2,1,0:T(8,128)S(1)} collective-permute-done((f32[3,4,32,256]{3,2,1,0:T(8,128)S(1)}, f32[3,4,32,256]{3,2,1,0:T(8,128)S(1)}, u32[]{:S(2)}, u32[]{:S(2)}) %collective-permute-start.11) | collective-permute-done | bytes 393248 | tf_op jit(solution)/shard_map/ppermute | solution.py:46
  72.1 3.2 %collective-permute-done.8 = f32[3,4,32,256]{3,2,1,0:T(8,128)S(1)} collective-permute-done((f32[3,4,32,256]{3,2,1,0:T(8,128)S(1)}, f32[3,4,32,256]{3,2,1,0:T(8,128)S(1)}, u32[]{:S(2)}, u32[]{:S(2)}) %collective-permute-start.8) | collective-permute-done | bytes 393248 | tf_op jit(solution)/shard_map/ppermute | solution.py:45
  75.4 16.5 %collective-permute-done.12 = f32[3,4,64,256]{3,2,1,0:T(8,128)S(1)} collective-permute-done((f32[3,4,64,256]{3,2,1,0:T(8,128)S(1)}, f32[3,4,64,256]{3,2,1,0:T(8,128)S(1)}, u32[]{:S(2)}, u32[]{:S(2)}) %collective-permute-start.12) | collective-permute-done | bytes 786464 | tf_op jit(solution)/shard_map/ppermute | solution.py:59
  92.0 0.1 maximum_add_fusion
  92.1 0.7 fusion.15
  92.8 1.1 copy.13
  94.0 7.5 %all-to-all-start = ((f32[2,4,64,256]{3,1,0,2:T(4,128)}), f32[2,4,64,256]{3,1,0,2:T(4,128)S(1)}, u32[]{:S(2)}, u32[]{:S(2)}) async-start(f32[2,4,64,256]{3,1,0,2:T(4,128)} %copy.13), calls=%async_computation | async-start | bytes 1048576 | tf_op jit(solution)/shard_map/all_to_all | solution.py:100
  101.5 0.1 fusion.69
  101.6 14.6 %all-to-all-done = f32[2,4,64,256]{3,1,0,2:T(4,128)S(1)} async-done(((f32[2,4,64,256]{3,1,0,2:T(4,128)}), f32[2,4,64,256]{3,1,0,2:T(4,128)S(1)}, u32[]{:S(2)}, u32[]{:S(2)}) %all-to-all-start) | async-done | bytes 524320 | tf_op jit(solution)/shard_map/all_to_all | solution.py:100
  116.2 0.3 copy.14
  116.5 1.0 convolution_bitcast_fusion
  117.5 1.0 copy.16
  118.5 5.9 %all-to-all-start.1 = ((f32[2,128,2,256]{3,2,0,1:T(2,128)}), f32[2,128,2,256]{3,2,0,1:T(2,128)S(1)}, u32[]{:S(2)}, u32[]{:S(2)}) async-start(f32[2,128,2,256]{3,2,0,1:T(2,128)} %copy.16), calls=%async_computation.1 | async-start | bytes 1048576 | tf_op jit(solution)/shard_map/all_to_all | solution.py:103
  124.4 0.5 fusion.14
  124.9 0.4 fusion.13
  125.3 2.6 %constant_dynamic-slice_fusion.24 = (f32[512,32]{1,0:T(8,128)S(1)}, f32[512,32]{1,0:T(8,128)S(1)}, f32[512,32]{1,0:T(8,128)S(1)}, f32[512,32]{1,0:T(8,128)S(1)},...) fusion(f32[512,512]{1,0:T(8,128)S(1)} %fusion.13, ...), kind=kLoop, calls=%fused_computation.178 | loop fusion | bytes 2097216 | tf_op jit(solution)/shard_map/dynamic_slice | solution.py:84
  127.9 3.3 %concatenate.15 = f32[512,512]{1,0:T(8,128)S(1)} concatenate(f32[512,32]{1,0:T(8,128)} %get-tuple-element.73, f32[512,32]{1,0:T(8,128)} %get-tuple-element.72, f32[512,32]{1,0:T(8,128)} %get-tuple-element.71, f32[512,32]{1,0:T(8,128)} %get-tuple-element.70, f32[512,32]{1,0:T(8,128)} %get-tuple-element.69, f32[512,32]{1,0:T(8,128)} %get-tuple-element.68, ...), dimensions={1} | concatenate | bytes 2097152 | tf_op jit(solution)/shard_map/concatenate | solution.py:83
  131.3 0.2 convolution_bitcast_fusion.1
  131.5 7.6 %all-to-all-done.1 = f32[2,128,2,256]{3,2,0,1:T(2,128)S(1)} async-done(((f32[2,128,2,256]{3,2,0,1:T(2,128)}), f32[2,128,2,256]{3,2,0,1:T(2,128)S(1)}, u32[]{:S(2)}, u32[]{:S(2)}) %all-to-all-start.1) | async-done | bytes 524320 | tf_op jit(solution)/shard_map/all_to_all | solution.py:103
  139.1 0.2 copy.18
  139.3 0.4 all_to_all.33
  139.8 3.2 %collective-permute-start.14 = (f32[2,4,32,256]{3,2,1,0:T(8,128)S(1)}, f32[2,4,32,256]{3,2,1,0:T(8,128)S(1)}, u32[]{:S(2)}, u32[]{:S(2)}) collective-permute-start(f32[2,4,32,256]{3,2,1,0:T(8,128)S(1)} %get-tuple-element.86), channel_id=1, source_target_pairs={{0,96},{32,0},{64,32},{96,64},{128,224},{160,128},{192,160},{224,1... | collective-permute-start | bytes 786440 | tf_op jit(solution)/shard_map/ppermute | solution.py:79
  143.0 5.1 %collective-permute-start.19 = (f32[2,4,64,256]{3,2,1,0:T(8,128)S(1)}, f32[2,4,64,256]{3,2,1,0:T(8,128)S(1)}, u32[]{:S(2)}, u32[]{:S(2)}) collective-permute-start(f32[2,4,64,256]{3,2,1,0:T(8,128)S(1)} %all_to_all.33), channel_id=1, source_target_pairs={{0,128},{32,160},{64,192},{96,224},{128,0},{160,32},{192,64},{224,... | collective-permute-start | bytes 1572872 | tf_op jit(solution)/shard_map/ppermute | solution.py:71
  148.2 2.0 collective-permute-done.13
  150.1 3.2 %collective-permute-start.16 = (f32[2,4,32,256]{3,2,1,0:T(8,128)S(1)}, f32[2,4,32,256]{3,2,1,0:T(8,128)S(1)}, u32[]{:S(2)}, u32[]{:S(2)}) collective-permute-start(f32[2,4,32,256]{3,2,1,0:T(8,128)S(1)} %collective-permute-done.14), channel_id=1, source_target_pairs={{0,96},{32,0},{64,32},{96,64},{128,224},{160,128},{192,160},{224,1... | collective-permute-start | bytes 786440 | tf_op jit(solution)/shard_map/ppermute | solution.py:79
  153.4 19.2 %collective-permute-done.19 = f32[2,4,64,256]{3,2,1,0:T(8,128)S(1)} collective-permute-done((f32[2,4,64,256]{3,2,1,0:T(8,128)S(1)}, f32[2,4,64,256]{3,2,1,0:T(8,128)S(1)}, u32[]{:S(2)}, u32[]{:S(2)}) %collective-permute-start.19) | collective-permute-done | bytes 524320 | tf_op jit(solution)/shard_map/ppermute | solution.py:71
  172.8 3.2 %collective-permute-start.21 = (f32[2,4,32,256]{3,2,1,0:T(8,128)S(1)}, f32[2,4,32,256]{3,2,1,0:T(8,128)S(1)}, u32[]{:S(2)}, u32[]{:S(2)}) collective-permute-start(f32[2,4,32,256]{3,2,1,0:T(8,128)S(1)} %get-tuple-element.84), channel_id=1, source_target_pairs={{0,96},{32,0},{64,32},{96,64},{128,224},{160,128},{192,160},{224,1... | collective-permute-start | bytes 786440 | tf_op jit(solution)/shard_map/ppermute | solution.py:79
  176.0 3.2 %collective-permute-start.18 = (f32[2,4,32,256]{3,2,1,0:T(8,128)S(1)}, f32[2,4,32,256]{3,2,1,0:T(8,128)S(1)}, u32[]{:S(2)}, u32[]{:S(2)}) collective-permute-start(f32[2,4,32,256]{3,2,1,0:T(8,128)S(1)} %collective-permute-done.16), channel_id=1, source_target_pairs={{0,96},{32,0},{64,32},{96,64},{128,224},{160,128},{192,160},{224,1... | collective-permute-start | bytes 786440 | tf_op jit(solution)/shard_map/ppermute | solution.py:79
  179.3 3.9 %collective-permute-done.20 = f32[2,4,32,256]{3,2,1,0:T(8,128)S(1)} collective-permute-done((f32[2,4,32,256]{3,2,1,0:T(8,128)S(1)}, f32[2,4,32,256]{3,2,1,0:T(8,128)S(1)}, u32[]{:S(2)}, u32[]{:S(2)}) %collective-permute-start.20) | collective-permute-done | bytes 262176 | tf_op jit(solution)/shard_map/ppermute | solution.py:78
  183.2 3.2 %collective-permute-start.23 = (f32[2,4,32,256]{3,2,1,0:T(8,128)S(1)}, f32[2,4,32,256]{3,2,1,0:T(8,128)S(1)}, u32[]{:S(2)}, u32[]{:S(2)}) collective-permute-start(f32[2,4,32,256]{3,2,1,0:T(8,128)S(1)} %collective-permute-done.21), channel_id=1, source_target_pairs={{0,96},{32,0},{64,32},{96,64},{128,224},{160,128},{192,160},{224,1... | collective-permute-start | bytes 786440 | tf_op jit(solution)/shard_map/ppermute | solution.py:79
  186.5 2.4 %collective-permute-done.17 = f32[2,4,32,256]{3,2,1,0:T(8,128)S(1)} collective-permute-done((f32[2,4,32,256]{3,2,1,0:T(8,128)S(1)}, f32[2,4,32,256]{3,2,1,0:T(8,128)S(1)}, u32[]{:S(2)}, u32[]{:S(2)}) %collective-permute-start.17) | collective-permute-done | bytes 262176 | tf_op jit(solution)/shard_map/ppermute | solution.py:78
  189.0 4.0 %collective-permute-done.22 = f32[2,4,32,256]{3,2,1,0:T(8,128)S(1)} collective-permute-done((f32[2,4,32,256]{3,2,1,0:T(8,128)S(1)}, f32[2,4,32,256]{3,2,1,0:T(8,128)S(1)}, u32[]{:S(2)}, u32[]{:S(2)}) %collective-permute-start.22) | collective-permute-done | bytes 262176 | tf_op jit(solution)/shard_map/ppermute | solution.py:78
  193.0 3.2 %collective-permute-start.25 = (f32[2,4,32,256]{3,2,1,0:T(8,128)S(1)}, f32[2,4,32,256]{3,2,1,0:T(8,128)S(1)}, u32[]{:S(2)}, u32[]{:S(2)}) collective-permute-start(f32[2,4,32,256]{3,2,1,0:T(8,128)S(1)} %collective-permute-done.23), channel_id=1, source_target_pairs={{0,96},{32,0},{64,32},{96,64},{128,224},{160,128},{192,160},{224,1... | collective-permute-start | bytes 786440 | tf_op jit(solution)/shard_map/ppermute | solution.py:79
  196.3 4.8 %collective-permute-done.24 = f32[2,4,32,256]{3,2,1,0:T(8,128)S(1)} collective-permute-done((f32[2,4,32,256]{3,2,1,0:T(8,128)S(1)}, f32[2,4,32,256]{3,2,1,0:T(8,128)S(1)}, u32[]{:S(2)}, u32[]{:S(2)}) %collective-permute-start.24) | collective-permute-done | bytes 262176 | tf_op jit(solution)/shard_map/ppermute | solution.py:78
  201.2 4.9 %fusion.4 = f32[4,512,256]{2,1,0:T(8,128)} fusion(f32[4,512,256]{2,1,0:T(8,128)S(1)} %get-tuple-element.89, f32[512,512]{1,0:T(8,128)S(1)} %concatenate.15, f32[256]{0:T(256)S(1)} %bitcast.212), kind=kOutput, calls=%fused_computation.4 | convolution fusion | flops 3221749760 | bytes 5243904 | tf_op jit(solution)/shard_map/xij,xjz->xiz/dot_general | solution.py:90
  206.1 4.9 %fusion.7 = f32[4,512,256]{2,1,0:T(8,128)} fusion(f32[4,512,256]{2,1,0:T(8,128)S(1)} %get-tuple-element.88, f32[512,512]{1,0:T(8,128)S(1)} %concatenate.15, f32[256]{0:T(256)S(1)} %bitcast.211), kind=kOutput, calls=%fused_computation.5 | convolution fusion | flops 3221749760 | bytes 5243904 | tf_op jit(solution)/shard_map/xij,xjz->xiz/dot_general | solution.py:90
  (61 shorter events, 1.4 us)
Async XLA Ops:
  0.6 130.6 %copy-start = (f32[2,16]{1,0:T(2,128)S(1)}, f32[2,16]{1,0:T(2,128)}, u32[]{:S(2)}) copy-start(f32[2,16]{1,0:T(2,128)} %param.9) | copy-start | bytes 388
  0.6 2.0 copy-start.1
  4.2 11.5 %collective-permute-start.3 = (f32[3,4,32,256]{3,2,1,0:T(8,128)S(1)}, f32[3,4,32,256]{3,2,1,0:T(8,128)S(1)}, u32[]{:S(2)}, u32[]{:S(2)}) collective-permute-start(f32[3,4,32,256]{3,2,1,0:T(8,128)S(1)} %pad_maximum_fusion.2), channel_id=1, source_target_pairs={{0,96},{32,0},{64,32},{96,64},{128,224},{160,128},{192,160},{224,1... | collective-permute-start | bytes 1179656 | tf_op jit(solution)/shard_map/ppermute | solution.py:46
  7.4 12.2 %collective-permute-start = (f32[3,4,32,256]{3,2,1,0:T(8,128)S(1)}, f32[3,4,32,256]{3,2,1,0:T(8,128)S(1)}, u32[]{:S(2)}, u32[]{:S(2)}) collective-permute-start(f32[3,4,32,256]{3,2,1,0:T(8,128)S(1)} %pad_maximum_fusion.1), channel_id=1, source_target_pairs={{0,32},{32,64},{64,96},{96,0},{128,160},{160,192},{192,224},{224,1... | collective-permute-start | bytes 1179656 | tf_op jit(solution)/shard_map/ppermute | solution.py:45
  15.8 11.3 %collective-permute-start.4 = (f32[3,4,32,256]{3,2,1,0:T(8,128)S(1)}, f32[3,4,32,256]{3,2,1,0:T(8,128)S(1)}, u32[]{:S(2)}, u32[]{:S(2)}) collective-permute-start(f32[3,4,32,256]{3,2,1,0:T(8,128)S(1)} %maximum_add_fusion.4), channel_id=1, source_target_pairs={{0,96},{32,0},{64,32},{96,64},{128,224},{160,128},{192,160},{224,1... | collective-permute-start | bytes 1179656 | tf_op jit(solution)/shard_map/ppermute | solution.py:46
  19.6 11.3 %collective-permute-start.1 = (f32[3,4,32,256]{3,2,1,0:T(8,128)S(1)}, f32[3,4,32,256]{3,2,1,0:T(8,128)S(1)}, u32[]{:S(2)}, u32[]{:S(2)}) collective-permute-start(f32[3,4,32,256]{3,2,1,0:T(8,128)S(1)} %maximum_add_fusion.1), channel_id=1, source_target_pairs={{0,32},{32,64},{64,96},{96,0},{128,160},{160,192},{192,224},{224,1... | collective-permute-start | bytes 1179656 | tf_op jit(solution)/shard_map/ppermute | solution.py:45
  27.1 10.3 %collective-permute-start.5 = (f32[3,4,32,256]{3,2,1,0:T(8,128)S(1)}, f32[3,4,32,256]{3,2,1,0:T(8,128)}, u32[]{:S(2)}, u32[]{:S(2)}) collective-permute-start(f32[3,4,32,256]{3,2,1,0:T(8,128)S(1)} %maximum_add_fusion.5), channel_id=1, source_target_pairs={{0,96},{32,0},{64,32},{96,64},{128,224},{160,128},{192,160},{224,1... | collective-permute-start | bytes 1179656 | tf_op jit(solution)/shard_map/ppermute | solution.py:46
  31.7 10.3 %collective-permute-start.2 = (f32[3,4,32,256]{3,2,1,0:T(8,128)}, f32[3,4,32,256]{3,2,1,0:T(8,128)}, u32[]{:S(2)}, u32[]{:S(2)}) collective-permute-start(f32[3,4,32,256]{3,2,1,0:T(8,128)} %maximum_add_fusion.2), channel_id=1, source_target_pairs={{0,32},{32,64},{64,96},{96,0},{128,160},{160,192},{192,224},{224,1... | collective-permute-start | bytes 1179656 | tf_op jit(solution)/shard_map/ppermute | solution.py:45
  43.1 1.6 copy-start.2
  43.1 2.2 %copy-start.3 = (f32[1,4,512,256]{3,2,1,0:T(8,128)S(1)}, f32[1,4,512,256]{3,2,1,0:T(8,128)}, u32[]{:S(2)}) copy-start(f32[1,4,512,256]{3,2,1,0:T(8,128)} %param.7) | copy-start | bytes 6291460
  45.5 9.2 %collective-permute-start.9 = (f32[3,4,32,256]{3,2,1,0:T(8,128)S(1)}, f32[3,4,32,256]{3,2,1,0:T(8,128)S(1)}, u32[]{:S(2)}, u32[]{:S(2)}) collective-permute-start(f32[3,4,32,256]{3,2,1,0:T(8,128)S(1)} %pad_maximum_fusion.4), channel_id=1, source_target_pairs={{0,96},{32,0},{64,32},{96,64},{128,224},{160,128},{192,160},{224,1... | collective-permute-start | bytes 1179656 | tf_op jit(solution)/shard_map/ppermute | solution.py:46
  45.9 9.5 %collective-permute-start.6 = (f32[3,4,32,256]{3,2,1,0:T(8,128)S(1)}, f32[3,4,32,256]{3,2,1,0:T(8,128)S(1)}, u32[]{:S(2)}, u32[]{:S(2)}) collective-permute-start(f32[3,4,32,256]{3,2,1,0:T(8,128)S(1)} %pad_maximum_fusion.3), channel_id=1, source_target_pairs={{0,32},{32,64},{64,96},{96,0},{128,160},{160,192},{192,224},{224,1... | collective-permute-start | bytes 1179656 | tf_op jit(solution)/shard_map/ppermute | solution.py:45
  54.7 9.4 %collective-permute-start.10 = (f32[3,4,32,256]{3,2,1,0:T(8,128)S(1)}, f32[3,4,32,256]{3,2,1,0:T(8,128)S(1)}, u32[]{:S(2)}, u32[]{:S(2)}) collective-permute-start(f32[3,4,32,256]{3,2,1,0:T(8,128)S(1)} %maximum_add_fusion.10), channel_id=1, source_target_pairs={{0,96},{32,0},{64,32},{96,64},{128,224},{160,128},{192,160},{224,1... | collective-permute-start | bytes 1179656 | tf_op jit(solution)/shard_map/ppermute | solution.py:46
  55.4 10.6 %collective-permute-start.7 = (f32[3,4,32,256]{3,2,1,0:T(8,128)S(1)}, f32[3,4,32,256]{3,2,1,0:T(8,128)S(1)}, u32[]{:S(2)}, u32[]{:S(2)}) collective-permute-start(f32[3,4,32,256]{3,2,1,0:T(8,128)S(1)} %maximum_add_fusion.7), channel_id=1, source_target_pairs={{0,32},{32,64},{64,96},{96,0},{128,160},{160,192},{192,224},{224,1... | collective-permute-start | bytes 1179656 | tf_op jit(solution)/shard_map/ppermute | solution.py:45
  57.0 35.0 %collective-permute-start.12 = (f32[3,4,64,256]{3,2,1,0:T(8,128)S(1)}, f32[3,4,64,256]{3,2,1,0:T(8,128)S(1)}, u32[]{:S(2)}, u32[]{:S(2)}) collective-permute-start(f32[3,4,64,256]{3,2,1,0:T(8,128)S(1)} %pad_maximum_fusion), channel_id=1, source_target_pairs={{0,128},{32,160},{64,192},{96,224},{128,0},{160,32},{192,64},{224,... | collective-permute-start | bytes 2359304 | tf_op jit(solution)/shard_map/ppermute | solution.py:59
  64.2 7.9 %collective-permute-start.11 = (f32[3,4,32,256]{3,2,1,0:T(8,128)S(1)}, f32[3,4,32,256]{3,2,1,0:T(8,128)S(1)}, u32[]{:S(2)}, u32[]{:S(2)}) collective-permute-start(f32[3,4,32,256]{3,2,1,0:T(8,128)S(1)} %maximum_add_fusion.11), channel_id=1, source_target_pairs={{0,96},{32,0},{64,32},{96,64},{128,224},{160,128},{192,160},{224,1... | collective-permute-start | bytes 1179656 | tf_op jit(solution)/shard_map/ppermute | solution.py:46
  66.1 9.2 %collective-permute-start.8 = (f32[3,4,32,256]{3,2,1,0:T(8,128)S(1)}, f32[3,4,32,256]{3,2,1,0:T(8,128)S(1)}, u32[]{:S(2)}, u32[]{:S(2)}) collective-permute-start(f32[3,4,32,256]{3,2,1,0:T(8,128)S(1)} %maximum_add_fusion.8), channel_id=1, source_target_pairs={{0,32},{32,64},{64,96},{96,0},{128,160},{160,192},{192,224},{224,1... | collective-permute-start | bytes 1179656 | tf_op jit(solution)/shard_map/ppermute | solution.py:45
  94.0 22.2 %all-to-all-start = ((f32[2,4,64,256]{3,1,0,2:T(4,128)}), f32[2,4,64,256]{3,1,0,2:T(4,128)S(1)}, u32[]{:S(2)}, u32[]{:S(2)}) async-start(f32[2,4,64,256]{3,1,0,2:T(4,128)} %copy.13), calls=%async_computation | async-start | bytes 1048576 | tf_op jit(solution)/shard_map/all_to_all | solution.py:100
  118.5 20.6 %all-to-all-start.1 = ((f32[2,128,2,256]{3,2,0,1:T(2,128)}), f32[2,128,2,256]{3,2,0,1:T(2,128)S(1)}, u32[]{:S(2)}, u32[]{:S(2)}) async-start(f32[2,128,2,256]{3,2,0,1:T(2,128)} %copy.16), calls=%async_computation.1 | async-start | bytes 1048576 | tf_op jit(solution)/shard_map/all_to_all | solution.py:103
  127.9 3.4 %copy-start.4 = (s32[256]{0:T(256)S(1)}, s32[256]{0:T(256)}, u32[]{:S(2)}) copy-start(s32[256]{0:T(256)} %param.8) | copy-start | bytes 3076
  139.7 10.4 %collective-permute-start.13 = (f32[2,4,32,256]{3,2,1,0:T(8,128)S(1)}, f32[2,4,32,256]{3,2,1,0:T(8,128)S(1)}, u32[]{:S(2)}, u32[]{:S(2)}) collective-permute-start(f32[2,4,32,256]{3,2,1,0:T(8,128)S(1)} %get-tuple-element.87), channel_id=1, source_target_pairs={{0,32},{32,64},{64,96},{96,0},{128,160},{160,192},{192,224},{224,1... | collective-permute-start | bytes 786440 | tf_op jit(solution)/shard_map/ppermute | solution.py:78
  139.8 10.4 %collective-permute-start.14 = (f32[2,4,32,256]{3,2,1,0:T(8,128)S(1)}, f32[2,4,32,256]{3,2,1,0:T(8,128)S(1)}, u32[]{:S(2)}, u32[]{:S(2)}) collective-permute-start(f32[2,4,32,256]{3,2,1,0:T(8,128)S(1)} %get-tuple-element.86), channel_id=1, source_target_pairs={{0,96},{32,0},{64,32},{96,64},{128,224},{160,128},{192,160},{224,1... | collective-permute-start | bytes 786440 | tf_op jit(solution)/shard_map/ppermute | solution.py:79
  143.0 29.6 %collective-permute-start.19 = (f32[2,4,64,256]{3,2,1,0:T(8,128)S(1)}, f32[2,4,64,256]{3,2,1,0:T(8,128)S(1)}, u32[]{:S(2)}, u32[]{:S(2)}) collective-permute-start(f32[2,4,64,256]{3,2,1,0:T(8,128)S(1)} %all_to_all.33), channel_id=1, source_target_pairs={{0,128},{32,160},{64,192},{96,224},{128,0},{160,32},{192,64},{224,... | collective-permute-start | bytes 1572872 | tf_op jit(solution)/shard_map/ppermute | solution.py:71
  150.1 25.9 %collective-permute-start.15 = (f32[2,4,32,256]{3,2,1,0:T(8,128)S(1)}, f32[2,4,32,256]{3,2,1,0:T(8,128)S(1)}, u32[]{:S(2)}, u32[]{:S(2)}) collective-permute-start(f32[2,4,32,256]{3,2,1,0:T(8,128)S(1)} %collective-permute-done.13), channel_id=1, source_target_pairs={{0,32},{32,64},{64,96},{96,0},{128,160},{160,192},{192,224},{224,1... | collective-permute-start | bytes 786440 | tf_op jit(solution)/shard_map/ppermute | solution.py:78
  150.1 25.9 %collective-permute-start.16 = (f32[2,4,32,256]{3,2,1,0:T(8,128)S(1)}, f32[2,4,32,256]{3,2,1,0:T(8,128)S(1)}, u32[]{:S(2)}, u32[]{:S(2)}) collective-permute-start(f32[2,4,32,256]{3,2,1,0:T(8,128)S(1)} %collective-permute-done.14), channel_id=1, source_target_pairs={{0,96},{32,0},{64,32},{96,64},{128,224},{160,128},{192,160},{224,1... | collective-permute-start | bytes 786440 | tf_op jit(solution)/shard_map/ppermute | solution.py:79
  172.7 10.5 %collective-permute-start.20 = (f32[2,4,32,256]{3,2,1,0:T(8,128)S(1)}, f32[2,4,32,256]{3,2,1,0:T(8,128)S(1)}, u32[]{:S(2)}, u32[]{:S(2)}) collective-permute-start(f32[2,4,32,256]{3,2,1,0:T(8,128)S(1)} %get-tuple-element.85), channel_id=1, source_target_pairs={{0,32},{32,64},{64,96},{96,0},{128,160},{160,192},{192,224},{224,1... | collective-permute-start | bytes 786440 | tf_op jit(solution)/shard_map/ppermute | solution.py:78
  172.8 10.4 %collective-permute-start.21 = (f32[2,4,32,256]{3,2,1,0:T(8,128)S(1)}, f32[2,4,32,256]{3,2,1,0:T(8,128)S(1)}, u32[]{:S(2)}, u32[]{:S(2)}) collective-permute-start(f32[2,4,32,256]{3,2,1,0:T(8,128)S(1)} %get-tuple-element.84), channel_id=1, source_target_pairs={{0,96},{32,0},{64,32},{96,64},{128,224},{160,128},{192,160},{224,1... | collective-permute-start | bytes 786440 | tf_op jit(solution)/shard_map/ppermute | solution.py:79
  176.0 12.8 %collective-permute-start.17 = (f32[2,4,32,256]{3,2,1,0:T(8,128)S(1)}, f32[2,4,32,256]{3,2,1,0:T(8,128)S(1)}, u32[]{:S(2)}, u32[]{:S(2)}) collective-permute-start(f32[2,4,32,256]{3,2,1,0:T(8,128)S(1)} %collective-permute-done.15), channel_id=1, source_target_pairs={{0,32},{32,64},{64,96},{96,0},{128,160},{160,192},{192,224},{224,1... | collective-permute-start | bytes 786440 | tf_op jit(solution)/shard_map/ppermute | solution.py:78
  176.0 12.8 %collective-permute-start.18 = (f32[2,4,32,256]{3,2,1,0:T(8,128)S(1)}, f32[2,4,32,256]{3,2,1,0:T(8,128)S(1)}, u32[]{:S(2)}, u32[]{:S(2)}) collective-permute-start(f32[2,4,32,256]{3,2,1,0:T(8,128)S(1)} %collective-permute-done.16), channel_id=1, source_target_pairs={{0,96},{32,0},{64,32},{96,64},{128,224},{160,128},{192,160},{224,1... | collective-permute-start | bytes 786440 | tf_op jit(solution)/shard_map/ppermute | solution.py:79
  183.2 9.8 %collective-permute-start.22 = (f32[2,4,32,256]{3,2,1,0:T(8,128)S(1)}, f32[2,4,32,256]{3,2,1,0:T(8,128)S(1)}, u32[]{:S(2)}, u32[]{:S(2)}) collective-permute-start(f32[2,4,32,256]{3,2,1,0:T(8,128)S(1)} %collective-permute-done.20), channel_id=1, source_target_pairs={{0,32},{32,64},{64,96},{96,0},{128,160},{160,192},{192,224},{224,1... | collective-permute-start | bytes 786440 | tf_op jit(solution)/shard_map/ppermute | solution.py:78
  183.2 9.8 %collective-permute-start.23 = (f32[2,4,32,256]{3,2,1,0:T(8,128)S(1)}, f32[2,4,32,256]{3,2,1,0:T(8,128)S(1)}, u32[]{:S(2)}, u32[]{:S(2)}) collective-permute-start(f32[2,4,32,256]{3,2,1,0:T(8,128)S(1)} %collective-permute-done.21), channel_id=1, source_target_pairs={{0,96},{32,0},{64,32},{96,64},{128,224},{160,128},{192,160},{224,1... | collective-permute-start | bytes 786440 | tf_op jit(solution)/shard_map/ppermute | solution.py:79
  193.0 8.1 %collective-permute-start.24 = (f32[2,4,32,256]{3,2,1,0:T(8,128)S(1)}, f32[2,4,32,256]{3,2,1,0:T(8,128)S(1)}, u32[]{:S(2)}, u32[]{:S(2)}) collective-permute-start(f32[2,4,32,256]{3,2,1,0:T(8,128)S(1)} %collective-permute-done.22), channel_id=1, source_target_pairs={{0,32},{32,64},{64,96},{96,0},{128,160},{160,192},{192,224},{224,1... | collective-permute-start | bytes 786440 | tf_op jit(solution)/shard_map/ppermute | solution.py:78
  193.0 8.1 %collective-permute-start.25 = (f32[2,4,32,256]{3,2,1,0:T(8,128)S(1)}, f32[2,4,32,256]{3,2,1,0:T(8,128)S(1)}, u32[]{:S(2)}, u32[]{:S(2)}) collective-permute-start(f32[2,4,32,256]{3,2,1,0:T(8,128)S(1)} %collective-permute-done.23), channel_id=1, source_target_pairs={{0,96},{32,0},{64,32},{96,64},{128,224},{160,128},{192,160},{224,1... | collective-permute-start | bytes 786440 | tf_op jit(solution)/shard_map/ppermute | solution.py:79

commit v6 on v5

--- a/solution.py
+++ b/solution.py
@@ -30,7 +30,7 @@
     return lax.dynamic_slice_in_dim(field, start, size, axis=1)
 
 
-def ring_sum(fields, starts, size, n_shots):
+def ring_sum(fields, starts, size, n_shots, gate=None):
     idx = lax.axis_index("shots")
     r = idx % RING
     q = size // 2
@@ -44,6 +44,8 @@
     for t in range(1, RING):
         recv_f = lax.ppermute(acc_f, "shots", fwd)
         recv_b = lax.ppermute(acc_b, "shots", bwd)
+        if gate is not None and t == RING - 1:
+            recv_f, recv_b, gate = lax.optimization_barrier((recv_f, recv_b, gate))
         acc_f = recv_f + take(starts((r - 1 - t) % RING))
         acc_b = recv_b + take(starts((r + 1 + t) % RING) + q)
     return jnp.concatenate([acc_f, acc_b], axis=2)
@@ -57,7 +59,7 @@
     theirs = ring_sum(fields, lambda c: c * chunk + (1 - h) * half, half, n_shots)
     fields, theirs = lax.optimization_barrier((tuple(fields), theirs))
     got = lax.ppermute(theirs, "shots", hi_pairs(n_shots))
-    mine = ring_sum(fields, lambda c: c * chunk + h * half, half, n_shots)
+    mine = ring_sum(fields, lambda c: c * chunk + h * half, half, n_shots, gate=got)
     return mine + got
 
 

time: 211 us -> 213 us (level)
  starting transfers between devices: 62.8 us -> 66.4 us
    ppermute x6, waiting for transfers between devices: 33.6 us -> 21.4 us  [ring_sum(): recv_b = lax.ppermute(acc_b, 'shots', bwd)]
    ppermute x1, waiting for transfers between devices: 16.5 us -> 24.6 us  [reduce_scatter_shots(): got = lax.ppermute(theirs, 'shots', hi_pairs(n_shots))]
    ppermute x6, starting transfers between devices: 13.5 us -> 20.7 us  [ring_sum(): recv_b = lax.ppermute(acc_b, 'shots', bwd)]
    ppermute x6, starting transfers between devices: 4.01 us -> 0.42 us  [ring_sum(): recv_f = lax.ppermute(acc_f, 'shots', fwd)]
    ppermute x6, waiting for transfers between devices: 6.71 us -> 9.27 us  [ring_sum(): recv_f = lax.ppermute(acc_f, 'shots', fwd)]
  transfers between devices with their start and end apart: 28 -> 28, of which waited for: 16 -> 14; matrix products, arithmetic and copies ran while one was open for 5% -> 5% of each run, Pallas kernels for 0% -> 0%
where the time goes in v6:
time: 213 us
  waiting for transfers between devices  114 us (54%)
  starting transfers between devices  66.4 us (31%)
  local copies, waits for them, and re-layouts  14.9 us (7%)
  matrix products  11.7 us (5%)
  other arithmetic  5.02 us (2%)
    ppermute x1, waiting for transfers between devices, reduce_scatter_shots(): got = lax.ppermute(theirs, 'shots', hi_pairs(n_shots))  24.6 us
    ppermute x6, waiting for transfers between devices, ring_sum(): recv_b = lax.ppermute(acc_b, 'shots', bwd)  21.4 us
    ppermute x6, starting transfers between devices, ring_sum(): recv_b = lax.ppermute(acc_b, 'shots', bwd)  20.7 us
    ppermute x6, starting transfers between devices, all_gather_smooth_shots(): cur_b = lax.ppermute(cur_b, 'shots', bwd)  19.4 us
    ppermute x1, waiting for transfers between devices, all_gather_smooth_shots(): other = lax.ppermute(blocks, 'shots', hi_pairs(n_shots))  19.2 us
    ppermute x6, waiting for transfers between devices, all_gather_smooth_shots(): cur_f = lax.ppermute(cur_f, 'shots', fwd)  17.1 us
    all_to_all x1, waiting for transfers between devices, smooth_along_x(): cols = lax.all_to_all(both, 'slab', split_axis=2, concat_axis=1, tiled=True)  14.6 us
    dot_general x2, matrix products, all_gather_smooth_shots(): outs.append(jnp.einsum('xij,xjz->xiz', wide, joined, precision=HP))  9.79 us
  transfers between devices with their start and end apart: 28, of which 14 were waited for; matrix products, arithmetic and copies ran while one was open for 5% of the time, Pallas kernels for 0%

profile of v6, /device:TPU:2, one launch (start us, length us, event | category | flops | bytes accessed | tf_op | source)
XLA Modules:
  0.0 213.1 jit_solution(6431057777997423933)
XLA Ops:
  0.8 1.5 constant_dynamic-slice_fusion.14
  2.3 0.3 copy-done.1
  2.7 1.5 constant_dynamic-slice_fusion.12
  4.2 3.1 %collective-permute-start.3 = (f32[3,4,32,256]{3,2,1,0:T(8,128)S(1)}, f32[3,4,32,256]{3,2,1,0:T(8,128)S(1)}, u32[]{:S(2)}, u32[]{:S(2)}) collective-permute-start(f32[3,4,32,256]{3,2,1,0:T(8,128)S(1)} %pad_maximum_fusion.2), channel_id=1, source_target_pairs={{0,96},{32,0},{64,32},{96,64},{128,224},{160,128},{192,160},{224,1... | collective-permute-start | bytes 1179656 | tf_op jit(solution)/shard_map/ppermute | solution.py:46
  7.5 8.2 %collective-permute-done.3 = f32[3,4,32,256]{3,2,1,0:T(8,128)S(1)} collective-permute-done((f32[3,4,32,256]{3,2,1,0:T(8,128)S(1)}, f32[3,4,32,256]{3,2,1,0:T(8,128)S(1)}, u32[]{:S(2)}, u32[]{:S(2)}) %collective-permute-start.3) | collective-permute-done | bytes 393248 | tf_op jit(solution)/shard_map/ppermute | solution.py:46
  15.8 3.8 %collective-permute-start.4 = (f32[3,4,32,256]{3,2,1,0:T(8,128)S(1)}, f32[3,4,32,256]{3,2,1,0:T(8,128)S(1)}, u32[]{:S(2)}, u32[]{:S(2)}) collective-permute-start(f32[3,4,32,256]{3,2,1,0:T(8,128)S(1)} %maximum_add_fusion.4), channel_id=1, source_target_pairs={{0,96},{32,0},{64,32},{96,64},{128,224},{160,128},{192,160},{224,1... | collective-permute-start | bytes 1179656 | tf_op jit(solution)/shard_map/ppermute | solution.py:46
  19.6 0.1 collective-permute-start.1
  19.7 7.3 %collective-permute-done.4 = f32[3,4,32,256]{3,2,1,0:T(8,128)S(1)} collective-permute-done((f32[3,4,32,256]{3,2,1,0:T(8,128)S(1)}, f32[3,4,32,256]{3,2,1,0:T(8,128)S(1)}, u32[]{:S(2)}, u32[]{:S(2)}) %collective-permute-start.4) | collective-permute-done | bytes 393248 | tf_op jit(solution)/shard_map/ppermute | solution.py:46
  27.1 3.8 %collective-permute-start.5 = (f32[3,4,32,256]{3,2,1,0:T(8,128)S(1)}, f32[3,4,32,256]{3,2,1,0:T(8,128)}, u32[]{:S(2)}, u32[]{:S(2)}) collective-permute-start(f32[3,4,32,256]{3,2,1,0:T(8,128)S(1)} %maximum_add_fusion.5), channel_id=1, source_target_pairs={{0,96},{32,0},{64,32},{96,64},{128,224},{160,128},{192,160},{224,1... | collective-permute-start | bytes 1179656 | tf_op jit(solution)/shard_map/ppermute | solution.py:46
  30.9 0.8 maximum_add_fusion.2
  31.7 5.8 %collective-permute-done.5 = f32[3,4,32,256]{3,2,1,0:T(8,128)} collective-permute-done((f32[3,4,32,256]{3,2,1,0:T(8,128)S(1)}, f32[3,4,32,256]{3,2,1,0:T(8,128)}, u32[]{:S(2)}, u32[]{:S(2)}) %collective-permute-start.5) | collective-permute-done | bytes 393248 | tf_op jit(solution)/shard_map/ppermute | solution.py:46
  37.5 1.1 maximum_add_fusion.6
  38.5 3.5 %collective-permute-done.2 = f32[3,4,32,256]{3,2,1,0:T(8,128)} collective-permute-done((f32[3,4,32,256]{3,2,1,0:T(8,128)}, f32[3,4,32,256]{3,2,1,0:T(8,128)}, u32[]{:S(2)}, u32[]{:S(2)}) %collective-permute-start.2) | collective-permute-done | bytes 393248 | tf_op jit(solution)/shard_map/ppermute | solution.py:45
  42.0 1.1 maximum_add_fusion.3
  43.2 0.1 dynamic-slice_bitcast_fusion.3
  43.3 1.4 copy-done.2
  44.7 0.1 dynamic-slice_bitcast_fusion.4
  44.8 0.5 copy-done.3
  45.3 0.1 dynamic-slice_bitcast_fusion.5
  45.5 0.1 collective-permute-start.6
  45.6 3.3 %collective-permute-start.9 = (f32[3,4,32,256]{3,2,1,0:T(8,128)S(1)}, f32[3,4,32,256]{3,2,1,0:T(8,128)S(1)}, u32[]{:S(2)}, u32[]{:S(2)}) collective-permute-start(f32[3,4,32,256]{3,2,1,0:T(8,128)S(1)} %pad_maximum_fusion.4), channel_id=1, source_target_pairs={{0,96},{32,0},{64,32},{96,64},{128,224},{160,128},{192,160},{224,1... | collective-permute-start | bytes 1179656 | tf_op jit(solution)/shard_map/ppermute | solution.py:46
  48.9 5.8 %collective-permute-done.6 = f32[3,4,32,256]{3,2,1,0:T(8,128)S(1)} collective-permute-done((f32[3,4,32,256]{3,2,1,0:T(8,128)S(1)}, f32[3,4,32,256]{3,2,1,0:T(8,128)S(1)}, u32[]{:S(2)}, u32[]{:S(2)}) %collective-permute-start.6) | collective-permute-done | bytes 393248 | tf_op jit(solution)/shard_map/ppermute | solution.py:45
  54.7 0.1 collective-permute-start.7
  54.9 3.3 %collective-permute-start.10 = (f32[3,4,32,256]{3,2,1,0:T(8,128)S(1)}, f32[3,4,32,256]{3,2,1,0:T(8,128)S(1)}, u32[]{:S(2)}, u32[]{:S(2)}) collective-permute-start(f32[3,4,32,256]{3,2,1,0:T(8,128)S(1)} %maximum_add_fusion.9), channel_id=1, source_target_pairs={{0,96},{32,0},{64,32},{96,64},{128,224},{160,128},{192,160},{224,1... | collective-permute-start | bytes 1179656 | tf_op jit(solution)/shard_map/ppermute | solution.py:46
  58.2 7.2 %collective-permute-start.12 = (f32[3,4,64,256]{3,2,1,0:T(8,128)S(1)}, f32[3,4,64,256]{3,2,1,0:T(8,128)S(1)}, u32[]{:S(2)}, u32[]{:S(2)}) collective-permute-start(f32[3,4,64,256]{3,2,1,0:T(8,128)S(1)} %pad_maximum_fusion), channel_id=1, source_target_pairs={{0,128},{32,160},{64,192},{96,224},{128,0},{160,32},{192,64},{224,... | collective-permute-start | bytes 2359304 | tf_op jit(solution)/shard_map/ppermute | solution.py:61
  65.5 0.1 collective-permute-start.8
  65.7 3.5 %collective-permute-start.11 = (f32[3,4,32,256]{3,2,1,0:T(8,128)S(1)}, f32[3,4,32,256]{3,2,1,0:T(8,128)S(1)}, u32[]{:S(2)}, u32[]{:S(2)}) collective-permute-start(f32[3,4,32,256]{3,2,1,0:T(8,128)S(1)} %maximum_add_fusion.10), channel_id=1, source_target_pairs={{0,96},{32,0},{64,32},{96,64},{128,224},{160,128},{192,160},{224,1... | collective-permute-start | bytes 1179656 | tf_op jit(solution)/shard_map/ppermute | solution.py:46
  69.1 0.2 fusion.26
  69.3 24.6 %collective-permute-done.12 = f32[3,4,64,256]{3,2,1,0:T(8,128)S(1)} collective-permute-done((f32[3,4,64,256]{3,2,1,0:T(8,128)S(1)}, f32[3,4,64,256]{3,2,1,0:T(8,128)S(1)}, u32[]{:S(2)}, u32[]{:S(2)}) %collective-permute-start.12) | collective-permute-done | bytes 786464 | tf_op jit(solution)/shard_map/ppermute | solution.py:61
  94.0 0.1 maximum_add_fusion
  94.2 0.7 fusion.15
  94.9 1.1 copy.13
  96.1 7.5 %all-to-all-start = ((f32[2,4,64,256]{3,1,0,2:T(4,128)}), f32[2,4,64,256]{3,1,0,2:T(4,128)S(1)}, u32[]{:S(2)}, u32[]{:S(2)}) async-start(f32[2,4,64,256]{3,1,0,2:T(4,128)} %copy.13), calls=%async_computation | async-start | bytes 1048576 | tf_op jit(solution)/shard_map/all_to_all | solution.py:102
  103.6 0.1 fusion.69
  103.7 14.6 %all-to-all-done = f32[2,4,64,256]{3,1,0,2:T(4,128)S(1)} async-done(((f32[2,4,64,256]{3,1,0,2:T(4,128)}), f32[2,4,64,256]{3,1,0,2:T(4,128)S(1)}, u32[]{:S(2)}, u32[]{:S(2)}) %all-to-all-start) | async-done | bytes 524320 | tf_op jit(solution)/shard_map/all_to_all | solution.py:102
  118.3 0.3 copy.14
  118.6 1.0 convolution_bitcast_fusion
  119.6 1.0 copy.16
  120.6 5.9 %all-to-all-start.1 = ((f32[2,128,2,256]{3,2,0,1:T(2,128)}), f32[2,128,2,256]{3,2,0,1:T(2,128)S(1)}, u32[]{:S(2)}, u32[]{:S(2)}) async-start(f32[2,128,2,256]{3,2,0,1:T(2,128)} %copy.16), calls=%async_computation.1 | async-start | bytes 1048576 | tf_op jit(solution)/shard_map/all_to_all | solution.py:105
  126.5 0.5 fusion.14
  127.0 0.4 fusion.13
  127.4 2.6 %constant_dynamic-slice_fusion.24 = (f32[512,32]{1,0:T(8,128)S(1)}, f32[512,32]{1,0:T(8,128)S(1)}, f32[512,32]{1,0:T(8,128)S(1)}, f32[512,32]{1,0:T(8,128)S(1)},...) fusion(f32[512,512]{1,0:T(8,128)S(1)} %fusion.13, ...), kind=kLoop, calls=%fused_computation.178 | loop fusion | bytes 2097216 | tf_op jit(solution)/shard_map/dynamic_slice | solution.py:86
  130.0 3.3 %concatenate.15 = f32[512,512]{1,0:T(8,128)S(1)} concatenate(f32[512,32]{1,0:T(8,128)} %get-tuple-element.77, f32[512,32]{1,0:T(8,128)} %get-tuple-element.76, f32[512,32]{1,0:T(8,128)} %get-tuple-element.75, f32[512,32]{1,0:T(8,128)} %get-tuple-element.74, f32[512,32]{1,0:T(8,128)} %get-tuple-element.73, f32[512,32]{1,0:T(8,128)} %get-tuple-element.72, ...), dimensions={1} | concatenate | bytes 2097152 | tf_op jit(solution)/shard_map/concatenate | solution.py:85
  133.4 0.2 convolution_bitcast_fusion.1
  133.6 7.6 %all-to-all-done.1 = f32[2,128,2,256]{3,2,0,1:T(2,128)S(1)} async-done(((f32[2,128,2,256]{3,2,0,1:T(2,128)}), f32[2,128,2,256]{3,2,0,1:T(2,128)S(1)}, u32[]{:S(2)}, u32[]{:S(2)}) %all-to-all-start.1) | async-done | bytes 524320 | tf_op jit(solution)/shard_map/all_to_all | solution.py:105
  141.2 0.2 copy.18
  141.4 0.4 all_to_all.33
  141.8 0.1 collective-permute-start.13
  141.9 3.2 %collective-permute-start.14 = (f32[2,4,32,256]{3,2,1,0:T(8,128)S(1)}, f32[2,4,32,256]{3,2,1,0:T(8,128)S(1)}, u32[]{:S(2)}, u32[]{:S(2)}) collective-permute-start(f32[2,4,32,256]{3,2,1,0:T(8,128)S(1)} %get-tuple-element.90), channel_id=1, source_target_pairs={{0,96},{32,0},{64,32},{96,64},{128,224},{160,128},{192,160},{224,1... | collective-permute-start | bytes 786440 | tf_op jit(solution)/shard_map/ppermute | solution.py:81
  145.1 5.1 %collective-permute-start.19 = (f32[2,4,64,256]{3,2,1,0:T(8,128)S(1)}, f32[2,4,64,256]{3,2,1,0:T(8,128)S(1)}, u32[]{:S(2)}, u32[]{:S(2)}) collective-permute-start(f32[2,4,64,256]{3,2,1,0:T(8,128)S(1)} %all_to_all.33), channel_id=1, source_target_pairs={{0,128},{32,160},{64,192},{96,224},{128,0},{160,32},{192,64},{224,... | collective-permute-start | bytes 1572872 | tf_op jit(solution)/shard_map/ppermute | solution.py:73
  150.3 2.0 collective-permute-done.13
  152.2 3.2 %collective-permute-start.16 = (f32[2,4,32,256]{3,2,1,0:T(8,128)S(1)}, f32[2,4,32,256]{3,2,1,0:T(8,128)S(1)}, u32[]{:S(2)}, u32[]{:S(2)}) collective-permute-start(f32[2,4,32,256]{3,2,1,0:T(8,128)S(1)} %collective-permute-done.14), channel_id=1, source_target_pairs={{0,96},{32,0},{64,32},{96,64},{128,224},{160,128},{192,160},{224,1... | collective-permute-start | bytes 786440 | tf_op jit(solution)/shard_map/ppermute | solution.py:81
  155.5 19.2 %collective-permute-done.19 = f32[2,4,64,256]{3,2,1,0:T(8,128)S(1)} collective-permute-done((f32[2,4,64,256]{3,2,1,0:T(8,128)S(1)}, f32[2,4,64,256]{3,2,1,0:T(8,128)S(1)}, u32[]{:S(2)}, u32[]{:S(2)}) %collective-permute-start.19) | collective-permute-done | bytes 524320 | tf_op jit(solution)/shard_map/ppermute | solution.py:73
  174.8 0.1 collective-permute-start.20
  174.9 3.2 %collective-permute-start.21 = (f32[2,4,32,256]{3,2,1,0:T(8,128)S(1)}, f32[2,4,32,256]{3,2,1,0:T(8,128)S(1)}, u32[]{:S(2)}, u32[]{:S(2)}) collective-permute-start(f32[2,4,32,256]{3,2,1,0:T(8,128)S(1)} %get-tuple-element.88), channel_id=1, source_target_pairs={{0,96},{32,0},{64,32},{96,64},{128,224},{160,128},{192,160},{224,1... | collective-permute-start | bytes 786440 | tf_op jit(solution)/shard_map/ppermute | solution.py:81
  178.1 3.2 %collective-permute-start.18 = (f32[2,4,32,256]{3,2,1,0:T(8,128)S(1)}, f32[2,4,32,256]{3,2,1,0:T(8,128)S(1)}, u32[]{:S(2)}, u32[]{:S(2)}) collective-permute-start(f32[2,4,32,256]{3,2,1,0:T(8,128)S(1)} %collective-permute-done.16), channel_id=1, source_target_pairs={{0,96},{32,0},{64,32},{96,64},{128,224},{160,128},{192,160},{224,1... | collective-permute-start | bytes 786440 | tf_op jit(solution)/shard_map/ppermute | solution.py:81
  181.4 3.9 %collective-permute-done.20 = f32[2,4,32,256]{3,2,1,0:T(8,128)S(1)} collective-permute-done((f32[2,4,32,256]{3,2,1,0:T(8,128)S(1)}, f32[2,4,32,256]{3,2,1,0:T(8,128)S(1)}, u32[]{:S(2)}, u32[]{:S(2)}) %collective-permute-start.20) | collective-permute-done | bytes 262176 | tf_op jit(solution)/shard_map/ppermute | solution.py:80
  185.3 3.2 %collective-permute-start.23 = (f32[2,4,32,256]{3,2,1,0:T(8,128)S(1)}, f32[2,4,32,256]{3,2,1,0:T(8,128)S(1)}, u32[]{:S(2)}, u32[]{:S(2)}) collective-permute-start(f32[2,4,32,256]{3,2,1,0:T(8,128)S(1)} %collective-permute-done.21), channel_id=1, source_target_pairs={{0,96},{32,0},{64,32},{96,64},{128,224},{160,128},{192,160},{224,1... | collective-permute-start | bytes 786440 | tf_op jit(solution)/shard_map/ppermute | solution.py:81
  188.5 2.4 %collective-permute-done.17 = f32[2,4,32,256]{3,2,1,0:T(8,128)S(1)} collective-permute-done((f32[2,4,32,256]{3,2,1,0:T(8,128)S(1)}, f32[2,4,32,256]{3,2,1,0:T(8,128)S(1)}, u32[]{:S(2)}, u32[]{:S(2)}) %collective-permute-start.17) | collective-permute-done | bytes 262176 | tf_op jit(solution)/shard_map/ppermute | solution.py:80
  191.1 4.0 %collective-permute-done.22 = f32[2,4,32,256]{3,2,1,0:T(8,128)S(1)} collective-permute-done((f32[2,4,32,256]{3,2,1,0:T(8,128)S(1)}, f32[2,4,32,256]{3,2,1,0:T(8,128)S(1)}, u32[]{:S(2)}, u32[]{:S(2)}) %collective-permute-start.22) | collective-permute-done | bytes 262176 | tf_op jit(solution)/shard_map/ppermute | solution.py:80
  195.1 3.2 %collective-permute-start.25 = (f32[2,4,32,256]{3,2,1,0:T(8,128)S(1)}, f32[2,4,32,256]{3,2,1,0:T(8,128)S(1)}, u32[]{:S(2)}, u32[]{:S(2)}) collective-permute-start(f32[2,4,32,256]{3,2,1,0:T(8,128)S(1)} %collective-permute-done.23), channel_id=1, source_target_pairs={{0,96},{32,0},{64,32},{96,64},{128,224},{160,128},{192,160},{224,1... | collective-permute-start | bytes 786440 | tf_op jit(solution)/shard_map/ppermute | solution.py:81
  198.4 4.8 %collective-permute-done.24 = f32[2,4,32,256]{3,2,1,0:T(8,128)S(1)} collective-permute-done((f32[2,4,32,256]{3,2,1,0:T(8,128)S(1)}, f32[2,4,32,256]{3,2,1,0:T(8,128)S(1)}, u32[]{:S(2)}, u32[]{:S(2)}) %collective-permute-start.24) | collective-permute-done | bytes 262176 | tf_op jit(solution)/shard_map/ppermute | solution.py:80
  203.3 4.9 %fusion.4 = f32[4,512,256]{2,1,0:T(8,128)} fusion(f32[4,512,256]{2,1,0:T(8,128)S(1)} %get-tuple-element.93, f32[512,512]{1,0:T(8,128)S(1)} %concatenate.15, f32[256]{0:T(256)S(1)} %bitcast.212), kind=kOutput, calls=%fused_computation.4 | convolution fusion | flops 3221749760 | bytes 5243904 | tf_op jit(solution)/shard_map/xij,xjz->xiz/dot_general | solution.py:92
  208.2 4.9 %fusion.7 = f32[4,512,256]{2,1,0:T(8,128)} fusion(f32[4,512,256]{2,1,0:T(8,128)S(1)} %get-tuple-element.92, f32[512,512]{1,0:T(8,128)S(1)} %concatenate.15, f32[256]{0:T(256)S(1)} %bitcast.211), kind=kOutput, calls=%fused_computation.5 | convolution fusion | flops 3221749760 | bytes 5243904 | tf_op jit(solution)/shard_map/xij,xjz->xiz/dot_general | solution.py:92
  (61 shorter events, 1.3 us)
Async XLA Ops:
  0.6 132.7 %copy-start = (f32[2,16]{1,0:T(2,128)S(1)}, f32[2,16]{1,0:T(2,128)}, u32[]{:S(2)}) copy-start(f32[2,16]{1,0:T(2,128)} %param.9) | copy-start | bytes 388
  0.6 2.0 copy-start.1
  4.2 11.5 %collective-permute-start.3 = (f32[3,4,32,256]{3,2,1,0:T(8,128)S(1)}, f32[3,4,32,256]{3,2,1,0:T(8,128)S(1)}, u32[]{:S(2)}, u32[]{:S(2)}) collective-permute-start(f32[3,4,32,256]{3,2,1,0:T(8,128)S(1)} %pad_maximum_fusion.2), channel_id=1, source_target_pairs={{0,96},{32,0},{64,32},{96,64},{128,224},{160,128},{192,160},{224,1... | collective-permute-start | bytes 1179656 | tf_op jit(solution)/shard_map/ppermute | solution.py:46
  7.4 12.2 %collective-permute-start = (f32[3,4,32,256]{3,2,1,0:T(8,128)S(1)}, f32[3,4,32,256]{3,2,1,0:T(8,128)S(1)}, u32[]{:S(2)}, u32[]{:S(2)}) collective-permute-start(f32[3,4,32,256]{3,2,1,0:T(8,128)S(1)} %pad_maximum_fusion.1), channel_id=1, source_target_pairs={{0,32},{32,64},{64,96},{96,0},{128,160},{160,192},{192,224},{224,1... | collective-permute-start | bytes 1179656 | tf_op jit(solution)/shard_map/ppermute | solution.py:45
  15.8 11.3 %collective-permute-start.4 = (f32[3,4,32,256]{3,2,1,0:T(8,128)S(1)}, f32[3,4,32,256]{3,2,1,0:T(8,128)S(1)}, u32[]{:S(2)}, u32[]{:S(2)}) collective-permute-start(f32[3,4,32,256]{3,2,1,0:T(8,128)S(1)} %maximum_add_fusion.4), channel_id=1, source_target_pairs={{0,96},{32,0},{64,32},{96,64},{128,224},{160,128},{192,160},{224,1... | collective-permute-start | bytes 1179656 | tf_op jit(solution)/shard_map/ppermute | solution.py:46
  19.6 11.3 %collective-permute-start.1 = (f32[3,4,32,256]{3,2,1,0:T(8,128)S(1)}, f32[3,4,32,256]{3,2,1,0:T(8,128)S(1)}, u32[]{:S(2)}, u32[]{:S(2)}) collective-permute-start(f32[3,4,32,256]{3,2,1,0:T(8,128)S(1)} %maximum_add_fusion.1), channel_id=1, source_target_pairs={{0,32},{32,64},{64,96},{96,0},{128,160},{160,192},{192,224},{224,1... | collective-permute-start | bytes 1179656 | tf_op jit(solution)/shard_map/ppermute | solution.py:45
  27.1 10.3 %collective-permute-start.5 = (f32[3,4,32,256]{3,2,1,0:T(8,128)S(1)}, f32[3,4,32,256]{3,2,1,0:T(8,128)}, u32[]{:S(2)}, u32[]{:S(2)}) collective-permute-start(f32[3,4,32,256]{3,2,1,0:T(8,128)S(1)} %maximum_add_fusion.5), channel_id=1, source_target_pairs={{0,96},{32,0},{64,32},{96,64},{128,224},{160,128},{192,160},{224,1... | collective-permute-start | bytes 1179656 | tf_op jit(solution)/shard_map/ppermute | solution.py:46
  31.7 10.3 %collective-permute-start.2 = (f32[3,4,32,256]{3,2,1,0:T(8,128)}, f32[3,4,32,256]{3,2,1,0:T(8,128)}, u32[]{:S(2)}, u32[]{:S(2)}) collective-permute-start(f32[3,4,32,256]{3,2,1,0:T(8,128)} %maximum_add_fusion.2), channel_id=1, source_target_pairs={{0,32},{32,64},{64,96},{96,0},{128,160},{160,192},{192,224},{224,1... | collective-permute-start | bytes 1179656 | tf_op jit(solution)/shard_map/ppermute | solution.py:45
  43.1 1.6 copy-start.2
  43.1 2.2 %copy-start.3 = (f32[1,4,512,256]{3,2,1,0:T(8,128)S(1)}, f32[1,4,512,256]{3,2,1,0:T(8,128)}, u32[]{:S(2)}) copy-start(f32[1,4,512,256]{3,2,1,0:T(8,128)} %param.7) | copy-start | bytes 6291460
  45.5 9.2 %collective-permute-start.6 = (f32[3,4,32,256]{3,2,1,0:T(8,128)S(1)}, f32[3,4,32,256]{3,2,1,0:T(8,128)S(1)}, u32[]{:S(2)}, u32[]{:S(2)}) collective-permute-start(f32[3,4,32,256]{3,2,1,0:T(8,128)S(1)} %pad_maximum_fusion.3), channel_id=1, source_target_pairs={{0,32},{32,64},{64,96},{96,0},{128,160},{160,192},{192,224},{224,1... | collective-permute-start | bytes 1179656 | tf_op jit(solution)/shard_map/ppermute | solution.py:45
  45.6 9.2 %collective-permute-start.9 = (f32[3,4,32,256]{3,2,1,0:T(8,128)S(1)}, f32[3,4,32,256]{3,2,1,0:T(8,128)S(1)}, u32[]{:S(2)}, u32[]{:S(2)}) collective-permute-start(f32[3,4,32,256]{3,2,1,0:T(8,128)S(1)} %pad_maximum_fusion.4), channel_id=1, source_target_pairs={{0,96},{32,0},{64,32},{96,64},{128,224},{160,128},{192,160},{224,1... | collective-permute-start | bytes 1179656 | tf_op jit(solution)/shard_map/ppermute | solution.py:46
  54.7 10.7 %collective-permute-start.7 = (f32[3,4,32,256]{3,2,1,0:T(8,128)S(1)}, f32[3,4,32,256]{3,2,1,0:T(8,128)S(1)}, u32[]{:S(2)}, u32[]{:S(2)}) collective-permute-start(f32[3,4,32,256]{3,2,1,0:T(8,128)S(1)} %maximum_add_fusion.7), channel_id=1, source_target_pairs={{0,32},{32,64},{64,96},{96,0},{128,160},{160,192},{192,224},{224,1... | collective-permute-start | bytes 1179656 | tf_op jit(solution)/shard_map/ppermute | solution.py:45
  54.9 10.7 %collective-permute-start.10 = (f32[3,4,32,256]{3,2,1,0:T(8,128)S(1)}, f32[3,4,32,256]{3,2,1,0:T(8,128)S(1)}, u32[]{:S(2)}, u32[]{:S(2)}) collective-permute-start(f32[3,4,32,256]{3,2,1,0:T(8,128)S(1)} %maximum_add_fusion.9), channel_id=1, source_target_pairs={{0,96},{32,0},{64,32},{96,64},{128,224},{160,128},{192,160},{224,1... | collective-permute-start | bytes 1179656 | tf_op jit(solution)/shard_map/ppermute | solution.py:46
  58.2 35.7 %collective-permute-start.12 = (f32[3,4,64,256]{3,2,1,0:T(8,128)S(1)}, f32[3,4,64,256]{3,2,1,0:T(8,128)S(1)}, u32[]{:S(2)}, u32[]{:S(2)}) collective-permute-start(f32[3,4,64,256]{3,2,1,0:T(8,128)S(1)} %pad_maximum_fusion), channel_id=1, source_target_pairs={{0,128},{32,160},{64,192},{96,224},{128,0},{160,32},{192,64},{224,... | collective-permute-start | bytes 2359304 | tf_op jit(solution)/shard_map/ppermute | solution.py:61
  65.5 28.4 %collective-permute-start.8 = (f32[3,4,32,256]{3,2,1,0:T(8,128)S(1)}, f32[3,4,32,256]{3,2,1,0:T(8,128)S(1)}, u32[]{:S(2)}, u32[]{:S(2)}) collective-permute-start(f32[3,4,32,256]{3,2,1,0:T(8,128)S(1)} %maximum_add_fusion.8), channel_id=1, source_target_pairs={{0,32},{32,64},{64,96},{96,0},{128,160},{160,192},{192,224},{224,1... | collective-permute-start | bytes 1179656 | tf_op jit(solution)/shard_map/ppermute | solution.py:45
  65.7 28.3 %collective-permute-start.11 = (f32[3,4,32,256]{3,2,1,0:T(8,128)S(1)}, f32[3,4,32,256]{3,2,1,0:T(8,128)S(1)}, u32[]{:S(2)}, u32[]{:S(2)}) collective-permute-start(f32[3,4,32,256]{3,2,1,0:T(8,128)S(1)} %maximum_add_fusion.10), channel_id=1, source_target_pairs={{0,96},{32,0},{64,32},{96,64},{128,224},{160,128},{192,160},{224,1... | collective-permute-start | bytes 1179656 | tf_op jit(solution)/shard_map/ppermute | solution.py:46
  96.1 22.2 %all-to-all-start = ((f32[2,4,64,256]{3,1,0,2:T(4,128)}), f32[2,4,64,256]{3,1,0,2:T(4,128)S(1)}, u32[]{:S(2)}, u32[]{:S(2)}) async-start(f32[2,4,64,256]{3,1,0,2:T(4,128)} %copy.13), calls=%async_computation | async-start | bytes 1048576 | tf_op jit(solution)/shard_map/all_to_all | solution.py:102
  120.6 20.6 %all-to-all-start.1 = ((f32[2,128,2,256]{3,2,0,1:T(2,128)}), f32[2,128,2,256]{3,2,0,1:T(2,128)S(1)}, u32[]{:S(2)}, u32[]{:S(2)}) async-start(f32[2,128,2,256]{3,2,0,1:T(2,128)} %copy.16), calls=%async_computation.1 | async-start | bytes 1048576 | tf_op jit(solution)/shard_map/all_to_all | solution.py:105
  130.0 3.4 %copy-start.4 = (s32[256]{0:T(256)S(1)}, s32[256]{0:T(256)}, u32[]{:S(2)}) copy-start(s32[256]{0:T(256)} %param.8) | copy-start | bytes 3076
  141.8 10.4 %collective-permute-start.13 = (f32[2,4,32,256]{3,2,1,0:T(8,128)S(1)}, f32[2,4,32,256]{3,2,1,0:T(8,128)S(1)}, u32[]{:S(2)}, u32[]{:S(2)}) collective-permute-start(f32[2,4,32,256]{3,2,1,0:T(8,128)S(1)} %get-tuple-element.91), channel_id=1, source_target_pairs={{0,32},{32,64},{64,96},{96,0},{128,160},{160,192},{192,224},{224,1... | collective-permute-start | bytes 786440 | tf_op jit(solution)/shard_map/ppermute | solution.py:80
  141.9 10.4 %collective-permute-start.14 = (f32[2,4,32,256]{3,2,1,0:T(8,128)S(1)}, f32[2,4,32,256]{3,2,1,0:T(8,128)S(1)}, u32[]{:S(2)}, u32[]{:S(2)}) collective-permute-start(f32[2,4,32,256]{3,2,1,0:T(8,128)S(1)} %get-tuple-element.90), channel_id=1, source_target_pairs={{0,96},{32,0},{64,32},{96,64},{128,224},{160,128},{192,160},{224,1... | collective-permute-start | bytes 786440 | tf_op jit(solution)/shard_map/ppermute | solution.py:81
  145.1 29.6 %collective-permute-start.19 = (f32[2,4,64,256]{3,2,1,0:T(8,128)S(1)}, f32[2,4,64,256]{3,2,1,0:T(8,128)S(1)}, u32[]{:S(2)}, u32[]{:S(2)}) collective-permute-start(f32[2,4,64,256]{3,2,1,0:T(8,128)S(1)} %all_to_all.33), channel_id=1, source_target_pairs={{0,128},{32,160},{64,192},{96,224},{128,0},{160,32},{192,64},{224,... | collective-permute-start | bytes 1572872 | tf_op jit(solution)/shard_map/ppermute | solution.py:73
  152.2 25.9 %collective-permute-start.15 = (f32[2,4,32,256]{3,2,1,0:T(8,128)S(1)}, f32[2,4,32,256]{3,2,1,0:T(8,128)S(1)}, u32[]{:S(2)}, u32[]{:S(2)}) collective-permute-start(f32[2,4,32,256]{3,2,1,0:T(8,128)S(1)} %collective-permute-done.13), channel_id=1, source_target_pairs={{0,32},{32,64},{64,96},{96,0},{128,160},{160,192},{192,224},{224,1... | collective-permute-start | bytes 786440 | tf_op jit(solution)/shard_map/ppermute | solution.py:80
  152.2 25.9 %collective-permute-start.16 = (f32[2,4,32,256]{3,2,1,0:T(8,128)S(1)}, f32[2,4,32,256]{3,2,1,0:T(8,128)S(1)}, u32[]{:S(2)}, u32[]{:S(2)}) collective-permute-start(f32[2,4,32,256]{3,2,1,0:T(8,128)S(1)} %collective-permute-done.14), channel_id=1, source_target_pairs={{0,96},{32,0},{64,32},{96,64},{128,224},{160,128},{192,160},{224,1... | collective-permute-start | bytes 786440 | tf_op jit(solution)/shard_map/ppermute | solution.py:81
  174.8 10.5 %collective-permute-start.20 = (f32[2,4,32,256]{3,2,1,0:T(8,128)S(1)}, f32[2,4,32,256]{3,2,1,0:T(8,128)S(1)}, u32[]{:S(2)}, u32[]{:S(2)}) collective-permute-start(f32[2,4,32,256]{3,2,1,0:T(8,128)S(1)} %get-tuple-element.89), channel_id=1, source_target_pairs={{0,32},{32,64},{64,96},{96,0},{128,160},{160,192},{192,224},{224,1... | collective-permute-start | bytes 786440 | tf_op jit(solution)/shard_map/ppermute | solution.py:80
  174.9 10.4 %collective-permute-start.21 = (f32[2,4,32,256]{3,2,1,0:T(8,128)S(1)}, f32[2,4,32,256]{3,2,1,0:T(8,128)S(1)}, u32[]{:S(2)}, u32[]{:S(2)}) collective-permute-start(f32[2,4,32,256]{3,2,1,0:T(8,128)S(1)} %get-tuple-element.88), channel_id=1, source_target_pairs={{0,96},{32,0},{64,32},{96,64},{128,224},{160,128},{192,160},{224,1... | collective-permute-start | bytes 786440 | tf_op jit(solution)/shard_map/ppermute | solution.py:81
  178.1 12.8 %collective-permute-start.17 = (f32[2,4,32,256]{3,2,1,0:T(8,128)S(1)}, f32[2,4,32,256]{3,2,1,0:T(8,128)S(1)}, u32[]{:S(2)}, u32[]{:S(2)}) collective-permute-start(f32[2,4,32,256]{3,2,1,0:T(8,128)S(1)} %collective-permute-done.15), channel_id=1, source_target_pairs={{0,32},{32,64},{64,96},{96,0},{128,160},{160,192},{192,224},{224,1... | collective-permute-start | bytes 786440 | tf_op jit(solution)/shard_map/ppermute | solution.py:80
  178.1 12.8 %collective-permute-start.18 = (f32[2,4,32,256]{3,2,1,0:T(8,128)S(1)}, f32[2,4,32,256]{3,2,1,0:T(8,128)S(1)}, u32[]{:S(2)}, u32[]{:S(2)}) collective-permute-start(f32[2,4,32,256]{3,2,1,0:T(8,128)S(1)} %collective-permute-done.16), channel_id=1, source_target_pairs={{0,96},{32,0},{64,32},{96,64},{128,224},{160,128},{192,160},{224,1... | collective-permute-start | bytes 786440 | tf_op jit(solution)/shard_map/ppermute | solution.py:81
  185.3 9.8 %collective-permute-start.22 = (f32[2,4,32,256]{3,2,1,0:T(8,128)S(1)}, f32[2,4,32,256]{3,2,1,0:T(8,128)S(1)}, u32[]{:S(2)}, u32[]{:S(2)}) collective-permute-start(f32[2,4,32,256]{3,2,1,0:T(8,128)S(1)} %collective-permute-done.20), channel_id=1, source_target_pairs={{0,32},{32,64},{64,96},{96,0},{128,160},{160,192},{192,224},{224,1... | collective-permute-start | bytes 786440 | tf_op jit(solution)/shard_map/ppermute | solution.py:80
  185.3 9.8 %collective-permute-start.23 = (f32[2,4,32,256]{3,2,1,0:T(8,128)S(1)}, f32[2,4,32,256]{3,2,1,0:T(8,128)S(1)}, u32[]{:S(2)}, u32[]{:S(2)}) collective-permute-start(f32[2,4,32,256]{3,2,1,0:T(8,128)S(1)} %collective-permute-done.21), channel_id=1, source_target_pairs={{0,96},{32,0},{64,32},{96,64},{128,224},{160,128},{192,160},{224,1... | collective-permute-start | bytes 786440 | tf_op jit(solution)/shard_map/ppermute | solution.py:81
  195.1 8.1 %collective-permute-start.24 = (f32[2,4,32,256]{3,2,1,0:T(8,128)S(1)}, f32[2,4,32,256]{3,2,1,0:T(8,128)S(1)}, u32[]{:S(2)}, u32[]{:S(2)}) collective-permute-start(f32[2,4,32,256]{3,2,1,0:T(8,128)S(1)} %collective-permute-done.22), channel_id=1, source_target_pairs={{0,32},{32,64},{64,96},{96,0},{128,160},{160,192},{192,224},{224,1... | collective-permute-start | bytes 786440 | tf_op jit(solution)/shard_map/ppermute | solution.py:80
  195.1 8.1 %collective-permute-start.25 = (f32[2,4,32,256]{3,2,1,0:T(8,128)S(1)}, f32[2,4,32,256]{3,2,1,0:T(8,128)S(1)}, u32[]{:S(2)}, u32[]{:S(2)}) collective-permute-start(f32[2,4,32,256]{3,2,1,0:T(8,128)S(1)} %collective-permute-done.23), channel_id=1, source_target_pairs={{0,96},{32,0},{64,32},{96,64},{128,224},{160,128},{192,160},{224,1... | collective-permute-start | bytes 786440 | tf_op jit(solution)/shard_map/ppermute | solution.py:81

commit v7 on v5

--- a/solution.py
+++ b/solution.py
@@ -30,7 +30,7 @@
     return lax.dynamic_slice_in_dim(field, start, size, axis=1)
 
 
-def ring_sum(fields, starts, size, n_shots):
+def ring_sum(fields, starts, size, n_shots, gates=None):
     idx = lax.axis_index("shots")
     r = idx % RING
     q = size // 2
@@ -44,6 +44,8 @@
     for t in range(1, RING):
         recv_f = lax.ppermute(acc_f, "shots", fwd)
         recv_b = lax.ppermute(acc_b, "shots", bwd)
+        if gates is not None and t in gates:
+            recv_f, recv_b, gates[t] = lax.optimization_barrier((recv_f, recv_b, gates[t]))
         acc_f = recv_f + take(starts((r - 1 - t) % RING))
         acc_b = recv_b + take(starts((r + 1 + t) % RING) + q)
     return jnp.concatenate([acc_f, acc_b], axis=2)
@@ -56,9 +58,13 @@
     half = chunk // 2
     theirs = ring_sum(fields, lambda c: c * chunk + (1 - h) * half, half, n_shots)
     fields, theirs = lax.optimization_barrier((tuple(fields), theirs))
-    got = lax.ppermute(theirs, "shots", hi_pairs(n_shots))
-    mine = ring_sum(fields, lambda c: c * chunk + h * half, half, n_shots)
-    return mine + got
+    q = half // 2
+    gates = {
+        RING - 2: lax.ppermute(theirs[:, :, :q], "shots", hi_pairs(n_shots)),
+        RING - 1: lax.ppermute(theirs[:, :, q:], "shots", hi_pairs(n_shots)),
+    }
+    mine = ring_sum(fields, lambda c: c * chunk + h * half, half, n_shots, gates)
+    return mine + jnp.concatenate([gates[RING - 2], gates[RING - 1]], axis=2)
 
 
 def all_gather_smooth_shots(blocks, n_shots, total):

time: 211 us -> 209 us (level)
  waiting for transfers between devices: 115 us -> 100 us
  starting transfers between devices: 62.8 us -> 76 us
    ppermute x6, waiting for transfers between devices: 33.6 us -> 21.4 us  [ring_sum(): recv_b = lax.ppermute(acc_b, 'shots', bwd)]
    ppermute x6, starting transfers between devices: 13.5 us -> 20.9 us  [ring_sum(): recv_b = lax.ppermute(acc_b, 'shots', bwd)]
    ppermute x1 -> x2, starting transfers between devices: 7.19 us -> 13 us  [the longest x1 7.28 us: reduce_scatter_shots(): lax.ppermute(theirs[:, :, :q], 'shots', hi_pairs(n_shots))]
    ppermute x6, starting transfers between devices: 4.01 us -> 0.42 us  [ring_sum(): recv_f = lax.ppermute(acc_f, 'shots', fwd)]
    all_to_all x1, starting transfers between devices: 7.53 us -> 10.8 us  [smooth_along_x(): cols = lax.all_to_all(both, 'slab', split_axis=2, concat_axis=1, tiled=True)]
    ppermute x6, waiting for transfers between devices: 6.71 us -> 4.08 us  [ring_sum(): recv_f = lax.ppermute(acc_f, 'shots', fwd)]
    ppermute x1 -> x2, waiting for transfers between devices: 16.5 us -> 15.5 us  [the longest x1 15.5 us: reduce_scatter_shots(): lax.ppermute(theirs[:, :, q:], 'shots', hi_pairs(n_shots))]
  transfers between devices with their start and end apart: 28 -> 29, of which waited for: 16 -> 14; matrix products, arithmetic and copies ran while one was open for 5% -> 5% of each run, Pallas kernels for 0% -> 0%
where the time goes in v7:
time: 209 us
  waiting for transfers between devices  100 us (48%)
  starting transfers between devices  76 us (36%)
  local copies, waits for them, and re-layouts  14.9 us (7%)
  matrix products  11.7 us (6%)
  other arithmetic  5.01 us (2%)
    ppermute x6, waiting for transfers between devices, ring_sum(): recv_b = lax.ppermute(acc_b, 'shots', bwd)  21.4 us
    ppermute x6, starting transfers between devices, ring_sum(): recv_b = lax.ppermute(acc_b, 'shots', bwd)  20.9 us
    ppermute x6, starting transfers between devices, all_gather_smooth_shots(): cur_b = lax.ppermute(cur_b, 'shots', bwd)  19.9 us
    ppermute x1, waiting for transfers between devices, all_gather_smooth_shots(): other = lax.ppermute(blocks, 'shots', hi_pairs(n_shots))  19.5 us
    ppermute x6, waiting for transfers between devices, all_gather_smooth_shots(): cur_f = lax.ppermute(cur_f, 'shots', fwd)  17.3 us
    ppermute x1, waiting for transfers between devices, reduce_scatter_shots(): lax.ppermute(theirs[:, :, q:], 'shots', hi_pairs(n_shots))  15.5 us
    all_to_all x1, waiting for transfers between devices, smooth_along_x(): cols = lax.all_to_all(both, 'slab', split_axis=2, concat_axis=1, tiled=True)  14.6 us
    all_to_all x1, starting transfers between devices, smooth_along_x(): cols = lax.all_to_all(both, 'slab', split_axis=2, concat_axis=1, tiled=True)  10.8 us
  transfers between devices with their start and end apart: 29, of which 14 were waited for; matrix products, arithmetic and copies ran while one was open for 5% of the time, Pallas kernels for 0%

profile of v7, /device:TPU:2, one launch (start us, length us, event | category | flops | bytes accessed | tf_op | source)
XLA Modules:
  0.0 209.0 jit_solution(14761846833666516307)
XLA Ops:
  0.8 1.5 constant_dynamic-slice_fusion.14
  2.3 0.3 copy-done.1
  2.7 1.5 constant_dynamic-slice_fusion.12
  4.2 3.1 %collective-permute-start.3 = (f32[3,4,32,256]{3,2,1,0:T(8,128)S(1)}, f32[3,4,32,256]{3,2,1,0:T(8,128)S(1)}, u32[]{:S(2)}, u32[]{:S(2)}) collective-permute-start(f32[3,4,32,256]{3,2,1,0:T(8,128)S(1)} %pad_maximum_fusion.2), channel_id=1, source_target_pairs={{0,96},{32,0},{64,32},{96,64},{128,224},{160,128},{192,160},{224,1... | collective-permute-start | bytes 1179656 | tf_op jit(solution)/shard_map/ppermute | solution.py:46
  7.4 0.1 collective-permute-start
  7.5 8.2 %collective-permute-done.3 = f32[3,4,32,256]{3,2,1,0:T(8,128)S(1)} collective-permute-done((f32[3,4,32,256]{3,2,1,0:T(8,128)S(1)}, f32[3,4,32,256]{3,2,1,0:T(8,128)S(1)}, u32[]{:S(2)}, u32[]{:S(2)}) %collective-permute-start.3) | collective-permute-done | bytes 393248 | tf_op jit(solution)/shard_map/ppermute | solution.py:46
  15.8 3.8 %collective-permute-start.4 = (f32[3,4,32,256]{3,2,1,0:T(8,128)S(1)}, f32[3,4,32,256]{3,2,1,0:T(8,128)S(1)}, u32[]{:S(2)}, u32[]{:S(2)}) collective-permute-start(f32[3,4,32,256]{3,2,1,0:T(8,128)S(1)} %maximum_add_fusion.4), channel_id=1, source_target_pairs={{0,96},{32,0},{64,32},{96,64},{128,224},{160,128},{192,160},{224,1... | collective-permute-start | bytes 1179656 | tf_op jit(solution)/shard_map/ppermute | solution.py:46
  19.6 0.1 collective-permute-start.1
  19.7 7.3 %collective-permute-done.4 = f32[3,4,32,256]{3,2,1,0:T(8,128)S(1)} collective-permute-done((f32[3,4,32,256]{3,2,1,0:T(8,128)S(1)}, f32[3,4,32,256]{3,2,1,0:T(8,128)S(1)}, u32[]{:S(2)}, u32[]{:S(2)}) %collective-permute-start.4) | collective-permute-done | bytes 393248 | tf_op jit(solution)/shard_map/ppermute | solution.py:46
  27.1 3.8 %collective-permute-start.5 = (f32[3,4,32,256]{3,2,1,0:T(8,128)S(1)}, f32[3,4,32,256]{3,2,1,0:T(8,128)}, u32[]{:S(2)}, u32[]{:S(2)}) collective-permute-start(f32[3,4,32,256]{3,2,1,0:T(8,128)S(1)} %maximum_add_fusion.5), channel_id=1, source_target_pairs={{0,96},{32,0},{64,32},{96,64},{128,224},{160,128},{192,160},{224,1... | collective-permute-start | bytes 1179656 | tf_op jit(solution)/shard_map/ppermute | solution.py:46
  30.9 0.8 maximum_add_fusion.2
  31.7 5.8 %collective-permute-done.5 = f32[3,4,32,256]{3,2,1,0:T(8,128)} collective-permute-done((f32[3,4,32,256]{3,2,1,0:T(8,128)S(1)}, f32[3,4,32,256]{3,2,1,0:T(8,128)}, u32[]{:S(2)}, u32[]{:S(2)}) %collective-permute-start.5) | collective-permute-done | bytes 393248 | tf_op jit(solution)/shard_map/ppermute | solution.py:46
  37.5 1.1 maximum_add_fusion.6
  38.5 3.5 %collective-permute-done.2 = f32[3,4,32,256]{3,2,1,0:T(8,128)} collective-permute-done((f32[3,4,32,256]{3,2,1,0:T(8,128)}, f32[3,4,32,256]{3,2,1,0:T(8,128)}, u32[]{:S(2)}, u32[]{:S(2)}) %collective-permute-start.2) | collective-permute-done | bytes 393248 | tf_op jit(solution)/shard_map/ppermute | solution.py:45
  42.0 1.1 maximum_add_fusion.3
  43.2 0.1 dynamic-slice_bitcast_fusion.3
  43.3 1.4 copy-done.2
  44.7 0.1 dynamic-slice_bitcast_fusion.4
  44.8 0.5 copy-done.3
  45.3 0.1 dynamic-slice_bitcast_fusion.5
  45.5 0.1 collective-permute-start.6
  45.6 3.3 %collective-permute-start.8 = (f32[3,4,32,256]{3,2,1,0:T(8,128)S(1)}, f32[3,4,32,256]{3,2,1,0:T(8,128)S(1)}, u32[]{:S(2)}, u32[]{:S(2)}) collective-permute-start(f32[3,4,32,256]{3,2,1,0:T(8,128)S(1)} %pad_maximum_fusion.4), channel_id=1, source_target_pairs={{0,96},{32,0},{64,32},{96,64},{128,224},{160,128},{192,160},{224,1... | collective-permute-start | bytes 1179656 | tf_op jit(solution)/shard_map/ppermute | solution.py:46
  48.9 7.3 %collective-permute-start.10 = (f32[3,4,32,256]{3,2,1,0:T(8,128)S(1)}, f32[3,4,32,256]{3,2,1,0:T(8,128)S(1)}, u32[]{:S(2)}, u32[]{:S(2)}) collective-permute-start(f32[3,4,32,256]{3,2,1,0:T(8,128)S(1)} %get-tuple-element.89), channel_id=1, source_target_pairs={{0,128},{32,160},{64,192},{96,224},{128,0},{160,32},{192,64},{224,... | collective-permute-start | bytes 1179656 | tf_op jit(solution)/shard_map/ppermute | solution.py:63
  56.4 3.3 %collective-permute-start.9 = (f32[3,4,32,256]{3,2,1,0:T(8,128)S(1)}, f32[3,4,32,256]{3,2,1,0:T(8,128)S(1)}, u32[]{:S(2)}, u32[]{:S(2)}) collective-permute-start(f32[3,4,32,256]{3,2,1,0:T(8,128)S(1)} %maximum_add_fusion.8), channel_id=1, source_target_pairs={{0,96},{32,0},{64,32},{96,64},{128,224},{160,128},{192,160},{224,1... | collective-permute-start | bytes 1179656 | tf_op jit(solution)/shard_map/ppermute | solution.py:46
  59.7 5.7 %collective-permute-start.13 = (f32[3,4,32,256]{3,2,1,0:T(8,128)S(1)}, f32[3,4,32,256]{3,2,1,0:T(8,128)S(1)}, u32[]{:S(2)}, u32[]{:S(2)}) collective-permute-start(f32[3,4,32,256]{3,2,1,0:T(8,128)S(1)} %get-tuple-element.88), channel_id=1, source_target_pairs={{0,128},{32,160},{64,192},{96,224},{128,0},{160,32},{192,64},{224,... | collective-permute-start | bytes 1179656 | tf_op jit(solution)/shard_map/ppermute | solution.py:64
  65.4 0.6 collective-permute-done.7
  66.1 0.1 collective-permute-start.11
  66.3 3.7 %collective-permute-start.12 = (f32[3,4,32,256]{3,2,1,0:T(8,128)S(1)}, f32[3,4,32,256]{3,2,1,0:T(8,128)S(1)}, u32[]{:S(2)}, u32[]{:S(2)}) collective-permute-start(f32[3,4,32,256]{3,2,1,0:T(8,128)S(1)} %maximum_add_fusion.10), channel_id=1, source_target_pairs={{0,96},{32,0},{64,32},{96,64},{128,224},{160,128},{192,160},{224,1... | collective-permute-start | bytes 1179656 | tf_op jit(solution)/shard_map/ppermute | solution.py:46
  70.0 0.2 fusion.26
  70.2 15.5 %collective-permute-done.13 = f32[3,4,32,256]{3,2,1,0:T(8,128)S(1)} collective-permute-done((f32[3,4,32,256]{3,2,1,0:T(8,128)S(1)}, f32[3,4,32,256]{3,2,1,0:T(8,128)S(1)}, u32[]{:S(2)}, u32[]{:S(2)}) %collective-permute-start.13) | collective-permute-done | bytes 393248 | tf_op jit(solution)/shard_map/ppermute | solution.py:64
  85.8 0.1 maximum_add_fusion
  86.0 0.7 fusion.15
  86.7 1.1 copy.13
  87.8 10.8 %all-to-all-start = ((f32[2,4,64,256]{3,1,0,2:T(4,128)}), f32[2,4,64,256]{3,1,0,2:T(4,128)S(1)}, u32[]{:S(2)}, u32[]{:S(2)}) async-start(f32[2,4,64,256]{3,1,0,2:T(4,128)} %copy.13), calls=%async_computation | async-start | bytes 1048576 | tf_op jit(solution)/shard_map/all_to_all | solution.py:106
  98.6 0.1 fusion.69
  98.8 14.6 %all-to-all-done = f32[2,4,64,256]{3,1,0,2:T(4,128)S(1)} async-done(((f32[2,4,64,256]{3,1,0,2:T(4,128)}), f32[2,4,64,256]{3,1,0,2:T(4,128)S(1)}, u32[]{:S(2)}, u32[]{:S(2)}) %all-to-all-start) | async-done | bytes 524320 | tf_op jit(solution)/shard_map/all_to_all | solution.py:106
  113.3 0.3 copy.14
  113.6 1.0 convolution_bitcast_fusion
  114.6 1.0 copy.16
  115.6 5.9 %all-to-all-start.1 = ((f32[2,128,2,256]{3,2,0,1:T(2,128)}), f32[2,128,2,256]{3,2,0,1:T(2,128)S(1)}, u32[]{:S(2)}, u32[]{:S(2)}) async-start(f32[2,128,2,256]{3,2,0,1:T(2,128)} %copy.16), calls=%async_computation.1 | async-start | bytes 1048576 | tf_op jit(solution)/shard_map/all_to_all | solution.py:109
  121.5 0.5 fusion.14
  122.0 0.4 fusion.13
  122.4 2.6 %constant_dynamic-slice_fusion.24 = (f32[512,32]{1,0:T(8,128)S(1)}, f32[512,32]{1,0:T(8,128)S(1)}, f32[512,32]{1,0:T(8,128)S(1)}, f32[512,32]{1,0:T(8,128)S(1)},...) fusion(f32[512,512]{1,0:T(8,128)S(1)} %fusion.13, ...), kind=kLoop, calls=%fused_computation.178 | loop fusion | bytes 2097216 | tf_op jit(solution)/shard_map/dynamic_slice | solution.py:90
  125.0 3.3 %concatenate.18 = f32[512,512]{1,0:T(8,128)S(1)} concatenate(f32[512,32]{1,0:T(8,128)} %get-tuple-element.85, f32[512,32]{1,0:T(8,128)} %get-tuple-element.84, f32[512,32]{1,0:T(8,128)} %get-tuple-element.83, f32[512,32]{1,0:T(8,128)} %get-tuple-element.82, f32[512,32]{1,0:T(8,128)} %get-tuple-element.81, f32[512,32]{1,0:T(8,128)} %get-tuple-element.80, ...), dimensions={1} | concatenate | bytes 2097152 | tf_op jit(solution)/shard_map/concatenate | solution.py:89
  128.4 0.2 convolution_bitcast_fusion.1
  128.6 7.6 %all-to-all-done.1 = f32[2,128,2,256]{3,2,0,1:T(2,128)S(1)} async-done(((f32[2,128,2,256]{3,2,0,1:T(2,128)}), f32[2,128,2,256]{3,2,0,1:T(2,128)S(1)}, u32[]{:S(2)}, u32[]{:S(2)}) %all-to-all-start.1) | async-done | bytes 524320 | tf_op jit(solution)/shard_map/all_to_all | solution.py:109
  136.2 0.2 copy.18
  136.4 0.4 all_to_all.33
  136.8 0.1 collective-permute-start.14
  136.9 3.3 %collective-permute-start.15 = (f32[2,4,32,256]{3,2,1,0:T(8,128)S(1)}, f32[2,4,32,256]{3,2,1,0:T(8,128)S(1)}, u32[]{:S(2)}, u32[]{:S(2)}) collective-permute-start(f32[2,4,32,256]{3,2,1,0:T(8,128)S(1)} %get-tuple-element.100), channel_id=1, source_target_pairs={{0,96},{32,0},{64,32},{96,64},{128,224},{160,128},{192,160},{224,1... | collective-permute-start | bytes 786440 | tf_op jit(solution)/shard_map/ppermute | solution.py:85
  140.3 5.0 %collective-permute-start.20 = (f32[2,4,64,256]{3,2,1,0:T(8,128)S(1)}, f32[2,4,64,256]{3,2,1,0:T(8,128)S(1)}, u32[]{:S(2)}, u32[]{:S(2)}) collective-permute-start(f32[2,4,64,256]{3,2,1,0:T(8,128)S(1)} %all_to_all.33), channel_id=1, source_target_pairs={{0,128},{32,160},{64,192},{96,224},{128,0},{160,32},{192,64},{224,... | collective-permute-start | bytes 1572872 | tf_op jit(solution)/shard_map/ppermute | solution.py:77
  145.2 1.8 collective-permute-done.14
  147.0 3.6 %collective-permute-start.17 = (f32[2,4,32,256]{3,2,1,0:T(8,128)S(1)}, f32[2,4,32,256]{3,2,1,0:T(8,128)S(1)}, u32[]{:S(2)}, u32[]{:S(2)}) collective-permute-start(f32[2,4,32,256]{3,2,1,0:T(8,128)S(1)} %collective-permute-done.15), channel_id=1, source_target_pairs={{0,96},{32,0},{64,32},{96,64},{128,224},{160,128},{192,160},{224,1... | collective-permute-start | bytes 786440 | tf_op jit(solution)/shard_map/ppermute | solution.py:85
  150.6 19.5 %collective-permute-done.20 = f32[2,4,64,256]{3,2,1,0:T(8,128)S(1)} collective-permute-done((f32[2,4,64,256]{3,2,1,0:T(8,128)S(1)}, f32[2,4,64,256]{3,2,1,0:T(8,128)S(1)}, u32[]{:S(2)}, u32[]{:S(2)}) %collective-permute-start.20) | collective-permute-done | bytes 524320 | tf_op jit(solution)/shard_map/ppermute | solution.py:77
  170.3 3.2 %collective-permute-start.22 = (f32[2,4,32,256]{3,2,1,0:T(8,128)S(1)}, f32[2,4,32,256]{3,2,1,0:T(8,128)S(1)}, u32[]{:S(2)}, u32[]{:S(2)}) collective-permute-start(f32[2,4,32,256]{3,2,1,0:T(8,128)S(1)} %get-tuple-element.98), channel_id=1, source_target_pairs={{0,96},{32,0},{64,32},{96,64},{128,224},{160,128},{192,160},{224,1... | collective-permute-start | bytes 786440 | tf_op jit(solution)/shard_map/ppermute | solution.py:85
  173.6 3.2 %collective-permute-start.19 = (f32[2,4,32,256]{3,2,1,0:T(8,128)S(1)}, f32[2,4,32,256]{3,2,1,0:T(8,128)S(1)}, u32[]{:S(2)}, u32[]{:S(2)}) collective-permute-start(f32[2,4,32,256]{3,2,1,0:T(8,128)S(1)} %collective-permute-done.17), channel_id=1, source_target_pairs={{0,96},{32,0},{64,32},{96,64},{128,224},{160,128},{192,160},{224,1... | collective-permute-start | bytes 786440 | tf_op jit(solution)/shard_map/ppermute | solution.py:85
  176.8 3.9 %collective-permute-done.21 = f32[2,4,32,256]{3,2,1,0:T(8,128)S(1)} collective-permute-done((f32[2,4,32,256]{3,2,1,0:T(8,128)S(1)}, f32[2,4,32,256]{3,2,1,0:T(8,128)S(1)}, u32[]{:S(2)}, u32[]{:S(2)}) %collective-permute-start.21) | collective-permute-done | bytes 262176 | tf_op jit(solution)/shard_map/ppermute | solution.py:84
  180.7 3.3 %collective-permute-start.24 = (f32[2,4,32,256]{3,2,1,0:T(8,128)S(1)}, f32[2,4,32,256]{3,2,1,0:T(8,128)S(1)}, u32[]{:S(2)}, u32[]{:S(2)}) collective-permute-start(f32[2,4,32,256]{3,2,1,0:T(8,128)S(1)} %collective-permute-done.22), channel_id=1, source_target_pairs={{0,96},{32,0},{64,32},{96,64},{128,224},{160,128},{192,160},{224,1... | collective-permute-start | bytes 786440 | tf_op jit(solution)/shard_map/ppermute | solution.py:85
  184.0 2.3 %collective-permute-done.18 = f32[2,4,32,256]{3,2,1,0:T(8,128)S(1)} collective-permute-done((f32[2,4,32,256]{3,2,1,0:T(8,128)S(1)}, f32[2,4,32,256]{3,2,1,0:T(8,128)S(1)}, u32[]{:S(2)}, u32[]{:S(2)}) %collective-permute-start.18) | collective-permute-done | bytes 262176 | tf_op jit(solution)/shard_map/ppermute | solution.py:84
  186.5 4.3 %collective-permute-done.23 = f32[2,4,32,256]{3,2,1,0:T(8,128)S(1)} collective-permute-done((f32[2,4,32,256]{3,2,1,0:T(8,128)S(1)}, f32[2,4,32,256]{3,2,1,0:T(8,128)S(1)}, u32[]{:S(2)}, u32[]{:S(2)}) %collective-permute-start.23) | collective-permute-done | bytes 262176 | tf_op jit(solution)/shard_map/ppermute | solution.py:84
  190.8 3.2 %collective-permute-start.26 = (f32[2,4,32,256]{3,2,1,0:T(8,128)S(1)}, f32[2,4,32,256]{3,2,1,0:T(8,128)S(1)}, u32[]{:S(2)}, u32[]{:S(2)}) collective-permute-start(f32[2,4,32,256]{3,2,1,0:T(8,128)S(1)} %collective-permute-done.24), channel_id=1, source_target_pairs={{0,96},{32,0},{64,32},{96,64},{128,224},{160,128},{192,160},{224,1... | collective-permute-start | bytes 786440 | tf_op jit(solution)/shard_map/ppermute | solution.py:85
  194.1 5.1 %collective-permute-done.25 = f32[2,4,32,256]{3,2,1,0:T(8,128)S(1)} collective-permute-done((f32[2,4,32,256]{3,2,1,0:T(8,128)S(1)}, f32[2,4,32,256]{3,2,1,0:T(8,128)S(1)}, u32[]{:S(2)}, u32[]{:S(2)}) %collective-permute-start.25) | collective-permute-done | bytes 262176 | tf_op jit(solution)/shard_map/ppermute | solution.py:84
  199.2 4.9 %fusion.4 = f32[4,512,256]{2,1,0:T(8,128)} fusion(f32[4,512,256]{2,1,0:T(8,128)S(1)} %get-tuple-element.103, f32[512,512]{1,0:T(8,128)S(1)} %concatenate.18, f32[256]{0:T(256)S(1)} %bitcast.212), kind=kOutput, calls=%fused_computation.4 | convolution fusion | flops 3221749760 | bytes 5243904 | tf_op jit(solution)/shard_map/xij,xjz->xiz/dot_general | solution.py:96
  204.1 4.9 %fusion.7 = f32[4,512,256]{2,1,0:T(8,128)} fusion(f32[4,512,256]{2,1,0:T(8,128)S(1)} %get-tuple-element.102, f32[512,512]{1,0:T(8,128)S(1)} %concatenate.18, f32[256]{0:T(256)S(1)} %bitcast.211), kind=kOutput, calls=%fused_computation.5 | convolution fusion | flops 3221749760 | bytes 5243904 | tf_op jit(solution)/shard_map/xij,xjz->xiz/dot_general | solution.py:96
  (64 shorter events, 1.4 us)
Async XLA Ops:
  0.6 127.7 %copy-start = (f32[2,16]{1,0:T(2,128)S(1)}, f32[2,16]{1,0:T(2,128)}, u32[]{:S(2)}) copy-start(f32[2,16]{1,0:T(2,128)} %param.9) | copy-start | bytes 388
  0.6 2.0 copy-start.1
  4.2 11.5 %collective-permute-start.3 = (f32[3,4,32,256]{3,2,1,0:T(8,128)S(1)}, f32[3,4,32,256]{3,2,1,0:T(8,128)S(1)}, u32[]{:S(2)}, u32[]{:S(2)}) collective-permute-start(f32[3,4,32,256]{3,2,1,0:T(8,128)S(1)} %pad_maximum_fusion.2), channel_id=1, source_target_pairs={{0,96},{32,0},{64,32},{96,64},{128,224},{160,128},{192,160},{224,1... | collective-permute-start | bytes 1179656 | tf_op jit(solution)/shard_map/ppermute | solution.py:46
  7.4 12.2 %collective-permute-start = (f32[3,4,32,256]{3,2,1,0:T(8,128)S(1)}, f32[3,4,32,256]{3,2,1,0:T(8,128)S(1)}, u32[]{:S(2)}, u32[]{:S(2)}) collective-permute-start(f32[3,4,32,256]{3,2,1,0:T(8,128)S(1)} %pad_maximum_fusion.1), channel_id=1, source_target_pairs={{0,32},{32,64},{64,96},{96,0},{128,160},{160,192},{192,224},{224,1... | collective-permute-start | bytes 1179656 | tf_op jit(solution)/shard_map/ppermute | solution.py:45
  15.8 11.3 %collective-permute-start.4 = (f32[3,4,32,256]{3,2,1,0:T(8,128)S(1)}, f32[3,4,32,256]{3,2,1,0:T(8,128)S(1)}, u32[]{:S(2)}, u32[]{:S(2)}) collective-permute-start(f32[3,4,32,256]{3,2,1,0:T(8,128)S(1)} %maximum_add_fusion.4), channel_id=1, source_target_pairs={{0,96},{32,0},{64,32},{96,64},{128,224},{160,128},{192,160},{224,1... | collective-permute-start | bytes 1179656 | tf_op jit(solution)/shard_map/ppermute | solution.py:46
  19.6 11.3 %collective-permute-start.1 = (f32[3,4,32,256]{3,2,1,0:T(8,128)S(1)}, f32[3,4,32,256]{3,2,1,0:T(8,128)S(1)}, u32[]{:S(2)}, u32[]{:S(2)}) collective-permute-start(f32[3,4,32,256]{3,2,1,0:T(8,128)S(1)} %maximum_add_fusion.1), channel_id=1, source_target_pairs={{0,32},{32,64},{64,96},{96,0},{128,160},{160,192},{192,224},{224,1... | collective-permute-start | bytes 1179656 | tf_op jit(solution)/shard_map/ppermute | solution.py:45
  27.1 10.3 %collective-permute-start.5 = (f32[3,4,32,256]{3,2,1,0:T(8,128)S(1)}, f32[3,4,32,256]{3,2,1,0:T(8,128)}, u32[]{:S(2)}, u32[]{:S(2)}) collective-permute-start(f32[3,4,32,256]{3,2,1,0:T(8,128)S(1)} %maximum_add_fusion.5), channel_id=1, source_target_pairs={{0,96},{32,0},{64,32},{96,64},{128,224},{160,128},{192,160},{224,1... | collective-permute-start | bytes 1179656 | tf_op jit(solution)/shard_map/ppermute | solution.py:46
  31.7 10.3 %collective-permute-start.2 = (f32[3,4,32,256]{3,2,1,0:T(8,128)}, f32[3,4,32,256]{3,2,1,0:T(8,128)}, u32[]{:S(2)}, u32[]{:S(2)}) collective-permute-start(f32[3,4,32,256]{3,2,1,0:T(8,128)} %maximum_add_fusion.2), channel_id=1, source_target_pairs={{0,32},{32,64},{64,96},{96,0},{128,160},{160,192},{192,224},{224,1... | collective-permute-start | bytes 1179656 | tf_op jit(solution)/shard_map/ppermute | solution.py:45
  43.1 1.6 copy-start.2
  43.1 2.2 %copy-start.3 = (f32[1,4,512,256]{3,2,1,0:T(8,128)S(1)}, f32[1,4,512,256]{3,2,1,0:T(8,128)}, u32[]{:S(2)}) copy-start(f32[1,4,512,256]{3,2,1,0:T(8,128)} %param.7) | copy-start | bytes 6291460
  45.5 10.8 %collective-permute-start.6 = (f32[3,4,32,256]{3,2,1,0:T(8,128)S(1)}, f32[3,4,32,256]{3,2,1,0:T(8,128)S(1)}, u32[]{:S(2)}, u32[]{:S(2)}) collective-permute-start(f32[3,4,32,256]{3,2,1,0:T(8,128)S(1)} %pad_maximum_fusion.3), channel_id=1, source_target_pairs={{0,32},{32,64},{64,96},{96,0},{128,160},{160,192},{192,224},{224,1... | collective-permute-start | bytes 1179656 | tf_op jit(solution)/shard_map/ppermute | solution.py:45
  45.6 10.8 %collective-permute-start.8 = (f32[3,4,32,256]{3,2,1,0:T(8,128)S(1)}, f32[3,4,32,256]{3,2,1,0:T(8,128)S(1)}, u32[]{:S(2)}, u32[]{:S(2)}) collective-permute-start(f32[3,4,32,256]{3,2,1,0:T(8,128)S(1)} %pad_maximum_fusion.4), channel_id=1, source_target_pairs={{0,96},{32,0},{64,32},{96,64},{128,224},{160,128},{192,160},{224,1... | collective-permute-start | bytes 1179656 | tf_op jit(solution)/shard_map/ppermute | solution.py:46
  48.9 16.5 %collective-permute-start.10 = (f32[3,4,32,256]{3,2,1,0:T(8,128)S(1)}, f32[3,4,32,256]{3,2,1,0:T(8,128)S(1)}, u32[]{:S(2)}, u32[]{:S(2)}) collective-permute-start(f32[3,4,32,256]{3,2,1,0:T(8,128)S(1)} %get-tuple-element.89), channel_id=1, source_target_pairs={{0,128},{32,160},{64,192},{96,224},{128,0},{160,32},{192,64},{224,... | collective-permute-start | bytes 1179656 | tf_op jit(solution)/shard_map/ppermute | solution.py:63
  56.3 9.8 %collective-permute-start.7 = (f32[3,4,32,256]{3,2,1,0:T(8,128)S(1)}, f32[3,4,32,256]{3,2,1,0:T(8,128)S(1)}, u32[]{:S(2)}, u32[]{:S(2)}) collective-permute-start(f32[3,4,32,256]{3,2,1,0:T(8,128)S(1)} %maximum_add_fusion.7), channel_id=1, source_target_pairs={{0,32},{32,64},{64,96},{96,0},{128,160},{160,192},{192,224},{224,1... | collective-permute-start | bytes 1179656 | tf_op jit(solution)/shard_map/ppermute | solution.py:45
  56.4 9.6 %collective-permute-start.9 = (f32[3,4,32,256]{3,2,1,0:T(8,128)S(1)}, f32[3,4,32,256]{3,2,1,0:T(8,128)S(1)}, u32[]{:S(2)}, u32[]{:S(2)}) collective-permute-start(f32[3,4,32,256]{3,2,1,0:T(8,128)S(1)} %maximum_add_fusion.8), channel_id=1, source_target_pairs={{0,96},{32,0},{64,32},{96,64},{128,224},{160,128},{192,160},{224,1... | collective-permute-start | bytes 1179656 | tf_op jit(solution)/shard_map/ppermute | solution.py:46
  59.7 26.0 %collective-permute-start.13 = (f32[3,4,32,256]{3,2,1,0:T(8,128)S(1)}, f32[3,4,32,256]{3,2,1,0:T(8,128)S(1)}, u32[]{:S(2)}, u32[]{:S(2)}) collective-permute-start(f32[3,4,32,256]{3,2,1,0:T(8,128)S(1)} %get-tuple-element.88), channel_id=1, source_target_pairs={{0,128},{32,160},{64,192},{96,224},{128,0},{160,32},{192,64},{224,... | collective-permute-start | bytes 1179656 | tf_op jit(solution)/shard_map/ppermute | solution.py:64
  66.1 19.6 %collective-permute-start.11 = (f32[3,4,32,256]{3,2,1,0:T(8,128)S(1)}, f32[3,4,32,256]{3,2,1,0:T(8,128)S(1)}, u32[]{:S(2)}, u32[]{:S(2)}) collective-permute-start(f32[3,4,32,256]{3,2,1,0:T(8,128)S(1)} %maximum_add_fusion.9), channel_id=1, source_target_pairs={{0,32},{32,64},{64,96},{96,0},{128,160},{160,192},{192,224},{224,1... | collective-permute-start | bytes 1179656 | tf_op jit(solution)/shard_map/ppermute | solution.py:45
  66.3 19.4 %collective-permute-start.12 = (f32[3,4,32,256]{3,2,1,0:T(8,128)S(1)}, f32[3,4,32,256]{3,2,1,0:T(8,128)S(1)}, u32[]{:S(2)}, u32[]{:S(2)}) collective-permute-start(f32[3,4,32,256]{3,2,1,0:T(8,128)S(1)} %maximum_add_fusion.10), channel_id=1, source_target_pairs={{0,96},{32,0},{64,32},{96,64},{128,224},{160,128},{192,160},{224,1... | collective-permute-start | bytes 1179656 | tf_op jit(solution)/shard_map/ppermute | solution.py:46
  87.8 25.5 %all-to-all-start = ((f32[2,4,64,256]{3,1,0,2:T(4,128)}), f32[2,4,64,256]{3,1,0,2:T(4,128)S(1)}, u32[]{:S(2)}, u32[]{:S(2)}) async-start(f32[2,4,64,256]{3,1,0,2:T(4,128)} %copy.13), calls=%async_computation | async-start | bytes 1048576 | tf_op jit(solution)/shard_map/all_to_all | solution.py:106
  115.6 20.6 %all-to-all-start.1 = ((f32[2,128,2,256]{3,2,0,1:T(2,128)}), f32[2,128,2,256]{3,2,0,1:T(2,128)S(1)}, u32[]{:S(2)}, u32[]{:S(2)}) async-start(f32[2,128,2,256]{3,2,0,1:T(2,128)} %copy.16), calls=%async_computation.1 | async-start | bytes 1048576 | tf_op jit(solution)/shard_map/all_to_all | solution.py:109
  125.0 3.4 %copy-start.4 = (s32[256]{0:T(256)S(1)}, s32[256]{0:T(256)}, u32[]{:S(2)}) copy-start(s32[256]{0:T(256)} %param.8) | copy-start | bytes 3076
  136.8 10.2 %collective-permute-start.14 = (f32[2,4,32,256]{3,2,1,0:T(8,128)S(1)}, f32[2,4,32,256]{3,2,1,0:T(8,128)S(1)}, u32[]{:S(2)}, u32[]{:S(2)}) collective-permute-start(f32[2,4,32,256]{3,2,1,0:T(8,128)S(1)} %get-tuple-element.101), channel_id=1, source_target_pairs={{0,32},{32,64},{64,96},{96,0},{128,160},{160,192},{192,224},{224,1... | collective-permute-start | bytes 786440 | tf_op jit(solution)/shard_map/ppermute | solution.py:84
  136.9 10.1 %collective-permute-start.15 = (f32[2,4,32,256]{3,2,1,0:T(8,128)S(1)}, f32[2,4,32,256]{3,2,1,0:T(8,128)S(1)}, u32[]{:S(2)}, u32[]{:S(2)}) collective-permute-start(f32[2,4,32,256]{3,2,1,0:T(8,128)S(1)} %get-tuple-element.100), channel_id=1, source_target_pairs={{0,96},{32,0},{64,32},{96,64},{128,224},{160,128},{192,160},{224,1... | collective-permute-start | bytes 786440 | tf_op jit(solution)/shard_map/ppermute | solution.py:85
  140.3 29.9 %collective-permute-start.20 = (f32[2,4,64,256]{3,2,1,0:T(8,128)S(1)}, f32[2,4,64,256]{3,2,1,0:T(8,128)S(1)}, u32[]{:S(2)}, u32[]{:S(2)}) collective-permute-start(f32[2,4,64,256]{3,2,1,0:T(8,128)S(1)} %all_to_all.33), channel_id=1, source_target_pairs={{0,128},{32,160},{64,192},{96,224},{128,0},{160,32},{192,64},{224,... | collective-permute-start | bytes 1572872 | tf_op jit(solution)/shard_map/ppermute | solution.py:77
  147.0 26.6 %collective-permute-start.16 = (f32[2,4,32,256]{3,2,1,0:T(8,128)S(1)}, f32[2,4,32,256]{3,2,1,0:T(8,128)S(1)}, u32[]{:S(2)}, u32[]{:S(2)}) collective-permute-start(f32[2,4,32,256]{3,2,1,0:T(8,128)S(1)} %collective-permute-done.14), channel_id=1, source_target_pairs={{0,32},{32,64},{64,96},{96,0},{128,160},{160,192},{192,224},{224,1... | collective-permute-start | bytes 786440 | tf_op jit(solution)/shard_map/ppermute | solution.py:84
  147.0 26.6 %collective-permute-start.17 = (f32[2,4,32,256]{3,2,1,0:T(8,128)S(1)}, f32[2,4,32,256]{3,2,1,0:T(8,128)S(1)}, u32[]{:S(2)}, u32[]{:S(2)}) collective-permute-start(f32[2,4,32,256]{3,2,1,0:T(8,128)S(1)} %collective-permute-done.15), channel_id=1, source_target_pairs={{0,96},{32,0},{64,32},{96,64},{128,224},{160,128},{192,160},{224,1... | collective-permute-start | bytes 786440 | tf_op jit(solution)/shard_map/ppermute | solution.py:85
  170.2 10.5 %collective-permute-start.21 = (f32[2,4,32,256]{3,2,1,0:T(8,128)S(1)}, f32[2,4,32,256]{3,2,1,0:T(8,128)S(1)}, u32[]{:S(2)}, u32[]{:S(2)}) collective-permute-start(f32[2,4,32,256]{3,2,1,0:T(8,128)S(1)} %get-tuple-element.99), channel_id=1, source_target_pairs={{0,32},{32,64},{64,96},{96,0},{128,160},{160,192},{192,224},{224,1... | collective-permute-start | bytes 786440 | tf_op jit(solution)/shard_map/ppermute | solution.py:84
  170.3 10.4 %collective-permute-start.22 = (f32[2,4,32,256]{3,2,1,0:T(8,128)S(1)}, f32[2,4,32,256]{3,2,1,0:T(8,128)S(1)}, u32[]{:S(2)}, u32[]{:S(2)}) collective-permute-start(f32[2,4,32,256]{3,2,1,0:T(8,128)S(1)} %get-tuple-element.98), channel_id=1, source_target_pairs={{0,96},{32,0},{64,32},{96,64},{128,224},{160,128},{192,160},{224,1... | collective-permute-start | bytes 786440 | tf_op jit(solution)/shard_map/ppermute | solution.py:85
  173.6 12.8 %collective-permute-start.18 = (f32[2,4,32,256]{3,2,1,0:T(8,128)S(1)}, f32[2,4,32,256]{3,2,1,0:T(8,128)S(1)}, u32[]{:S(2)}, u32[]{:S(2)}) collective-permute-start(f32[2,4,32,256]{3,2,1,0:T(8,128)S(1)} %collective-permute-done.16), channel_id=1, source_target_pairs={{0,32},{32,64},{64,96},{96,0},{128,160},{160,192},{192,224},{224,1... | collective-permute-start | bytes 786440 | tf_op jit(solution)/shard_map/ppermute | solution.py:84
  173.6 12.8 %collective-permute-start.19 = (f32[2,4,32,256]{3,2,1,0:T(8,128)S(1)}, f32[2,4,32,256]{3,2,1,0:T(8,128)S(1)}, u32[]{:S(2)}, u32[]{:S(2)}) collective-permute-start(f32[2,4,32,256]{3,2,1,0:T(8,128)S(1)} %collective-permute-done.17), channel_id=1, source_target_pairs={{0,96},{32,0},{64,32},{96,64},{128,224},{160,128},{192,160},{224,1... | collective-permute-start | bytes 786440 | tf_op jit(solution)/shard_map/ppermute | solution.py:85
  180.7 10.0 %collective-permute-start.23 = (f32[2,4,32,256]{3,2,1,0:T(8,128)S(1)}, f32[2,4,32,256]{3,2,1,0:T(8,128)S(1)}, u32[]{:S(2)}, u32[]{:S(2)}) collective-permute-start(f32[2,4,32,256]{3,2,1,0:T(8,128)S(1)} %collective-permute-done.21), channel_id=1, source_target_pairs={{0,32},{32,64},{64,96},{96,0},{128,160},{160,192},{192,224},{224,1... | collective-permute-start | bytes 786440 | tf_op jit(solution)/shard_map/ppermute | solution.py:84
  180.7 10.0 %collective-permute-start.24 = (f32[2,4,32,256]{3,2,1,0:T(8,128)S(1)}, f32[2,4,32,256]{3,2,1,0:T(8,128)S(1)}, u32[]{:S(2)}, u32[]{:S(2)}) collective-permute-start(f32[2,4,32,256]{3,2,1,0:T(8,128)S(1)} %collective-permute-done.22), channel_id=1, source_target_pairs={{0,96},{32,0},{64,32},{96,64},{128,224},{160,128},{192,160},{224,1... | collective-permute-start | bytes 786440 | tf_op jit(solution)/shard_map/ppermute | solution.py:85
  190.8 8.3 %collective-permute-start.25 = (f32[2,4,32,256]{3,2,1,0:T(8,128)S(1)}, f32[2,4,32,256]{3,2,1,0:T(8,128)S(1)}, u32[]{:S(2)}, u32[]{:S(2)}) collective-permute-start(f32[2,4,32,256]{3,2,1,0:T(8,128)S(1)} %collective-permute-done.23), channel_id=1, source_target_pairs={{0,32},{32,64},{64,96},{96,0},{128,160},{160,192},{192,224},{224,1... | collective-permute-start | bytes 786440 | tf_op jit(solution)/shard_map/ppermute | solution.py:84
  190.8 8.4 %collective-permute-start.26 = (f32[2,4,32,256]{3,2,1,0:T(8,128)S(1)}, f32[2,4,32,256]{3,2,1,0:T(8,128)S(1)}, u32[]{:S(2)}, u32[]{:S(2)}) collective-permute-start(f32[2,4,32,256]{3,2,1,0:T(8,128)S(1)} %collective-permute-done.24), channel_id=1, source_target_pairs={{0,96},{32,0},{64,32},{96,64},{128,224},{160,128},{192,160},{224,1... | collective-permute-start | bytes 786440 | tf_op jit(solution)/shard_map/ppermute | solution.py:85

commit v8 on v7

--- a/solution.py
+++ b/solution.py
@@ -74,10 +74,11 @@
     half = chunk // 2
     q = half // 2
     fwd, bwd = ring_pairs(n_shots, 1), ring_pairs(n_shots, -1)
-    other = lax.ppermute(blocks, "shots", hi_pairs(n_shots))
+    other_f = lax.ppermute(blocks[:, :, :q], "shots", hi_pairs(n_shots))
+    rest, other_f = lax.optimization_barrier((blocks[:, :, q:], other_f))
+    other_b = lax.ppermute(rest, "shots", hi_pairs(n_shots))
     pieces, starts = [], []
-    for block, side in ((blocks, h), (other, 1 - h)):
-        cur_f, cur_b = block[:, :, :q], block[:, :, q:]
+    for (cur_f, cur_b), side in (((blocks[:, :, :q], blocks[:, :, q:]), h), ((other_f, other_b), 1 - h)):
         pieces += [cur_f, cur_b]
         starts += [r * chunk + side * half, r * chunk + side * half + q]
         for t in range(1, RING):

time: 209 us -> 214 us (1.024)
  starting transfers between devices: 76 us -> 79.2 us
    ppermute x6, waiting for transfers between devices: 0.02 us -> 15.5 us  [all_gather_smooth_shots(): cur_b = lax.ppermute(cur_b, 'shots', bwd)]
    ppermute x1 -> x2, waiting for transfers between devices: 19.5 us -> 10.6 us  [the longest x1 10.6 us: all_gather_smooth_shots(): other_f = lax.ppermute(blocks[:, :, :q], 'shots', hi_pairs(n_shots))]
    ppermute x6, waiting for transfers between devices: 17.3 us -> 10.6 us  [all_gather_smooth_shots(): cur_f = lax.ppermute(cur_f, 'shots', fwd)]
    ppermute x6, starting transfers between devices: 0.18 us -> 6.26 us  [all_gather_smooth_shots(): cur_f = lax.ppermute(cur_f, 'shots', fwd)]
    ppermute x6, starting transfers between devices: 19.9 us -> 14.4 us  [all_gather_smooth_shots(): cur_b = lax.ppermute(cur_b, 'shots', bwd)]
    ppermute x1 -> x2, starting transfers between devices: 4.97 us -> 7.58 us  [the longest x1 4.97 us: all_gather_smooth_shots(): other_f = lax.ppermute(blocks[:, :, :q], 'shots', hi_pairs(n_shots))]
  transfers between devices with their start and end apart: 29 -> 30, of which waited for: 14 -> 14; matrix products, arithmetic and copies ran while one was open for 5% -> 5% of each run, Pallas kernels for 0% -> 0%
where the time goes in v8:
time: 214 us; the launch traced here: 212 us
  waiting for transfers between devices  99.9 us (47%)
  starting transfers between devices  79.2 us (37%)
  local copies, waits for them, and re-layouts  14.9 us (7%)
  matrix products  11.7 us (5%)
  other arithmetic  5.01 us (2%)
    ppermute x6, waiting for transfers between devices, ring_sum(): recv_b = lax.ppermute(acc_b, 'shots', bwd)  21.4 us
    ppermute x6, starting transfers between devices, ring_sum(): recv_b = lax.ppermute(acc_b, 'shots', bwd)  20.9 us
    ppermute x1, waiting for transfers between devices, reduce_scatter_shots(): lax.ppermute(theirs[:, :, q:], 'shots', hi_pairs(n_shots))  15.5 us
    ppermute x6, waiting for transfers between devices, all_gather_smooth_shots(): cur_b = lax.ppermute(cur_b, 'shots', bwd)  15.5 us
    all_to_all x1, waiting for transfers between devices, smooth_along_x(): cols = lax.all_to_all(both, 'slab', split_axis=2, concat_axis=1, tiled=True)  14.6 us
    ppermute x6, starting transfers between devices, all_gather_smooth_shots(): cur_b = lax.ppermute(cur_b, 'shots', bwd)  14.4 us
    all_to_all x1, starting transfers between devices, smooth_along_x(): cols = lax.all_to_all(both, 'slab', split_axis=2, concat_axis=1, tiled=True)  10.8 us
    ppermute x6, waiting for transfers between devices, all_gather_smooth_shots(): cur_f = lax.ppermute(cur_f, 'shots', fwd)  10.6 us
  transfers between devices with their start and end apart: 30, of which 14 were waited for; matrix products, arithmetic and copies ran while one was open for 5% of the time, Pallas kernels for 0%

profile of v8, /device:TPU:2, one launch (start us, length us, event | category | flops | bytes accessed | tf_op | source)
XLA Modules:
  0.0 212.1 jit_solution(14040902444027611490)
XLA Ops:
  0.8 1.5 constant_dynamic-slice_fusion.14
  2.3 0.3 copy-done.1
  2.7 1.5 constant_dynamic-slice_fusion.12
  4.2 3.1 %collective-permute-start.3 = (f32[3,4,32,256]{3,2,1,0:T(8,128)S(1)}, f32[3,4,32,256]{3,2,1,0:T(8,128)S(1)}, u32[]{:S(2)}, u32[]{:S(2)}) collective-permute-start(f32[3,4,32,256]{3,2,1,0:T(8,128)S(1)} %pad_maximum_fusion.2), channel_id=1, source_target_pairs={{0,96},{32,0},{64,32},{96,64},{128,224},{160,128},{192,160},{224,1... | collective-permute-start | bytes 1179656 | tf_op jit(solution)/shard_map/ppermute | solution.py:46
  7.5 8.2 %collective-permute-done.3 = f32[3,4,32,256]{3,2,1,0:T(8,128)S(1)} collective-permute-done((f32[3,4,32,256]{3,2,1,0:T(8,128)S(1)}, f32[3,4,32,256]{3,2,1,0:T(8,128)S(1)}, u32[]{:S(2)}, u32[]{:S(2)}) %collective-permute-start.3) | collective-permute-done | bytes 393248 | tf_op jit(solution)/shard_map/ppermute | solution.py:46
  15.8 3.8 %collective-permute-start.4 = (f32[3,4,32,256]{3,2,1,0:T(8,128)S(1)}, f32[3,4,32,256]{3,2,1,0:T(8,128)S(1)}, u32[]{:S(2)}, u32[]{:S(2)}) collective-permute-start(f32[3,4,32,256]{3,2,1,0:T(8,128)S(1)} %maximum_add_fusion.4), channel_id=1, source_target_pairs={{0,96},{32,0},{64,32},{96,64},{128,224},{160,128},{192,160},{224,1... | collective-permute-start | bytes 1179656 | tf_op jit(solution)/shard_map/ppermute | solution.py:46
  19.7 7.3 %collective-permute-done.4 = f32[3,4,32,256]{3,2,1,0:T(8,128)S(1)} collective-permute-done((f32[3,4,32,256]{3,2,1,0:T(8,128)S(1)}, f32[3,4,32,256]{3,2,1,0:T(8,128)S(1)}, u32[]{:S(2)}, u32[]{:S(2)}) %collective-permute-start.4) | collective-permute-done | bytes 393248 | tf_op jit(solution)/shard_map/ppermute | solution.py:46
  27.1 3.8 %collective-permute-start.5 = (f32[3,4,32,256]{3,2,1,0:T(8,128)S(1)}, f32[3,4,32,256]{3,2,1,0:T(8,128)}, u32[]{:S(2)}, u32[]{:S(2)}) collective-permute-start(f32[3,4,32,256]{3,2,1,0:T(8,128)S(1)} %maximum_add_fusion.5), channel_id=1, source_target_pairs={{0,96},{32,0},{64,32},{96,64},{128,224},{160,128},{192,160},{224,1... | collective-permute-start | bytes 1179656 | tf_op jit(solution)/shard_map/ppermute | solution.py:46
  30.9 0.8 maximum_add_fusion.2
  31.7 5.8 %collective-permute-done.5 = f32[3,4,32,256]{3,2,1,0:T(8,128)} collective-permute-done((f32[3,4,32,256]{3,2,1,0:T(8,128)S(1)}, f32[3,4,32,256]{3,2,1,0:T(8,128)}, u32[]{:S(2)}, u32[]{:S(2)}) %collective-permute-start.5) | collective-permute-done | bytes 393248 | tf_op jit(solution)/shard_map/ppermute | solution.py:46
  37.5 1.1 maximum_add_fusion.6
  38.5 3.5 %collective-permute-done.2 = f32[3,4,32,256]{3,2,1,0:T(8,128)} collective-permute-done((f32[3,4,32,256]{3,2,1,0:T(8,128)}, f32[3,4,32,256]{3,2,1,0:T(8,128)}, u32[]{:S(2)}, u32[]{:S(2)}) %collective-permute-start.2) | collective-permute-done | bytes 393248 | tf_op jit(solution)/shard_map/ppermute | solution.py:45
  42.0 1.1 maximum_add_fusion.3
  43.2 0.1 dynamic-slice_bitcast_fusion.3
  43.3 1.4 copy-done.2
  44.7 0.1 dynamic-slice_bitcast_fusion.4
  44.8 0.5 copy-done.3
  45.3 0.1 dynamic-slice_bitcast_fusion.5
  45.6 3.3 %collective-permute-start.8 = (f32[3,4,32,256]{3,2,1,0:T(8,128)S(1)}, f32[3,4,32,256]{3,2,1,0:T(8,128)S(1)}, u32[]{:S(2)}, u32[]{:S(2)}) collective-permute-start(f32[3,4,32,256]{3,2,1,0:T(8,128)S(1)} %pad_maximum_fusion.4), channel_id=1, source_target_pairs={{0,96},{32,0},{64,32},{96,64},{128,224},{160,128},{192,160},{224,1... | collective-permute-start | bytes 1179656 | tf_op jit(solution)/shard_map/ppermute | solution.py:46
  48.9 7.3 %collective-permute-start.10 = (f32[3,4,32,256]{3,2,1,0:T(8,128)S(1)}, f32[3,4,32,256]{3,2,1,0:T(8,128)S(1)}, u32[]{:S(2)}, u32[]{:S(2)}) collective-permute-start(f32[3,4,32,256]{3,2,1,0:T(8,128)S(1)} %get-tuple-element.93), channel_id=1, source_target_pairs={{0,128},{32,160},{64,192},{96,224},{128,0},{160,32},{192,64},{224,... | collective-permute-start | bytes 1179656 | tf_op jit(solution)/shard_map/ppermute | solution.py:63
  56.4 3.3 %collective-permute-start.9 = (f32[3,4,32,256]{3,2,1,0:T(8,128)S(1)}, f32[3,4,32,256]{3,2,1,0:T(8,128)S(1)}, u32[]{:S(2)}, u32[]{:S(2)}) collective-permute-start(f32[3,4,32,256]{3,2,1,0:T(8,128)S(1)} %maximum_add_fusion.8), channel_id=1, source_target_pairs={{0,96},{32,0},{64,32},{96,64},{128,224},{160,128},{192,160},{224,1... | collective-permute-start | bytes 1179656 | tf_op jit(solution)/shard_map/ppermute | solution.py:46
  59.7 5.7 %collective-permute-start.13 = (f32[3,4,32,256]{3,2,1,0:T(8,128)S(1)}, f32[3,4,32,256]{3,2,1,0:T(8,128)S(1)}, u32[]{:S(2)}, u32[]{:S(2)}) collective-permute-start(f32[3,4,32,256]{3,2,1,0:T(8,128)S(1)} %get-tuple-element.92), channel_id=1, source_target_pairs={{0,128},{32,160},{64,192},{96,224},{128,0},{160,32},{192,64},{224,... | collective-permute-start | bytes 1179656 | tf_op jit(solution)/shard_map/ppermute | solution.py:64
  65.4 0.6 collective-permute-done.7
  66.3 3.7 %collective-permute-start.12 = (f32[3,4,32,256]{3,2,1,0:T(8,128)S(1)}, f32[3,4,32,256]{3,2,1,0:T(8,128)S(1)}, u32[]{:S(2)}, u32[]{:S(2)}) collective-permute-start(f32[3,4,32,256]{3,2,1,0:T(8,128)S(1)} %maximum_add_fusion.10), channel_id=1, source_target_pairs={{0,96},{32,0},{64,32},{96,64},{128,224},{160,128},{192,160},{224,1... | collective-permute-start | bytes 1179656 | tf_op jit(solution)/shard_map/ppermute | solution.py:46
  70.0 0.2 fusion.26
  70.2 15.5 %collective-permute-done.13 = f32[3,4,32,256]{3,2,1,0:T(8,128)S(1)} collective-permute-done((f32[3,4,32,256]{3,2,1,0:T(8,128)S(1)}, f32[3,4,32,256]{3,2,1,0:T(8,128)S(1)}, u32[]{:S(2)}, u32[]{:S(2)}) %collective-permute-start.13) | collective-permute-done | bytes 393248 | tf_op jit(solution)/shard_map/ppermute | solution.py:64
  85.8 0.1 maximum_add_fusion
  86.0 0.7 fusion.15
  86.7 1.1 copy.13
  87.8 10.8 %all-to-all-start = ((f32[2,4,64,256]{3,1,0,2:T(4,128)}), f32[2,4,64,256]{3,1,0,2:T(4,128)S(1)}, u32[]{:S(2)}, u32[]{:S(2)}) async-start(f32[2,4,64,256]{3,1,0,2:T(4,128)} %copy.13), calls=%async_computation | async-start | bytes 1048576 | tf_op jit(solution)/shard_map/all_to_all | solution.py:107
  98.6 0.1 fusion.67
  98.8 14.6 %all-to-all-done = f32[2,4,64,256]{3,1,0,2:T(4,128)S(1)} async-done(((f32[2,4,64,256]{3,1,0,2:T(4,128)}), f32[2,4,64,256]{3,1,0,2:T(4,128)S(1)}, u32[]{:S(2)}, u32[]{:S(2)}) %all-to-all-start) | async-done | bytes 524320 | tf_op jit(solution)/shard_map/all_to_all | solution.py:107
  113.3 0.3 copy.14
  113.6 1.0 convolution_bitcast_fusion
  114.6 1.0 copy.16
  115.6 5.9 %all-to-all-start.1 = ((f32[2,128,2,256]{3,2,0,1:T(2,128)}), f32[2,128,2,256]{3,2,0,1:T(2,128)S(1)}, u32[]{:S(2)}, u32[]{:S(2)}) async-start(f32[2,128,2,256]{3,2,0,1:T(2,128)} %copy.16), calls=%async_computation.1 | async-start | bytes 1048576 | tf_op jit(solution)/shard_map/all_to_all | solution.py:110
  121.5 0.5 fusion.14
  122.0 0.4 fusion.13
  122.4 2.6 %constant_dynamic-slice_fusion.24 = (f32[512,32]{1,0:T(8,128)S(1)}, f32[512,32]{1,0:T(8,128)S(1)}, f32[512,32]{1,0:T(8,128)S(1)}, f32[512,32]{1,0:T(8,128)S(1)},...) fusion(f32[512,512]{1,0:T(8,128)S(1)} %fusion.13, ...), kind=kLoop, calls=%fused_computation.176 | loop fusion | bytes 2097216 | tf_op jit(solution)/shard_map/dynamic_slice | solution.py:91
  125.0 3.3 %concatenate.18 = f32[512,512]{1,0:T(8,128)S(1)} concatenate(f32[512,32]{1,0:T(8,128)} %get-tuple-element.89, f32[512,32]{1,0:T(8,128)} %get-tuple-element.88, f32[512,32]{1,0:T(8,128)} %get-tuple-element.87, f32[512,32]{1,0:T(8,128)} %get-tuple-element.86, f32[512,32]{1,0:T(8,128)} %get-tuple-element.85, f32[512,32]{1,0:T(8,128)} %get-tuple-element.84, ...), dimensions={1} | concatenate | bytes 2097152 | tf_op jit(solution)/shard_map/concatenate | solution.py:90
  128.4 0.2 convolution_bitcast_fusion.1
  128.6 7.6 %all-to-all-done.1 = f32[2,128,2,256]{3,2,0,1:T(2,128)S(1)} async-done(((f32[2,128,2,256]{3,2,0,1:T(2,128)}), f32[2,128,2,256]{3,2,0,1:T(2,128)S(1)}, u32[]{:S(2)}, u32[]{:S(2)}) %all-to-all-start.1) | async-done | bytes 524320 | tf_op jit(solution)/shard_map/all_to_all | solution.py:110
  136.2 0.2 copy.18
  136.4 0.4 all_to_all.33
  136.9 5.0 %collective-permute-start.20 = (f32[2,4,32,256]{3,2,1,0:T(8,128)S(1)}, f32[2,4,32,256]{3,2,1,0:T(8,128)S(1)}, u32[]{:S(2)}, u32[]{:S(2)}) collective-permute-start(f32[2,4,32,256]{3,2,1,0:T(8,128)S(1)} %get-tuple-element.99), channel_id=1, source_target_pairs={{0,128},{32,160},{64,192},{96,224},{128,0},{160,32},{192,64},{224,... | collective-permute-start | bytes 786440 | tf_op jit(solution)/shard_map/ppermute | solution.py:77
  141.9 3.3 %collective-permute-start.15 = (f32[2,4,32,256]{3,2,1,0:T(8,128)S(1)}, f32[2,4,32,256]{3,2,1,0:T(8,128)S(1)}, u32[]{:S(2)}, u32[]{:S(2)}) collective-permute-start(f32[2,4,32,256]{3,2,1,0:T(8,128)S(1)} %get-tuple-element.25), channel_id=1, source_target_pairs={{0,96},{32,0},{64,32},{96,64},{128,224},{160,128},{192,160},{224,1... | collective-permute-start | bytes 786440 | tf_op jit(solution)/shard_map/ppermute | solution.py:86
  145.2 10.6 %collective-permute-done.20 = f32[2,4,32,256]{3,2,1,0:T(8,128)S(1)} collective-permute-done((f32[2,4,32,256]{3,2,1,0:T(8,128)S(1)}, f32[2,4,32,256]{3,2,1,0:T(8,128)S(1)}, u32[]{:S(2)}, u32[]{:S(2)}) %collective-permute-start.20) | collective-permute-done | bytes 262176 | tf_op jit(solution)/shard_map/ppermute | solution.py:77
  155.8 2.6 %collective-permute-start.21 = (f32[2,4,32,256]{3,2,1,0:T(8,128)S(1)}, f32[2,4,32,256]{3,2,1,0:T(8,128)S(1)}, u32[]{:S(2)}, u32[]{:S(2)}) collective-permute-start(f32[2,4,32,256]{3,2,1,0:T(8,128)S(1)} %get-tuple-element.25), channel_id=1, source_target_pairs={{0,128},{32,160},{64,192},{96,224},{128,0},{160,32},{192,64},{224,... | collective-permute-start | bytes 786440 | tf_op jit(solution)/shard_map/ppermute | solution.py:79
  158.4 1.4 collective-permute-start.22
  159.8 3.0 %collective-permute-start.16 = (f32[2,4,32,256]{3,2,1,0:T(8,128)S(1)}, f32[2,4,32,256]{3,2,1,0:T(8,128)S(1)}, u32[]{:S(2)}, u32[]{:S(2)}) collective-permute-start(f32[2,4,32,256]{3,2,1,0:T(8,128)S(1)} %collective-permute-done.14), channel_id=1, source_target_pairs={{0,32},{32,64},{64,96},{96,0},{128,160},{160,192},{192,224},{224,1... | collective-permute-start | bytes 786440 | tf_op jit(solution)/shard_map/ppermute | solution.py:85
  162.7 0.3 collective-permute-start.17
  163.1 10.5 %collective-permute-done.16 = f32[2,4,32,256]{3,2,1,0:T(8,128)S(1)} collective-permute-done((f32[2,4,32,256]{3,2,1,0:T(8,128)S(1)}, f32[2,4,32,256]{3,2,1,0:T(8,128)S(1)}, u32[]{:S(2)}, u32[]{:S(2)}) %collective-permute-start.16) | collective-permute-done | bytes 262176 | tf_op jit(solution)/shard_map/ppermute | solution.py:85
  173.5 0.3 collective-permute-start.18
  173.8 3.0 %collective-permute-start.19 = (f32[2,4,32,256]{3,2,1,0:T(8,128)S(1)}, f32[2,4,32,256]{3,2,1,0:T(8,128)S(1)}, u32[]{:S(2)}, u32[]{:S(2)}) collective-permute-start(f32[2,4,32,256]{3,2,1,0:T(8,128)S(1)} %collective-permute-done.17), channel_id=1, source_target_pairs={{0,96},{32,0},{64,32},{96,64},{128,224},{160,128},{192,160},{224,1... | collective-permute-start | bytes 786440 | tf_op jit(solution)/shard_map/ppermute | solution.py:86
  176.8 0.5 collective-permute-start.23
  177.3 1.5 collective-permute-start.24
  178.9 8.2 %collective-permute-done.23 = f32[2,4,32,256]{3,2,1,0:T(8,128)S(1)} collective-permute-done((f32[2,4,32,256]{3,2,1,0:T(8,128)S(1)}, f32[2,4,32,256]{3,2,1,0:T(8,128)S(1)}, u32[]{:S(2)}, u32[]{:S(2)}) %collective-permute-start.23) | collective-permute-done | bytes 262176 | tf_op jit(solution)/shard_map/ppermute | solution.py:86
  187.1 3.7 %collective-permute-start.25 = (f32[2,4,32,256]{3,2,1,0:T(8,128)S(1)}, f32[2,4,32,256]{3,2,1,0:T(8,128)S(1)}, u32[]{:S(2)}, u32[]{:S(2)}) collective-permute-start(f32[2,4,32,256]{3,2,1,0:T(8,128)S(1)} %collective-permute-done.23), channel_id=1, source_target_pairs={{0,96},{32,0},{64,32},{96,64},{128,224},{160,128},{192,160},{224,1... | collective-permute-start | bytes 786440 | tf_op jit(solution)/shard_map/ppermute | solution.py:86
  191.1 3.6 %collective-permute-done.25 = f32[2,4,32,256]{3,2,1,0:T(8,128)S(1)} collective-permute-done((f32[2,4,32,256]{3,2,1,0:T(8,128)S(1)}, f32[2,4,32,256]{3,2,1,0:T(8,128)S(1)}, u32[]{:S(2)}, u32[]{:S(2)}) %collective-permute-start.25) | collective-permute-done | bytes 262176 | tf_op jit(solution)/shard_map/ppermute | solution.py:86
  194.7 3.7 %collective-permute-start.27 = (f32[2,4,32,256]{3,2,1,0:T(8,128)S(1)}, f32[2,4,32,256]{3,2,1,0:T(8,128)S(1)}, u32[]{:S(2)}, u32[]{:S(2)}) collective-permute-start(f32[2,4,32,256]{3,2,1,0:T(8,128)S(1)} %collective-permute-done.25), channel_id=1, source_target_pairs={{0,96},{32,0},{64,32},{96,64},{128,224},{160,128},{192,160},{224,1... | collective-permute-start | bytes 786440 | tf_op jit(solution)/shard_map/ppermute | solution.py:86
  198.4 0.2 collective-permute-done.26
  198.6 3.7 %collective-permute-done.27 = f32[2,4,32,256]{3,2,1,0:T(8,128)S(1)} collective-permute-done((f32[2,4,32,256]{3,2,1,0:T(8,128)S(1)}, f32[2,4,32,256]{3,2,1,0:T(8,128)S(1)}, u32[]{:S(2)}, u32[]{:S(2)}) %collective-permute-start.27) | collective-permute-done | bytes 262176 | tf_op jit(solution)/shard_map/ppermute | solution.py:86
  202.3 4.9 %fusion.4 = f32[4,512,256]{2,1,0:T(8,128)} fusion(f32[4,512,256]{2,1,0:T(8,128)S(1)} %get-tuple-element.101, f32[512,512]{1,0:T(8,128)S(1)} %concatenate.18, f32[256]{0:T(256)S(1)} %bitcast.208), kind=kOutput, calls=%fused_computation.4 | convolution fusion | flops 3221749760 | bytes 5243904 | tf_op jit(solution)/shard_map/xij,xjz->xiz/dot_general | solution.py:97
  207.2 4.9 %fusion.7 = f32[4,512,256]{2,1,0:T(8,128)} fusion(f32[4,512,256]{2,1,0:T(8,128)S(1)} %get-tuple-element.100, f32[512,512]{1,0:T(8,128)S(1)} %concatenate.18, f32[256]{0:T(256)S(1)} %bitcast.207), kind=kOutput, calls=%fused_computation.5 | convolution fusion | flops 3221749760 | bytes 5243904 | tf_op jit(solution)/shard_map/xij,xjz->xiz/dot_general | solution.py:97
  (65 shorter events, 1.8 us)
Async XLA Ops:
  0.6 127.7 %copy-start = (f32[2,16]{1,0:T(2,128)S(1)}, f32[2,16]{1,0:T(2,128)}, u32[]{:S(2)}) copy-start(f32[2,16]{1,0:T(2,128)} %param.9) | copy-start | bytes 388
  0.6 2.0 copy-start.1
  4.2 11.5 %collective-permute-start.3 = (f32[3,4,32,256]{3,2,1,0:T(8,128)S(1)}, f32[3,4,32,256]{3,2,1,0:T(8,128)S(1)}, u32[]{:S(2)}, u32[]{:S(2)}) collective-permute-start(f32[3,4,32,256]{3,2,1,0:T(8,128)S(1)} %pad_maximum_fusion.2), channel_id=1, source_target_pairs={{0,96},{32,0},{64,32},{96,64},{128,224},{160,128},{192,160},{224,1... | collective-permute-start | bytes 1179656 | tf_op jit(solution)/shard_map/ppermute | solution.py:46
  7.4 12.2 %collective-permute-start = (f32[3,4,32,256]{3,2,1,0:T(8,128)S(1)}, f32[3,4,32,256]{3,2,1,0:T(8,128)S(1)}, u32[]{:S(2)}, u32[]{:S(2)}) collective-permute-start(f32[3,4,32,256]{3,2,1,0:T(8,128)S(1)} %pad_maximum_fusion.1), channel_id=1, source_target_pairs={{0,32},{32,64},{64,96},{96,0},{128,160},{160,192},{192,224},{224,1... | collective-permute-start | bytes 1179656 | tf_op jit(solution)/shard_map/ppermute | solution.py:45
  15.8 11.3 %collective-permute-start.4 = (f32[3,4,32,256]{3,2,1,0:T(8,128)S(1)}, f32[3,4,32,256]{3,2,1,0:T(8,128)S(1)}, u32[]{:S(2)}, u32[]{:S(2)}) collective-permute-start(f32[3,4,32,256]{3,2,1,0:T(8,128)S(1)} %maximum_add_fusion.4), channel_id=1, source_target_pairs={{0,96},{32,0},{64,32},{96,64},{128,224},{160,128},{192,160},{224,1... | collective-permute-start | bytes 1179656 | tf_op jit(solution)/shard_map/ppermute | solution.py:46
  19.6 11.3 %collective-permute-start.1 = (f32[3,4,32,256]{3,2,1,0:T(8,128)S(1)}, f32[3,4,32,256]{3,2,1,0:T(8,128)S(1)}, u32[]{:S(2)}, u32[]{:S(2)}) collective-permute-start(f32[3,4,32,256]{3,2,1,0:T(8,128)S(1)} %maximum_add_fusion.1), channel_id=1, source_target_pairs={{0,32},{32,64},{64,96},{96,0},{128,160},{160,192},{192,224},{224,1... | collective-permute-start | bytes 1179656 | tf_op jit(solution)/shard_map/ppermute | solution.py:45
  27.1 10.3 %collective-permute-start.5 = (f32[3,4,32,256]{3,2,1,0:T(8,128)S(1)}, f32[3,4,32,256]{3,2,1,0:T(8,128)}, u32[]{:S(2)}, u32[]{:S(2)}) collective-permute-start(f32[3,4,32,256]{3,2,1,0:T(8,128)S(1)} %maximum_add_fusion.5), channel_id=1, source_target_pairs={{0,96},{32,0},{64,32},{96,64},{128,224},{160,128},{192,160},{224,1... | collective-permute-start | bytes 1179656 | tf_op jit(solution)/shard_map/ppermute | solution.py:46
  31.7 10.3 %collective-permute-start.2 = (f32[3,4,32,256]{3,2,1,0:T(8,128)}, f32[3,4,32,256]{3,2,1,0:T(8,128)}, u32[]{:S(2)}, u32[]{:S(2)}) collective-permute-start(f32[3,4,32,256]{3,2,1,0:T(8,128)} %maximum_add_fusion.2), channel_id=1, source_target_pairs={{0,32},{32,64},{64,96},{96,0},{128,160},{160,192},{192,224},{224,1... | collective-permute-start | bytes 1179656 | tf_op jit(solution)/shard_map/ppermute | solution.py:45
  43.1 1.6 copy-start.2
  43.1 2.2 %copy-start.3 = (f32[1,4,512,256]{3,2,1,0:T(8,128)S(1)}, f32[1,4,512,256]{3,2,1,0:T(8,128)}, u32[]{:S(2)}) copy-start(f32[1,4,512,256]{3,2,1,0:T(8,128)} %param.7) | copy-start | bytes 6291460
  45.5 10.8 %collective-permute-start.6 = (f32[3,4,32,256]{3,2,1,0:T(8,128)S(1)}, f32[3,4,32,256]{3,2,1,0:T(8,128)S(1)}, u32[]{:S(2)}, u32[]{:S(2)}) collective-permute-start(f32[3,4,32,256]{3,2,1,0:T(8,128)S(1)} %pad_maximum_fusion.3), channel_id=1, source_target_pairs={{0,32},{32,64},{64,96},{96,0},{128,160},{160,192},{192,224},{224,1... | collective-permute-start | bytes 1179656 | tf_op jit(solution)/shard_map/ppermute | solution.py:45
  45.6 10.8 %collective-permute-start.8 = (f32[3,4,32,256]{3,2,1,0:T(8,128)S(1)}, f32[3,4,32,256]{3,2,1,0:T(8,128)S(1)}, u32[]{:S(2)}, u32[]{:S(2)}) collective-permute-start(f32[3,4,32,256]{3,2,1,0:T(8,128)S(1)} %pad_maximum_fusion.4), channel_id=1, source_target_pairs={{0,96},{32,0},{64,32},{96,64},{128,224},{160,128},{192,160},{224,1... | collective-permute-start | bytes 1179656 | tf_op jit(solution)/shard_map/ppermute | solution.py:46
  48.9 16.5 %collective-permute-start.10 = (f32[3,4,32,256]{3,2,1,0:T(8,128)S(1)}, f32[3,4,32,256]{3,2,1,0:T(8,128)S(1)}, u32[]{:S(2)}, u32[]{:S(2)}) collective-permute-start(f32[3,4,32,256]{3,2,1,0:T(8,128)S(1)} %get-tuple-element.93), channel_id=1, source_target_pairs={{0,128},{32,160},{64,192},{96,224},{128,0},{160,32},{192,64},{224,... | collective-permute-start | bytes 1179656 | tf_op jit(solution)/shard_map/ppermute | solution.py:63
  56.3 9.8 %collective-permute-start.7 = (f32[3,4,32,256]{3,2,1,0:T(8,128)S(1)}, f32[3,4,32,256]{3,2,1,0:T(8,128)S(1)}, u32[]{:S(2)}, u32[]{:S(2)}) collective-permute-start(f32[3,4,32,256]{3,2,1,0:T(8,128)S(1)} %maximum_add_fusion.7), channel_id=1, source_target_pairs={{0,32},{32,64},{64,96},{96,0},{128,160},{160,192},{192,224},{224,1... | collective-permute-start | bytes 1179656 | tf_op jit(solution)/shard_map/ppermute | solution.py:45
  56.4 9.6 %collective-permute-start.9 = (f32[3,4,32,256]{3,2,1,0:T(8,128)S(1)}, f32[3,4,32,256]{3,2,1,0:T(8,128)S(1)}, u32[]{:S(2)}, u32[]{:S(2)}) collective-permute-start(f32[3,4,32,256]{3,2,1,0:T(8,128)S(1)} %maximum_add_fusion.8), channel_id=1, source_target_pairs={{0,96},{32,0},{64,32},{96,64},{128,224},{160,128},{192,160},{224,1... | collective-permute-start | bytes 1179656 | tf_op jit(solution)/shard_map/ppermute | solution.py:46
  59.7 26.0 %collective-permute-start.13 = (f32[3,4,32,256]{3,2,1,0:T(8,128)S(1)}, f32[3,4,32,256]{3,2,1,0:T(8,128)S(1)}, u32[]{:S(2)}, u32[]{:S(2)}) collective-permute-start(f32[3,4,32,256]{3,2,1,0:T(8,128)S(1)} %get-tuple-element.92), channel_id=1, source_target_pairs={{0,128},{32,160},{64,192},{96,224},{128,0},{160,32},{192,64},{224,... | collective-permute-start | bytes 1179656 | tf_op jit(solution)/shard_map/ppermute | solution.py:64
  66.1 19.6 %collective-permute-start.11 = (f32[3,4,32,256]{3,2,1,0:T(8,128)S(1)}, f32[3,4,32,256]{3,2,1,0:T(8,128)S(1)}, u32[]{:S(2)}, u32[]{:S(2)}) collective-permute-start(f32[3,4,32,256]{3,2,1,0:T(8,128)S(1)} %maximum_add_fusion.9), channel_id=1, source_target_pairs={{0,32},{32,64},{64,96},{96,0},{128,160},{160,192},{192,224},{224,1... | collective-permute-start | bytes 1179656 | tf_op jit(solution)/shard_map/ppermute | solution.py:45
  66.3 19.4 %collective-permute-start.12 = (f32[3,4,32,256]{3,2,1,0:T(8,128)S(1)}, f32[3,4,32,256]{3,2,1,0:T(8,128)S(1)}, u32[]{:S(2)}, u32[]{:S(2)}) collective-permute-start(f32[3,4,32,256]{3,2,1,0:T(8,128)S(1)} %maximum_add_fusion.10), channel_id=1, source_target_pairs={{0,96},{32,0},{64,32},{96,64},{128,224},{160,128},{192,160},{224,1... | collective-permute-start | bytes 1179656 | tf_op jit(solution)/shard_map/ppermute | solution.py:46
  87.8 25.5 %all-to-all-start = ((f32[2,4,64,256]{3,1,0,2:T(4,128)}), f32[2,4,64,256]{3,1,0,2:T(4,128)S(1)}, u32[]{:S(2)}, u32[]{:S(2)}) async-start(f32[2,4,64,256]{3,1,0,2:T(4,128)} %copy.13), calls=%async_computation | async-start | bytes 1048576 | tf_op jit(solution)/shard_map/all_to_all | solution.py:107
  115.6 20.6 %all-to-all-start.1 = ((f32[2,128,2,256]{3,2,0,1:T(2,128)}), f32[2,128,2,256]{3,2,0,1:T(2,128)S(1)}, u32[]{:S(2)}, u32[]{:S(2)}) async-start(f32[2,128,2,256]{3,2,0,1:T(2,128)} %copy.16), calls=%async_computation.1 | async-start | bytes 1048576 | tf_op jit(solution)/shard_map/all_to_all | solution.py:110
  125.0 3.4 %copy-start.4 = (s32[256]{0:T(256)S(1)}, s32[256]{0:T(256)}, u32[]{:S(2)}) copy-start(s32[256]{0:T(256)} %param.8) | copy-start | bytes 3076
  136.8 23.0 %collective-permute-start.14 = (f32[2,4,32,256]{3,2,1,0:T(8,128)S(1)}, f32[2,4,32,256]{3,2,1,0:T(8,128)S(1)}, u32[]{:S(2)}, u32[]{:S(2)}) collective-permute-start(f32[2,4,32,256]{3,2,1,0:T(8,128)S(1)} %get-tuple-element.99), channel_id=1, source_target_pairs={{0,32},{32,64},{64,96},{96,0},{128,160},{160,192},{192,224},{224,1... | collective-permute-start | bytes 786440 | tf_op jit(solution)/shard_map/ppermute | solution.py:85
  136.9 18.9 %collective-permute-start.20 = (f32[2,4,32,256]{3,2,1,0:T(8,128)S(1)}, f32[2,4,32,256]{3,2,1,0:T(8,128)S(1)}, u32[]{:S(2)}, u32[]{:S(2)}) collective-permute-start(f32[2,4,32,256]{3,2,1,0:T(8,128)S(1)} %get-tuple-element.99), channel_id=1, source_target_pairs={{0,128},{32,160},{64,192},{96,224},{128,0},{160,32},{192,64},{224,... | collective-permute-start | bytes 786440 | tf_op jit(solution)/shard_map/ppermute | solution.py:77
  141.9 20.9 %collective-permute-start.15 = (f32[2,4,32,256]{3,2,1,0:T(8,128)S(1)}, f32[2,4,32,256]{3,2,1,0:T(8,128)S(1)}, u32[]{:S(2)}, u32[]{:S(2)}) collective-permute-start(f32[2,4,32,256]{3,2,1,0:T(8,128)S(1)} %get-tuple-element.25), channel_id=1, source_target_pairs={{0,96},{32,0},{64,32},{96,64},{128,224},{160,128},{192,160},{224,1... | collective-permute-start | bytes 786440 | tf_op jit(solution)/shard_map/ppermute | solution.py:86
  155.8 21.0 %collective-permute-start.21 = (f32[2,4,32,256]{3,2,1,0:T(8,128)S(1)}, f32[2,4,32,256]{3,2,1,0:T(8,128)S(1)}, u32[]{:S(2)}, u32[]{:S(2)}) collective-permute-start(f32[2,4,32,256]{3,2,1,0:T(8,128)S(1)} %get-tuple-element.25), channel_id=1, source_target_pairs={{0,128},{32,160},{64,192},{96,224},{128,0},{160,32},{192,64},{224,... | collective-permute-start | bytes 786440 | tf_op jit(solution)/shard_map/ppermute | solution.py:79
  158.4 18.9 %collective-permute-start.22 = (f32[2,4,32,256]{3,2,1,0:T(8,128)S(1)}, f32[2,4,32,256]{3,2,1,0:T(8,128)S(1)}, u32[]{:S(2)}, u32[]{:S(2)}) collective-permute-start(f32[2,4,32,256]{3,2,1,0:T(8,128)S(1)} %collective-permute-done.20), channel_id=1, source_target_pairs={{0,32},{32,64},{64,96},{96,0},{128,160},{160,192},{192,224},{224,1... | collective-permute-start | bytes 786440 | tf_op jit(solution)/shard_map/ppermute | solution.py:85
  159.8 13.8 %collective-permute-start.16 = (f32[2,4,32,256]{3,2,1,0:T(8,128)S(1)}, f32[2,4,32,256]{3,2,1,0:T(8,128)S(1)}, u32[]{:S(2)}, u32[]{:S(2)}) collective-permute-start(f32[2,4,32,256]{3,2,1,0:T(8,128)S(1)} %collective-permute-done.14), channel_id=1, source_target_pairs={{0,32},{32,64},{64,96},{96,0},{128,160},{160,192},{192,224},{224,1... | collective-permute-start | bytes 786440 | tf_op jit(solution)/shard_map/ppermute | solution.py:85
  162.7 11.1 %collective-permute-start.17 = (f32[2,4,32,256]{3,2,1,0:T(8,128)S(1)}, f32[2,4,32,256]{3,2,1,0:T(8,128)S(1)}, u32[]{:S(2)}, u32[]{:S(2)}) collective-permute-start(f32[2,4,32,256]{3,2,1,0:T(8,128)S(1)} %collective-permute-done.15), channel_id=1, source_target_pairs={{0,96},{32,0},{64,32},{96,64},{128,224},{160,128},{192,160},{224,1... | collective-permute-start | bytes 786440 | tf_op jit(solution)/shard_map/ppermute | solution.py:86
  173.5 17.2 %collective-permute-start.18 = (f32[2,4,32,256]{3,2,1,0:T(8,128)S(1)}, f32[2,4,32,256]{3,2,1,0:T(8,128)S(1)}, u32[]{:S(2)}, u32[]{:S(2)}) collective-permute-start(f32[2,4,32,256]{3,2,1,0:T(8,128)S(1)} %collective-permute-done.16), channel_id=1, source_target_pairs={{0,32},{32,64},{64,96},{96,0},{128,160},{160,192},{192,224},{224,1... | collective-permute-start | bytes 786440 | tf_op jit(solution)/shard_map/ppermute | solution.py:85
  173.8 17.0 %collective-permute-start.19 = (f32[2,4,32,256]{3,2,1,0:T(8,128)S(1)}, f32[2,4,32,256]{3,2,1,0:T(8,128)S(1)}, u32[]{:S(2)}, u32[]{:S(2)}) collective-permute-start(f32[2,4,32,256]{3,2,1,0:T(8,128)S(1)} %collective-permute-done.17), channel_id=1, source_target_pairs={{0,96},{32,0},{64,32},{96,64},{128,224},{160,128},{192,160},{224,1... | collective-permute-start | bytes 786440 | tf_op jit(solution)/shard_map/ppermute | solution.py:86
  176.8 10.3 %collective-permute-start.23 = (f32[2,4,32,256]{3,2,1,0:T(8,128)S(1)}, f32[2,4,32,256]{3,2,1,0:T(8,128)S(1)}, u32[]{:S(2)}, u32[]{:S(2)}) collective-permute-start(f32[2,4,32,256]{3,2,1,0:T(8,128)S(1)} %collective-permute-done.21), channel_id=1, source_target_pairs={{0,96},{32,0},{64,32},{96,64},{128,224},{160,128},{192,160},{224,1... | collective-permute-start | bytes 786440 | tf_op jit(solution)/shard_map/ppermute | solution.py:86
  177.3 13.5 %collective-permute-start.24 = (f32[2,4,32,256]{3,2,1,0:T(8,128)S(1)}, f32[2,4,32,256]{3,2,1,0:T(8,128)S(1)}, u32[]{:S(2)}, u32[]{:S(2)}) collective-permute-start(f32[2,4,32,256]{3,2,1,0:T(8,128)S(1)} %collective-permute-done.22), channel_id=1, source_target_pairs={{0,32},{32,64},{64,96},{96,0},{128,160},{160,192},{192,224},{224,1... | collective-permute-start | bytes 786440 | tf_op jit(solution)/shard_map/ppermute | solution.py:85
  187.1 7.6 %collective-permute-start.25 = (f32[2,4,32,256]{3,2,1,0:T(8,128)S(1)}, f32[2,4,32,256]{3,2,1,0:T(8,128)S(1)}, u32[]{:S(2)}, u32[]{:S(2)}) collective-permute-start(f32[2,4,32,256]{3,2,1,0:T(8,128)S(1)} %collective-permute-done.23), channel_id=1, source_target_pairs={{0,96},{32,0},{64,32},{96,64},{128,224},{160,128},{192,160},{224,1... | collective-permute-start | bytes 786440 | tf_op jit(solution)/shard_map/ppermute | solution.py:86
  190.9 7.7 %collective-permute-start.26 = (f32[2,4,32,256]{3,2,1,0:T(8,128)S(1)}, f32[2,4,32,256]{3,2,1,0:T(8,128)S(1)}, u32[]{:S(2)}, u32[]{:S(2)}) collective-permute-start(f32[2,4,32,256]{3,2,1,0:T(8,128)S(1)} %collective-permute-done.24), channel_id=1, source_target_pairs={{0,32},{32,64},{64,96},{96,0},{128,160},{160,192},{192,224},{224,1... | collective-permute-start | bytes 786440 | tf_op jit(solution)/shard_map/ppermute | solution.py:85
  194.7 7.6 %collective-permute-start.27 = (f32[2,4,32,256]{3,2,1,0:T(8,128)S(1)}, f32[2,4,32,256]{3,2,1,0:T(8,128)S(1)}, u32[]{:S(2)}, u32[]{:S(2)}) collective-permute-start(f32[2,4,32,256]{3,2,1,0:T(8,128)S(1)} %collective-permute-done.25), channel_id=1, source_target_pairs={{0,96},{32,0},{64,32},{96,64},{128,224},{160,128},{192,160},{224,1... | collective-permute-start | bytes 786440 | tf_op jit(solution)/shard_map/ppermute | solution.py:86

commit v9 on v7

--- a/solution.py
+++ b/solution.py
@@ -58,13 +58,13 @@
     half = chunk // 2
     theirs = ring_sum(fields, lambda c: c * chunk + (1 - h) * half, half, n_shots)
     fields, theirs = lax.optimization_barrier((tuple(fields), theirs))
-    q = half // 2
+    cuts = [0, half // 4, half // 4 + 3 * half // 8, half]
     gates = {
-        RING - 2: lax.ppermute(theirs[:, :, :q], "shots", hi_pairs(n_shots)),
-        RING - 1: lax.ppermute(theirs[:, :, q:], "shots", hi_pairs(n_shots)),
+        t: lax.ppermute(theirs[:, :, cuts[t - 1]:cuts[t]], "shots", hi_pairs(n_shots))
+        for t in range(1, RING)
     }
     mine = ring_sum(fields, lambda c: c * chunk + h * half, half, n_shots, gates)
-    return mine + jnp.concatenate([gates[RING - 2], gates[RING - 1]], axis=2)
+    return mine + jnp.concatenate([gates[t] for t in range(1, RING)], axis=2)
 
 
 def all_gather_smooth_shots(blocks, n_shots, total):

time: 209 us -> 216 us (1.033)
  waiting for transfers between devices: 100 us -> 107 us
    ppermute x2 -> x3, waiting for transfers between devices: 15.5 us -> 23.2 us  [reduce_scatter_shots(): lax.ppermute(theirs[:, :, cuts[t - 1]:cuts[t]], 'shots', hi_pairs(n_shots))]
    ppermute x2 -> x3, starting transfers between devices: 13 us -> 19.8 us  [reduce_scatter_shots(): lax.ppermute(theirs[:, :, cuts[t - 1]:cuts[t]], 'shots', hi_pairs(n_shots))]
    all_to_all x1, starting transfers between devices: 10.8 us -> 4.99 us  [smooth_along_x(): cols = lax.all_to_all(both, 'slab', split_axis=2, concat_axis=1, tiled=True)]
  transfers between devices with their start and end apart: 29 -> 30, of which waited for: 14 -> 15; matrix products, arithmetic and copies ran while one was open for 5% -> 5% of each run, Pallas kernels for 0% -> 0%
where the time goes in v9:
time: 216 us
  waiting for transfers between devices  107 us (50%)
  starting transfers between devices  75.3 us (35%)
  local copies, waits for them, and re-layouts  14.9 us (7%)
  matrix products  11.7 us (5%)
  other arithmetic  5.01 us (2%)
    ppermute x3, waiting for transfers between devices, reduce_scatter_shots(): lax.ppermute(theirs[:, :, cuts[t - 1]:cuts[t]], 'shots', hi_pairs(n_shots))  23.2 us
    ppermute x6, waiting for transfers between devices, ring_sum(): recv_b = lax.ppermute(acc_b, 'shots', bwd)  21.4 us
    ppermute x6, starting transfers between devices, ring_sum(): recv_b = lax.ppermute(acc_b, 'shots', bwd)  20.5 us
    ppermute x3, starting transfers between devices, reduce_scatter_shots(): lax.ppermute(theirs[:, :, cuts[t - 1]:cuts[t]], 'shots', hi_pairs(n_shots))  19.8 us
    ppermute x6, starting transfers between devices, all_gather_smooth_shots(): cur_b = lax.ppermute(cur_b, 'shots', bwd)  19.4 us
    ppermute x1, waiting for transfers between devices, all_gather_smooth_shots(): other = lax.ppermute(blocks, 'shots', hi_pairs(n_shots))  19.1 us
    ppermute x6, waiting for transfers between devices, all_gather_smooth_shots(): cur_f = lax.ppermute(cur_f, 'shots', fwd)  18.1 us
    all_to_all x1, waiting for transfers between devices, smooth_along_x(): cols = lax.all_to_all(both, 'slab', split_axis=2, concat_axis=1, tiled=True)  14.6 us
  transfers between devices with their start and end apart: 30, of which 15 were waited for; matrix products, arithmetic and copies ran while one was open for 5% of the time, Pallas kernels for 0%

profile of v9, /device:TPU:2, one launch (start us, length us, event | category | flops | bytes accessed | tf_op | source)
XLA Modules:
  0.0 215.7 jit_solution(7570086771804433138)
XLA Ops:
  0.8 1.5 constant_dynamic-slice_fusion.14
  2.3 0.3 copy-done.1
  2.7 1.5 constant_dynamic-slice_fusion.12
  4.2 3.1 %collective-permute-start.3 = (f32[3,4,32,256]{3,2,1,0:T(8,128)S(1)}, f32[3,4,32,256]{3,2,1,0:T(8,128)S(1)}, u32[]{:S(2)}, u32[]{:S(2)}) collective-permute-start(f32[3,4,32,256]{3,2,1,0:T(8,128)S(1)} %pad_maximum_fusion.2), channel_id=1, source_target_pairs={{0,96},{32,0},{64,32},{96,64},{128,224},{160,128},{192,160},{224,1... | collective-permute-start | bytes 1179656 | tf_op jit(solution)/shard_map/ppermute | solution.py:46
  7.5 8.2 %collective-permute-done.3 = f32[3,4,32,256]{3,2,1,0:T(8,128)S(1)} collective-permute-done((f32[3,4,32,256]{3,2,1,0:T(8,128)S(1)}, f32[3,4,32,256]{3,2,1,0:T(8,128)S(1)}, u32[]{:S(2)}, u32[]{:S(2)}) %collective-permute-start.3) | collective-permute-done | bytes 393248 | tf_op jit(solution)/shard_map/ppermute | solution.py:46
  15.8 3.8 %collective-permute-start.4 = (f32[3,4,32,256]{3,2,1,0:T(8,128)S(1)}, f32[3,4,32,256]{3,2,1,0:T(8,128)S(1)}, u32[]{:S(2)}, u32[]{:S(2)}) collective-permute-start(f32[3,4,32,256]{3,2,1,0:T(8,128)S(1)} %maximum_add_fusion.4), channel_id=1, source_target_pairs={{0,96},{32,0},{64,32},{96,64},{128,224},{160,128},{192,160},{224,1... | collective-permute-start | bytes 1179656 | tf_op jit(solution)/shard_map/ppermute | solution.py:46
  19.6 0.1 collective-permute-start.1
  19.7 7.3 %collective-permute-done.4 = f32[3,4,32,256]{3,2,1,0:T(8,128)S(1)} collective-permute-done((f32[3,4,32,256]{3,2,1,0:T(8,128)S(1)}, f32[3,4,32,256]{3,2,1,0:T(8,128)S(1)}, u32[]{:S(2)}, u32[]{:S(2)}) %collective-permute-start.4) | collective-permute-done | bytes 393248 | tf_op jit(solution)/shard_map/ppermute | solution.py:46
  27.1 3.8 %collective-permute-start.5 = (f32[3,4,32,256]{3,2,1,0:T(8,128)S(1)}, f32[3,4,32,256]{3,2,1,0:T(8,128)}, u32[]{:S(2)}, u32[]{:S(2)}) collective-permute-start(f32[3,4,32,256]{3,2,1,0:T(8,128)S(1)} %maximum_add_fusion.5), channel_id=1, source_target_pairs={{0,96},{32,0},{64,32},{96,64},{128,224},{160,128},{192,160},{224,1... | collective-permute-start | bytes 1179656 | tf_op jit(solution)/shard_map/ppermute | solution.py:46
  30.9 0.8 maximum_add_fusion.2
  31.7 5.8 %collective-permute-done.5 = f32[3,4,32,256]{3,2,1,0:T(8,128)} collective-permute-done((f32[3,4,32,256]{3,2,1,0:T(8,128)S(1)}, f32[3,4,32,256]{3,2,1,0:T(8,128)}, u32[]{:S(2)}, u32[]{:S(2)}) %collective-permute-start.5) | collective-permute-done | bytes 393248 | tf_op jit(solution)/shard_map/ppermute | solution.py:46
  37.5 1.1 maximum_add_fusion.6
  38.5 3.5 %collective-permute-done.2 = f32[3,4,32,256]{3,2,1,0:T(8,128)} collective-permute-done((f32[3,4,32,256]{3,2,1,0:T(8,128)}, f32[3,4,32,256]{3,2,1,0:T(8,128)}, u32[]{:S(2)}, u32[]{:S(2)}) %collective-permute-start.2) | collective-permute-done | bytes 393248 | tf_op jit(solution)/shard_map/ppermute | solution.py:45
  42.0 1.1 maximum_add_fusion.3
  43.2 0.1 dynamic-slice_bitcast_fusion.3
  43.3 1.4 copy-done.2
  44.7 0.1 dynamic-slice_bitcast_fusion.4
  44.8 0.5 copy-done.3
  45.3 0.1 dynamic-slice_bitcast_fusion.5
  45.5 0.1 collective-permute-start.6
  45.6 3.3 %collective-permute-start.7 = (f32[3,4,32,256]{3,2,1,0:T(8,128)S(1)}, f32[3,4,32,256]{3,2,1,0:T(8,128)S(1)}, u32[]{:S(2)}, u32[]{:S(2)}) collective-permute-start(f32[3,4,32,256]{3,2,1,0:T(8,128)S(1)} %pad_maximum_fusion.4), channel_id=1, source_target_pairs={{0,96},{32,0},{64,32},{96,64},{128,224},{160,128},{192,160},{224,1... | collective-permute-start | bytes 1179656 | tf_op jit(solution)/shard_map/ppermute | solution.py:46
  48.9 7.3 %collective-permute-start.8 = (f32[3,4,16,256]{3,2,1,0:T(8,128)S(1)}, f32[3,4,16,256]{3,2,1,0:T(8,128)S(1)}, u32[]{:S(2)}, u32[]{:S(2)}) collective-permute-start(f32[3,4,16,256]{3,2,1,0:T(8,128)S(1)} %slice.132), channel_id=1, source_target_pairs={{0,128},{32,160},{64,192},{96,224},{128,0},{160,32},{192,64},{224,... | collective-permute-start | bytes 589832 | tf_op jit(solution)/shard_map/ppermute | solution.py:63
  56.2 4.5 %collective-permute-done.8 = f32[3,4,16,256]{3,2,1,0:T(8,128)S(1)} collective-permute-done((f32[3,4,16,256]{3,2,1,0:T(8,128)S(1)}, f32[3,4,16,256]{3,2,1,0:T(8,128)S(1)}, u32[]{:S(2)}, u32[]{:S(2)}) %collective-permute-start.8) | collective-permute-done | bytes 196640 | tf_op jit(solution)/shard_map/ppermute | solution.py:63
  60.8 0.1 collective-permute-start.9
  60.9 3.3 %collective-permute-start.10 = (f32[3,4,32,256]{3,2,1,0:T(8,128)S(1)}, f32[3,4,32,256]{3,2,1,0:T(8,128)S(1)}, u32[]{:S(2)}, u32[]{:S(2)}) collective-permute-start(f32[3,4,32,256]{3,2,1,0:T(8,128)S(1)} %maximum_add_fusion.8), channel_id=1, source_target_pairs={{0,96},{32,0},{64,32},{96,64},{128,224},{160,128},{192,160},{224,1... | collective-permute-start | bytes 1179656 | tf_op jit(solution)/shard_map/ppermute | solution.py:46
  64.3 5.5 %collective-permute-start.11 = (f32[3,4,24,256]{3,2,1,0:T(8,128)S(1)}, f32[3,4,24,256]{3,2,1,0:T(8,128)S(1)}, u32[]{:S(2)}, u32[]{:S(2)}) collective-permute-start(f32[3,4,24,256]{3,2,1,0:T(8,128)S(1)} %get-tuple-element.95), channel_id=1, source_target_pairs={{0,128},{32,160},{64,192},{96,224},{128,0},{160,32},{192,64},{224,... | collective-permute-start | bytes 884744 | tf_op jit(solution)/shard_map/ppermute | solution.py:63
  69.8 7.8 %collective-permute-done.11 = f32[3,4,24,256]{3,2,1,0:T(8,128)S(1)} collective-permute-done((f32[3,4,24,256]{3,2,1,0:T(8,128)S(1)}, f32[3,4,24,256]{3,2,1,0:T(8,128)S(1)}, u32[]{:S(2)}, u32[]{:S(2)}) %collective-permute-start.11) | collective-permute-done | bytes 294944 | tf_op jit(solution)/shard_map/ppermute | solution.py:63
  77.8 3.3 %collective-permute-start.13 = (f32[3,4,32,256]{3,2,1,0:T(8,128)S(1)}, f32[3,4,32,256]{3,2,1,0:T(8,128)S(1)}, u32[]{:S(2)}, u32[]{:S(2)}) collective-permute-start(f32[3,4,32,256]{3,2,1,0:T(8,128)S(1)} %maximum_add_fusion.10), channel_id=1, source_target_pairs={{0,96},{32,0},{64,32},{96,64},{128,224},{160,128},{192,160},{224,1... | collective-permute-start | bytes 1179656 | tf_op jit(solution)/shard_map/ppermute | solution.py:46
  81.1 7.0 %collective-permute-start.14 = (f32[3,4,24,256]{3,2,1,0:T(8,128)S(1)}, f32[3,4,24,256]{3,2,1,0:T(8,128)S(1)}, u32[]{:S(2)}, u32[]{:S(2)}) collective-permute-start(f32[3,4,24,256]{3,2,1,0:T(8,128)S(1)} %get-tuple-element.94), channel_id=1, source_target_pairs={{0,128},{32,160},{64,192},{96,224},{128,0},{160,32},{192,64},{224,... | collective-permute-start | bytes 884744 | tf_op jit(solution)/shard_map/ppermute | solution.py:63
  88.1 0.2 fusion.26
  88.3 10.9 %collective-permute-done.14 = f32[3,4,24,256]{3,2,1,0:T(8,128)S(1)} collective-permute-done((f32[3,4,24,256]{3,2,1,0:T(8,128)S(1)}, f32[3,4,24,256]{3,2,1,0:T(8,128)S(1)}, u32[]{:S(2)}, u32[]{:S(2)}) %collective-permute-start.14) | collective-permute-done | bytes 294944 | tf_op jit(solution)/shard_map/ppermute | solution.py:63
  99.3 0.1 maximum_add_fusion
  99.5 0.7 fusion.15
  100.2 1.1 copy.13
  101.3 5.0 %all-to-all-start = ((f32[2,4,64,256]{3,1,0,2:T(4,128)}), f32[2,4,64,256]{3,1,0,2:T(4,128)S(1)}, u32[]{:S(2)}, u32[]{:S(2)}) async-start(f32[2,4,64,256]{3,1,0,2:T(4,128)} %copy.13), calls=%async_computation | async-start | bytes 1048576 | tf_op jit(solution)/shard_map/all_to_all | solution.py:106
  106.3 0.1 fusion.69
  106.4 14.6 %all-to-all-done = f32[2,4,64,256]{3,1,0,2:T(4,128)S(1)} async-done(((f32[2,4,64,256]{3,1,0,2:T(4,128)}), f32[2,4,64,256]{3,1,0,2:T(4,128)S(1)}, u32[]{:S(2)}, u32[]{:S(2)}) %all-to-all-start) | async-done | bytes 524320 | tf_op jit(solution)/shard_map/all_to_all | solution.py:106
  121.0 0.3 copy.14
  121.3 1.0 convolution_bitcast_fusion
  122.3 1.0 copy.16
  123.3 5.9 %all-to-all-start.1 = ((f32[2,128,2,256]{3,2,0,1:T(2,128)}), f32[2,128,2,256]{3,2,0,1:T(2,128)S(1)}, u32[]{:S(2)}, u32[]{:S(2)}) async-start(f32[2,128,2,256]{3,2,0,1:T(2,128)} %copy.16), calls=%async_computation.1 | async-start | bytes 1048576 | tf_op jit(solution)/shard_map/all_to_all | solution.py:109
  129.2 0.5 fusion.14
  129.7 0.4 fusion.13
  130.1 2.6 %constant_dynamic-slice_fusion.24 = (f32[512,32]{1,0:T(8,128)S(1)}, f32[512,32]{1,0:T(8,128)S(1)}, f32[512,32]{1,0:T(8,128)S(1)}, f32[512,32]{1,0:T(8,128)S(1)},...) fusion(f32[512,512]{1,0:T(8,128)S(1)} %fusion.13, ...), kind=kLoop, calls=%fused_computation.178 | loop fusion | bytes 2097216 | tf_op jit(solution)/shard_map/dynamic_slice | solution.py:90
  132.7 3.3 %concatenate.18 = f32[512,512]{1,0:T(8,128)S(1)} concatenate(f32[512,32]{1,0:T(8,128)} %get-tuple-element.91, f32[512,32]{1,0:T(8,128)} %get-tuple-element.90, f32[512,32]{1,0:T(8,128)} %get-tuple-element.89, f32[512,32]{1,0:T(8,128)} %get-tuple-element.88, f32[512,32]{1,0:T(8,128)} %get-tuple-element.87, f32[512,32]{1,0:T(8,128)} %get-tuple-element.86, ...), dimensions={1} | concatenate | bytes 2097152 | tf_op jit(solution)/shard_map/concatenate | solution.py:89
  136.1 0.2 convolution_bitcast_fusion.1
  136.3 7.6 %all-to-all-done.1 = f32[2,128,2,256]{3,2,0,1:T(2,128)S(1)} async-done(((f32[2,128,2,256]{3,2,0,1:T(2,128)}), f32[2,128,2,256]{3,2,0,1:T(2,128)S(1)}, u32[]{:S(2)}, u32[]{:S(2)}) %all-to-all-start.1) | async-done | bytes 524320 | tf_op jit(solution)/shard_map/all_to_all | solution.py:109
  143.9 0.2 copy.18
  144.1 0.4 all_to_all.33
  144.6 3.2 %collective-permute-start.16 = (f32[2,4,32,256]{3,2,1,0:T(8,128)S(1)}, f32[2,4,32,256]{3,2,1,0:T(8,128)S(1)}, u32[]{:S(2)}, u32[]{:S(2)}) collective-permute-start(f32[2,4,32,256]{3,2,1,0:T(8,128)S(1)} %get-tuple-element.106), channel_id=1, source_target_pairs={{0,96},{32,0},{64,32},{96,64},{128,224},{160,128},{192,160},{224,1... | collective-permute-start | bytes 786440 | tf_op jit(solution)/shard_map/ppermute | solution.py:85
  147.8 4.2 %collective-permute-start.21 = (f32[2,4,64,256]{3,2,1,0:T(8,128)S(1)}, f32[2,4,64,256]{3,2,1,0:T(8,128)S(1)}, u32[]{:S(2)}, u32[]{:S(2)}) collective-permute-start(f32[2,4,64,256]{3,2,1,0:T(8,128)S(1)} %all_to_all.33), channel_id=1, source_target_pairs={{0,128},{32,160},{64,192},{96,224},{128,0},{160,32},{192,64},{224,... | collective-permute-start | bytes 1572872 | tf_op jit(solution)/shard_map/ppermute | solution.py:77
  152.0 2.9 %collective-permute-done.15 = f32[2,4,32,256]{3,2,1,0:T(8,128)S(1)} collective-permute-done((f32[2,4,32,256]{3,2,1,0:T(8,128)S(1)}, f32[2,4,32,256]{3,2,1,0:T(8,128)S(1)}, u32[]{:S(2)}, u32[]{:S(2)}) %collective-permute-start.15) | collective-permute-done | bytes 262176 | tf_op jit(solution)/shard_map/ppermute | solution.py:84
  154.9 3.2 %collective-permute-start.18 = (f32[2,4,32,256]{3,2,1,0:T(8,128)S(1)}, f32[2,4,32,256]{3,2,1,0:T(8,128)S(1)}, u32[]{:S(2)}, u32[]{:S(2)}) collective-permute-start(f32[2,4,32,256]{3,2,1,0:T(8,128)S(1)} %collective-permute-done.16), channel_id=1, source_target_pairs={{0,96},{32,0},{64,32},{96,64},{128,224},{160,128},{192,160},{224,1... | collective-permute-start | bytes 786440 | tf_op jit(solution)/shard_map/ppermute | solution.py:85
  158.2 19.1 %collective-permute-done.21 = f32[2,4,64,256]{3,2,1,0:T(8,128)S(1)} collective-permute-done((f32[2,4,64,256]{3,2,1,0:T(8,128)S(1)}, f32[2,4,64,256]{3,2,1,0:T(8,128)S(1)}, u32[]{:S(2)}, u32[]{:S(2)}) %collective-permute-start.21) | collective-permute-done | bytes 524320 | tf_op jit(solution)/shard_map/ppermute | solution.py:77
  177.5 3.2 %collective-permute-start.23 = (f32[2,4,32,256]{3,2,1,0:T(8,128)S(1)}, f32[2,4,32,256]{3,2,1,0:T(8,128)S(1)}, u32[]{:S(2)}, u32[]{:S(2)}) collective-permute-start(f32[2,4,32,256]{3,2,1,0:T(8,128)S(1)} %get-tuple-element.104), channel_id=1, source_target_pairs={{0,96},{32,0},{64,32},{96,64},{128,224},{160,128},{192,160},{224,1... | collective-permute-start | bytes 786440 | tf_op jit(solution)/shard_map/ppermute | solution.py:85
  180.7 3.2 %collective-permute-start.20 = (f32[2,4,32,256]{3,2,1,0:T(8,128)S(1)}, f32[2,4,32,256]{3,2,1,0:T(8,128)S(1)}, u32[]{:S(2)}, u32[]{:S(2)}) collective-permute-start(f32[2,4,32,256]{3,2,1,0:T(8,128)S(1)} %collective-permute-done.18), channel_id=1, source_target_pairs={{0,96},{32,0},{64,32},{96,64},{128,224},{160,128},{192,160},{224,1... | collective-permute-start | bytes 786440 | tf_op jit(solution)/shard_map/ppermute | solution.py:85
  184.0 3.9 %collective-permute-done.22 = f32[2,4,32,256]{3,2,1,0:T(8,128)S(1)} collective-permute-done((f32[2,4,32,256]{3,2,1,0:T(8,128)S(1)}, f32[2,4,32,256]{3,2,1,0:T(8,128)S(1)}, u32[]{:S(2)}, u32[]{:S(2)}) %collective-permute-start.22) | collective-permute-done | bytes 262176 | tf_op jit(solution)/shard_map/ppermute | solution.py:84
  187.9 3.2 %collective-permute-start.25 = (f32[2,4,32,256]{3,2,1,0:T(8,128)S(1)}, f32[2,4,32,256]{3,2,1,0:T(8,128)S(1)}, u32[]{:S(2)}, u32[]{:S(2)}) collective-permute-start(f32[2,4,32,256]{3,2,1,0:T(8,128)S(1)} %collective-permute-done.23), channel_id=1, source_target_pairs={{0,96},{32,0},{64,32},{96,64},{128,224},{160,128},{192,160},{224,1... | collective-permute-start | bytes 786440 | tf_op jit(solution)/shard_map/ppermute | solution.py:85
  191.2 2.4 %collective-permute-done.19 = f32[2,4,32,256]{3,2,1,0:T(8,128)S(1)} collective-permute-done((f32[2,4,32,256]{3,2,1,0:T(8,128)S(1)}, f32[2,4,32,256]{3,2,1,0:T(8,128)S(1)}, u32[]{:S(2)}, u32[]{:S(2)}) %collective-permute-start.19) | collective-permute-done | bytes 262176 | tf_op jit(solution)/shard_map/ppermute | solution.py:84
  193.7 4.0 %collective-permute-done.24 = f32[2,4,32,256]{3,2,1,0:T(8,128)S(1)} collective-permute-done((f32[2,4,32,256]{3,2,1,0:T(8,128)S(1)}, f32[2,4,32,256]{3,2,1,0:T(8,128)S(1)}, u32[]{:S(2)}, u32[]{:S(2)}) %collective-permute-start.24) | collective-permute-done | bytes 262176 | tf_op jit(solution)/shard_map/ppermute | solution.py:84
  197.7 3.2 %collective-permute-start.27 = (f32[2,4,32,256]{3,2,1,0:T(8,128)S(1)}, f32[2,4,32,256]{3,2,1,0:T(8,128)S(1)}, u32[]{:S(2)}, u32[]{:S(2)}) collective-permute-start(f32[2,4,32,256]{3,2,1,0:T(8,128)S(1)} %collective-permute-done.25), channel_id=1, source_target_pairs={{0,96},{32,0},{64,32},{96,64},{128,224},{160,128},{192,160},{224,1... | collective-permute-start | bytes 786440 | tf_op jit(solution)/shard_map/ppermute | solution.py:85
  201.0 4.8 %collective-permute-done.26 = f32[2,4,32,256]{3,2,1,0:T(8,128)S(1)} collective-permute-done((f32[2,4,32,256]{3,2,1,0:T(8,128)S(1)}, f32[2,4,32,256]{3,2,1,0:T(8,128)S(1)}, u32[]{:S(2)}, u32[]{:S(2)}) %collective-permute-start.26) | collective-permute-done | bytes 262176 | tf_op jit(solution)/shard_map/ppermute | solution.py:84
  205.9 4.9 %fusion.4 = f32[4,512,256]{2,1,0:T(8,128)} fusion(f32[4,512,256]{2,1,0:T(8,128)S(1)} %get-tuple-element.109, f32[512,512]{1,0:T(8,128)S(1)} %concatenate.18, f32[256]{0:T(256)S(1)} %bitcast.212), kind=kOutput, calls=%fused_computation.4 | convolution fusion | flops 3221749760 | bytes 5243904 | tf_op jit(solution)/shard_map/xij,xjz->xiz/dot_general | solution.py:96
  210.8 4.9 %fusion.7 = f32[4,512,256]{2,1,0:T(8,128)} fusion(f32[4,512,256]{2,1,0:T(8,128)S(1)} %get-tuple-element.108, f32[512,512]{1,0:T(8,128)S(1)} %concatenate.18, f32[256]{0:T(256)S(1)} %bitcast.211), kind=kOutput, calls=%fused_computation.5 | convolution fusion | flops 3221749760 | bytes 5243904 | tf_op jit(solution)/shard_map/xij,xjz->xiz/dot_general | solution.py:96
  (67 shorter events, 1.6 us)
Async XLA Ops:
  0.6 135.4 %copy-start = (f32[2,16]{1,0:T(2,128)S(1)}, f32[2,16]{1,0:T(2,128)}, u32[]{:S(2)}) copy-start(f32[2,16]{1,0:T(2,128)} %param.9) | copy-start | bytes 388
  0.6 2.0 copy-start.1
  4.2 11.5 %collective-permute-start.3 = (f32[3,4,32,256]{3,2,1,0:T(8,128)S(1)}, f32[3,4,32,256]{3,2,1,0:T(8,128)S(1)}, u32[]{:S(2)}, u32[]{:S(2)}) collective-permute-start(f32[3,4,32,256]{3,2,1,0:T(8,128)S(1)} %pad_maximum_fusion.2), channel_id=1, source_target_pairs={{0,96},{32,0},{64,32},{96,64},{128,224},{160,128},{192,160},{224,1... | collective-permute-start | bytes 1179656 | tf_op jit(solution)/shard_map/ppermute | solution.py:46
  7.4 12.2 %collective-permute-start = (f32[3,4,32,256]{3,2,1,0:T(8,128)S(1)}, f32[3,4,32,256]{3,2,1,0:T(8,128)S(1)}, u32[]{:S(2)}, u32[]{:S(2)}) collective-permute-start(f32[3,4,32,256]{3,2,1,0:T(8,128)S(1)} %pad_maximum_fusion.1), channel_id=1, source_target_pairs={{0,32},{32,64},{64,96},{96,0},{128,160},{160,192},{192,224},{224,1... | collective-permute-start | bytes 1179656 | tf_op jit(solution)/shard_map/ppermute | solution.py:45
  15.8 11.3 %collective-permute-start.4 = (f32[3,4,32,256]{3,2,1,0:T(8,128)S(1)}, f32[3,4,32,256]{3,2,1,0:T(8,128)S(1)}, u32[]{:S(2)}, u32[]{:S(2)}) collective-permute-start(f32[3,4,32,256]{3,2,1,0:T(8,128)S(1)} %maximum_add_fusion.4), channel_id=1, source_target_pairs={{0,96},{32,0},{64,32},{96,64},{128,224},{160,128},{192,160},{224,1... | collective-permute-start | bytes 1179656 | tf_op jit(solution)/shard_map/ppermute | solution.py:46
  19.6 11.3 %collective-permute-start.1 = (f32[3,4,32,256]{3,2,1,0:T(8,128)S(1)}, f32[3,4,32,256]{3,2,1,0:T(8,128)S(1)}, u32[]{:S(2)}, u32[]{:S(2)}) collective-permute-start(f32[3,4,32,256]{3,2,1,0:T(8,128)S(1)} %maximum_add_fusion.1), channel_id=1, source_target_pairs={{0,32},{32,64},{64,96},{96,0},{128,160},{160,192},{192,224},{224,1... | collective-permute-start | bytes 1179656 | tf_op jit(solution)/shard_map/ppermute | solution.py:45
  27.1 10.3 %collective-permute-start.5 = (f32[3,4,32,256]{3,2,1,0:T(8,128)S(1)}, f32[3,4,32,256]{3,2,1,0:T(8,128)}, u32[]{:S(2)}, u32[]{:S(2)}) collective-permute-start(f32[3,4,32,256]{3,2,1,0:T(8,128)S(1)} %maximum_add_fusion.5), channel_id=1, source_target_pairs={{0,96},{32,0},{64,32},{96,64},{128,224},{160,128},{192,160},{224,1... | collective-permute-start | bytes 1179656 | tf_op jit(solution)/shard_map/ppermute | solution.py:46
  31.7 10.3 %collective-permute-start.2 = (f32[3,4,32,256]{3,2,1,0:T(8,128)}, f32[3,4,32,256]{3,2,1,0:T(8,128)}, u32[]{:S(2)}, u32[]{:S(2)}) collective-permute-start(f32[3,4,32,256]{3,2,1,0:T(8,128)} %maximum_add_fusion.2), channel_id=1, source_target_pairs={{0,32},{32,64},{64,96},{96,0},{128,160},{160,192},{192,224},{224,1... | collective-permute-start | bytes 1179656 | tf_op jit(solution)/shard_map/ppermute | solution.py:45
  43.1 1.6 copy-start.2
  43.1 2.2 %copy-start.3 = (f32[1,4,512,256]{3,2,1,0:T(8,128)S(1)}, f32[1,4,512,256]{3,2,1,0:T(8,128)}, u32[]{:S(2)}) copy-start(f32[1,4,512,256]{3,2,1,0:T(8,128)} %param.7) | copy-start | bytes 6291460
  45.5 15.2 %collective-permute-start.6 = (f32[3,4,32,256]{3,2,1,0:T(8,128)S(1)}, f32[3,4,32,256]{3,2,1,0:T(8,128)S(1)}, u32[]{:S(2)}, u32[]{:S(2)}) collective-permute-start(f32[3,4,32,256]{3,2,1,0:T(8,128)S(1)} %pad_maximum_fusion.3), channel_id=1, source_target_pairs={{0,32},{32,64},{64,96},{96,0},{128,160},{160,192},{192,224},{224,1... | collective-permute-start | bytes 1179656 | tf_op jit(solution)/shard_map/ppermute | solution.py:45
  45.6 15.1 %collective-permute-start.7 = (f32[3,4,32,256]{3,2,1,0:T(8,128)S(1)}, f32[3,4,32,256]{3,2,1,0:T(8,128)S(1)}, u32[]{:S(2)}, u32[]{:S(2)}) collective-permute-start(f32[3,4,32,256]{3,2,1,0:T(8,128)S(1)} %pad_maximum_fusion.4), channel_id=1, source_target_pairs={{0,96},{32,0},{64,32},{96,64},{128,224},{160,128},{192,160},{224,1... | collective-permute-start | bytes 1179656 | tf_op jit(solution)/shard_map/ppermute | solution.py:46
  48.9 11.8 %collective-permute-start.8 = (f32[3,4,16,256]{3,2,1,0:T(8,128)S(1)}, f32[3,4,16,256]{3,2,1,0:T(8,128)S(1)}, u32[]{:S(2)}, u32[]{:S(2)}) collective-permute-start(f32[3,4,16,256]{3,2,1,0:T(8,128)S(1)} %slice.132), channel_id=1, source_target_pairs={{0,128},{32,160},{64,192},{96,224},{128,0},{160,32},{192,64},{224,... | collective-permute-start | bytes 589832 | tf_op jit(solution)/shard_map/ppermute | solution.py:63
  60.8 16.8 %collective-permute-start.9 = (f32[3,4,32,256]{3,2,1,0:T(8,128)S(1)}, f32[3,4,32,256]{3,2,1,0:T(8,128)S(1)}, u32[]{:S(2)}, u32[]{:S(2)}) collective-permute-start(f32[3,4,32,256]{3,2,1,0:T(8,128)S(1)} %maximum_add_fusion.7), channel_id=1, source_target_pairs={{0,32},{32,64},{64,96},{96,0},{128,160},{160,192},{192,224},{224,1... | collective-permute-start | bytes 1179656 | tf_op jit(solution)/shard_map/ppermute | solution.py:45
  60.9 16.7 %collective-permute-start.10 = (f32[3,4,32,256]{3,2,1,0:T(8,128)S(1)}, f32[3,4,32,256]{3,2,1,0:T(8,128)S(1)}, u32[]{:S(2)}, u32[]{:S(2)}) collective-permute-start(f32[3,4,32,256]{3,2,1,0:T(8,128)S(1)} %maximum_add_fusion.8), channel_id=1, source_target_pairs={{0,96},{32,0},{64,32},{96,64},{128,224},{160,128},{192,160},{224,1... | collective-permute-start | bytes 1179656 | tf_op jit(solution)/shard_map/ppermute | solution.py:46
  64.3 13.3 %collective-permute-start.11 = (f32[3,4,24,256]{3,2,1,0:T(8,128)S(1)}, f32[3,4,24,256]{3,2,1,0:T(8,128)S(1)}, u32[]{:S(2)}, u32[]{:S(2)}) collective-permute-start(f32[3,4,24,256]{3,2,1,0:T(8,128)S(1)} %get-tuple-element.95), channel_id=1, source_target_pairs={{0,128},{32,160},{64,192},{96,224},{128,0},{160,32},{192,64},{224,... | collective-permute-start | bytes 884744 | tf_op jit(solution)/shard_map/ppermute | solution.py:63
  77.6 21.5 %collective-permute-start.12 = (f32[3,4,32,256]{3,2,1,0:T(8,128)S(1)}, f32[3,4,32,256]{3,2,1,0:T(8,128)S(1)}, u32[]{:S(2)}, u32[]{:S(2)}) collective-permute-start(f32[3,4,32,256]{3,2,1,0:T(8,128)S(1)} %maximum_add_fusion.9), channel_id=1, source_target_pairs={{0,32},{32,64},{64,96},{96,0},{128,160},{160,192},{192,224},{224,1... | collective-permute-start | bytes 1179656 | tf_op jit(solution)/shard_map/ppermute | solution.py:45
  77.8 21.4 %collective-permute-start.13 = (f32[3,4,32,256]{3,2,1,0:T(8,128)S(1)}, f32[3,4,32,256]{3,2,1,0:T(8,128)S(1)}, u32[]{:S(2)}, u32[]{:S(2)}) collective-permute-start(f32[3,4,32,256]{3,2,1,0:T(8,128)S(1)} %maximum_add_fusion.10), channel_id=1, source_target_pairs={{0,96},{32,0},{64,32},{96,64},{128,224},{160,128},{192,160},{224,1... | collective-permute-start | bytes 1179656 | tf_op jit(solution)/shard_map/ppermute | solution.py:46
  81.1 18.1 %collective-permute-start.14 = (f32[3,4,24,256]{3,2,1,0:T(8,128)S(1)}, f32[3,4,24,256]{3,2,1,0:T(8,128)S(1)}, u32[]{:S(2)}, u32[]{:S(2)}) collective-permute-start(f32[3,4,24,256]{3,2,1,0:T(8,128)S(1)} %get-tuple-element.94), channel_id=1, source_target_pairs={{0,128},{32,160},{64,192},{96,224},{128,0},{160,32},{192,64},{224,... | collective-permute-start | bytes 884744 | tf_op jit(solution)/shard_map/ppermute | solution.py:63
  101.3 19.7 %all-to-all-start = ((f32[2,4,64,256]{3,1,0,2:T(4,128)}), f32[2,4,64,256]{3,1,0,2:T(4,128)S(1)}, u32[]{:S(2)}, u32[]{:S(2)}) async-start(f32[2,4,64,256]{3,1,0,2:T(4,128)} %copy.13), calls=%async_computation | async-start | bytes 1048576 | tf_op jit(solution)/shard_map/all_to_all | solution.py:106
  123.3 20.6 %all-to-all-start.1 = ((f32[2,128,2,256]{3,2,0,1:T(2,128)}), f32[2,128,2,256]{3,2,0,1:T(2,128)S(1)}, u32[]{:S(2)}, u32[]{:S(2)}) async-start(f32[2,128,2,256]{3,2,0,1:T(2,128)} %copy.16), calls=%async_computation.1 | async-start | bytes 1048576 | tf_op jit(solution)/shard_map/all_to_all | solution.py:109
  132.7 3.4 %copy-start.4 = (s32[256]{0:T(256)S(1)}, s32[256]{0:T(256)}, u32[]{:S(2)}) copy-start(s32[256]{0:T(256)} %param.8) | copy-start | bytes 3076
  144.5 10.4 %collective-permute-start.15 = (f32[2,4,32,256]{3,2,1,0:T(8,128)S(1)}, f32[2,4,32,256]{3,2,1,0:T(8,128)S(1)}, u32[]{:S(2)}, u32[]{:S(2)}) collective-permute-start(f32[2,4,32,256]{3,2,1,0:T(8,128)S(1)} %get-tuple-element.107), channel_id=1, source_target_pairs={{0,32},{32,64},{64,96},{96,0},{128,160},{160,192},{192,224},{224,1... | collective-permute-start | bytes 786440 | tf_op jit(solution)/shard_map/ppermute | solution.py:84
  144.6 10.4 %collective-permute-start.16 = (f32[2,4,32,256]{3,2,1,0:T(8,128)S(1)}, f32[2,4,32,256]{3,2,1,0:T(8,128)S(1)}, u32[]{:S(2)}, u32[]{:S(2)}) collective-permute-start(f32[2,4,32,256]{3,2,1,0:T(8,128)S(1)} %get-tuple-element.106), channel_id=1, source_target_pairs={{0,96},{32,0},{64,32},{96,64},{128,224},{160,128},{192,160},{224,1... | collective-permute-start | bytes 786440 | tf_op jit(solution)/shard_map/ppermute | solution.py:85
  147.8 29.5 %collective-permute-start.21 = (f32[2,4,64,256]{3,2,1,0:T(8,128)S(1)}, f32[2,4,64,256]{3,2,1,0:T(8,128)S(1)}, u32[]{:S(2)}, u32[]{:S(2)}) collective-permute-start(f32[2,4,64,256]{3,2,1,0:T(8,128)S(1)} %all_to_all.33), channel_id=1, source_target_pairs={{0,128},{32,160},{64,192},{96,224},{128,0},{160,32},{192,64},{224,... | collective-permute-start | bytes 1572872 | tf_op jit(solution)/shard_map/ppermute | solution.py:77
  154.9 25.8 %collective-permute-start.17 = (f32[2,4,32,256]{3,2,1,0:T(8,128)S(1)}, f32[2,4,32,256]{3,2,1,0:T(8,128)S(1)}, u32[]{:S(2)}, u32[]{:S(2)}) collective-permute-start(f32[2,4,32,256]{3,2,1,0:T(8,128)S(1)} %collective-permute-done.15), channel_id=1, source_target_pairs={{0,32},{32,64},{64,96},{96,0},{128,160},{160,192},{192,224},{224,1... | collective-permute-start | bytes 786440 | tf_op jit(solution)/shard_map/ppermute | solution.py:84
  154.9 25.8 %collective-permute-start.18 = (f32[2,4,32,256]{3,2,1,0:T(8,128)S(1)}, f32[2,4,32,256]{3,2,1,0:T(8,128)S(1)}, u32[]{:S(2)}, u32[]{:S(2)}) collective-permute-start(f32[2,4,32,256]{3,2,1,0:T(8,128)S(1)} %collective-permute-done.16), channel_id=1, source_target_pairs={{0,96},{32,0},{64,32},{96,64},{128,224},{160,128},{192,160},{224,1... | collective-permute-start | bytes 786440 | tf_op jit(solution)/shard_map/ppermute | solution.py:85
  177.4 10.5 %collective-permute-start.22 = (f32[2,4,32,256]{3,2,1,0:T(8,128)S(1)}, f32[2,4,32,256]{3,2,1,0:T(8,128)S(1)}, u32[]{:S(2)}, u32[]{:S(2)}) collective-permute-start(f32[2,4,32,256]{3,2,1,0:T(8,128)S(1)} %get-tuple-element.105), channel_id=1, source_target_pairs={{0,32},{32,64},{64,96},{96,0},{128,160},{160,192},{192,224},{224,1... | collective-permute-start | bytes 786440 | tf_op jit(solution)/shard_map/ppermute | solution.py:84
  177.5 10.4 %collective-permute-start.23 = (f32[2,4,32,256]{3,2,1,0:T(8,128)S(1)}, f32[2,4,32,256]{3,2,1,0:T(8,128)S(1)}, u32[]{:S(2)}, u32[]{:S(2)}) collective-permute-start(f32[2,4,32,256]{3,2,1,0:T(8,128)S(1)} %get-tuple-element.104), channel_id=1, source_target_pairs={{0,96},{32,0},{64,32},{96,64},{128,224},{160,128},{192,160},{224,1... | collective-permute-start | bytes 786440 | tf_op jit(solution)/shard_map/ppermute | solution.py:85
  180.7 12.8 %collective-permute-start.19 = (f32[2,4,32,256]{3,2,1,0:T(8,128)S(1)}, f32[2,4,32,256]{3,2,1,0:T(8,128)S(1)}, u32[]{:S(2)}, u32[]{:S(2)}) collective-permute-start(f32[2,4,32,256]{3,2,1,0:T(8,128)S(1)} %collective-permute-done.17), channel_id=1, source_target_pairs={{0,32},{32,64},{64,96},{96,0},{128,160},{160,192},{192,224},{224,1... | collective-permute-start | bytes 786440 | tf_op jit(solution)/shard_map/ppermute | solution.py:84
  180.7 12.8 %collective-permute-start.20 = (f32[2,4,32,256]{3,2,1,0:T(8,128)S(1)}, f32[2,4,32,256]{3,2,1,0:T(8,128)S(1)}, u32[]{:S(2)}, u32[]{:S(2)}) collective-permute-start(f32[2,4,32,256]{3,2,1,0:T(8,128)S(1)} %collective-permute-done.18), channel_id=1, source_target_pairs={{0,96},{32,0},{64,32},{96,64},{128,224},{160,128},{192,160},{224,1... | collective-permute-start | bytes 786440 | tf_op jit(solution)/shard_map/ppermute | solution.py:85
  187.9 9.8 %collective-permute-start.24 = (f32[2,4,32,256]{3,2,1,0:T(8,128)S(1)}, f32[2,4,32,256]{3,2,1,0:T(8,128)S(1)}, u32[]{:S(2)}, u32[]{:S(2)}) collective-permute-start(f32[2,4,32,256]{3,2,1,0:T(8,128)S(1)} %collective-permute-done.22), channel_id=1, source_target_pairs={{0,32},{32,64},{64,96},{96,0},{128,160},{160,192},{192,224},{224,1... | collective-permute-start | bytes 786440 | tf_op jit(solution)/shard_map/ppermute | solution.py:84
  187.9 9.8 %collective-permute-start.25 = (f32[2,4,32,256]{3,2,1,0:T(8,128)S(1)}, f32[2,4,32,256]{3,2,1,0:T(8,128)S(1)}, u32[]{:S(2)}, u32[]{:S(2)}) collective-permute-start(f32[2,4,32,256]{3,2,1,0:T(8,128)S(1)} %collective-permute-done.23), channel_id=1, source_target_pairs={{0,96},{32,0},{64,32},{96,64},{128,224},{160,128},{192,160},{224,1... | collective-permute-start | bytes 786440 | tf_op jit(solution)/shard_map/ppermute | solution.py:85
  197.7 8.1 %collective-permute-start.26 = (f32[2,4,32,256]{3,2,1,0:T(8,128)S(1)}, f32[2,4,32,256]{3,2,1,0:T(8,128)S(1)}, u32[]{:S(2)}, u32[]{:S(2)}) collective-permute-start(f32[2,4,32,256]{3,2,1,0:T(8,128)S(1)} %collective-permute-done.24), channel_id=1, source_target_pairs={{0,32},{32,64},{64,96},{96,0},{128,160},{160,192},{192,224},{224,1... | collective-permute-start | bytes 786440 | tf_op jit(solution)/shard_map/ppermute | solution.py:84
  197.7 8.1 %collective-permute-start.27 = (f32[2,4,32,256]{3,2,1,0:T(8,128)S(1)}, f32[2,4,32,256]{3,2,1,0:T(8,128)S(1)}, u32[]{:S(2)}, u32[]{:S(2)}) collective-permute-start(f32[2,4,32,256]{3,2,1,0:T(8,128)S(1)} %collective-permute-done.25), channel_id=1, source_target_pairs={{0,96},{32,0},{64,32},{96,64},{128,224},{160,128},{192,160},{224,1... | collective-permute-start | bytes 786440 | tf_op jit(solution)/shard_map/ppermute | solution.py:85
